TPU v7x, 512 devices: a whole 4x4x16 slice. The times are simulated.
512 devices in a mesh: mx: 32 (over z, core), my: 4 (over y), layer: 4 (over x).
Axes of the slice: x: 4, y: 4, z: 16, core: 2. Of those that a mesh axis runs over, the one named last changes fastest.
Arguments:
- ssa_velocity: float32 [2, 2048, 1024], P(None, 'mx', 'my'), may hold values from -6 to 6
- shelf_viscosity: float32 [2048, 1024], P('mx', 'my'), may hold values from 0.3 to 3
- basal_friction: float32 [2048, 1024], P('mx', 'my'), may hold values from 0.1 to 3
- driving_stress: float32 [2, 2048, 1024], P(None, 'mx', 'my'), may hold values from -6 to 6
- stokes_velocity: float32 [3, 12, 512, 1024], P(None, 'layer', 'mx', 'my'), may hold values from -6 to 6
- ice_viscosity: float32 [12, 512, 1024], P('layer', 'mx', 'my'), may hold values from 0.3 to 3
- body_force: float32 [3, 12, 512, 1024], P(None, 'layer', 'mx', 'my'), may hold values from -6 to 6
- diagonals: int32 [512, 1024], P('mx', 'my'), may hold values 0 or 1
- element_matrix: float32 [18, 18], replicated, may hold values from -0.1 to 1.5, as said below
- iface_columns: int32 [128, 9, 128], P(('mx', 'my')), may hold values from -1 to 4095, as said below
- iface_nodes: int32 [128, 9, 128], P(('mx', 'my')), may hold values from -1 to 16383, as said below
Outputs:
- coupled_residual: float32 [2, 2048, 1024], P(None, 'mx', 'my')
- stokes_residual: float32 [3, 12, 512, 1024], P(None, 'layer', 'mx', 'my')
Inputs may be any that keep to these rules, and one draw needn't show every extreme that they name: `iface_columns`: slots toward blocks outside the map are empty; in each block and direction the live slots come first; all 128 slots toward a block's own direction (d = 4) are live; the live columns of one block are distinct. `iface_nodes`: slot (o, d, k) is live exactly where its partner slot (s, 8 - d, k) of iface_columns is live, s the block at offset d from o, and then names a node of o's 64 x 256 block (row-major). `element_matrix`: the diagonal dominates each row.
All inputs are finite; a program needn't handle non-finite values. No bound on the sum of `diagonals` on one device may be relied on, other than what follows from the above.
Results may differ from a plain program's by a relative error of at most 0.0001.
Values sent between devices are 32-bit elements; how exact they have to be, the bound alone decides.
No kernel may reach another device: no remote copies, remote signals or barrier semaphores. Data moves between devices by JAX's collectives and lax.ppermute only.
A program may use at most 64 MiB of HBM per device.

v0:
```python
import jax
import jax.numpy as jnp
from jax import lax
from jax.sharding import PartitionSpec as P


def with_halo(array, sides, width):
    for axis, dim in sides:
        devices, length = (lax.axis_size(axis), array.shape[dim])
        up = [(i, (i + 1) % devices) for i in range(devices - 1)]
        down = [(j, i) for i, j in up]
        last = lax.slice_in_dim(array, length - width, length, axis=dim)
        initial = lax.slice_in_dim(array, 0, width, axis=dim)
        before = lax.ppermute(last, axis, up)
        after = lax.ppermute(initial, axis, down)
        array = jnp.concatenate([before, array, after], axis=dim)
    return array


def cell_dx(plane):
    return 0.5 * (plane[1:, :-1] + plane[1:, 1:] - (plane[:-1, :-1] + plane[:-1, 1:]))


def cell_dy(plane):
    return 0.5 * (plane[:-1, 1:] + plane[1:, 1:] - (plane[:-1, :-1] + plane[1:, :-1]))


def shelf_residual(padded, friction, driving):
    u_field = padded[0]
    v_field = padded[1]
    h_field = padded[2]
    du_dx = cell_dx(u_field)
    du_dy = cell_dy(u_field)
    dv_dx = cell_dx(v_field)
    dv_dy = cell_dy(v_field)
    h_cell = 0.25 * (h_field[1:, :-1] + h_field[1:, 1:] + h_field[:-1, :-1] + h_field[:-1, 1:])
    tau_xx = h_cell * (4.0 * du_dx + 2.0 * dv_dy)
    tau_yy = h_cell * (4.0 * dv_dy + 2.0 * du_dx)
    tau_xy = h_cell * (du_dy + dv_dx)
    res_x = cell_dx(tau_xx) + cell_dy(tau_xy) - friction * u_field[1:-1, 1:-1] - driving[0]
    res_y = cell_dy(tau_yy) + cell_dx(tau_xy) - friction * v_field[1:-1, 1:-1] - driving[1]
    return jnp.stack([res_x, res_y])


def triangle(stiffness, lows, ups, weight):
    values = jnp.stack(
        [plane[comp] for group in (lows, ups) for comp in range(3) for plane in group]
    )
    viscous = (
        (lows[0][3] + lows[1][3] + lows[2][3] + ups[0][3] + ups[1][3] + ups[2][3]) / 6.0 * weight
    )
    response = (
        jnp.einsum("ab,bxy->axy", stiffness, values, precision=lax.Precision.HIGHEST) * viscous
    )
    return response.reshape((2, 3, 3) + response.shape[1:])


def cell_terms(lower, upper, flag_cells, stiffness, weight):
    low_a, low_b, low_c, low_d = (
        lower[:, :-1, :-1],
        lower[:, 1:, :-1],
        lower[:, :-1, 1:],
        lower[:, 1:, 1:],
    )
    up_a, up_b, up_c, up_d = (
        upper[:, :-1, :-1],
        upper[:, 1:, :-1],
        upper[:, :-1, 1:],
        upper[:, 1:, 1:],
    )
    main_diag = (flag_cells == 0)[None]
    low_far = jnp.where(main_diag, low_d, low_c)
    up_far = jnp.where(main_diag, up_d, up_c)
    low_near = jnp.where(main_diag, low_a, low_b)
    up_near = jnp.where(main_diag, up_a, up_b)
    tri_one = triangle(stiffness, (low_a, low_b, low_far), (up_a, up_b, up_far), weight)
    tri_two = triangle(stiffness, (low_near, low_d, low_c), (up_near, up_d, up_c), weight)
    result = []
    for height in range(2):
        resp_one = tri_one[height]
        resp_two = tri_two[height]
        corner_a = resp_one[:, 0] + jnp.where(main_diag, resp_two[:, 0], 0.0)
        corner_b = resp_one[:, 1] + jnp.where(main_diag, 0.0, resp_two[:, 0])
        corner_c = resp_two[:, 2] + jnp.where(main_diag, 0.0, resp_one[:, 2])
        corner_d = resp_two[:, 1] + jnp.where(main_diag, resp_one[:, 2], 0.0)
        result.append((corner_a, corner_b, corner_c, corner_d))
    return (result[0], result[1])


def add_corners(total, extra):
    if total is None:
        return extra
    return tuple((first_term + other_term for first_term, other_term in zip(total, extra)))


def scaled_by(corners, factor):
    return tuple((member * factor for member in corners))


def own_nodes(corners):
    corner_a, corner_b, corner_c, corner_d = corners
    return corner_a[:, 1:, 1:] + corner_b[:, :-1, 1:] + corner_c[:, 1:, :-1] + corner_d[:, :-1, :-1]


def per_device(
    ssa_velocity,
    shelf_viscosity,
    basal_friction,
    driving_stress,
    stokes_velocity,
    ice_viscosity,
    body_force,
    diagonals,
    element_matrix,
    iface_columns,
    iface_nodes,
):
    row_count = ssa_velocity.shape[1]
    col_count = ssa_velocity.shape[2]
    stacked = jnp.concatenate([ssa_velocity, shelf_viscosity[None]], 0)
    padded = with_halo(stacked, (("mx", 1), ("my", 2)), 1)
    shelf_res = shelf_residual(padded, basal_friction, driving_stress)
    owner_nodes = iface_nodes[0]
    node_live = owner_nodes >= 0
    flat_vel = ssa_velocity.reshape(2, row_count * col_count)
    outgoing = jnp.where(node_live[None], flat_vel[:, jnp.maximum(owner_nodes, 0)], 0.0)
    slot_count = outgoing.shape[2]
    grid_out = outgoing.reshape(2, 3, 3, slot_count)
    extended = with_halo(grid_out, (("mx", 1), ("my", 2)), 1)
    returned = extended[:, 0::2, 0::2].reshape(2, 9, slot_count)
    depth_count = stokes_velocity.shape[1]
    block_x = stokes_velocity.shape[2]
    block_y = stokes_velocity.shape[3]
    column_count = block_x * block_y
    columns = iface_columns[0]
    col_live = columns >= 0
    target = jnp.where(col_live, columns, column_count).reshape(-1)
    placed = (
        jnp.zeros((2, column_count + 1), jnp.float32)
        .at[:, target]
        .add(returned.reshape(2, -1))[:, :column_count]
    )
    marked = jnp.zeros((column_count + 1,), jnp.float32).at[target].add(1.0)[:column_count] > 0.0
    uv_part = jnp.where(
        marked.reshape(1, 1, block_x, block_y),
        placed.reshape(2, 1, block_x, block_y),
        stokes_velocity[:2],
    )
    stokes_field = jnp.concatenate([uv_part, stokes_velocity[2:3], ice_viscosity[None]], 0)
    planes = jnp.concatenate(
        [
            stokes_field.reshape(4 * depth_count, block_x, block_y),
            diagonals.astype(jnp.float32)[None],
        ],
        0,
    )
    widened = with_halo(planes, (("mx", 1), ("my", 2)), 1)
    flag_cells = widened[-1, :-1, :-1]
    field_ext = widened[:-1].reshape(4, depth_count, block_x + 2, block_y + 2)
    count_x = lax.axis_size("mx")
    count_y = lax.axis_size("my")
    place_x = lax.axis_index("mx")
    place_y = lax.axis_index("my")
    global_x = place_x * block_x + jnp.arange(block_x + 1, dtype=jnp.int32) - 1
    global_y = place_y * block_y + jnp.arange(block_y + 1, dtype=jnp.int32) - 1
    valid_x = (global_x >= 0) & (global_x <= count_x * block_x - 2)
    valid_y = (global_y >= 0) & (global_y <= count_y * block_y - 2)
    weight = (valid_x[:, None] & valid_y[None, :]).astype(jnp.float32)
    layer_index = lax.axis_index("layer")
    layer_count = lax.axis_size("layer")
    below_live = (layer_index > 0).astype(jnp.float32)
    above_live = (layer_index < layer_count - 1).astype(jnp.float32)
    extended_layers = with_halo(field_ext, (("layer", 1),), 1)
    collected = [None for height in range(depth_count)]
    for height in range(depth_count + 1):
        lower_part, upper_part = cell_terms(
            extended_layers[:, height],
            extended_layers[:, height + 1],
            flag_cells,
            element_matrix,
            weight,
        )
        if height > 0:
            if height == depth_count:
                lower_part = scaled_by(lower_part, above_live)
            collected[height - 1] = add_corners(collected[height - 1], lower_part)
        if height < depth_count:
            if height == 0:
                upper_part = scaled_by(upper_part, below_live)
            collected[height] = add_corners(collected[height], upper_part)
    owned = [own_nodes(corners) for corners in collected]
    stokes_residual = jnp.stack(owned, axis=1) - body_force
    depth_sum = jnp.sum(stokes_residual[:2], axis=1).reshape(2, column_count)
    bucket = jnp.where(col_live[None], depth_sum[:, jnp.maximum(columns, 0)], 0.0)
    depth_total = lax.psum(bucket, "layer")
    grid_back = depth_total.reshape(2, 3, 3, slot_count)
    extended_back = with_halo(grid_back, (("mx", 1), ("my", 2)), 1)
    at_owner = extended_back[:, 0::2, 0::2].reshape(2, 9, slot_count)
    node_index = jnp.where(node_live, owner_nodes, row_count * col_count).reshape(-1)
    node_force = (
        jnp.zeros((2, row_count * col_count + 1), jnp.float32)
        .at[:, node_index]
        .add(at_owner.reshape(2, -1))
    )
    node_force = node_force[:, : row_count * col_count].reshape(2, row_count, col_count)
    coupled_residual = shelf_res - node_force
    return (coupled_residual, stokes_residual)


def solution(mesh):
    return jax.shard_map(
        per_device,
        mesh=mesh,
        in_specs=(
            P(None, "mx", "my"),
            P("mx", "my"),
            P("mx", "my"),
            P(None, "mx", "my"),
            P(None, "layer", "mx", "my"),
            P("layer", "mx", "my"),
            P(None, "layer", "mx", "my"),
            P("mx", "my"),
            P(),
            P(("mx", "my"), None, None),
            P(("mx", "my"), None, None),
        ),
        out_specs=(P(None, "mx", "my"), P(None, "layer", "mx", "my")),
        check_vma=False,
    )
```

profile of v0, /device:TPU:225, one launch (start us, length us, event | category | flops | bytes accessed | tf_op | source)
XLA Modules:
  0.0 200.9 jit_solution(2747815549716672843)
XLA Ops:
  2.9 5.5 %copy.172 = f32[2,64,256]{0,2,1:T(8,128)} copy(f32[2,64,256]{2,1,0:T(8,128)} %param.11) | data formatting | bytes 262144 | tf_op args[0]
  9.0 5.8 %gather_fusion = f32[1152,2]{1,0:T(8,128)S(1)} fusion(f32[2,16384]{0,1:T(8,128)} %bitcast.297, s32[2048]{0:T(1024)S(1)} %get-tuple-element.199), kind=kCustom, calls=%fused_computation | custom fusion | bytes 23040 | tf_op jit(solution)/shard_map/gather | solution.py:126
  15.1 5.3 %collective-permute-start.4 = (f32[2,1,3,128]{3,0,2,1:T(2,128)S(1)}, f32[2,1,3,128]{3,0,2,1:T(2,128)S(1)}, u32[]{:S(2)}, u32[]{:S(2)}) collective-permute-start(f32[2,1,3,128]{3,0,2,1:T(2,128)S(1)} %get-tuple-element.196), channel_id=1, source_target_pairs={{0,16},{16,32},{32,48},{48,64},{64,80},{80,96},{96,112},{112,128},... | collective-permute-start | bytes 9224 | tf_op jit(solution)/shard_map/ppermute | solution.py:14
  20.5 1.9 collective-permute-start.5
  22.4 4.9 %collective-permute-start = (f32[3,1,256]{2,1,0:T(1,128)S(1)}, f32[3,1,256]{2,1,0:T(1,128)S(1)}, u32[]{:S(2)}, u32[]{:S(2)}) collective-permute-start(f32[3,1,256]{2,1,0:T(1,128)S(1)} %get-tuple-element.76), channel_id=1, source_target_pairs={{0,16},{16,32},{32,48},{48,64},{64,80},{80,96},{96,112},{112,128},... | collective-permute-start | bytes 9224 | tf_op jit(solution)/shard_map/ppermute | solution.py:14
  27.3 1.9 collective-permute-start.1
  29.9 8.6 %scatter_custom_fusion = f32[4097]{0:T(1024)S(1)} fusion(s32[1152]{0:T(1024)S(1)} %fusion.75, f32[1152]{0:T(1024)S(1)} %broadcast.299, f32[]{:T(128)} %constant.32.clone.1), kind=kCustom, calls=%fused_computation.252 | custom fusion | flops 1152 | bytes 16392 | tf_op jit(solution)/shard_map/scatter-add | solution.py:143
  39.4 2.9 %collective-permute-start.2 = (f32[3,66,1]{2,1,0:T(8,128)S(1)}, f32[3,66,1]{2,1,0:T(8,128)S(1)}, u32[]{:S(2)}, u32[]{:S(2)}) collective-permute-start(f32[3,66,1]{2,1,0:T(8,128)S(1)} %get-tuple-element.74), channel_id=1, source_target_pairs={{0,4},{4,8},{8,12},{1,5},{5,9},{9,13},{2,6},{6,10},{10,14},{3,7},{... | collective-permute-start | bytes 2384 | tf_op jit(solution)/shard_map/ppermute | solution.py:14
  43.6 4.0 %collective-permute-start.6 = (f32[2,5,1,128]{3,0,2,1:T(2,128)S(1)}, f32[2,5,1,128]{3,0,2,1:T(2,128)S(1)}, u32[]{:S(2)}, u32[]{:S(2)}) collective-permute-start(f32[2,5,1,128]{3,0,2,1:T(2,128)S(1)} %get-tuple-element.182), channel_id=1, source_target_pairs={{0,4},{4,8},{8,12},{1,5},{5,9},{9,13},{2,6},{6,10},{10,14},{3,7},{... | collective-permute-start | bytes 15368 | tf_op jit(solution)/shard_map/ppermute | solution.py:14
  49.2 2.8 %collective-permute-done.7 = f32[2,5,1,128]{3,0,2,1:T(2,128)S(1)} collective-permute-done((f32[2,5,1,128]{3,0,2,1:T(2,128)S(1)}, f32[2,5,1,128]{3,0,2,1:T(2,128)S(1)}, u32[]{:S(2)}, u32[]{:S(2)}) %collective-permute-start.7) | collective-permute-done | bytes 5152 | tf_op jit(solution)/shard_map/ppermute | solution.py:15
  52.2 10.5 %scatter_custom_fusion.1 = f32[2,4097]{0,1:T(8,128)S(1)} fusion(s32[1152]{0:T(1024)S(1)} %fusion.75, f32[1152,2]{1,0:T(8,128)S(1)} %copy.174, f32[]{:T(128)} %constant.32.clone.1), kind=kCustom, calls=%fused_computation.23 | custom fusion | flops 2304 | bytes 32780 | tf_op jit(solution)/shard_map/scatter-add | solution.py:141
  64.2 2.2 %copy.175 = f32[2,16,256]{2,1,0:T(8,128)S(1)} copy(f32[2,16,256]{0,2,1:T(8,128)} %bitcast.298) | data formatting | bytes 65536 | tf_op jit(solution)/shard_map/jit(_where)/broadcast_in_dim | solution.py:144
  66.6 7.0 %collective-permute-start.8 = (f32[13,1,256]{2,0,1:T(8,128)S(1)}, f32[13,1,256]{2,0,1:T(8,128)S(1)}, u32[]{:S(2)}, u32[]{:S(2)}) collective-permute-start(f32[13,1,256]{2,0,1:T(8,128)S(1)} %get-tuple-element.64), channel_id=1, source_target_pairs={{0,16},{16,32},{32,48},{48,64},{64,80},{80,96},{96,112},{112,128},... | collective-permute-start | bytes 39944 | tf_op jit(solution)/shard_map/ppermute | solution.py:14
  73.6 1.9 collective-permute-start.9
  75.8 4.1 %collective-permute-done.9 = f32[13,1,256]{2,0,1:T(8,128)S(1)} collective-permute-done((f32[13,1,256]{2,0,1:T(8,128)S(1)}, f32[13,1,256]{2,0,1:T(8,128)S(1)}, u32[]{:S(2)}, u32[]{:S(2)}) %collective-permute-start.9) | collective-permute-done | bytes 13344 | tf_op jit(solution)/shard_map/ppermute | solution.py:15
  80.0 2.7 %collective-permute-start.10 = (f32[13,18,1]{2,0,1:T(8,128)S(1)}, f32[13,18,1]{2,0,1:T(8,128)S(1)}, u32[]{:S(2)}, u32[]{:S(2)}) collective-permute-start(f32[13,18,1]{2,0,1:T(8,128)S(1)} %get-tuple-element.62), channel_id=1, source_target_pairs={{0,4},{4,8},{8,12},{1,5},{5,9},{9,13},{2,6},{6,10},{10,14},{3,7},{... | collective-permute-start | bytes 2816 | tf_op jit(solution)/shard_map/ppermute | solution.py:14
  84.8 3.8 %collective-permute-done.11 = f32[13,18,1]{2,0,1:T(8,128)S(1)} collective-permute-done((f32[13,18,1]{2,0,1:T(8,128)S(1)}, f32[13,18,1]{2,0,1:T(8,128)S(1)}, u32[]{:S(2)}, u32[]{:S(2)}) %collective-permute-start.11) | collective-permute-done | bytes 968 | tf_op jit(solution)/shard_map/ppermute | solution.py:15
  89.2 3.1 %collective-permute-start.12 = (f32[4,1,18,258]{3,0,2,1:T(4,128)S(1)}, f32[4,1,18,258]{3,0,2,1:T(4,128)S(1)}, u32[]{:S(2)}, u32[]{:S(2)}) collective-permute-start(f32[4,1,18,258]{3,0,2,1:T(4,128)S(1)} %copy.245), channel_id=1, source_target_pairs={{0,1},{1,2},{2,3},{4,5},{5,6},{6,7},{8,9},{9,10},{10,11},{12,13},{... | collective-permute-start | bytes 222920 | tf_op jit(solution)/shard_map/ppermute | solution.py:14
  103.3 1.8 and_select_fusion.1
  105.8 2.2 %stack.48 = f32[18,17,257]{2,0,1:T(8,128)S(1)} concatenate(f32[1,17,257]{2,0,1:T(1,128)} %get-tuple-element.106, f32[1,17,257]{2,0,1:T(1,128)} %get-tuple-element.105, f32[1,17,257]{2,0,1:T(1,128)} %get-tuple-element.152, f32[1,17,257]{2,0,1:T(1,128)} %get-tuple-element.103, f32[1,17,257]{2,0,1:T(1,128)S(1)} %get-tuple-element.102, f32[1,17,257]{2,0,1:T(1,128)} %get-tuple-element.151, ...), dimensions={0} | concatenate | bytes 629136 | tf_op jit(solution)/shard_map/stack | solution.py:46
  123.0 1.5 stack.54
  126.8 2.3 %stack.56 = f32[18,17,257]{2,0,1:T(8,128)S(1)} concatenate(f32[1,17,257]{2,0,1:T(1,128)S(1)} %get-tuple-element.142, f32[1,17,257]{2,0,1:T(1,128)S(1)} %get-tuple-element.141, f32[1,17,257]{2,0,1:T(1,128)S(1)} %copy-done.5, f32[1,17,257]{2,0,1:T(1,128)S(1)} %get-tuple-element.140, f32[1,17,257]{2,0,1:T(1,128)S(1)} %get-tuple-element.139, f32[1,17,257]{2,0,1:T(1,128)S(1)} %get-tuple-element.166, ...), dimensions={0} | concatenate | bytes 629136 | tf_op jit(solution)/shard_map/stack | solution.py:46
  132.1 2.3 %stack.57 = f32[18,17,257]{2,0,1:T(8,128)S(1)} concatenate(f32[1,17,257]{2,0,1:T(1,128)S(1)} %get-tuple-element.176, f32[1,17,257]{2,0,1:T(1,128)S(1)} %get-tuple-element.137, f32[1,17,257]{2,0,1:T(1,128)S(1)} %get-tuple-element.118, f32[1,17,257]{2,0,1:T(1,128)S(1)} %get-tuple-element.175, f32[1,17,257]{2,0,1:T(1,128)S(1)} %get-tuple-element.117, ...), dimensions={0} | concatenate | bytes 629136 | tf_op jit(solution)/shard_map/stack | solution.py:46
  140.8 2.9 %gather_fusion.1 = f32[1152,2]{1,0:T(8,128)S(1)} fusion(f32[2,4096]{0,1:T(8,128)S(1)} %bitcast.305, s32[2048]{0:T(1024)} %get-tuple-element.198), kind=kCustom, calls=%fused_computation.1 | custom fusion | bytes 23040 | tf_op jit(solution)/shard_map/gather | solution.py:194
  144.8 9.6 %psum.7 = f32[2,3,3,128]{3,0,2,1:T(2,128)S(1)} all-reduce(f32[2,3,3,128]{3,0,2,1:T(2,128)S(1)} %bitcast.339), channel_id=1, replica_groups=mesh['mx'=32,'my'=4,'layer'=4] {'layer'}, use_global_device_ids=true, to_apply=%region_3.4 | all-reduce | flops 2304 | bytes 18432 | tf_op jit(solution)/shard_map/psum | solution.py:195
  154.4 5.9 %collective-permute-start.14 = (f32[2,1,3,128]{3,0,2,1:T(2,128)S(1)}, f32[2,1,3,128]{3,0,2,1:T(2,128)S(1)}, u32[]{:S(2)}, u32[]{:S(2)}) collective-permute-start(f32[2,1,3,128]{3,0,2,1:T(2,128)S(1)} %get-tuple-element.185), channel_id=1, source_target_pairs={{0,16},{16,32},{32,48},{48,64},{64,80},{80,96},{96,112},{112,128},... | collective-permute-start | bytes 9224 | tf_op jit(solution)/shard_map/ppermute | solution.py:14
  161.3 1.9 collective-permute-start.15
  163.3 4.2 %collective-permute-done.15 = f32[2,1,3,128]{3,0,2,1:T(2,128)S(1)} collective-permute-done((f32[2,1,3,128]{3,0,2,1:T(2,128)S(1)}, f32[2,1,3,128]{3,0,2,1:T(2,128)S(1)}, u32[]{:S(2)}, u32[]{:S(2)}) %collective-permute-start.15) | collective-permute-done | bytes 3104 | tf_op jit(solution)/shard_map/ppermute | solution.py:15
  167.5 3.2 %collective-permute-start.16 = (f32[2,5,1,128]{3,0,2,1:T(2,128)S(1)}, f32[2,5,1,128]{3,0,2,1:T(2,128)S(1)}, u32[]{:S(2)}, u32[]{:S(2)}) collective-permute-start(f32[2,5,1,128]{3,0,2,1:T(2,128)S(1)} %get-tuple-element.180), channel_id=1, source_target_pairs={{0,4},{4,8},{8,12},{1,5},{5,9},{9,13},{2,6},{6,10},{10,14},{3,7},{... | collective-permute-start | bytes 15368 | tf_op jit(solution)/shard_map/ppermute | solution.py:14
  175.3 14.0 %scatter_custom_fusion.2 = f32[2,16385]{0,1:T(8,128)} fusion(s32[1152]{0:T(1024)} %fusion.74, f32[1152,2]{1,0:T(8,128)S(1)} %copy.231, f32[]{:T(128)} %constant.32.clone.1), kind=kCustom, calls=%fused_computation.5 | custom fusion | flops 2304 | bytes 131592 | tf_op jit(solution)/shard_map/scatter-add | solution.py:203
  189.3 5.7 %slice.1543 = f32[2,16384]{0,1:T(8,128)} slice(f32[2,16385]{0,1:T(8,128)} %scatter_custom_fusion.2), slice={[0:2], [0:16384]} | slice | bytes 262144 | tf_op jit(solution)/shard_map/slice | solution.py:205
  195.0 5.2 %copy.232 = f32[2,64,256]{2,1,0:T(8,128)S(1)} copy(f32[2,64,256]{0,2,1:T(8,128)} %bitcast.284) | data formatting | bytes 262144 | tf_op jit(solution)/shard_map/reshape | solution.py:205
  (213 shorter events, 57.3 us)
Async XLA Ops:
  0.6 107.4 %copy-start = (f32[18,18]{1,0:T(8,128)S(1)}, f32[18,18]{1,0:T(8,128)}, u32[]{:S(2)}) copy-start(f32[18,18]{1,0:T(8,128)} %param.19) | copy-start | bytes 3892
  0.6 28.6 %copy-start.23 = (s32[1,9,128]{2,0,1:T(1,128)S(1)}, s32[1,9,128]{2,0,1:T(1,128)}, u32[]{:S(2)}) copy-start(s32[1,9,128]{2,0,1:T(1,128)} %param.21) | copy-start | bytes 13828
  0.7 28.6 %copy-start.22 = (s32[1,9,128]{2,0,1:T(1,128)S(1)}, s32[1,9,128]{2,0,1:T(1,128)}, u32[]{:S(2)}) copy-start(s32[1,9,128]{2,0,1:T(1,128)} %param.20) | copy-start | bytes 13828
  0.7 21.7 %copy-start.1 = (f32[2,64,256]{2,1,0:T(8,128)S(1)}, f32[2,64,256]{2,1,0:T(8,128)}, u32[]{:S(2)}) copy-start(f32[2,64,256]{2,1,0:T(8,128)} %param.11) | copy-start | bytes 393220
  0.7 21.7 %copy-start.2 = (f32[64,256]{1,0:T(8,128)S(1)}, f32[64,256]{1,0:T(8,128)}, u32[]{:S(2)}) copy-start(f32[64,256]{1,0:T(8,128)} %param.12) | copy-start | bytes 196612
  0.7 37.9 %copy-start.24 = (s32[16,256]{1,0:T(8,128)S(1)}, s32[16,256]{1,0:T(8,128)}, u32[]{:S(2)}) copy-start(s32[16,256]{1,0:T(8,128)} %param.18) | copy-start | bytes 49156
  8.4 58.0 %copy-start.10 = (f32[3,3,16,256]{3,2,1,0:T(8,128)S(1)}, f32[3,3,16,256]{3,2,1,0:T(8,128)}, u32[]{:S(2)}) copy-start(f32[3,3,16,256]{3,2,1,0:T(8,128)} %param.15) | copy-start | bytes 442372
  8.4 58.0 %slice-start = ((f32[3,3,16,256]{3,2,1,0:T(8,128)}), f32[1,3,16,256]{3,2,1,0:T(8,128)S(1)}, s32[]{:S(2)}) async-start(f32[3,3,16,256]{3,2,1,0:T(8,128)} %param.15), calls=%async_computation | async-start | bytes 98304 | tf_op jit(solution)/shard_map/slice | solution.py:149
  8.4 58.0 %copy-start.21 = (f32[3,16,256]{2,1,0:T(8,128)S(1)}, f32[3,16,256]{2,1,0:T(8,128)}, u32[]{:S(2)}) copy-start(f32[3,16,256]{2,1,0:T(8,128)} %param.16) | copy-start | bytes 147460
  15.1 28.4 %collective-permute-start.4 = (f32[2,1,3,128]{3,0,2,1:T(2,128)S(1)}, f32[2,1,3,128]{3,0,2,1:T(2,128)S(1)}, u32[]{:S(2)}, u32[]{:S(2)}) collective-permute-start(f32[2,1,3,128]{3,0,2,1:T(2,128)S(1)} %get-tuple-element.196), channel_id=1, source_target_pairs={{0,16},{16,32},{32,48},{48,64},{64,80},{80,96},{96,112},{112,128},... | collective-permute-start | bytes 9224 | tf_op jit(solution)/shard_map/ppermute | solution.py:14
  20.5 23.1 %collective-permute-start.5 = (f32[2,1,3,128]{3,0,2,1:T(2,128)S(1)}, f32[2,1,3,128]{3,0,2,1:T(2,128)S(1)}, u32[]{:S(2)}, u32[]{:S(2)}) collective-permute-start(f32[2,1,3,128]{3,0,2,1:T(2,128)S(1)} %get-tuple-element.197), channel_id=1, source_target_pairs={{16,0},{32,16},{48,32},{64,48},{80,64},{96,80},{112,96},{128,112},... | collective-permute-start | bytes 9224 | tf_op jit(solution)/shard_map/ppermute | solution.py:15
  22.4 16.8 %collective-permute-start = (f32[3,1,256]{2,1,0:T(1,128)S(1)}, f32[3,1,256]{2,1,0:T(1,128)S(1)}, u32[]{:S(2)}, u32[]{:S(2)}) collective-permute-start(f32[3,1,256]{2,1,0:T(1,128)S(1)} %get-tuple-element.76), channel_id=1, source_target_pairs={{0,16},{16,32},{32,48},{48,64},{64,80},{80,96},{96,112},{112,128},... | collective-permute-start | bytes 9224 | tf_op jit(solution)/shard_map/ppermute | solution.py:14
  27.3 11.9 %collective-permute-start.1 = (f32[3,1,256]{2,1,0:T(1,128)S(1)}, f32[3,1,256]{2,1,0:T(1,128)S(1)}, u32[]{:S(2)}, u32[]{:S(2)}) collective-permute-start(f32[3,1,256]{2,1,0:T(1,128)S(1)} %get-tuple-element.77), channel_id=1, source_target_pairs={{16,0},{32,16},{48,32},{64,48},{80,64},{96,80},{112,96},{128,112},... | collective-permute-start | bytes 9224 | tf_op jit(solution)/shard_map/ppermute | solution.py:15
  38.6 61.5 %copy-start.25 = (pred[257]{0:T(512)(128)(4,1)}, pred[257]{0:T(512)(128)(4,1)S(1)}, u32[]{:S(2)}) copy-start(pred[257]{0:T(512)(128)(4,1)S(1)} %fusion.78) | copy-start | bytes 775
  39.4 9.5 %collective-permute-start.2 = (f32[3,66,1]{2,1,0:T(8,128)S(1)}, f32[3,66,1]{2,1,0:T(8,128)S(1)}, u32[]{:S(2)}, u32[]{:S(2)}) collective-permute-start(f32[3,66,1]{2,1,0:T(8,128)S(1)} %get-tuple-element.74), channel_id=1, source_target_pairs={{0,4},{4,8},{8,12},{1,5},{5,9},{9,13},{2,6},{6,10},{10,14},{3,7},{... | collective-permute-start | bytes 2384 | tf_op jit(solution)/shard_map/ppermute | solution.py:14
  42.3 6.6 %collective-permute-start.3 = (f32[3,66,1]{2,1,0:T(8,128)S(1)}, f32[3,66,1]{2,1,0:T(8,128)S(1)}, u32[]{:S(2)}, u32[]{:S(2)}) collective-permute-start(f32[3,66,1]{2,1,0:T(8,128)S(1)} %get-tuple-element.75), channel_id=1, source_target_pairs={{4,0},{8,4},{12,8},{5,1},{9,5},{13,9},{6,2},{10,6},{14,10},{7,3},{... | collective-permute-start | bytes 2384 | tf_op jit(solution)/shard_map/ppermute | solution.py:15
  43.6 5.6 %collective-permute-start.6 = (f32[2,5,1,128]{3,0,2,1:T(2,128)S(1)}, f32[2,5,1,128]{3,0,2,1:T(2,128)S(1)}, u32[]{:S(2)}, u32[]{:S(2)}) collective-permute-start(f32[2,5,1,128]{3,0,2,1:T(2,128)S(1)} %get-tuple-element.182), channel_id=1, source_target_pairs={{0,4},{4,8},{8,12},{1,5},{5,9},{9,13},{2,6},{6,10},{10,14},{3,7},{... | collective-permute-start | bytes 15368 | tf_op jit(solution)/shard_map/ppermute | solution.py:14
  47.6 4.4 %collective-permute-start.7 = (f32[2,5,1,128]{3,0,2,1:T(2,128)S(1)}, f32[2,5,1,128]{3,0,2,1:T(2,128)S(1)}, u32[]{:S(2)}, u32[]{:S(2)}) collective-permute-start(f32[2,5,1,128]{3,0,2,1:T(2,128)S(1)} %get-tuple-element.183), channel_id=1, source_target_pairs={{4,0},{8,4},{12,8},{5,1},{9,5},{13,9},{6,2},{10,6},{14,10},{7,3},{... | collective-permute-start | bytes 15368 | tf_op jit(solution)/shard_map/ppermute | solution.py:15
  66.6 9.2 %collective-permute-start.8 = (f32[13,1,256]{2,0,1:T(8,128)S(1)}, f32[13,1,256]{2,0,1:T(8,128)S(1)}, u32[]{:S(2)}, u32[]{:S(2)}) collective-permute-start(f32[13,1,256]{2,0,1:T(8,128)S(1)} %get-tuple-element.64), channel_id=1, source_target_pairs={{0,16},{16,32},{32,48},{48,64},{64,80},{80,96},{96,112},{112,128},... | collective-permute-start | bytes 39944 | tf_op jit(solution)/shard_map/ppermute | solution.py:14
  73.6 6.3 %collective-permute-start.9 = (f32[13,1,256]{2,0,1:T(8,128)S(1)}, f32[13,1,256]{2,0,1:T(8,128)S(1)}, u32[]{:S(2)}, u32[]{:S(2)}) collective-permute-start(f32[13,1,256]{2,0,1:T(8,128)S(1)} %get-tuple-element.65), channel_id=1, source_target_pairs={{16,0},{32,16},{48,32},{64,48},{80,64},{96,80},{112,96},{128,112},... | collective-permute-start | bytes 39944 | tf_op jit(solution)/shard_map/ppermute | solution.py:15
  80.0 4.8 %collective-permute-start.10 = (f32[13,18,1]{2,0,1:T(8,128)S(1)}, f32[13,18,1]{2,0,1:T(8,128)S(1)}, u32[]{:S(2)}, u32[]{:S(2)}) collective-permute-start(f32[13,18,1]{2,0,1:T(8,128)S(1)} %get-tuple-element.62), channel_id=1, source_target_pairs={{0,4},{4,8},{8,12},{1,5},{5,9},{9,13},{2,6},{6,10},{10,14},{3,7},{... | collective-permute-start | bytes 2816 | tf_op jit(solution)/shard_map/ppermute | solution.py:14
  82.8 5.9 %collective-permute-start.11 = (f32[13,18,1]{2,0,1:T(8,128)S(1)}, f32[13,18,1]{2,0,1:T(8,128)S(1)}, u32[]{:S(2)}, u32[]{:S(2)}) collective-permute-start(f32[13,18,1]{2,0,1:T(8,128)S(1)} %get-tuple-element.63), channel_id=1, source_target_pairs={{4,0},{8,4},{12,8},{5,1},{9,5},{13,9},{6,2},{10,6},{14,10},{7,3},{... | collective-permute-start | bytes 2816 | tf_op jit(solution)/shard_map/ppermute | solution.py:15
  89.2 5.9 %collective-permute-start.12 = (f32[4,1,18,258]{3,0,2,1:T(4,128)S(1)}, f32[4,1,18,258]{3,0,2,1:T(4,128)S(1)}, u32[]{:S(2)}, u32[]{:S(2)}) collective-permute-start(f32[4,1,18,258]{3,0,2,1:T(4,128)S(1)} %copy.245), channel_id=1, source_target_pairs={{0,1},{1,2},{2,3},{4,5},{5,6},{6,7},{8,9},{9,10},{10,11},{12,13},{... | collective-permute-start | bytes 222920 | tf_op jit(solution)/shard_map/ppermute | solution.py:14
  93.6 7.7 %collective-permute-start.13 = (f32[4,1,18,258]{3,0,2,1:T(4,128)S(1)}, f32[4,1,18,258]{3,0,2,1:T(4,128)S(1)}, u32[]{:S(2)}, u32[]{:S(2)}) collective-permute-start(f32[4,1,18,258]{3,0,2,1:T(4,128)S(1)} %copy.246), channel_id=1, source_target_pairs={{1,0},{2,1},{3,2},{5,4},{6,5},{7,6},{9,8},{10,9},{11,10},{13,12},{... | collective-permute-start | bytes 222920 | tf_op jit(solution)/shard_map/ppermute | solution.py:15
  100.0 15.1 %copy-start.6 = (f32[1,17,257]{2,0,1:T(1,128)}, f32[1,17,257]{2,0,1:T(1,128)S(1)}, u32[]{:S(2)}) copy-start(f32[1,17,257]{2,0,1:T(1,128)S(1)} %get-tuple-element.177) | copy-start | bytes 52432
  100.0 15.1 %copy-start.8 = (f32[1,17,257]{2,0,1:T(1,128)}, f32[1,17,257]{2,0,1:T(1,128)S(1)}, u32[]{:S(2)}) copy-start(f32[1,17,257]{2,0,1:T(1,128)S(1)} %get-tuple-element.178) | copy-start | bytes 52432
  100.0 19.7 %copy-start.4 = (f32[1,17,257]{2,0,1:T(1,128)}, f32[1,17,257]{2,0,1:T(1,128)S(1)}, u32[]{:S(2)}) copy-start(f32[1,17,257]{2,0,1:T(1,128)S(1)} %get-tuple-element.167) | copy-start | bytes 52432
  129.8 30.5 %copy-start.3 = (f32[64,256]{1,0:T(8,128)S(1)}, f32[64,256]{1,0:T(8,128)}, u32[]{:S(2)}) copy-start(f32[64,256]{1,0:T(8,128)} %param.13) | copy-start | bytes 196612
  154.4 8.9 %collective-permute-start.14 = (f32[2,1,3,128]{3,0,2,1:T(2,128)S(1)}, f32[2,1,3,128]{3,0,2,1:T(2,128)S(1)}, u32[]{:S(2)}, u32[]{:S(2)}) collective-permute-start(f32[2,1,3,128]{3,0,2,1:T(2,128)S(1)} %get-tuple-element.185), channel_id=1, source_target_pairs={{0,16},{16,32},{32,48},{48,64},{64,80},{80,96},{96,112},{112,128},... | collective-permute-start | bytes 9224 | tf_op jit(solution)/shard_map/ppermute | solution.py:14
  161.3 6.1 %collective-permute-start.15 = (f32[2,1,3,128]{3,0,2,1:T(2,128)S(1)}, f32[2,1,3,128]{3,0,2,1:T(2,128)S(1)}, u32[]{:S(2)}, u32[]{:S(2)}) collective-permute-start(f32[2,1,3,128]{3,0,2,1:T(2,128)S(1)} %get-tuple-element.184), channel_id=1, source_target_pairs={{16,0},{32,16},{48,32},{64,48},{80,64},{96,80},{112,96},{128,112},... | collective-permute-start | bytes 9224 | tf_op jit(solution)/shard_map/ppermute | solution.py:15
  167.5 6.2 %collective-permute-start.16 = (f32[2,5,1,128]{3,0,2,1:T(2,128)S(1)}, f32[2,5,1,128]{3,0,2,1:T(2,128)S(1)}, u32[]{:S(2)}, u32[]{:S(2)}) collective-permute-start(f32[2,5,1,128]{3,0,2,1:T(2,128)S(1)} %get-tuple-element.180), channel_id=1, source_target_pairs={{0,4},{4,8},{8,12},{1,5},{5,9},{9,13},{2,6},{6,10},{10,14},{3,7},{... | collective-permute-start | bytes 15368 | tf_op jit(solution)/shard_map/ppermute | solution.py:14
  170.7 4.4 %collective-permute-start.17 = (f32[2,5,1,128]{3,0,2,1:T(2,128)S(1)}, f32[2,5,1,128]{3,0,2,1:T(2,128)S(1)}, u32[]{:S(2)}, u32[]{:S(2)}) collective-permute-start(f32[2,5,1,128]{3,0,2,1:T(2,128)S(1)} %get-tuple-element.181), channel_id=1, source_target_pairs={{4,0},{8,4},{12,8},{5,1},{9,5},{13,9},{6,2},{10,6},{14,10},{7,3},{... | collective-permute-start | bytes 15368 | tf_op jit(solution)/shard_map/ppermute | solution.py:15
  (13 other events, 136.4 us)
where the time goes:
time: 203 us; the launch traced here: 201 us
  local copies, waits for them, and re-layouts  62.5 us (31%)
  starting transfers between devices  53.3 us (26%)
  other arithmetic  51.4 us (25%)
  waiting for transfers between devices  16.8 us (8%)
  blocking collectives  9.58 us (5%)
  matrix products  5.27 us (3%)
    ppermute x9, starting transfers between devices, with_halo(): before = lax.ppermute(last, axis, up)  39 us
    ppermute x9, waiting for transfers between devices, with_halo(): after = lax.ppermute(initial, axis, down)  16.2 us
    ppermute x9, starting transfers between devices, with_halo(): after = lax.ppermute(initial, axis, down)  14.3 us
    scatter-add x1, other arithmetic, per_device(): node_force = jnp.zeros((2, row_count * col_count + 1), jnp.float32).at[:,...  14 us
    another operation x8, local copies, waits for them, and re-layouts, triangle(): jnp.stack([plane[comp] for group in (lows, ups) for comp in range(3) for...  11.7 us
    unnamed x71, local copies, waits for them, and re-layouts  10.8 us
    scatter-add x1, other arithmetic, per_device(): placed = jnp.zeros((2, column_count + 1), jnp.float32).at[:, target].add(...  10.5 us
    psum x1, blocking collectives, per_device(): depth_total = lax.psum(bucket, 'layer')  9.58 us
  transfers between devices with their start and end apart: 18, of which 6 were waited for; matrix products, arithmetic and copies ran while one was open for 10% of the time, Pallas kernels for 0%

commit v1 on v0

--- a/solution.py
+++ b/solution.py
@@ -15,6 +15,45 @@
         after = lax.ppermute(initial, axis, down)
         array = jnp.concatenate([before, array, after], axis=dim)
     return array
+
+
+HIGH = lax.Precision.HIGHEST
+
+
+def slot_selectors(index, rows, cols):
+    live = index >= 0
+    row_of = jnp.where(live, index // cols, -1)
+    col_of = jnp.where(live, index % cols, -1)
+    pick_row = (row_of[:, None] == jnp.arange(rows, dtype=jnp.int32)[None]).astype(jnp.float32)
+    pick_col = col_of[:, None] == jnp.arange(cols, dtype=jnp.int32)[None]
+    return pick_row, pick_col
+
+
+def gather_slots(field, pick_row, pick_col):
+    rows_taken = jnp.einsum("sr,krc->ksc", pick_row, field, precision=HIGH)
+    return jnp.sum(jnp.where(pick_col[None], rows_taken, 0.0), axis=-1)
+
+
+def scatter_slots(values, pick_row, pick_col):
+    spread = jnp.where(pick_col[None], values[:, :, None], 0.0)
+    return jnp.einsum("sr,ksc->krc", pick_row, spread, precision=HIGH)
+
+
+def layer_total(part):
+    count = lax.axis_size("layer")
+    place = lax.axis_index("layer")
+    received = [part]
+    for shift in range(1, count):
+        pairs = [(i, (i + shift) % count) for i in range(count)]
+        received.append(lax.ppermute(part, "layer", pairs))
+    total = None
+    for source in range(count):
+        wanted = (place - source) % count
+        value = received[0]
+        for shift in range(1, count):
+            value = jnp.where(wanted == shift, received[shift], value)
+        total = value if total is None else total + value
+    return total
 
 
 def cell_dx(plane):
@@ -122,9 +161,9 @@
     shelf_res = shelf_residual(padded, basal_friction, driving_stress)
     owner_nodes = iface_nodes[0]
     node_live = owner_nodes >= 0
-    flat_vel = ssa_velocity.reshape(2, row_count * col_count)
-    outgoing = jnp.where(node_live[None], flat_vel[:, jnp.maximum(owner_nodes, 0)], 0.0)
-    slot_count = outgoing.shape[2]
+    slot_count = owner_nodes.shape[1]
+    node_row, node_col = slot_selectors(owner_nodes.reshape(-1), row_count, col_count)
+    outgoing = gather_slots(ssa_velocity, node_row, node_col).reshape(2, 9, slot_count)
     grid_out = outgoing.reshape(2, 3, 3, slot_count)
     extended = with_halo(grid_out, (("mx", 1), ("my", 2)), 1)
     returned = extended[:, 0::2, 0::2].reshape(2, 9, slot_count)
@@ -134,13 +173,9 @@
     column_count = block_x * block_y
     columns = iface_columns[0]
     col_live = columns >= 0
-    target = jnp.where(col_live, columns, column_count).reshape(-1)
-    placed = (
-        jnp.zeros((2, column_count + 1), jnp.float32)
-        .at[:, target]
-        .add(returned.reshape(2, -1))[:, :column_count]
-    )
-    marked = jnp.zeros((column_count + 1,), jnp.float32).at[target].add(1.0)[:column_count] > 0.0
+    col_row, col_col = slot_selectors(columns.reshape(-1), block_x, block_y)
+    placed = scatter_slots(returned.reshape(2, -1), col_row, col_col)
+    marked = jnp.einsum("sr,sc->rc", col_row, col_col.astype(jnp.float32)) > 0.0
     uv_part = jnp.where(
         marked.reshape(1, 1, block_x, block_y),
         placed.reshape(2, 1, block_x, block_y),
@@ -190,19 +225,13 @@
             collected[height] = add_corners(collected[height], upper_part)
     owned = [own_nodes(corners) for corners in collected]
     stokes_residual = jnp.stack(owned, axis=1) - body_force
-    depth_sum = jnp.sum(stokes_residual[:2], axis=1).reshape(2, column_count)
-    bucket = jnp.where(col_live[None], depth_sum[:, jnp.maximum(columns, 0)], 0.0)
-    depth_total = lax.psum(bucket, "layer")
+    depth_sum = jnp.sum(stokes_residual[:2], axis=1)
+    bucket = gather_slots(depth_sum, col_row, col_col).reshape(2, 9, slot_count)
+    depth_total = layer_total(bucket)
     grid_back = depth_total.reshape(2, 3, 3, slot_count)
     extended_back = with_halo(grid_back, (("mx", 1), ("my", 2)), 1)
     at_owner = extended_back[:, 0::2, 0::2].reshape(2, 9, slot_count)
-    node_index = jnp.where(node_live, owner_nodes, row_count * col_count).reshape(-1)
-    node_force = (
-        jnp.zeros((2, row_count * col_count + 1), jnp.float32)
-        .at[:, node_index]
-        .add(at_owner.reshape(2, -1))
-    )
-    node_force = node_force[:, : row_count * col_count].reshape(2, row_count, col_count)
+    node_force = scatter_slots(at_owner.reshape(2, -1), node_row, node_col)
     coupled_residual = shelf_res - node_force
     return (coupled_residual, stokes_residual)
 

time: 203 us -> 142 us (0.70)
  other arithmetic: 51.4 us -> 11.6 us
  local copies, waits for them, and re-layouts: 62.5 us -> 28.7 us
  starting transfers between devices: 53.3 us -> 63.6 us
  blocking collectives: 9.58 us -> 0 us
  matrix products: 5.27 us -> 13.3 us
  waiting for transfers between devices: 16.8 us -> 20.8 us
    scatter-add x3 -> x0, other arithmetic: 33.1 us -> none  [the longest x1 14 us: per_device(): node_force = jnp.zeros((2, row_count * col_count + 1), jnp.float32).at[:,...]
    ppermute x0 -> x3, starting transfers between devices: none -> 10.2 us  [layer_total(): received.append(lax.ppermute(part, 'layer', pairs))]
    psum x1 -> x0, blocking collectives: 9.58 us -> none  [per_device(): depth_total = lax.psum(bucket, 'layer')]
    gather x3 -> x0, local copies, waits for them, and re-layouts: 8.88 us -> none  [the longest x2 6.02 us: per_device(): flat_vel[:, jnp.maximum(owner_nodes, 0)]]
    unnamed x71 -> x173, local copies, waits for them, and re-layouts: 10.8 us -> 2.9 us
    dot_general x0 -> x5, matrix products: none -> 7.27 us  [the longest x2 3.56 us: gather_slots(): rows_taken = jnp.einsum('sr,krc->ksc', pick_row, field, precision=HIGH)]
    slice x2 -> x0, local copies, waits for them, and re-layouts: 7.21 us -> none  [the longest x1 5.74 us: per_device(): node_force[:, :row_count * col_count].reshape(2, row_count, col_count)]
    reshape x1, local copies, waits for them, and re-layouts: 5.21 us -> 0.01 us  [per_device(): bucket = gather_slots(depth_sum, col_row, col_col).reshape(2, 9, slot_count)]
  transfers between devices with their start and end apart: 18 -> 21, of which waited for: 6 -> 8; matrix products, arithmetic and copies ran while one was open for 10% -> 9% of each run, Pallas kernels for 0% -> 0%
where the time goes in v1:
time: 142 us; the launch traced here: 141 us
  starting transfers between devices  63.6 us (45%)
  local copies, waits for them, and re-layouts  28.7 us (20%)
  waiting for transfers between devices  20.8 us (15%)
  matrix products  13.3 us (9%)
  other arithmetic  11.6 us (8%)
  between operations  2.69 us (2%)
    ppermute x9, starting transfers between devices, with_halo(): before = lax.ppermute(last, axis, up)  39 us
    ppermute x9, waiting for transfers between devices, with_halo(): after = lax.ppermute(initial, axis, down)  17.2 us
    ppermute x9, starting transfers between devices, with_halo(): after = lax.ppermute(initial, axis, down)  14.3 us
    another operation x8, local copies, waits for them, and re-layouts, triangle(): jnp.stack([plane[comp] for group in (lows, ups) for comp in range(3) for...  10.3 us
    ppermute x3, starting transfers between devices, layer_total(): received.append(lax.ppermute(part, 'layer', pairs))  10.2 us
    squeeze x12, local copies, waits for them, and re-layouts, cell_terms(): corner_a = resp_one[:, 0] + jnp.where(main_diag, resp_two[:, 0], 0.0)  7.09 us
    dot_general x8, matrix products, triangle(): jnp.einsum('ab,bxy->axy', stiffness, values, precision=lax.Precision.HIGH...  6.06 us
    slice x10, local copies, waits for them, and re-layouts, triangle(): plane[comp]  5.63 us
  transfers between devices with their start and end apart: 21, of which 8 were waited for; matrix products, arithmetic and copies ran while one was open for 9% of the time, Pallas kernels for 0%

profile of v1, /device:TPU:225, one launch (start us, length us, event | category | flops | bytes accessed | tf_op | source)
XLA Modules:
  0.0 140.6 jit_solution(4457158396675752550)
XLA Ops:
  1.4 5.3 %collective-permute-start = (f32[3,1,256]{2,1,0:T(1,128)S(1)}, f32[3,1,256]{2,1,0:T(1,128)S(1)}, u32[]{:S(2)}, u32[]{:S(2)}) collective-permute-start(f32[3,1,256]{2,1,0:T(1,128)S(1)} %get-tuple-element.72), channel_id=1, source_target_pairs={{0,16},{16,32},{32,48},{48,64},{64,80},{80,96},{96,112},{112,128},... | collective-permute-start | bytes 9224 | tf_op jit(solution)/shard_map/ppermute | solution.py:14
  6.7 1.9 %collective-permute-start.1 = (f32[3,1,256]{2,1,0:T(1,128)S(1)}, f32[3,1,256]{2,1,0:T(1,128)S(1)}, u32[]{:S(2)}, u32[]{:S(2)}) collective-permute-start(f32[3,1,256]{2,1,0:T(1,128)S(1)} %get-tuple-element.73), channel_id=1, source_target_pairs={{16,0},{32,16},{48,32},{64,48},{80,64},{96,80},{112,96},{128,112},... | collective-permute-start | bytes 9224 | tf_op jit(solution)/shard_map/ppermute | solution.py:15
  10.0 2.2 %fusion.5 = f32[1152,2]{0,1:T(2,128)S(1)} fusion(f32[2,64,256]{2,1,0:T(8,128)} %param.11, pred[1152,256]{0,1:T(8,128)(4,1)S(1)} %iota_compare_fusion.1, s32[1152]{0:T(1024)S(1)} %get-tuple-element.196), kind=kOutput, calls=%fused_computation.7 | convolution fusion | flops 454235904 | bytes 439808 | tf_op jit(solution)/shard_map/sr,krc->ksc/dot_general | solution.py:33
  12.3 5.0 %collective-permute-start.4 = (f32[2,1,3,128]{3,2,1,0:T(4,128)S(1)}, f32[2,1,3,128]{3,2,1,0:T(4,128)S(1)}, u32[]{:S(2)}, u32[]{:S(2)}) collective-permute-start(f32[2,1,3,128]{3,2,1,0:T(4,128)S(1)} %get-tuple-element.181), channel_id=1, source_target_pairs={{0,16},{16,32},{32,48},{48,64},{64,80},{80,96},{96,112},{112,128},... | collective-permute-start | bytes 9224 | tf_op jit(solution)/shard_map/ppermute | solution.py:14
  17.3 1.9 %collective-permute-start.5 = (f32[2,1,3,128]{3,2,1,0:T(4,128)S(1)}, f32[2,1,3,128]{3,2,1,0:T(4,128)S(1)}, u32[]{:S(2)}, u32[]{:S(2)}) collective-permute-start(f32[2,1,3,128]{3,2,1,0:T(4,128)S(1)} %get-tuple-element.180), channel_id=1, source_target_pairs={{16,0},{32,16},{48,32},{64,48},{80,64},{96,80},{112,96},{128,112},... | collective-permute-start | bytes 9224 | tf_op jit(solution)/shard_map/ppermute | solution.py:15
  20.1 3.2 %collective-permute-start.2 = (f32[3,66,1]{2,1,0:T(8,128)S(1)}, f32[3,66,1]{2,1,0:T(8,128)S(1)}, u32[]{:S(2)}, u32[]{:S(2)}) collective-permute-start(f32[3,66,1]{2,1,0:T(8,128)S(1)} %get-tuple-element.70), channel_id=1, source_target_pairs={{0,4},{4,8},{8,12},{1,5},{5,9},{9,13},{2,6},{6,10},{10,14},{3,7},{... | collective-permute-start | bytes 2384 | tf_op jit(solution)/shard_map/ppermute | solution.py:14
  24.7 4.0 %collective-permute-start.6 = (f32[2,5,1,128]{3,2,1,0:T(1,128)S(1)}, f32[2,5,1,128]{3,2,1,0:T(1,128)S(1)}, u32[]{:S(2)}, u32[]{:S(2)}) collective-permute-start(f32[2,5,1,128]{3,2,1,0:T(1,128)S(1)} %get-tuple-element.176), channel_id=1, source_target_pairs={{0,4},{4,8},{8,12},{1,5},{5,9},{9,13},{2,6},{6,10},{10,14},{3,7},{... | collective-permute-start | bytes 15368 | tf_op jit(solution)/shard_map/ppermute | solution.py:14
  30.3 2.8 %collective-permute-done.7 = f32[2,5,1,128]{3,2,1,0:T(1,128)S(1)} collective-permute-done((f32[2,5,1,128]{3,2,1,0:T(1,128)S(1)}, f32[2,5,1,128]{3,2,1,0:T(1,128)S(1)}, u32[]{:S(2)}, u32[]{:S(2)}) %collective-permute-start.7) | collective-permute-done | bytes 5152 | tf_op jit(solution)/shard_map/ppermute | solution.py:15
  33.4 1.3 fusion.27
  35.0 6.8 %collective-permute-start.8 = (f32[13,1,256]{2,0,1:T(8,128)S(1)}, f32[13,1,256]{2,0,1:T(8,128)S(1)}, u32[]{:S(2)}, u32[]{:S(2)}) collective-permute-start(f32[13,1,256]{2,0,1:T(8,128)S(1)} %get-tuple-element.60), channel_id=1, source_target_pairs={{0,16},{16,32},{32,48},{48,64},{64,80},{80,96},{96,112},{112,128},... | collective-permute-start | bytes 39944 | tf_op jit(solution)/shard_map/ppermute | solution.py:14
  41.8 1.9 %collective-permute-start.9 = (f32[13,1,256]{2,0,1:T(8,128)S(1)}, f32[13,1,256]{2,0,1:T(8,128)S(1)}, u32[]{:S(2)}, u32[]{:S(2)}) collective-permute-start(f32[13,1,256]{2,0,1:T(8,128)S(1)} %get-tuple-element.61), channel_id=1, source_target_pairs={{16,0},{32,16},{48,32},{64,48},{80,64},{96,80},{112,96},{128,112},... | collective-permute-start | bytes 39944 | tf_op jit(solution)/shard_map/ppermute | solution.py:15
  43.8 4.3 %collective-permute-done.9 = f32[13,1,256]{2,0,1:T(8,128)S(1)} collective-permute-done((f32[13,1,256]{2,0,1:T(8,128)S(1)}, f32[13,1,256]{2,0,1:T(8,128)S(1)}, u32[]{:S(2)}, u32[]{:S(2)}) %collective-permute-start.9) | collective-permute-done | bytes 13344 | tf_op jit(solution)/shard_map/ppermute | solution.py:15
  48.2 3.2 %collective-permute-start.10 = (f32[13,18,1]{2,0,1:T(8,128)S(1)}, f32[13,18,1]{2,0,1:T(8,128)S(1)}, u32[]{:S(2)}, u32[]{:S(2)}) collective-permute-start(f32[13,18,1]{2,0,1:T(8,128)S(1)} %get-tuple-element.58), channel_id=1, source_target_pairs={{0,4},{4,8},{8,12},{1,5},{5,9},{9,13},{2,6},{6,10},{10,14},{3,7},{... | collective-permute-start | bytes 2816 | tf_op jit(solution)/shard_map/ppermute | solution.py:14
  53.5 3.8 %collective-permute-done.11 = f32[13,18,1]{2,0,1:T(8,128)S(1)} collective-permute-done((f32[13,18,1]{2,0,1:T(8,128)S(1)}, f32[13,18,1]{2,0,1:T(8,128)S(1)}, u32[]{:S(2)}, u32[]{:S(2)}) %collective-permute-start.11) | collective-permute-done | bytes 968 | tf_op jit(solution)/shard_map/ppermute | solution.py:15
  57.9 3.1 %collective-permute-start.12 = (f32[4,1,18,258]{3,0,2,1:T(4,128)S(1)}, f32[4,1,18,258]{3,0,2,1:T(4,128)S(1)}, u32[]{:S(2)}, u32[]{:S(2)}) collective-permute-start(f32[4,1,18,258]{3,0,2,1:T(4,128)S(1)} %copy.122), channel_id=1, source_target_pairs={{0,1},{1,2},{2,3},{4,5},{5,6},{6,7},{8,9},{9,10},{10,11},{12,13},{... | collective-permute-start | bytes 222920 | tf_op jit(solution)/shard_map/ppermute | solution.py:14
  62.9 1.5 %collective-permute-start.13 = (f32[4,1,18,258]{3,0,2,1:T(4,128)S(1)}, f32[4,1,18,258]{3,0,2,1:T(4,128)S(1)}, u32[]{:S(2)}, u32[]{:S(2)}) collective-permute-start(f32[4,1,18,258]{3,0,2,1:T(4,128)S(1)} %copy.123), channel_id=1, source_target_pairs={{1,0},{2,1},{3,2},{5,4},{6,5},{7,6},{9,8},{10,9},{11,10},{13,12},{... | collective-permute-start | bytes 222920 | tf_op jit(solution)/shard_map/ppermute | solution.py:15
  90.5 3.1 %stack.56 = f32[18,17,257]{2,0,1:T(8,128)S(1)} concatenate(f32[1,17,257]{2,0,1:T(1,128)} %get-tuple-element.138, f32[1,17,257]{2,0,1:T(1,128)} %get-tuple-element.137, f32[1,17,257]{2,0,1:T(1,128)S(1)} %copy-done.19, f32[1,17,257]{2,0,1:T(1,128)} %get-tuple-element.136, f32[1,17,257]{2,0,1:T(1,128)} %get-tuple-element.135, f32[1,17,257]{2,0,1:T(1,128)S(1)} %copy-done.17, ...), dimensions={0} | concatenate | bytes 629136 | tf_op jit(solution)/shard_map/stack | solution.py:85
  93.6 1.4 %fusion.8 = f32[18,17,257]{2,0,1:T(8,128)S(1)} fusion(f32[18,17,257]{2,0,1:T(8,128)S(1)} %stack.56, f32[17,257]{1,0:T(8,128)} %get-tuple-element.213, f32[18,18]{1,0:T(8,128)S(1)} %copy-done), kind=kOutput, calls=%fused_computation.12 | convolution fusion | flops 17065314 | bytes 647908 | tf_op jit(solution)/shard_map/ab,bxy->axy/dot_general | solution.py:92
  96.7 2.3 %stack.57 = f32[18,17,257]{2,0,1:T(8,128)S(1)} concatenate(f32[1,17,257]{2,0,1:T(1,128)S(1)} %copy-done.9, f32[1,17,257]{2,0,1:T(1,128)S(1)} %copy-done.27, f32[1,17,257]{2,0,1:T(1,128)S(1)} %copy-done.7, f32[1,17,257]{2,0,1:T(1,128)S(1)} %copy-done.11, f32[1,17,257]{2,0,1:T(1,128)S(1)} %get-tuple-element.113, f32[1,17,257]{2,0,1:T(1,128)S(1)} %get-tuple-element.112, ...), dimensions={0} | concatenate | bytes 629136 | tf_op jit(solution)/shard_map/stack | solution.py:85
  100.6 1.3 fusion.65
  101.9 1.3 fusion.73
  104.6 1.3 fusion.6
  105.9 5.3 %collective-permute-start.14 = (f32[2,9,128]{2,1,0:T(8,128)S(1)}, f32[2,9,128]{2,1,0:T(8,128)S(1)}, u32[]{:S(2)}, u32[]{:S(2)}) collective-permute-start(f32[2,9,128]{2,1,0:T(8,128)S(1)} %reshape.358), channel_id=1, source_target_pairs={{0,3},{1,0},{2,1},{3,2},{4,7},{5,4},{6,5},{7,6},{8,11},{9,8},{10,9... | collective-permute-start | bytes 27656 | tf_op jit(solution)/shard_map/ppermute | solution.py:48
  111.2 2.4 %collective-permute-start.15 = (f32[2,9,128]{2,1,0:T(8,128)S(1)}, f32[2,9,128]{2,1,0:T(8,128)S(1)}, u32[]{:S(2)}, u32[]{:S(2)}) collective-permute-start(f32[2,9,128]{2,1,0:T(8,128)S(1)} %reshape.358), channel_id=1, source_target_pairs={{0,2},{1,3},{2,0},{3,1},{4,6},{5,7},{6,4},{7,5},{8,10},{9,11},{10,... | collective-permute-start | bytes 27656 | tf_op jit(solution)/shard_map/ppermute | solution.py:48
  113.6 2.5 %collective-permute-start.16 = (f32[2,9,128]{2,1,0:T(8,128)S(1)}, f32[2,9,128]{2,1,0:T(8,128)S(1)}, u32[]{:S(2)}, u32[]{:S(2)}) collective-permute-start(f32[2,9,128]{2,1,0:T(8,128)S(1)} %reshape.358), channel_id=1, source_target_pairs={{0,1},{1,2},{2,3},{3,0},{4,5},{5,6},{6,7},{7,4},{8,9},{9,10},{10,1... | collective-permute-start | bytes 27656 | tf_op jit(solution)/shard_map/ppermute | solution.py:48
  117.2 2.3 %collective-permute-done.16 = f32[2,9,128]{2,1,0:T(8,128)S(1)} collective-permute-done((f32[2,9,128]{2,1,0:T(8,128)S(1)}, f32[2,9,128]{2,1,0:T(8,128)S(1)}, u32[]{:S(2)}, u32[]{:S(2)}) %collective-permute-start.16) | collective-permute-done | bytes 9248 | tf_op jit(solution)/shard_map/ppermute | solution.py:48
  119.5 5.5 %collective-permute-start.17 = (f32[2,1,3,128]{3,0,2,1:T(2,128)S(1)}, f32[2,1,3,128]{3,0,2,1:T(2,128)S(1)}, u32[]{:S(2)}, u32[]{:S(2)}) collective-permute-start(f32[2,1,3,128]{3,0,2,1:T(2,128)S(1)} %get-tuple-element.182), channel_id=1, source_target_pairs={{0,16},{16,32},{32,48},{48,64},{64,80},{80,96},{96,112},{112,128},... | collective-permute-start | bytes 9224 | tf_op jit(solution)/shard_map/ppermute | solution.py:14
  125.0 1.9 %collective-permute-start.18 = (f32[2,1,3,128]{3,0,2,1:T(2,128)S(1)}, f32[2,1,3,128]{3,0,2,1:T(2,128)S(1)}, u32[]{:S(2)}, u32[]{:S(2)}) collective-permute-start(f32[2,1,3,128]{3,0,2,1:T(2,128)S(1)} %get-tuple-element.183), channel_id=1, source_target_pairs={{16,0},{32,16},{48,32},{64,48},{80,64},{96,80},{112,96},{128,112},... | collective-permute-start | bytes 9224 | tf_op jit(solution)/shard_map/ppermute | solution.py:15
  127.2 4.0 %collective-permute-done.18 = f32[2,1,3,128]{3,0,2,1:T(2,128)S(1)} collective-permute-done((f32[2,1,3,128]{3,0,2,1:T(2,128)S(1)}, f32[2,1,3,128]{3,0,2,1:T(2,128)S(1)}, u32[]{:S(2)}, u32[]{:S(2)}) %collective-permute-start.18) | collective-permute-done | bytes 3104 | tf_op jit(solution)/shard_map/ppermute | solution.py:15
  131.1 2.9 %collective-permute-start.19 = (f32[2,5,1,128]{3,0,2,1:T(2,128)S(1)}, f32[2,5,1,128]{3,0,2,1:T(2,128)S(1)}, u32[]{:S(2)}, u32[]{:S(2)}) collective-permute-start(f32[2,5,1,128]{3,0,2,1:T(2,128)S(1)} %get-tuple-element.178), channel_id=1, source_target_pairs={{0,4},{4,8},{8,12},{1,5},{5,9},{9,13},{2,6},{6,10},{10,14},{3,7},{... | collective-permute-start | bytes 15368 | tf_op jit(solution)/shard_map/ppermute | solution.py:14
  136.2 2.2 %collective-permute-done.20 = f32[2,5,1,128]{3,0,2,1:T(2,128)S(1)} collective-permute-done((f32[2,5,1,128]{3,0,2,1:T(2,128)S(1)}, f32[2,5,1,128]{3,0,2,1:T(2,128)S(1)}, u32[]{:S(2)}, u32[]{:S(2)}) %collective-permute-start.20) | collective-permute-done | bytes 5152 | tf_op jit(solution)/shard_map/ppermute | solution.py:15
  138.4 2.1 %fusion.24 = f32[2,64,256]{2,1,0:T(8,128)} fusion(f32[2,1152]{1,0:T(2,128)S(1)} %bitcast.378, pred[1152,256]{0,1:T(8,128)(4,1)S(1)} %iota_compare_fusion.1, s32[1152]{0:T(1024)S(1)} %copy-done.76, f32[1,64,256]{2,1,0:T(8,128)S(1)} %fusion.41, f32[1,64,256]{2,1,0:T(8,128)S(1)} %fusion.47), kind=kOutput, calls=%fused_computation.34 | convolution fusion | flops 453713920 | bytes 570880 | tf_op jit(solution)/shard_map/sr,ksc->krc/dot_general | solution.py:39
  (303 shorter events, 43.5 us)
Async XLA Ops:
  0.6 73.6 %copy-start = (f32[18,18]{1,0:T(8,128)S(1)}, f32[18,18]{1,0:T(8,128)}, u32[]{:S(2)}) copy-start(f32[18,18]{1,0:T(8,128)} %param.19) | copy-start | bytes 3892
  1.4 18.6 %collective-permute-start = (f32[3,1,256]{2,1,0:T(1,128)S(1)}, f32[3,1,256]{2,1,0:T(1,128)S(1)}, u32[]{:S(2)}, u32[]{:S(2)}) collective-permute-start(f32[3,1,256]{2,1,0:T(1,128)S(1)} %get-tuple-element.72), channel_id=1, source_target_pairs={{0,16},{16,32},{32,48},{48,64},{64,80},{80,96},{96,112},{112,128},... | collective-permute-start | bytes 9224 | tf_op jit(solution)/shard_map/ppermute | solution.py:14
  6.7 13.3 %collective-permute-start.1 = (f32[3,1,256]{2,1,0:T(1,128)S(1)}, f32[3,1,256]{2,1,0:T(1,128)S(1)}, u32[]{:S(2)}, u32[]{:S(2)}) collective-permute-start(f32[3,1,256]{2,1,0:T(1,128)S(1)} %get-tuple-element.73), channel_id=1, source_target_pairs={{16,0},{32,16},{48,32},{64,48},{80,64},{96,80},{112,96},{128,112},... | collective-permute-start | bytes 9224 | tf_op jit(solution)/shard_map/ppermute | solution.py:15
  12.3 12.4 %collective-permute-start.4 = (f32[2,1,3,128]{3,2,1,0:T(4,128)S(1)}, f32[2,1,3,128]{3,2,1,0:T(4,128)S(1)}, u32[]{:S(2)}, u32[]{:S(2)}) collective-permute-start(f32[2,1,3,128]{3,2,1,0:T(4,128)S(1)} %get-tuple-element.181), channel_id=1, source_target_pairs={{0,16},{16,32},{32,48},{48,64},{64,80},{80,96},{96,112},{112,128},... | collective-permute-start | bytes 9224 | tf_op jit(solution)/shard_map/ppermute | solution.py:14
  17.3 7.4 %collective-permute-start.5 = (f32[2,1,3,128]{3,2,1,0:T(4,128)S(1)}, f32[2,1,3,128]{3,2,1,0:T(4,128)S(1)}, u32[]{:S(2)}, u32[]{:S(2)}) collective-permute-start(f32[2,1,3,128]{3,2,1,0:T(4,128)S(1)} %get-tuple-element.180), channel_id=1, source_target_pairs={{16,0},{32,16},{48,32},{64,48},{80,64},{96,80},{112,96},{128,112},... | collective-permute-start | bytes 9224 | tf_op jit(solution)/shard_map/ppermute | solution.py:15
  20.1 9.9 %collective-permute-start.2 = (f32[3,66,1]{2,1,0:T(8,128)S(1)}, f32[3,66,1]{2,1,0:T(8,128)S(1)}, u32[]{:S(2)}, u32[]{:S(2)}) collective-permute-start(f32[3,66,1]{2,1,0:T(8,128)S(1)} %get-tuple-element.70), channel_id=1, source_target_pairs={{0,4},{4,8},{8,12},{1,5},{5,9},{9,13},{2,6},{6,10},{10,14},{3,7},{... | collective-permute-start | bytes 2384 | tf_op jit(solution)/shard_map/ppermute | solution.py:14
  23.4 6.7 %collective-permute-start.3 = (f32[3,66,1]{2,1,0:T(8,128)S(1)}, f32[3,66,1]{2,1,0:T(8,128)S(1)}, u32[]{:S(2)}, u32[]{:S(2)}) collective-permute-start(f32[3,66,1]{2,1,0:T(8,128)S(1)} %get-tuple-element.71), channel_id=1, source_target_pairs={{4,0},{8,4},{12,8},{5,1},{9,5},{13,9},{6,2},{10,6},{14,10},{7,3},{... | collective-permute-start | bytes 2384 | tf_op jit(solution)/shard_map/ppermute | solution.py:15
  24.7 5.5 %collective-permute-start.6 = (f32[2,5,1,128]{3,2,1,0:T(1,128)S(1)}, f32[2,5,1,128]{3,2,1,0:T(1,128)S(1)}, u32[]{:S(2)}, u32[]{:S(2)}) collective-permute-start(f32[2,5,1,128]{3,2,1,0:T(1,128)S(1)} %get-tuple-element.176), channel_id=1, source_target_pairs={{0,4},{4,8},{8,12},{1,5},{5,9},{9,13},{2,6},{6,10},{10,14},{3,7},{... | collective-permute-start | bytes 15368 | tf_op jit(solution)/shard_map/ppermute | solution.py:14
  28.7 4.4 %collective-permute-start.7 = (f32[2,5,1,128]{3,2,1,0:T(1,128)S(1)}, f32[2,5,1,128]{3,2,1,0:T(1,128)S(1)}, u32[]{:S(2)}, u32[]{:S(2)}) collective-permute-start(f32[2,5,1,128]{3,2,1,0:T(1,128)S(1)} %get-tuple-element.177), channel_id=1, source_target_pairs={{4,0},{8,4},{12,8},{5,1},{9,5},{13,9},{6,2},{10,6},{14,10},{7,3},{... | collective-permute-start | bytes 15368 | tf_op jit(solution)/shard_map/ppermute | solution.py:15
  35.0 8.8 %collective-permute-start.8 = (f32[13,1,256]{2,0,1:T(8,128)S(1)}, f32[13,1,256]{2,0,1:T(8,128)S(1)}, u32[]{:S(2)}, u32[]{:S(2)}) collective-permute-start(f32[13,1,256]{2,0,1:T(8,128)S(1)} %get-tuple-element.60), channel_id=1, source_target_pairs={{0,16},{16,32},{32,48},{48,64},{64,80},{80,96},{96,112},{112,128},... | collective-permute-start | bytes 39944 | tf_op jit(solution)/shard_map/ppermute | solution.py:14
  41.8 6.3 %collective-permute-start.9 = (f32[13,1,256]{2,0,1:T(8,128)S(1)}, f32[13,1,256]{2,0,1:T(8,128)S(1)}, u32[]{:S(2)}, u32[]{:S(2)}) collective-permute-start(f32[13,1,256]{2,0,1:T(8,128)S(1)} %get-tuple-element.61), channel_id=1, source_target_pairs={{16,0},{32,16},{48,32},{64,48},{80,64},{96,80},{112,96},{128,112},... | collective-permute-start | bytes 39944 | tf_op jit(solution)/shard_map/ppermute | solution.py:15
  48.2 5.3 %collective-permute-start.10 = (f32[13,18,1]{2,0,1:T(8,128)S(1)}, f32[13,18,1]{2,0,1:T(8,128)S(1)}, u32[]{:S(2)}, u32[]{:S(2)}) collective-permute-start(f32[13,18,1]{2,0,1:T(8,128)S(1)} %get-tuple-element.58), channel_id=1, source_target_pairs={{0,4},{4,8},{8,12},{1,5},{5,9},{9,13},{2,6},{6,10},{10,14},{3,7},{... | collective-permute-start | bytes 2816 | tf_op jit(solution)/shard_map/ppermute | solution.py:14
  51.5 5.9 %collective-permute-start.11 = (f32[13,18,1]{2,0,1:T(8,128)S(1)}, f32[13,18,1]{2,0,1:T(8,128)S(1)}, u32[]{:S(2)}, u32[]{:S(2)}) collective-permute-start(f32[13,18,1]{2,0,1:T(8,128)S(1)} %get-tuple-element.59), channel_id=1, source_target_pairs={{4,0},{8,4},{12,8},{5,1},{9,5},{13,9},{6,2},{10,6},{14,10},{7,3},{... | collective-permute-start | bytes 2816 | tf_op jit(solution)/shard_map/ppermute | solution.py:15
  57.9 6.5 %collective-permute-start.12 = (f32[4,1,18,258]{3,0,2,1:T(4,128)S(1)}, f32[4,1,18,258]{3,0,2,1:T(4,128)S(1)}, u32[]{:S(2)}, u32[]{:S(2)}) collective-permute-start(f32[4,1,18,258]{3,0,2,1:T(4,128)S(1)} %copy.122), channel_id=1, source_target_pairs={{0,1},{1,2},{2,3},{4,5},{5,6},{6,7},{8,9},{9,10},{10,11},{12,13},{... | collective-permute-start | bytes 222920 | tf_op jit(solution)/shard_map/ppermute | solution.py:14
  62.2 16.0 %copy-start.36 = (f32[1,17,257]{2,0,1:T(1,128)}, f32[1,17,257]{2,0,1:T(1,128)S(1)}, u32[]{:S(2)}) copy-start(f32[1,17,257]{2,0,1:T(1,128)S(1)} %get-tuple-element.214) | copy-start | bytes 52432
  62.2 16.0 %copy-start.38 = (f32[1,17,257]{2,0,1:T(1,128)}, f32[1,17,257]{2,0,1:T(1,128)S(1)}, u32[]{:S(2)}) copy-start(f32[1,17,257]{2,0,1:T(1,128)S(1)} %get-tuple-element.215) | copy-start | bytes 52432
  62.2 16.0 %copy-start.40 = (f32[1,17,257]{2,0,1:T(1,128)}, f32[1,17,257]{2,0,1:T(1,128)S(1)}, u32[]{:S(2)}) copy-start(f32[1,17,257]{2,0,1:T(1,128)S(1)} %get-tuple-element.216) | copy-start | bytes 52432
  62.2 16.0 %copy-start.42 = (f32[1,17,257]{2,0,1:T(1,128)}, f32[1,17,257]{2,0,1:T(1,128)S(1)}, u32[]{:S(2)}) copy-start(f32[1,17,257]{2,0,1:T(1,128)S(1)} %get-tuple-element.217) | copy-start | bytes 52432
  62.2 16.0 %copy-start.44 = (f32[1,17,257]{2,0,1:T(1,128)}, f32[1,17,257]{2,0,1:T(1,128)S(1)}, u32[]{:S(2)}) copy-start(f32[1,17,257]{2,0,1:T(1,128)S(1)} %get-tuple-element.218) | copy-start | bytes 52432
  62.2 16.0 %copy-start.46 = (f32[1,17,257]{2,0,1:T(1,128)}, f32[1,17,257]{2,0,1:T(1,128)S(1)}, u32[]{:S(2)}) copy-start(f32[1,17,257]{2,0,1:T(1,128)S(1)} %get-tuple-element.220) | copy-start | bytes 52432
  62.3 18.3 %copy-start.34 = (f32[1,17,257]{2,0,1:T(1,128)}, f32[1,17,257]{2,0,1:T(1,128)S(1)}, u32[]{:S(2)}) copy-start(f32[1,17,257]{2,0,1:T(1,128)S(1)} %get-tuple-element.219) | copy-start | bytes 52432
  62.9 7.1 %collective-permute-start.13 = (f32[4,1,18,258]{3,0,2,1:T(4,128)S(1)}, f32[4,1,18,258]{3,0,2,1:T(4,128)S(1)}, u32[]{:S(2)}, u32[]{:S(2)}) collective-permute-start(f32[4,1,18,258]{3,0,2,1:T(4,128)S(1)} %copy.123), channel_id=1, source_target_pairs={{1,0},{2,1},{3,2},{5,4},{6,5},{7,6},{9,8},{10,9},{11,10},{13,12},{... | collective-permute-start | bytes 222920 | tf_op jit(solution)/shard_map/ppermute | solution.py:15
  69.9 14.7 %copy-start.16 = (f32[1,17,257]{2,0,1:T(1,128)}, f32[1,17,257]{2,0,1:T(1,128)S(1)}, u32[]{:S(2)}) copy-start(f32[1,17,257]{2,0,1:T(1,128)S(1)} %get-tuple-element.162) | copy-start | bytes 52432
  69.9 14.7 %copy-start.18 = (f32[1,17,257]{2,0,1:T(1,128)}, f32[1,17,257]{2,0,1:T(1,128)S(1)}, u32[]{:S(2)}) copy-start(f32[1,17,257]{2,0,1:T(1,128)S(1)} %get-tuple-element.163) | copy-start | bytes 52432
  71.4 16.0 %copy-start.6 = (f32[1,17,257]{2,0,1:T(1,128)}, f32[1,17,257]{2,0,1:T(1,128)S(1)}, u32[]{:S(2)}) copy-start(f32[1,17,257]{2,0,1:T(1,128)S(1)} %get-tuple-element.114) | copy-start | bytes 52432
  105.9 10.4 %collective-permute-start.14 = (f32[2,9,128]{2,1,0:T(8,128)S(1)}, f32[2,9,128]{2,1,0:T(8,128)S(1)}, u32[]{:S(2)}, u32[]{:S(2)}) collective-permute-start(f32[2,9,128]{2,1,0:T(8,128)S(1)} %reshape.358), channel_id=1, source_target_pairs={{0,3},{1,0},{2,1},{3,2},{4,7},{5,4},{6,5},{7,6},{8,11},{9,8},{10,9... | collective-permute-start | bytes 27656 | tf_op jit(solution)/shard_map/ppermute | solution.py:48
  111.2 6.0 %collective-permute-start.15 = (f32[2,9,128]{2,1,0:T(8,128)S(1)}, f32[2,9,128]{2,1,0:T(8,128)S(1)}, u32[]{:S(2)}, u32[]{:S(2)}) collective-permute-start(f32[2,9,128]{2,1,0:T(8,128)S(1)} %reshape.358), channel_id=1, source_target_pairs={{0,2},{1,3},{2,0},{3,1},{4,6},{5,7},{6,4},{7,5},{8,10},{9,11},{10,... | collective-permute-start | bytes 27656 | tf_op jit(solution)/shard_map/ppermute | solution.py:48
  113.6 5.8 %collective-permute-start.16 = (f32[2,9,128]{2,1,0:T(8,128)S(1)}, f32[2,9,128]{2,1,0:T(8,128)S(1)}, u32[]{:S(2)}, u32[]{:S(2)}) collective-permute-start(f32[2,9,128]{2,1,0:T(8,128)S(1)} %reshape.358), channel_id=1, source_target_pairs={{0,1},{1,2},{2,3},{3,0},{4,5},{5,6},{6,7},{7,4},{8,9},{9,10},{10,1... | collective-permute-start | bytes 27656 | tf_op jit(solution)/shard_map/ppermute | solution.py:48
  119.5 7.6 %collective-permute-start.17 = (f32[2,1,3,128]{3,0,2,1:T(2,128)S(1)}, f32[2,1,3,128]{3,0,2,1:T(2,128)S(1)}, u32[]{:S(2)}, u32[]{:S(2)}) collective-permute-start(f32[2,1,3,128]{3,0,2,1:T(2,128)S(1)} %get-tuple-element.182), channel_id=1, source_target_pairs={{0,16},{16,32},{32,48},{48,64},{64,80},{80,96},{96,112},{112,128},... | collective-permute-start | bytes 9224 | tf_op jit(solution)/shard_map/ppermute | solution.py:14
  125.0 6.1 %collective-permute-start.18 = (f32[2,1,3,128]{3,0,2,1:T(2,128)S(1)}, f32[2,1,3,128]{3,0,2,1:T(2,128)S(1)}, u32[]{:S(2)}, u32[]{:S(2)}) collective-permute-start(f32[2,1,3,128]{3,0,2,1:T(2,128)S(1)} %get-tuple-element.183), channel_id=1, source_target_pairs={{16,0},{32,16},{48,32},{64,48},{80,64},{96,80},{112,96},{128,112},... | collective-permute-start | bytes 9224 | tf_op jit(solution)/shard_map/ppermute | solution.py:15
  131.1 5.0 %collective-permute-start.19 = (f32[2,5,1,128]{3,0,2,1:T(2,128)S(1)}, f32[2,5,1,128]{3,0,2,1:T(2,128)S(1)}, u32[]{:S(2)}, u32[]{:S(2)}) collective-permute-start(f32[2,5,1,128]{3,0,2,1:T(2,128)S(1)} %get-tuple-element.178), channel_id=1, source_target_pairs={{0,4},{4,8},{8,12},{1,5},{5,9},{9,13},{2,6},{6,10},{10,14},{3,7},{... | collective-permute-start | bytes 15368 | tf_op jit(solution)/shard_map/ppermute | solution.py:14
  134.0 4.4 %collective-permute-start.20 = (f32[2,5,1,128]{3,0,2,1:T(2,128)S(1)}, f32[2,5,1,128]{3,0,2,1:T(2,128)S(1)}, u32[]{:S(2)}, u32[]{:S(2)}) collective-permute-start(f32[2,5,1,128]{3,0,2,1:T(2,128)S(1)} %get-tuple-element.179), channel_id=1, source_target_pairs={{4,0},{8,4},{12,8},{5,1},{9,5},{13,9},{6,2},{10,6},{14,10},{7,3},{... | collective-permute-start | bytes 15368 | tf_op jit(solution)/shard_map/ppermute | solution.py:15
  (70 other events, 203.4 us)

commit v2 on v1

--- a/solution.py
+++ b/solution.py
@@ -2,6 +2,106 @@
 import jax.numpy as jnp
 from jax import lax
 from jax.sharding import PartitionSpec as P
+from jax.experimental import pallas as pl
+from jax.experimental.pallas import tpu as pltpu
+
+ROWS_PAD, LANES_PAD = 24, 384
+
+
+def fem_kernel(fld_ref, main_ref, weight_ref, kmat_ref, live_ref, body_ref, out_ref, vals_ref, vis_ref, resp_ref):
+    main = main_ref[...] > 0.5
+    weight = weight_ref[...]
+    zero = jnp.zeros((ROWS_PAD, LANES_PAD), jnp.float32)
+    out_ref[...] = -body_ref[...]
+    pairs = fld_ref.shape[1] - 1
+    for pair in range(pairs):
+        vis_parts = [[], []]
+        for height in range(2):
+            layer = pair + height
+            for comp in range(4):
+                plane = fld_ref[comp, layer]
+                below = pltpu.roll(plane, ROWS_PAD - 1, 0)
+                right = pltpu.roll(plane, LANES_PAD - 1, 1)
+                diag = pltpu.roll(below, LANES_PAD - 1, 1)
+                far = jnp.where(main, diag, right)
+                near = jnp.where(main, plane, below)
+                if comp < 3:
+                    base = height * 9 + comp * 3
+                    vals_ref[0, base] = plane
+                    vals_ref[0, base + 1] = below
+                    vals_ref[0, base + 2] = far
+                    vals_ref[1, base] = near
+                    vals_ref[1, base + 1] = diag
+                    vals_ref[1, base + 2] = right
+                else:
+                    vis_parts[0] += [plane, below, far]
+                    vis_parts[1] += [near, diag, right]
+        for tri in range(2):
+            total = vis_parts[tri][0]
+            for term in vis_parts[tri][1:]:
+                total = total + term
+            vis_ref[tri] = total / 6.0 * weight
+
+        def tile_body(tile, carry):
+            row = pl.multiple_of((tile // 3) * 8, 8)
+            lane = pl.multiple_of((tile % 3) * 128, 128)
+            for tri in range(2):
+                vals = [vals_ref[tri, beta, pl.ds(row, 8), pl.ds(lane, 128)] for beta in range(18)]
+                vis = vis_ref[tri, pl.ds(row, 8), pl.ds(lane, 128)]
+                for alpha in range(18):
+                    acc = kmat_ref[alpha, 0] * vals[0]
+                    for beta in range(1, 18):
+                        acc = acc + kmat_ref[alpha, beta] * vals[beta]
+                    resp_ref[tri, alpha, pl.ds(row, 8), pl.ds(lane, 128)] = acc * vis
+            return carry
+
+        lax.fori_loop(0, 9, tile_body, 0)
+        for height in range(2):
+            own_layer = pair + height - 1
+            if own_layer < 0 or own_layer > pairs - 2:
+                continue
+            scale = None
+            if pair == 0 and height == 1:
+                scale = live_ref[0]
+            if pair == pairs - 1 and height == 0:
+                scale = live_ref[1]
+            for comp in range(3):
+                base = height * 9 + comp * 3
+                one = [resp_ref[0, base + v] for v in range(3)]
+                two = [resp_ref[1, base + v] for v in range(3)]
+                corner_a = one[0] + jnp.where(main, two[0], zero)
+                corner_b = one[1] + jnp.where(main, zero, two[0])
+                corner_c = two[2] + jnp.where(main, zero, one[2])
+                corner_d = two[1] + jnp.where(main, one[2], zero)
+                node = (pltpu.roll(pltpu.roll(corner_a, ROWS_PAD - 1, 0), LANES_PAD - 1, 1)
+                        + pltpu.roll(corner_b, LANES_PAD - 1, 1)
+                        + pltpu.roll(corner_c, ROWS_PAD - 1, 0) + corner_d)
+                part = node[0:16, 0:256]
+                if scale is not None:
+                    part = part * scale
+                out_ref[comp, own_layer] = out_ref[comp, own_layer] + part
+
+
+def fem_pallas(extended_layers, flag_cells, weight, element_matrix, below_live, above_live, body_force):
+    comps, layers, rows, lanes = extended_layers.shape
+    fld = jnp.pad(extended_layers, ((0, 0), (0, 0), (0, ROWS_PAD - rows), (0, LANES_PAD - lanes)))
+    cell_rows, cell_lanes = flag_cells.shape
+    main = jnp.pad((flag_cells == 0).astype(jnp.float32), ((0, ROWS_PAD - cell_rows), (0, LANES_PAD - cell_lanes)))
+    wpad = jnp.pad(weight, ((0, ROWS_PAD - cell_rows), (0, LANES_PAD - cell_lanes)))
+    live = jnp.stack([below_live, above_live]).astype(jnp.float32)
+    return pl.pallas_call(
+        fem_kernel,
+        out_shape=jax.ShapeDtypeStruct(body_force.shape, jnp.float32),
+        in_specs=[pl.BlockSpec(memory_space=pltpu.VMEM)] * 3
+        + [pl.BlockSpec(memory_space=pltpu.SMEM)] * 2
+        + [pl.BlockSpec(memory_space=pltpu.VMEM)],
+        out_specs=pl.BlockSpec(memory_space=pltpu.VMEM),
+        scratch_shapes=[
+            pltpu.VMEM((2, 18, ROWS_PAD, LANES_PAD), jnp.float32),
+            pltpu.VMEM((2, ROWS_PAD, LANES_PAD), jnp.float32),
+            pltpu.VMEM((2, 18, ROWS_PAD, LANES_PAD), jnp.float32),
+        ],
+    )(fld, main, wpad, element_matrix, live, body_force)
 
 
 def with_halo(array, sides, width):
@@ -206,25 +306,9 @@
     below_live = (layer_index > 0).astype(jnp.float32)
     above_live = (layer_index < layer_count - 1).astype(jnp.float32)
     extended_layers = with_halo(field_ext, (("layer", 1),), 1)
-    collected = [None for height in range(depth_count)]
-    for height in range(depth_count + 1):
-        lower_part, upper_part = cell_terms(
-            extended_layers[:, height],
-            extended_layers[:, height + 1],
-            flag_cells,
-            element_matrix,
-            weight,
-        )
-        if height > 0:
-            if height == depth_count:
-                lower_part = scaled_by(lower_part, above_live)
-            collected[height - 1] = add_corners(collected[height - 1], lower_part)
-        if height < depth_count:
-            if height == 0:
-                upper_part = scaled_by(upper_part, below_live)
-            collected[height] = add_corners(collected[height], upper_part)
-    owned = [own_nodes(corners) for corners in collected]
-    stokes_residual = jnp.stack(owned, axis=1) - body_force
+    stokes_residual = fem_pallas(
+        extended_layers, flag_cells, weight, element_matrix, below_live, above_live, body_force
+    )
     depth_sum = jnp.sum(stokes_residual[:2], axis=1)
     bucket = gather_slots(depth_sum, col_row, col_col).reshape(2, 9, slot_count)
     depth_total = layer_total(bucket)

time: 142 us -> 119 us (0.84)
  local copies, waits for them, and re-layouts: 28.7 us -> 0.63 us
  Pallas kernels: 0 us -> 12.9 us
  matrix products: 13.3 us -> 7.26 us
  waiting for transfers between devices: 20.8 us -> 26.2 us
  other arithmetic: 11.6 us -> 7.3 us
    pallas_call x0 -> x1, Pallas kernels: none -> 12.9 us  [fem_pallas(): pl.pallas_call(fem_kernel, out_shape=jax.ShapeDtypeStruct(body_force.shap...]
    another operation x8 -> x0, local copies, waits for them, and re-layouts: 10.3 us -> none  [triangle(): jnp.stack([plane[comp] for group in (lows, ups) for comp in range(3) for...]
    slice x33 -> x0, local copies, waits for them, and re-layouts: 7.72 us -> none  [the longest x10 5.63 us: triangle(): plane[comp]]
    squeeze x12 -> x0, local copies, waits for them, and re-layouts: 7.09 us -> none  [cell_terms(): corner_a = resp_one[:, 0] + jnp.where(main_diag, resp_two[:, 0], 0.0)]
    dot_general x8 -> x0, matrix products: 6.06 us -> none  [triangle(): jnp.einsum('ab,bxy->axy', stiffness, values, precision=lax.Precision.HIGH...]
    ppermute x9, waiting for transfers between devices: 17.2 us -> 21.9 us  [with_halo(): after = lax.ppermute(initial, axis, down)]
    mul x4 -> x0, other arithmetic: 3.45 us -> none  [triangle(): (lows[0][3] + lows[1][3] + lows[2][3] + ups[0][3] + ups[1][3] + ups[2][3]...]
    another operation x3 -> x1, other arithmetic: 3.89 us -> 0.67 us  [fem_pallas(): live = jnp.stack([below_live, above_live]).astype(jnp.float32)]
  transfers between devices with their start and end apart: 21 -> 21, of which waited for: 8 -> 9; matrix products, arithmetic and copies ran while one was open for 9% -> 6% of each run, Pallas kernels for 0% -> 0%
where the time goes in v2:
time: 119 us; the launch traced here: 118 us
  starting transfers between devices  62.6 us (53%)
  waiting for transfers between devices  26.2 us (22%)
  Pallas kernels  12.9 us (11%)
  other arithmetic  7.3 us (6%)
  matrix products  7.26 us (6%)
  between operations  1.3 us (1%)
    ppermute x9, starting transfers between devices, with_halo(): before = lax.ppermute(last, axis, up)  39.5 us
    ppermute x9, waiting for transfers between devices, with_halo(): after = lax.ppermute(initial, axis, down)  21.9 us
    ppermute x9, starting transfers between devices, with_halo(): after = lax.ppermute(initial, axis, down)  14.1 us
    pallas_call x1, Pallas kernels, fem_pallas(): pl.pallas_call(fem_kernel, out_shape=jax.ShapeDtypeStruct(body_force.shap...  12.9 us
    ppermute x3, starting transfers between devices, layer_total(): received.append(lax.ppermute(part, 'layer', pairs))  9.02 us
    dot_general x2, matrix products, gather_slots(): rows_taken = jnp.einsum('sr,krc->ksc', pick_row, field, precision=HIGH)  3.55 us
    dot_general x2, matrix products, scatter_slots(): return jnp.einsum('sr,ksc->krc', pick_row, spread, precision=HIGH)  3.43 us
    ppermute x3, waiting for transfers between devices, layer_total(): received.append(lax.ppermute(part, 'layer', pairs))  3.24 us
  transfers between devices with their start and end apart: 21, of which 9 were waited for; matrix products, arithmetic and copies ran while one was open for 6% of the time, Pallas kernels for 0%

profile of v2, /device:TPU:225, one launch (start us, length us, event | category | flops | bytes accessed | tf_op | source)
XLA Modules:
  0.0 118.2 jit_solution(10144943202733922109)
XLA Ops:
  1.4 5.3 %collective-permute-start = (f32[3,1,256]{2,1,0:T(1,128)S(1)}, f32[3,1,256]{2,1,0:T(1,128)S(1)}, u32[]{:S(2)}, u32[]{:S(2)}) collective-permute-start(f32[3,1,256]{2,1,0:T(1,128)S(1)} %get-tuple-element.17), channel_id=1, source_target_pairs={{0,16},{16,32},{32,48},{48,64},{64,80},{80,96},{96,112},{112,128},... | collective-permute-start | bytes 9224 | tf_op jit(solution)/shard_map/ppermute | solution.py:114
  6.7 1.9 %collective-permute-start.1 = (f32[3,1,256]{2,1,0:T(1,128)S(1)}, f32[3,1,256]{2,1,0:T(1,128)S(1)}, u32[]{:S(2)}, u32[]{:S(2)}) collective-permute-start(f32[3,1,256]{2,1,0:T(1,128)S(1)} %get-tuple-element.18), channel_id=1, source_target_pairs={{16,0},{32,16},{48,32},{64,48},{80,64},{96,80},{112,96},{128,112},... | collective-permute-start | bytes 9224 | tf_op jit(solution)/shard_map/ppermute | solution.py:115
  9.6 2.2 %fusion.5 = f32[1152,2]{0,1:T(2,128)S(1)} fusion(f32[2,64,256]{2,1,0:T(8,128)} %param.11, pred[1152,256]{0,1:T(8,128)(4,1)S(1)} %iota_compare_fusion.1, s32[1152]{0:T(1024)S(1)} %get-tuple-element.31), kind=kOutput, calls=%fused_computation.7 | convolution fusion | flops 454235904 | bytes 439808 | tf_op jit(solution)/shard_map/sr,krc->ksc/dot_general | solution.py:133
  11.9 5.0 %collective-permute-start.4 = (f32[2,1,3,128]{3,2,1,0:T(4,128)S(1)}, f32[2,1,3,128]{3,2,1,0:T(4,128)S(1)}, u32[]{:S(2)}, u32[]{:S(2)}) collective-permute-start(f32[2,1,3,128]{3,2,1,0:T(4,128)S(1)} %get-tuple-element.26), channel_id=1, source_target_pairs={{0,16},{16,32},{32,48},{48,64},{64,80},{80,96},{96,112},{112,128},... | collective-permute-start | bytes 9224 | tf_op jit(solution)/shard_map/ppermute | solution.py:114
  16.9 1.9 %collective-permute-start.5 = (f32[2,1,3,128]{3,2,1,0:T(4,128)S(1)}, f32[2,1,3,128]{3,2,1,0:T(4,128)S(1)}, u32[]{:S(2)}, u32[]{:S(2)}) collective-permute-start(f32[2,1,3,128]{3,2,1,0:T(4,128)S(1)} %get-tuple-element.25), channel_id=1, source_target_pairs={{16,0},{32,16},{48,32},{64,48},{80,64},{96,80},{112,96},{128,112},... | collective-permute-start | bytes 9224 | tf_op jit(solution)/shard_map/ppermute | solution.py:115
  20.9 3.2 %collective-permute-start.2 = (f32[3,66,1]{2,1,0:T(8,128)S(1)}, f32[3,66,1]{2,1,0:T(8,128)S(1)}, u32[]{:S(2)}, u32[]{:S(2)}) collective-permute-start(f32[3,66,1]{2,1,0:T(8,128)S(1)} %get-tuple-element.13), channel_id=1, source_target_pairs={{0,4},{4,8},{8,12},{1,5},{5,9},{9,13},{2,6},{6,10},{10,14},{3,7},{... | collective-permute-start | bytes 2384 | tf_op jit(solution)/shard_map/ppermute | solution.py:114
  24.1 1.3 %collective-permute-start.3 = (f32[3,66,1]{2,1,0:T(8,128)S(1)}, f32[3,66,1]{2,1,0:T(8,128)S(1)}, u32[]{:S(2)}, u32[]{:S(2)}) collective-permute-start(f32[3,66,1]{2,1,0:T(8,128)S(1)} %get-tuple-element.14), channel_id=1, source_target_pairs={{4,0},{8,4},{12,8},{5,1},{9,5},{13,9},{6,2},{10,6},{14,10},{7,3},{... | collective-permute-start | bytes 2384 | tf_op jit(solution)/shard_map/ppermute | solution.py:115
  25.5 4.0 %collective-permute-start.6 = (f32[2,5,1,128]{3,2,1,0:T(1,128)S(1)}, f32[2,5,1,128]{3,2,1,0:T(1,128)S(1)}, u32[]{:S(2)}, u32[]{:S(2)}) collective-permute-start(f32[2,5,1,128]{3,2,1,0:T(1,128)S(1)} %get-tuple-element.21), channel_id=1, source_target_pairs={{0,4},{4,8},{8,12},{1,5},{5,9},{9,13},{2,6},{6,10},{10,14},{3,7},{... | collective-permute-start | bytes 15368 | tf_op jit(solution)/shard_map/ppermute | solution.py:114
  29.5 1.3 %collective-permute-start.7 = (f32[2,5,1,128]{3,2,1,0:T(1,128)S(1)}, f32[2,5,1,128]{3,2,1,0:T(1,128)S(1)}, u32[]{:S(2)}, u32[]{:S(2)}) collective-permute-start(f32[2,5,1,128]{3,2,1,0:T(1,128)S(1)} %get-tuple-element.22), channel_id=1, source_target_pairs={{4,0},{8,4},{12,8},{5,1},{9,5},{13,9},{6,2},{10,6},{14,10},{7,3},{... | collective-permute-start | bytes 15368 | tf_op jit(solution)/shard_map/ppermute | solution.py:115
  31.0 2.8 %collective-permute-done.7 = f32[2,5,1,128]{3,2,1,0:T(1,128)S(1)} collective-permute-done((f32[2,5,1,128]{3,2,1,0:T(1,128)S(1)}, f32[2,5,1,128]{3,2,1,0:T(1,128)S(1)}, u32[]{:S(2)}, u32[]{:S(2)}) %collective-permute-start.7) | collective-permute-done | bytes 5152 | tf_op jit(solution)/shard_map/ppermute | solution.py:115
  34.2 1.3 %fusion.19 = f32[2,16,256]{2,1,0:T(8,128)S(1)} fusion(f32[2,1152]{1,0:T(2,128)S(1)} %broadcast_in_dim.104, pred[1152,256]{0,1:T(8,128)(4,1)S(1)} %iota_compare_fusion, s32[1152]{0:T(1024)S(1)} %get-tuple-element.29), kind=kOutput, calls=%fused_computation.19 | convolution fusion | flops 113854464 | bytes 341504 | tf_op jit(solution)/shard_map/sr,ksc->krc/dot_general | solution.py:139
  35.6 6.8 %collective-permute-start.8 = (f32[13,1,256]{2,1,0:T(1,128)S(1)}, f32[13,1,256]{2,1,0:T(1,128)S(1)}, u32[]{:S(2)}, u32[]{:S(2)}) collective-permute-start(f32[13,1,256]{2,1,0:T(1,128)S(1)} %get-tuple-element.15), channel_id=1, source_target_pairs={{0,16},{16,32},{32,48},{48,64},{64,80},{80,96},{96,112},{112,128},... | collective-permute-start | bytes 39944 | tf_op jit(solution)/shard_map/ppermute | solution.py:114
  42.4 1.9 %collective-permute-start.9 = (f32[13,1,256]{2,1,0:T(1,128)S(1)}, f32[13,1,256]{2,1,0:T(1,128)S(1)}, u32[]{:S(2)}, u32[]{:S(2)}) collective-permute-start(f32[13,1,256]{2,1,0:T(1,128)S(1)} %get-tuple-element.16), channel_id=1, source_target_pairs={{16,0},{32,16},{48,32},{64,48},{80,64},{96,80},{112,96},{128,112},... | collective-permute-start | bytes 39944 | tf_op jit(solution)/shard_map/ppermute | solution.py:115
  44.4 4.3 %collective-permute-done.9 = f32[13,1,256]{2,1,0:T(1,128)S(1)} collective-permute-done((f32[13,1,256]{2,1,0:T(1,128)S(1)}, f32[13,1,256]{2,1,0:T(1,128)S(1)}, u32[]{:S(2)}, u32[]{:S(2)}) %collective-permute-start.9) | collective-permute-done | bytes 13344 | tf_op jit(solution)/shard_map/ppermute | solution.py:115
  48.8 3.2 %collective-permute-start.10 = (f32[13,18,1]{2,1,0:T(8,128)S(1)}, f32[13,18,1]{2,1,0:T(8,128)S(1)}, u32[]{:S(2)}, u32[]{:S(2)}) collective-permute-start(f32[13,18,1]{2,1,0:T(8,128)S(1)} %get-tuple-element.11), channel_id=1, source_target_pairs={{0,4},{4,8},{8,12},{1,5},{5,9},{9,13},{2,6},{6,10},{10,14},{3,7},{... | collective-permute-start | bytes 2816 | tf_op jit(solution)/shard_map/ppermute | solution.py:114
  52.1 1.3 %collective-permute-start.11 = (f32[13,18,1]{2,1,0:T(8,128)S(1)}, f32[13,18,1]{2,1,0:T(8,128)S(1)}, u32[]{:S(2)}, u32[]{:S(2)}) collective-permute-start(f32[13,18,1]{2,1,0:T(8,128)S(1)} %get-tuple-element.12), channel_id=1, source_target_pairs={{4,0},{8,4},{12,8},{5,1},{9,5},{13,9},{6,2},{10,6},{14,10},{7,3},{... | collective-permute-start | bytes 2816 | tf_op jit(solution)/shard_map/ppermute | solution.py:115
  54.3 3.8 %collective-permute-done.11 = f32[13,18,1]{2,1,0:T(8,128)S(1)} collective-permute-done((f32[13,18,1]{2,1,0:T(8,128)S(1)}, f32[13,18,1]{2,1,0:T(8,128)S(1)}, u32[]{:S(2)}, u32[]{:S(2)}) %collective-permute-start.11) | collective-permute-done | bytes 968 | tf_op jit(solution)/shard_map/ppermute | solution.py:115
  58.4 3.1 %collective-permute-start.12 = (f32[4,1,18,258]{3,2,1,0:T(8,128)S(1)}, f32[4,1,18,258]{3,2,1,0:T(8,128)S(1)}, u32[]{:S(2)}, u32[]{:S(2)}) collective-permute-start(f32[4,1,18,258]{3,2,1,0:T(8,128)S(1)} %get-tuple-element.6), channel_id=1, source_target_pairs={{0,1},{1,2},{2,3},{4,5},{5,6},{6,7},{8,9},{9,10},{10,11},{12,13},{... | collective-permute-start | bytes 222920 | tf_op jit(solution)/shard_map/ppermute | solution.py:114
  61.6 1.3 %collective-permute-start.13 = (f32[4,1,18,258]{3,2,1,0:T(8,128)S(1)}, f32[4,1,18,258]{3,2,1,0:T(8,128)S(1)}, u32[]{:S(2)}, u32[]{:S(2)}) collective-permute-start(f32[4,1,18,258]{3,2,1,0:T(8,128)S(1)} %get-tuple-element.7), channel_id=1, source_target_pairs={{1,0},{2,1},{3,2},{5,4},{6,5},{7,6},{9,8},{10,9},{11,10},{13,12},{... | collective-permute-start | bytes 222920 | tf_op jit(solution)/shard_map/ppermute | solution.py:115
  63.9 4.1 %collective-permute-done.13 = f32[4,1,18,258]{3,2,1,0:T(8,128)S(1)} collective-permute-done((f32[4,1,18,258]{3,2,1,0:T(8,128)S(1)}, f32[4,1,18,258]{3,2,1,0:T(8,128)S(1)}, u32[]{:S(2)}, u32[]{:S(2)}) %collective-permute-start.13) | collective-permute-done | bytes 74336 | tf_op jit(solution)/shard_map/ppermute | solution.py:115
  69.0 12.9 %shard_map.122 = f32[3,3,16,256]{3,2,1,0:T(8,128)} custom-call(f32[4,5,24,384]{3,2,1,0:T(8,128)} %select_maximum_fusion.fld_ref, f32[24,384]{1,0:T(8,128)} %pad_convert_fusion.1.main_ref, f32[24,384]{1,0:T(8,128)} %pad_convert_fusion.weight_ref, f32[18,18]{1,0:T(8,128)} %kmat_ref.1, f32[2]{0:T(128)} %add_convert_fusion.live_ref, f32[3,3,16,256]{3,2,1,0:T(8,128)} %body_ref.1), custom_call_target="tpu_custom_call" | custom-call | tf_op jit(solution)/shard_map/pallas_call | solution.py:92
  82.8 1.3 %fusion.6 = f32[2,1152]{1,0:T(2,128)S(1)} fusion(f32[2,16,256]{2,1,0:T(8,128)S(1)} %slice_reduce_fusion, pred[1152,256]{0,1:T(8,128)(4,1)S(1)} %iota_compare_fusion, s32[1152]{0:T(1024)S(1)} %get-tuple-element.29), kind=kOutput, calls=%fused_computation.8 | convolution fusion | flops 114441984 | bytes 341504 | tf_op jit(solution)/shard_map/sr,krc->ksc/dot_general | solution.py:133
  84.2 2.7 %collective-permute-start.14 = (f32[2,9,128]{2,1,0:T(8,128)S(1)}, f32[2,9,128]{2,1,0:T(8,128)S(1)}, u32[]{:S(2)}, u32[]{:S(2)}) collective-permute-start(f32[2,9,128]{2,1,0:T(8,128)S(1)} %reshape.196), channel_id=1, source_target_pairs={{0,3},{1,0},{2,1},{3,2},{4,7},{5,4},{6,5},{7,6},{8,11},{9,8},{10,9... | collective-permute-start | bytes 27656 | tf_op jit(solution)/shard_map/ppermute | solution.py:148
  86.9 4.1 %collective-permute-start.15 = (f32[2,9,128]{2,1,0:T(8,128)S(1)}, f32[2,9,128]{2,1,0:T(8,128)S(1)}, u32[]{:S(2)}, u32[]{:S(2)}) collective-permute-start(f32[2,9,128]{2,1,0:T(8,128)S(1)} %reshape.196), channel_id=1, source_target_pairs={{0,2},{1,3},{2,0},{3,1},{4,6},{5,7},{6,4},{7,5},{8,10},{9,11},{10,... | collective-permute-start | bytes 27656 | tf_op jit(solution)/shard_map/ppermute | solution.py:148
  91.0 2.2 %collective-permute-start.16 = (f32[2,9,128]{2,1,0:T(8,128)S(1)}, f32[2,9,128]{2,1,0:T(8,128)S(1)}, u32[]{:S(2)}, u32[]{:S(2)}) collective-permute-start(f32[2,9,128]{2,1,0:T(8,128)S(1)} %reshape.196), channel_id=1, source_target_pairs={{0,1},{1,2},{2,3},{3,0},{4,5},{5,6},{6,7},{7,4},{8,9},{9,10},{10,1... | collective-permute-start | bytes 27656 | tf_op jit(solution)/shard_map/ppermute | solution.py:148
  93.5 3.2 %collective-permute-done.16 = f32[2,9,128]{2,1,0:T(8,128)S(1)} collective-permute-done((f32[2,9,128]{2,1,0:T(8,128)S(1)}, f32[2,9,128]{2,1,0:T(8,128)S(1)}, u32[]{:S(2)}, u32[]{:S(2)}) %collective-permute-start.16) | collective-permute-done | bytes 9248 | tf_op jit(solution)/shard_map/ppermute | solution.py:148
  96.8 5.9 %collective-permute-start.17 = (f32[2,1,3,128]{3,0,2,1:T(2,128)S(1)}, f32[2,1,3,128]{3,0,2,1:T(2,128)S(1)}, u32[]{:S(2)}, u32[]{:S(2)}) collective-permute-start(f32[2,1,3,128]{3,0,2,1:T(2,128)S(1)} %get-tuple-element.27), channel_id=1, source_target_pairs={{0,16},{16,32},{32,48},{48,64},{64,80},{80,96},{96,112},{112,128},... | collective-permute-start | bytes 9224 | tf_op jit(solution)/shard_map/ppermute | solution.py:114
  102.7 1.9 %collective-permute-start.18 = (f32[2,1,3,128]{3,0,2,1:T(2,128)S(1)}, f32[2,1,3,128]{3,0,2,1:T(2,128)S(1)}, u32[]{:S(2)}, u32[]{:S(2)}) collective-permute-start(f32[2,1,3,128]{3,0,2,1:T(2,128)S(1)} %get-tuple-element.28), channel_id=1, source_target_pairs={{16,0},{32,16},{48,32},{64,48},{80,64},{96,80},{112,96},{128,112},... | collective-permute-start | bytes 9224 | tf_op jit(solution)/shard_map/ppermute | solution.py:115
  104.8 4.0 %collective-permute-done.18 = f32[2,1,3,128]{3,0,2,1:T(2,128)S(1)} collective-permute-done((f32[2,1,3,128]{3,0,2,1:T(2,128)S(1)}, f32[2,1,3,128]{3,0,2,1:T(2,128)S(1)}, u32[]{:S(2)}, u32[]{:S(2)}) %collective-permute-start.18) | collective-permute-done | bytes 3104 | tf_op jit(solution)/shard_map/ppermute | solution.py:115
  108.8 2.9 %collective-permute-start.19 = (f32[2,5,1,128]{3,0,2,1:T(2,128)S(1)}, f32[2,5,1,128]{3,0,2,1:T(2,128)S(1)}, u32[]{:S(2)}, u32[]{:S(2)}) collective-permute-start(f32[2,5,1,128]{3,0,2,1:T(2,128)S(1)} %get-tuple-element.23), channel_id=1, source_target_pairs={{0,4},{4,8},{8,12},{1,5},{5,9},{9,13},{2,6},{6,10},{10,14},{3,7},{... | collective-permute-start | bytes 15368 | tf_op jit(solution)/shard_map/ppermute | solution.py:114
  113.2 2.9 %collective-permute-done.20 = f32[2,5,1,128]{3,0,2,1:T(2,128)S(1)} collective-permute-done((f32[2,5,1,128]{3,0,2,1:T(2,128)S(1)}, f32[2,5,1,128]{3,0,2,1:T(2,128)S(1)}, u32[]{:S(2)}, u32[]{:S(2)}) %collective-permute-start.20) | collective-permute-done | bytes 5152 | tf_op jit(solution)/shard_map/ppermute | solution.py:115
  116.1 2.1 %fusion.16 = f32[2,64,256]{2,1,0:T(8,128)} fusion(f32[2,1152]{1,0:T(2,128)S(1)} %bitcast.124, pred[1152,256]{0,1:T(8,128)(4,1)S(1)} %iota_compare_fusion.1, s32[1152]{0:T(1024)S(1)} %get-tuple-element.31, f32[1,64,256]{2,1,0:T(8,128)S(1)} %fusion.33, f32[1,64,256]{2,1,0:T(8,128)S(1)} %fusion.39), kind=kOutput, calls=%fused_computation.18 | convolution fusion | flops 453713920 | bytes 570880 | tf_op jit(solution)/shard_map/sr,ksc->krc/dot_general | solution.py:139
  (82 shorter events, 10.5 us)
Async XLA Ops:
  1.4 19.4 %collective-permute-start = (f32[3,1,256]{2,1,0:T(1,128)S(1)}, f32[3,1,256]{2,1,0:T(1,128)S(1)}, u32[]{:S(2)}, u32[]{:S(2)}) collective-permute-start(f32[3,1,256]{2,1,0:T(1,128)S(1)} %get-tuple-element.17), channel_id=1, source_target_pairs={{0,16},{16,32},{32,48},{48,64},{64,80},{80,96},{96,112},{112,128},... | collective-permute-start | bytes 9224 | tf_op jit(solution)/shard_map/ppermute | solution.py:114
  6.7 14.1 %collective-permute-start.1 = (f32[3,1,256]{2,1,0:T(1,128)S(1)}, f32[3,1,256]{2,1,0:T(1,128)S(1)}, u32[]{:S(2)}, u32[]{:S(2)}) collective-permute-start(f32[3,1,256]{2,1,0:T(1,128)S(1)} %get-tuple-element.18), channel_id=1, source_target_pairs={{16,0},{32,16},{48,32},{64,48},{80,64},{96,80},{112,96},{128,112},... | collective-permute-start | bytes 9224 | tf_op jit(solution)/shard_map/ppermute | solution.py:115
  9.5 9.3 %copy-start.7 = (s32[1,9,128]{2,0,1:T(1,128)S(1)}, s32[1,9,128]{2,0,1:T(1,128)}, u32[]{:S(2)}) copy-start(s32[1,9,128]{2,0,1:T(1,128)} %param.20) | copy-start | bytes 13828
  11.8 7.5 %copy-start.6 = (s32[16,256]{1,0:T(8,128)S(1)}, s32[16,256]{1,0:T(8,128)}, u32[]{:S(2)}) copy-start(s32[16,256]{1,0:T(8,128)} %param.18) | copy-start | bytes 49156
  11.8 9.0 %copy-start = (f32[2,64,256]{2,1,0:T(8,128)S(1)}, f32[2,64,256]{2,1,0:T(8,128)}, u32[]{:S(2)}) copy-start(f32[2,64,256]{2,1,0:T(8,128)} %param.11) | copy-start | bytes 393220
  11.8 9.0 %copy-start.1 = (f32[64,256]{1,0:T(8,128)S(1)}, f32[64,256]{1,0:T(8,128)}, u32[]{:S(2)}) copy-start(f32[64,256]{1,0:T(8,128)} %param.12) | copy-start | bytes 196612
  11.9 13.6 %collective-permute-start.4 = (f32[2,1,3,128]{3,2,1,0:T(4,128)S(1)}, f32[2,1,3,128]{3,2,1,0:T(4,128)S(1)}, u32[]{:S(2)}, u32[]{:S(2)}) collective-permute-start(f32[2,1,3,128]{3,2,1,0:T(4,128)S(1)} %get-tuple-element.26), channel_id=1, source_target_pairs={{0,16},{16,32},{32,48},{48,64},{64,80},{80,96},{96,112},{112,128},... | collective-permute-start | bytes 9224 | tf_op jit(solution)/shard_map/ppermute | solution.py:114
  16.9 8.6 %collective-permute-start.5 = (f32[2,1,3,128]{3,2,1,0:T(4,128)S(1)}, f32[2,1,3,128]{3,2,1,0:T(4,128)S(1)}, u32[]{:S(2)}, u32[]{:S(2)}) collective-permute-start(f32[2,1,3,128]{3,2,1,0:T(4,128)S(1)} %get-tuple-element.25), channel_id=1, source_target_pairs={{16,0},{32,16},{48,32},{64,48},{80,64},{96,80},{112,96},{128,112},... | collective-permute-start | bytes 9224 | tf_op jit(solution)/shard_map/ppermute | solution.py:115
  20.9 9.9 %collective-permute-start.2 = (f32[3,66,1]{2,1,0:T(8,128)S(1)}, f32[3,66,1]{2,1,0:T(8,128)S(1)}, u32[]{:S(2)}, u32[]{:S(2)}) collective-permute-start(f32[3,66,1]{2,1,0:T(8,128)S(1)} %get-tuple-element.13), channel_id=1, source_target_pairs={{0,4},{4,8},{8,12},{1,5},{5,9},{9,13},{2,6},{6,10},{10,14},{3,7},{... | collective-permute-start | bytes 2384 | tf_op jit(solution)/shard_map/ppermute | solution.py:114
  24.1 6.7 %collective-permute-start.3 = (f32[3,66,1]{2,1,0:T(8,128)S(1)}, f32[3,66,1]{2,1,0:T(8,128)S(1)}, u32[]{:S(2)}, u32[]{:S(2)}) collective-permute-start(f32[3,66,1]{2,1,0:T(8,128)S(1)} %get-tuple-element.14), channel_id=1, source_target_pairs={{4,0},{8,4},{12,8},{5,1},{9,5},{13,9},{6,2},{10,6},{14,10},{7,3},{... | collective-permute-start | bytes 2384 | tf_op jit(solution)/shard_map/ppermute | solution.py:115
  25.5 5.5 %collective-permute-start.6 = (f32[2,5,1,128]{3,2,1,0:T(1,128)S(1)}, f32[2,5,1,128]{3,2,1,0:T(1,128)S(1)}, u32[]{:S(2)}, u32[]{:S(2)}) collective-permute-start(f32[2,5,1,128]{3,2,1,0:T(1,128)S(1)} %get-tuple-element.21), channel_id=1, source_target_pairs={{0,4},{4,8},{8,12},{1,5},{5,9},{9,13},{2,6},{6,10},{10,14},{3,7},{... | collective-permute-start | bytes 15368 | tf_op jit(solution)/shard_map/ppermute | solution.py:114
  29.5 4.4 %collective-permute-start.7 = (f32[2,5,1,128]{3,2,1,0:T(1,128)S(1)}, f32[2,5,1,128]{3,2,1,0:T(1,128)S(1)}, u32[]{:S(2)}, u32[]{:S(2)}) collective-permute-start(f32[2,5,1,128]{3,2,1,0:T(1,128)S(1)} %get-tuple-element.22), channel_id=1, source_target_pairs={{4,0},{8,4},{12,8},{5,1},{9,5},{13,9},{6,2},{10,6},{14,10},{7,3},{... | collective-permute-start | bytes 15368 | tf_op jit(solution)/shard_map/ppermute | solution.py:115
  34.1 1.3 %copy-start.3 = (f32[3,3,16,256]{3,2,1,0:T(8,128)S(1)}, f32[3,3,16,256]{3,2,1,0:T(8,128)}, u32[]{:S(2)}) copy-start(f32[3,3,16,256]{3,2,1,0:T(8,128)} %param.15) | copy-start | bytes 442372
  34.2 1.4 %slice-start = ((f32[3,3,16,256]{3,2,1,0:T(8,128)}), f32[1,3,16,256]{3,2,1,0:T(8,128)S(1)}, s32[]{:S(2)}) async-start(f32[3,3,16,256]{3,2,1,0:T(8,128)} %param.15), calls=%async_computation | async-start | bytes 98304 | tf_op jit(solution)/shard_map/slice | solution.py:284
  34.2 1.4 %copy-start.5 = (f32[3,16,256]{2,1,0:T(8,128)S(1)}, f32[3,16,256]{2,1,0:T(8,128)}, u32[]{:S(2)}) copy-start(f32[3,16,256]{2,1,0:T(8,128)} %param.16) | copy-start | bytes 147460
  35.6 8.8 %collective-permute-start.8 = (f32[13,1,256]{2,1,0:T(1,128)S(1)}, f32[13,1,256]{2,1,0:T(1,128)S(1)}, u32[]{:S(2)}, u32[]{:S(2)}) collective-permute-start(f32[13,1,256]{2,1,0:T(1,128)S(1)} %get-tuple-element.15), channel_id=1, source_target_pairs={{0,16},{16,32},{32,48},{48,64},{64,80},{80,96},{96,112},{112,128},... | collective-permute-start | bytes 39944 | tf_op jit(solution)/shard_map/ppermute | solution.py:114
  42.4 6.2 %collective-permute-start.9 = (f32[13,1,256]{2,1,0:T(1,128)S(1)}, f32[13,1,256]{2,1,0:T(1,128)S(1)}, u32[]{:S(2)}, u32[]{:S(2)}) collective-permute-start(f32[13,1,256]{2,1,0:T(1,128)S(1)} %get-tuple-element.16), channel_id=1, source_target_pairs={{16,0},{32,16},{48,32},{64,48},{80,64},{96,80},{112,96},{128,112},... | collective-permute-start | bytes 39944 | tf_op jit(solution)/shard_map/ppermute | solution.py:115
  48.8 5.4 %collective-permute-start.10 = (f32[13,18,1]{2,1,0:T(8,128)S(1)}, f32[13,18,1]{2,1,0:T(8,128)S(1)}, u32[]{:S(2)}, u32[]{:S(2)}) collective-permute-start(f32[13,18,1]{2,1,0:T(8,128)S(1)} %get-tuple-element.11), channel_id=1, source_target_pairs={{0,4},{4,8},{8,12},{1,5},{5,9},{9,13},{2,6},{6,10},{10,14},{3,7},{... | collective-permute-start | bytes 2816 | tf_op jit(solution)/shard_map/ppermute | solution.py:114
  52.1 6.0 %collective-permute-start.11 = (f32[13,18,1]{2,1,0:T(8,128)S(1)}, f32[13,18,1]{2,1,0:T(8,128)S(1)}, u32[]{:S(2)}, u32[]{:S(2)}) collective-permute-start(f32[13,18,1]{2,1,0:T(8,128)S(1)} %get-tuple-element.12), channel_id=1, source_target_pairs={{4,0},{8,4},{12,8},{5,1},{9,5},{13,9},{6,2},{10,6},{14,10},{7,3},{... | collective-permute-start | bytes 2816 | tf_op jit(solution)/shard_map/ppermute | solution.py:115
  58.4 5.5 %collective-permute-start.12 = (f32[4,1,18,258]{3,2,1,0:T(8,128)S(1)}, f32[4,1,18,258]{3,2,1,0:T(8,128)S(1)}, u32[]{:S(2)}, u32[]{:S(2)}) collective-permute-start(f32[4,1,18,258]{3,2,1,0:T(8,128)S(1)} %get-tuple-element.6), channel_id=1, source_target_pairs={{0,1},{1,2},{2,3},{4,5},{5,6},{6,7},{8,9},{9,10},{10,11},{12,13},{... | collective-permute-start | bytes 222920 | tf_op jit(solution)/shard_map/ppermute | solution.py:114
  61.6 6.5 %collective-permute-start.13 = (f32[4,1,18,258]{3,2,1,0:T(8,128)S(1)}, f32[4,1,18,258]{3,2,1,0:T(8,128)S(1)}, u32[]{:S(2)}, u32[]{:S(2)}) collective-permute-start(f32[4,1,18,258]{3,2,1,0:T(8,128)S(1)} %get-tuple-element.7), channel_id=1, source_target_pairs={{1,0},{2,1},{3,2},{5,4},{6,5},{7,6},{9,8},{10,9},{11,10},{13,12},{... | collective-permute-start | bytes 222920 | tf_op jit(solution)/shard_map/ppermute | solution.py:115
  84.2 9.3 %collective-permute-start.14 = (f32[2,9,128]{2,1,0:T(8,128)S(1)}, f32[2,9,128]{2,1,0:T(8,128)S(1)}, u32[]{:S(2)}, u32[]{:S(2)}) collective-permute-start(f32[2,9,128]{2,1,0:T(8,128)S(1)} %reshape.196), channel_id=1, source_target_pairs={{0,3},{1,0},{2,1},{3,2},{4,7},{5,4},{6,5},{7,6},{8,11},{9,8},{10,9... | collective-permute-start | bytes 27656 | tf_op jit(solution)/shard_map/ppermute | solution.py:148
  86.9 6.6 %collective-permute-start.15 = (f32[2,9,128]{2,1,0:T(8,128)S(1)}, f32[2,9,128]{2,1,0:T(8,128)S(1)}, u32[]{:S(2)}, u32[]{:S(2)}) collective-permute-start(f32[2,9,128]{2,1,0:T(8,128)S(1)} %reshape.196), channel_id=1, source_target_pairs={{0,2},{1,3},{2,0},{3,1},{4,6},{5,7},{6,4},{7,5},{8,10},{9,11},{10,... | collective-permute-start | bytes 27656 | tf_op jit(solution)/shard_map/ppermute | solution.py:148
  91.0 5.7 %collective-permute-start.16 = (f32[2,9,128]{2,1,0:T(8,128)S(1)}, f32[2,9,128]{2,1,0:T(8,128)S(1)}, u32[]{:S(2)}, u32[]{:S(2)}) collective-permute-start(f32[2,9,128]{2,1,0:T(8,128)S(1)} %reshape.196), channel_id=1, source_target_pairs={{0,1},{1,2},{2,3},{3,0},{4,5},{5,6},{6,7},{7,4},{8,9},{9,10},{10,1... | collective-permute-start | bytes 27656 | tf_op jit(solution)/shard_map/ppermute | solution.py:148
  93.2 11.4 %copy-start.2 = (f32[64,256]{1,0:T(8,128)S(1)}, f32[64,256]{1,0:T(8,128)}, u32[]{:S(2)}) copy-start(f32[64,256]{1,0:T(8,128)} %param.13) | copy-start | bytes 196612
  93.2 11.4 %copy-start.4 = (f32[2,64,256]{2,1,0:T(8,128)S(1)}, f32[2,64,256]{2,1,0:T(8,128)}, u32[]{:S(2)}) copy-start(f32[2,64,256]{2,1,0:T(8,128)} %param.14) | copy-start | bytes 393220
  96.8 8.0 %collective-permute-start.17 = (f32[2,1,3,128]{3,0,2,1:T(2,128)S(1)}, f32[2,1,3,128]{3,0,2,1:T(2,128)S(1)}, u32[]{:S(2)}, u32[]{:S(2)}) collective-permute-start(f32[2,1,3,128]{3,0,2,1:T(2,128)S(1)} %get-tuple-element.27), channel_id=1, source_target_pairs={{0,16},{16,32},{32,48},{48,64},{64,80},{80,96},{96,112},{112,128},... | collective-permute-start | bytes 9224 | tf_op jit(solution)/shard_map/ppermute | solution.py:114
  102.7 6.1 %collective-permute-start.18 = (f32[2,1,3,128]{3,0,2,1:T(2,128)S(1)}, f32[2,1,3,128]{3,0,2,1:T(2,128)S(1)}, u32[]{:S(2)}, u32[]{:S(2)}) collective-permute-start(f32[2,1,3,128]{3,0,2,1:T(2,128)S(1)} %get-tuple-element.28), channel_id=1, source_target_pairs={{16,0},{32,16},{48,32},{64,48},{80,64},{96,80},{112,96},{128,112},... | collective-permute-start | bytes 9224 | tf_op jit(solution)/shard_map/ppermute | solution.py:115
  108.8 4.4 %collective-permute-start.19 = (f32[2,5,1,128]{3,0,2,1:T(2,128)S(1)}, f32[2,5,1,128]{3,0,2,1:T(2,128)S(1)}, u32[]{:S(2)}, u32[]{:S(2)}) collective-permute-start(f32[2,5,1,128]{3,0,2,1:T(2,128)S(1)} %get-tuple-element.23), channel_id=1, source_target_pairs={{0,4},{4,8},{8,12},{1,5},{5,9},{9,13},{2,6},{6,10},{10,14},{3,7},{... | collective-permute-start | bytes 15368 | tf_op jit(solution)/shard_map/ppermute | solution.py:114
  111.7 4.4 %collective-permute-start.20 = (f32[2,5,1,128]{3,0,2,1:T(2,128)S(1)}, f32[2,5,1,128]{3,0,2,1:T(2,128)S(1)}, u32[]{:S(2)}, u32[]{:S(2)}) collective-permute-start(f32[2,5,1,128]{3,0,2,1:T(2,128)S(1)} %get-tuple-element.24), channel_id=1, source_target_pairs={{4,0},{8,4},{12,8},{5,1},{9,5},{13,9},{6,2},{10,6},{14,10},{7,3},{... | collective-permute-start | bytes 15368 | tf_op jit(solution)/shard_map/ppermute | solution.py:115

commit v3 on v2

--- a/solution.py
+++ b/solution.py
@@ -241,6 +241,36 @@
     return corner_a[:, 1:, 1:] + corner_b[:, :-1, 1:] + corner_c[:, 1:, :-1] + corner_d[:, :-1, :-1]
 
 
+def exchange(axis, sent_up, sent_down):
+    count = lax.axis_size(axis)
+    up = [(i, i + 1) for i in range(count - 1)]
+    down = [(i + 1, i) for i in range(count - 1)]
+    return lax.ppermute(sent_up, axis, up), lax.ppermute(sent_down, axis, down)
+
+
+def packed_halo(arrays, dims, axis):
+    ups, downs, shapes = [], [], []
+    for array, dim in zip(arrays, dims):
+        length = array.shape[dim]
+        last = lax.slice_in_dim(array, length - 1, length, axis=dim)
+        first = lax.slice_in_dim(array, 0, 1, axis=dim)
+        shapes.append(last.shape)
+        ups.append(last.reshape(-1))
+        downs.append(first.reshape(-1))
+    before, after = exchange(axis, jnp.concatenate(ups), jnp.concatenate(downs))
+    widened = []
+    offset = 0
+    for array, dim, shape in zip(arrays, dims, shapes):
+        size = 1
+        for extent in shape:
+            size *= extent
+        head = before[offset:offset + size].reshape(shape)
+        tail = after[offset:offset + size].reshape(shape)
+        offset += size
+        widened.append(jnp.concatenate([head, array, tail], axis=dim))
+    return widened
+
+
 def per_device(
     ssa_velocity,
     shelf_viscosity,
@@ -256,42 +286,40 @@
 ):
     row_count = ssa_velocity.shape[1]
     col_count = ssa_velocity.shape[2]
-    stacked = jnp.concatenate([ssa_velocity, shelf_viscosity[None]], 0)
-    padded = with_halo(stacked, (("mx", 1), ("my", 2)), 1)
-    shelf_res = shelf_residual(padded, basal_friction, driving_stress)
-    owner_nodes = iface_nodes[0]
-    node_live = owner_nodes >= 0
-    slot_count = owner_nodes.shape[1]
-    node_row, node_col = slot_selectors(owner_nodes.reshape(-1), row_count, col_count)
-    outgoing = gather_slots(ssa_velocity, node_row, node_col).reshape(2, 9, slot_count)
-    grid_out = outgoing.reshape(2, 3, 3, slot_count)
-    extended = with_halo(grid_out, (("mx", 1), ("my", 2)), 1)
-    returned = extended[:, 0::2, 0::2].reshape(2, 9, slot_count)
     depth_count = stokes_velocity.shape[1]
     block_x = stokes_velocity.shape[2]
     block_y = stokes_velocity.shape[3]
-    column_count = block_x * block_y
-    columns = iface_columns[0]
-    col_live = columns >= 0
-    col_row, col_col = slot_selectors(columns.reshape(-1), block_x, block_y)
-    placed = scatter_slots(returned.reshape(2, -1), col_row, col_col)
-    marked = jnp.einsum("sr,sc->rc", col_row, col_col.astype(jnp.float32)) > 0.0
-    uv_part = jnp.where(
-        marked.reshape(1, 1, block_x, block_y),
-        placed.reshape(2, 1, block_x, block_y),
-        stokes_velocity[:2],
-    )
-    stokes_field = jnp.concatenate([uv_part, stokes_velocity[2:3], ice_viscosity[None]], 0)
-    planes = jnp.concatenate(
+    stacked = jnp.concatenate([ssa_velocity, shelf_viscosity[None]], 0)
+    owner_nodes = iface_nodes[0]
+    slot_count = owner_nodes.shape[1]
+    node_row, node_col = slot_selectors(owner_nodes.reshape(-1), row_count, col_count)
+    outgoing = gather_slots(ssa_velocity, node_row, node_col).reshape(2, 3, 3, slot_count)
+    raw_planes = jnp.concatenate(
         [
-            stokes_field.reshape(4 * depth_count, block_x, block_y),
+            stokes_velocity.reshape(3 * depth_count, block_x, block_y),
+            ice_viscosity,
             diagonals.astype(jnp.float32)[None],
         ],
         0,
     )
-    widened = with_halo(planes, (("mx", 1), ("my", 2)), 1)
+    shelf_x, planes_x, slots_x = packed_halo((stacked, raw_planes, outgoing), (1, 1, 1), "mx")
+    padded, widened, extended = packed_halo((shelf_x, planes_x, slots_x), (2, 2, 2), "my")
+    shelf_res = shelf_residual(padded, basal_friction, driving_stress)
+    returned = extended[:, 0::2, 0::2].reshape(2, 9, slot_count)
+    columns = iface_columns[0]
+    col_row, col_col = slot_selectors(columns.reshape(-1), block_x, block_y)
+    placed = scatter_slots(returned.reshape(2, -1), col_row, col_col)
+    marked = jnp.einsum("sr,sc->rc", col_row, col_col.astype(jnp.float32))
+    ring = jnp.concatenate([jnp.minimum(marked, 1.0)[None], placed], 0)
+    field_ext = widened[:-1].reshape(4, depth_count, block_x + 2, block_y + 2)
     flag_cells = widened[-1, :-1, :-1]
-    field_ext = widened[:-1].reshape(4, depth_count, block_x + 2, block_y + 2)
+    below_raw, above_raw = exchange("layer", field_ext[:, -1], field_ext[:, 0])
+    (ring_x,) = packed_halo((ring,), (1,), "mx")
+    (ring_ext,) = packed_halo((ring_x,), (2,), "my")
+    imposed_at = ring_ext[0] > 0.5
+    all_layers = jnp.concatenate([below_raw[:, None], field_ext, above_raw[:, None]], 1)
+    uv_ext = jnp.where(imposed_at[None, None], ring_ext[1:3, None], all_layers[:2])
+    extended_layers = jnp.concatenate([uv_ext, all_layers[2:]], 0)
     count_x = lax.axis_size("mx")
     count_y = lax.axis_size("my")
     place_x = lax.axis_index("mx")
@@ -305,7 +333,6 @@
     layer_count = lax.axis_size("layer")
     below_live = (layer_index > 0).astype(jnp.float32)
     above_live = (layer_index < layer_count - 1).astype(jnp.float32)
-    extended_layers = with_halo(field_ext, (("layer", 1),), 1)
     stokes_residual = fem_pallas(
         extended_layers, flag_cells, weight, element_matrix, below_live, above_live, body_force
     )
@@ -313,7 +340,8 @@
     bucket = gather_slots(depth_sum, col_row, col_col).reshape(2, 9, slot_count)
     depth_total = layer_total(bucket)
     grid_back = depth_total.reshape(2, 3, 3, slot_count)
-    extended_back = with_halo(grid_back, (("mx", 1), ("my", 2)), 1)
+    (back_x,) = packed_halo((grid_back,), (1,), "mx")
+    (extended_back,) = packed_halo((back_x,), (2,), "my")
     at_owner = extended_back[:, 0::2, 0::2].reshape(2, 9, slot_count)
     node_force = scatter_slots(at_owner.reshape(2, -1), node_row, node_col)
     coupled_residual = shelf_res - node_force

time: 119 us -> 97.9 us (0.82)
  the two profiles are of different devices: /device:TPU:225 before, /device:TPU:408 now
where the time goes in v3:
time: 97.9 us; the launch traced here: 97.3 us
  starting transfers between devices  41.4 us (42%)
  waiting for transfers between devices  24.4 us (25%)
  Pallas kernels  12.9 us (13%)
  matrix products  7.34 us (7%)
  other arithmetic  6.34 us (6%)
  local copies, waits for them, and re-layouts  3.32 us (3%)
  between operations  1.48 us (2%)
    ppermute x7, waiting for transfers between devices, exchange(): lax.ppermute(sent_up, axis, up)  20.6 us
    ppermute x7, starting transfers between devices, exchange(): lax.ppermute(sent_down, axis, down)  16.1 us
    ppermute x7, starting transfers between devices, exchange(): lax.ppermute(sent_up, axis, up)  15.1 us
    pallas_call x1, Pallas kernels, fem_pallas(): pl.pallas_call(fem_kernel, out_shape=jax.ShapeDtypeStruct(body_force.shap...  12.9 us
    ppermute x3, starting transfers between devices, layer_total(): received.append(lax.ppermute(part, 'layer', pairs))  10.2 us
    ppermute x3, waiting for transfers between devices, layer_total(): received.append(lax.ppermute(part, 'layer', pairs))  3.79 us
    dot_general x2, matrix products, gather_slots(): rows_taken = jnp.einsum('sr,krc->ksc', pick_row, field, precision=HIGH)  3.64 us
    dot_general x2, matrix products, scatter_slots(): return jnp.einsum('sr,ksc->krc', pick_row, spread, precision=HIGH)  3.44 us
  transfers between devices with their start and end apart: 17, of which 7 were waited for; matrix products, arithmetic and copies ran while one was open for 7% of the time, Pallas kernels for 0%

profile of v3, /device:TPU:408, one launch (start us, length us, event | category | flops | bytes accessed | tf_op | source)
XLA Modules:
  0.0 97.3 jit_solution(7272163272677682984)
XLA Ops:
  0.6 0.7 reduce.3
  1.6 2.3 %fusion.5 = f32[1152,2]{0,1:T(2,128)S(1)} fusion(f32[2,64,256]{2,1,0:T(8,128)} %param.11, pred[1152,256]{0,1:T(8,128)(4,1)S(1)} %iota_compare_fusion.1, s32[1152]{0:T(1024)S(1)} %get-tuple-element.41), kind=kOutput, calls=%fused_computation.7 | convolution fusion | flops 454235904 | bytes 439808 | tf_op jit(solution)/shard_map/sr,krc->ksc/dot_general | solution.py:133
  4.2 3.6 %collective-permute-start.1 = (f32[4864]{0:T(1024)S(1)}, f32[4864]{0:T(1024)S(1)}, u32[]{:S(2)}, u32[]{:S(2)}) collective-permute-start(f32[4864]{0:T(1024)S(1)} %pad_maximum_fusion.24), channel_id=1, source_target_pairs={{16,0},{32,16},{48,32},{64,48},{80,64},{96,80},{112,96},{128,112},... | collective-permute-start | bytes 58376 | tf_op jit(solution)/shard_map/ppermute | solution.py:248
  7.8 1.9 %collective-permute-start = (f32[4864]{0:T(1024)S(1)}, f32[4864]{0:T(1024)S(1)}, u32[]{:S(2)}, u32[]{:S(2)}) collective-permute-start(f32[4864]{0:T(1024)S(1)} %pad_maximum_fusion.23), channel_id=1, source_target_pairs={{0,16},{16,32},{32,48},{48,64},{64,80},{80,96},{96,112},{112,128},... | collective-permute-start | bytes 58376 | tf_op jit(solution)/shard_map/ppermute | solution.py:248
  10.4 3.7 %collective-permute-done = f32[4864]{0:T(1024)S(1)} collective-permute-done((f32[4864]{0:T(1024)S(1)}, f32[4864]{0:T(1024)S(1)}, u32[]{:S(2)}, u32[]{:S(2)}) %collective-permute-start) | collective-permute-done | bytes 19488 | tf_op jit(solution)/shard_map/ppermute | solution.py:248
  15.1 2.6 %collective-permute-start.3 = (f32[1712]{0:T(1024)S(1)}, f32[1712]{0:T(1024)S(1)}, u32[]{:S(2)}, u32[]{:S(2)}) collective-permute-start(f32[1712]{0:T(1024)S(1)} %concatenate.68), channel_id=1, source_target_pairs={{4,0},{8,4},{12,8},{5,1},{9,5},{13,9},{6,2},{10,6},{14,10},{7,3},{... | collective-permute-start | bytes 20552 | tf_op jit(solution)/shard_map/ppermute | solution.py:248
  18.0 1.3 %collective-permute-start.2 = (f32[1712]{0:T(1024)S(1)}, f32[1712]{0:T(1024)S(1)}, u32[]{:S(2)}, u32[]{:S(2)}) collective-permute-start(f32[1712]{0:T(1024)S(1)} %concatenate.67), channel_id=1, source_target_pairs={{0,4},{4,8},{8,12},{1,5},{5,9},{9,13},{2,6},{6,10},{10,14},{3,7},{... | collective-permute-start | bytes 20552 | tf_op jit(solution)/shard_map/ppermute | solution.py:248
  20.2 3.3 %collective-permute-done.2 = f32[1712]{0:T(1024)S(1)} collective-permute-done((f32[1712]{0:T(1024)S(1)}, f32[1712]{0:T(1024)S(1)}, u32[]{:S(2)}, u32[]{:S(2)}) %collective-permute-start.2) | collective-permute-done | bytes 6880 | tf_op jit(solution)/shard_map/ppermute | solution.py:248
  24.2 1.3 %collective-permute-start.9 = (f32[4,18,258]{2,1,0:T(8,128)S(1)}, f32[4,18,258]{2,1,0:T(8,128)S(1)}, u32[]{:S(2)}, u32[]{:S(2)}) collective-permute-start(f32[4,18,258]{2,1,0:T(8,128)S(1)} %get-tuple-element.23), channel_id=1, source_target_pairs={{1,0},{2,1},{3,2},{5,4},{6,5},{7,6},{9,8},{10,9},{11,10},{13,12},{... | collective-permute-start | bytes 222920 | tf_op jit(solution)/shard_map/ppermute | solution.py:248
  25.5 4.6 %collective-permute-start.8 = (f32[4,18,258]{2,1,0:T(8,128)S(1)}, f32[4,18,258]{2,1,0:T(8,128)S(1)}, u32[]{:S(2)}, u32[]{:S(2)}) collective-permute-start(f32[4,18,258]{2,1,0:T(8,128)S(1)} %get-tuple-element.22), channel_id=1, source_target_pairs={{0,1},{1,2},{2,3},{4,5},{5,6},{6,7},{8,9},{9,10},{10,11},{12,13},{... | collective-permute-start | bytes 222920 | tf_op jit(solution)/shard_map/ppermute | solution.py:248
  30.5 1.3 %fusion.19 = f32[2,16,256]{2,1,0:T(8,128)S(1)} fusion(f32[2,1152]{1,0:T(2,128)S(1)} %broadcast_in_dim.113, pred[1152,256]{0,1:T(8,128)(4,1)S(1)} %iota_compare_fusion, s32[1152]{0:T(1024)S(1)} %get-tuple-element.39), kind=kOutput, calls=%fused_computation.19 | convolution fusion | flops 113854464 | bytes 341504 | tf_op jit(solution)/shard_map/sr,ksc->krc/dot_general | solution.py:139
  31.9 1.9 %collective-permute-start.5 = (f32[768]{0:T(1024)S(1)}, f32[768]{0:T(1024)S(1)}, u32[]{:S(2)}, u32[]{:S(2)}) collective-permute-start(f32[768]{0:T(1024)S(1)} %reshape.367), channel_id=1, source_target_pairs={{16,0},{32,16},{48,32},{64,48},{80,64},{96,80},{112,96},{128,112},... | collective-permute-start | bytes 9224 | tf_op jit(solution)/shard_map/ppermute | solution.py:248
  33.8 2.4 %collective-permute-start.4 = (f32[768]{0:T(1024)S(1)}, f32[768]{0:T(1024)S(1)}, u32[]{:S(2)}, u32[]{:S(2)}) collective-permute-start(f32[768]{0:T(1024)S(1)} %reshape.365), channel_id=1, source_target_pairs={{0,16},{16,32},{32,48},{48,64},{64,80},{80,96},{96,112},{112,128},... | collective-permute-start | bytes 9224 | tf_op jit(solution)/shard_map/ppermute | solution.py:248
  37.3 2.7 %collective-permute-done.4 = f32[768]{0:T(1024)S(1)} collective-permute-done((f32[768]{0:T(1024)S(1)}, f32[768]{0:T(1024)S(1)}, u32[]{:S(2)}, u32[]{:S(2)}) %collective-permute-start.4) | collective-permute-done | bytes 3104 | tf_op jit(solution)/shard_map/ppermute | solution.py:248
  40.2 2.4 %collective-permute-start.7 = (f32[54]{0:T(128)S(1)}, f32[54]{0:T(128)S(1)}, u32[]{:S(2)}, u32[]{:S(2)}) collective-permute-start(f32[54]{0:T(128)S(1)} %reshape.371), channel_id=1, source_target_pairs={{4,0},{8,4},{12,8},{5,1},{9,5},{13,9},{6,2},{10,6},{14,10},{7,3},{... | collective-permute-start | bytes 656 | tf_op jit(solution)/shard_map/ppermute | solution.py:248
  42.7 1.3 %collective-permute-start.6 = (f32[54]{0:T(128)S(1)}, f32[54]{0:T(128)S(1)}, u32[]{:S(2)}, u32[]{:S(2)}) collective-permute-start(f32[54]{0:T(128)S(1)} %reshape.369), channel_id=1, source_target_pairs={{0,4},{4,8},{8,12},{1,5},{5,9},{9,13},{2,6},{6,10},{10,14},{3,7},{... | collective-permute-start | bytes 656 | tf_op jit(solution)/shard_map/ppermute | solution.py:248
  44.7 3.4 %collective-permute-done.6 = f32[54]{0:T(128)S(1)} collective-permute-done((f32[54]{0:T(128)S(1)}, f32[54]{0:T(128)S(1)}, u32[]{:S(2)}, u32[]{:S(2)}) %collective-permute-start.6) | collective-permute-done | bytes 248 | tf_op jit(solution)/shard_map/ppermute | solution.py:248
  48.6 0.9 select_maximum_fusion.fld_ref
  49.5 12.9 %shard_map.122 = f32[3,3,16,256]{3,2,1,0:T(8,128)} custom-call(f32[4,5,24,384]{3,2,1,0:T(8,128)} %select_maximum_fusion.fld_ref, f32[24,384]{1,0:T(8,128)} %get-tuple-element.44.main_ref, f32[24,384]{1,0:T(8,128)} %get-tuple-element.43.weight_ref, f32[18,18]{1,0:T(8,128)} %kmat_ref.1, f32[2]{0:T(128)} %add_convert_fusion.live_ref, f32[3,3,16,256]{3,2,1,0:T(8,128)} %body_ref.1), custom_call_target="tpu_custom_call" | custom-call | tf_op jit(solution)/shard_map/pallas_call | solution.py:92
  62.5 0.9 slice_reduce_fusion.4
  63.4 1.3 %fusion.6 = f32[2,1152]{1,0:T(2,128)S(1)} fusion(f32[2,16,256]{2,1,0:T(8,128)S(1)} %slice_reduce_fusion.4, pred[1152,256]{0,1:T(8,128)(4,1)S(1)} %iota_compare_fusion, s32[1152]{0:T(1024)S(1)} %get-tuple-element.39), kind=kOutput, calls=%fused_computation.8 | convolution fusion | flops 114441984 | bytes 341504 | tf_op jit(solution)/shard_map/sr,krc->ksc/dot_general | solution.py:133
  64.7 2.9 %collective-permute-start.10 = (f32[2,9,128]{2,1,0:T(8,128)S(1)}, f32[2,9,128]{2,1,0:T(8,128)S(1)}, u32[]{:S(2)}, u32[]{:S(2)}) collective-permute-start(f32[2,9,128]{2,1,0:T(8,128)S(1)} %reshape.376), channel_id=1, source_target_pairs={{0,3},{1,0},{2,1},{3,2},{4,7},{5,4},{6,5},{7,6},{8,11},{9,8},{10,9... | collective-permute-start | bytes 27656 | tf_op jit(solution)/shard_map/ppermute | solution.py:148
  67.6 4.5 %collective-permute-start.11 = (f32[2,9,128]{2,1,0:T(8,128)S(1)}, f32[2,9,128]{2,1,0:T(8,128)S(1)}, u32[]{:S(2)}, u32[]{:S(2)}) collective-permute-start(f32[2,9,128]{2,1,0:T(8,128)S(1)} %reshape.376), channel_id=1, source_target_pairs={{0,2},{1,3},{2,0},{3,1},{4,6},{5,7},{6,4},{7,5},{8,10},{9,11},{10,... | collective-permute-start | bytes 27656 | tf_op jit(solution)/shard_map/ppermute | solution.py:148
  72.1 2.8 %collective-permute-start.12 = (f32[2,9,128]{2,1,0:T(8,128)S(1)}, f32[2,9,128]{2,1,0:T(8,128)S(1)}, u32[]{:S(2)}, u32[]{:S(2)}) collective-permute-start(f32[2,9,128]{2,1,0:T(8,128)S(1)} %reshape.376), channel_id=1, source_target_pairs={{0,1},{1,2},{2,3},{3,0},{4,5},{5,6},{6,7},{7,4},{8,9},{9,10},{10,1... | collective-permute-start | bytes 27656 | tf_op jit(solution)/shard_map/ppermute | solution.py:148
  75.2 3.8 %collective-permute-done.12 = f32[2,9,128]{2,1,0:T(8,128)S(1)} collective-permute-done((f32[2,9,128]{2,1,0:T(8,128)S(1)}, f32[2,9,128]{2,1,0:T(8,128)S(1)}, u32[]{:S(2)}, u32[]{:S(2)}) %collective-permute-start.12) | collective-permute-done | bytes 9248 | tf_op jit(solution)/shard_map/ppermute | solution.py:148
  79.0 1.9 %collective-permute-start.14 = (f32[768]{0:T(1024)S(1)}, f32[768]{0:T(1024)S(1)}, u32[]{:S(2)}, u32[]{:S(2)}) collective-permute-start(f32[768]{0:T(1024)S(1)} %reshape.380), channel_id=1, source_target_pairs={{16,0},{32,16},{48,32},{64,48},{80,64},{96,80},{112,96},{128,112},... | collective-permute-start | bytes 9224 | tf_op jit(solution)/shard_map/ppermute | solution.py:248
  81.0 2.4 %collective-permute-start.13 = (f32[768]{0:T(1024)S(1)}, f32[768]{0:T(1024)S(1)}, u32[]{:S(2)}, u32[]{:S(2)}) collective-permute-start(f32[768]{0:T(1024)S(1)} %reshape.378), channel_id=1, source_target_pairs={{0,16},{16,32},{32,48},{48,64},{64,80},{80,96},{96,112},{112,128},... | collective-permute-start | bytes 9224 | tf_op jit(solution)/shard_map/ppermute | solution.py:248
  83.6 3.5 %collective-permute-done.13 = f32[768]{0:T(1024)S(1)} collective-permute-done((f32[768]{0:T(1024)S(1)}, f32[768]{0:T(1024)S(1)}, u32[]{:S(2)}, u32[]{:S(2)}) %collective-permute-start.13) | collective-permute-done | bytes 3104 | tf_op jit(solution)/shard_map/ppermute | solution.py:248
  87.1 2.4 %collective-permute-start.16 = (f32[1280]{0:T(1024)S(1)}, f32[1280]{0:T(1024)S(1)}, u32[]{:S(2)}, u32[]{:S(2)}) collective-permute-start(f32[1280]{0:T(1024)S(1)} %reshape.384), channel_id=1, source_target_pairs={{4,0},{8,4},{12,8},{5,1},{9,5},{13,9},{6,2},{10,6},{14,10},{7,3},{... | collective-permute-start | bytes 15368 | tf_op jit(solution)/shard_map/ppermute | solution.py:248
  89.5 1.3 %collective-permute-start.15 = (f32[1280]{0:T(1024)S(1)}, f32[1280]{0:T(1024)S(1)}, u32[]{:S(2)}, u32[]{:S(2)}) collective-permute-start(f32[1280]{0:T(1024)S(1)} %reshape.382), channel_id=1, source_target_pairs={{0,4},{4,8},{8,12},{1,5},{5,9},{9,13},{2,6},{6,10},{10,14},{3,7},{... | collective-permute-start | bytes 15368 | tf_op jit(solution)/shard_map/ppermute | solution.py:248
  91.0 4.0 %collective-permute-done.15 = f32[1280]{0:T(1024)S(1)} collective-permute-done((f32[1280]{0:T(1024)S(1)}, f32[1280]{0:T(1024)S(1)}, u32[]{:S(2)}, u32[]{:S(2)}) %collective-permute-start.15) | collective-permute-done | bytes 5152 | tf_op jit(solution)/shard_map/ppermute | solution.py:248
  95.1 2.1 %fusion.16 = f32[2,64,256]{2,1,0:T(8,128)} fusion(f32[2,1152]{1,0:T(2,128)S(1)} %bitcast.152, pred[1152,256]{0,1:T(8,128)(4,1)S(1)} %iota_compare_fusion.1, s32[1152]{0:T(1024)S(1)} %get-tuple-element.41, f32[1,64,256]{2,1,0:T(8,128)S(1)} %fusion.34, f32[1,64,256]{2,1,0:T(8,128)S(1)} %fusion.40), kind=kOutput, calls=%fused_computation.18 | convolution fusion | flops 453713920 | bytes 570880 | tf_op jit(solution)/shard_map/sr,ksc->krc/dot_general | solution.py:139
  (135 shorter events, 7.4 us)
Async XLA Ops:
  1.5 2.4 %copy-start.6 = (s32[16,256]{1,0:T(8,128)S(1)}, s32[16,256]{1,0:T(8,128)}, u32[]{:S(2)}) copy-start(s32[16,256]{1,0:T(8,128)} %param.18) | copy-start | bytes 49156
  1.5 2.4 %copy-start = (f32[3,3,16,256]{3,2,1,0:T(8,128)S(1)}, f32[3,3,16,256]{3,2,1,0:T(8,128)}, u32[]{:S(2)}) copy-start(f32[3,3,16,256]{3,2,1,0:T(8,128)} %param.15) | copy-start | bytes 442372
  1.6 2.4 %copy-start.2 = (f32[3,16,256]{2,1,0:T(8,128)S(1)}, f32[3,16,256]{2,1,0:T(8,128)}, u32[]{:S(2)}) copy-start(f32[3,16,256]{2,1,0:T(8,128)} %param.16) | copy-start | bytes 147460
  1.6 2.5 %copy-start.1 = (f32[2,64,256]{2,1,0:T(8,128)S(1)}, f32[2,64,256]{2,1,0:T(8,128)}, u32[]{:S(2)}) copy-start(f32[2,64,256]{2,1,0:T(8,128)} %param.11) | copy-start | bytes 393220
  1.6 2.5 %copy-start.3 = (f32[64,256]{1,0:T(8,128)S(1)}, f32[64,256]{1,0:T(8,128)}, u32[]{:S(2)}) copy-start(f32[64,256]{1,0:T(8,128)} %param.12) | copy-start | bytes 196612
  1.6 8.1 %copy-start.7 = (s32[1,9,128]{2,0,1:T(1,128)S(1)}, s32[1,9,128]{2,0,1:T(1,128)}, u32[]{:S(2)}) copy-start(s32[1,9,128]{2,0,1:T(1,128)} %param.20) | copy-start | bytes 13828
  4.2 6.2 %collective-permute-start.1 = (f32[4864]{0:T(1024)S(1)}, f32[4864]{0:T(1024)S(1)}, u32[]{:S(2)}, u32[]{:S(2)}) collective-permute-start(f32[4864]{0:T(1024)S(1)} %pad_maximum_fusion.24), channel_id=1, source_target_pairs={{16,0},{32,16},{48,32},{64,48},{80,64},{96,80},{112,96},{128,112},... | collective-permute-start | bytes 58376 | tf_op jit(solution)/shard_map/ppermute | solution.py:248
  7.8 6.3 %collective-permute-start = (f32[4864]{0:T(1024)S(1)}, f32[4864]{0:T(1024)S(1)}, u32[]{:S(2)}, u32[]{:S(2)}) collective-permute-start(f32[4864]{0:T(1024)S(1)} %pad_maximum_fusion.23), channel_id=1, source_target_pairs={{0,16},{16,32},{32,48},{48,64},{64,80},{80,96},{96,112},{112,128},... | collective-permute-start | bytes 58376 | tf_op jit(solution)/shard_map/ppermute | solution.py:248
  15.1 4.8 %collective-permute-start.3 = (f32[1712]{0:T(1024)S(1)}, f32[1712]{0:T(1024)S(1)}, u32[]{:S(2)}, u32[]{:S(2)}) collective-permute-start(f32[1712]{0:T(1024)S(1)} %concatenate.68), channel_id=1, source_target_pairs={{4,0},{8,4},{12,8},{5,1},{9,5},{13,9},{6,2},{10,6},{14,10},{7,3},{... | collective-permute-start | bytes 20552 | tf_op jit(solution)/shard_map/ppermute | solution.py:248
  18.0 5.5 %collective-permute-start.2 = (f32[1712]{0:T(1024)S(1)}, f32[1712]{0:T(1024)S(1)}, u32[]{:S(2)}, u32[]{:S(2)}) collective-permute-start(f32[1712]{0:T(1024)S(1)} %concatenate.67), channel_id=1, source_target_pairs={{0,4},{4,8},{8,12},{1,5},{5,9},{9,13},{2,6},{6,10},{10,14},{3,7},{... | collective-permute-start | bytes 20552 | tf_op jit(solution)/shard_map/ppermute | solution.py:248
  24.2 24.3 %collective-permute-start.9 = (f32[4,18,258]{2,1,0:T(8,128)S(1)}, f32[4,18,258]{2,1,0:T(8,128)S(1)}, u32[]{:S(2)}, u32[]{:S(2)}) collective-permute-start(f32[4,18,258]{2,1,0:T(8,128)S(1)} %get-tuple-element.23), channel_id=1, source_target_pairs={{1,0},{2,1},{3,2},{5,4},{6,5},{7,6},{9,8},{10,9},{11,10},{13,12},{... | collective-permute-start | bytes 222920 | tf_op jit(solution)/shard_map/ppermute | solution.py:248
  25.5 23.0 %collective-permute-start.8 = (f32[4,18,258]{2,1,0:T(8,128)S(1)}, f32[4,18,258]{2,1,0:T(8,128)S(1)}, u32[]{:S(2)}, u32[]{:S(2)}) collective-permute-start(f32[4,18,258]{2,1,0:T(8,128)S(1)} %get-tuple-element.22), channel_id=1, source_target_pairs={{0,1},{1,2},{2,3},{4,5},{5,6},{6,7},{8,9},{9,10},{10,11},{12,13},{... | collective-permute-start | bytes 222920 | tf_op jit(solution)/shard_map/ppermute | solution.py:248
  31.9 5.4 %collective-permute-start.5 = (f32[768]{0:T(1024)S(1)}, f32[768]{0:T(1024)S(1)}, u32[]{:S(2)}, u32[]{:S(2)}) collective-permute-start(f32[768]{0:T(1024)S(1)} %reshape.367), channel_id=1, source_target_pairs={{16,0},{32,16},{48,32},{64,48},{80,64},{96,80},{112,96},{128,112},... | collective-permute-start | bytes 9224 | tf_op jit(solution)/shard_map/ppermute | solution.py:248
  33.8 6.1 %collective-permute-start.4 = (f32[768]{0:T(1024)S(1)}, f32[768]{0:T(1024)S(1)}, u32[]{:S(2)}, u32[]{:S(2)}) collective-permute-start(f32[768]{0:T(1024)S(1)} %reshape.365), channel_id=1, source_target_pairs={{0,16},{16,32},{32,48},{48,64},{64,80},{80,96},{96,112},{112,128},... | collective-permute-start | bytes 9224 | tf_op jit(solution)/shard_map/ppermute | solution.py:248
  40.2 4.4 %collective-permute-start.7 = (f32[54]{0:T(128)S(1)}, f32[54]{0:T(128)S(1)}, u32[]{:S(2)}, u32[]{:S(2)}) collective-permute-start(f32[54]{0:T(128)S(1)} %reshape.371), channel_id=1, source_target_pairs={{4,0},{8,4},{12,8},{5,1},{9,5},{13,9},{6,2},{10,6},{14,10},{7,3},{... | collective-permute-start | bytes 656 | tf_op jit(solution)/shard_map/ppermute | solution.py:248
  42.7 5.4 %collective-permute-start.6 = (f32[54]{0:T(128)S(1)}, f32[54]{0:T(128)S(1)}, u32[]{:S(2)}, u32[]{:S(2)}) collective-permute-start(f32[54]{0:T(128)S(1)} %reshape.369), channel_id=1, source_target_pairs={{0,4},{4,8},{8,12},{1,5},{5,9},{9,13},{2,6},{6,10},{10,14},{3,7},{... | collective-permute-start | bytes 656 | tf_op jit(solution)/shard_map/ppermute | solution.py:248
  64.7 10.4 %collective-permute-start.10 = (f32[2,9,128]{2,1,0:T(8,128)S(1)}, f32[2,9,128]{2,1,0:T(8,128)S(1)}, u32[]{:S(2)}, u32[]{:S(2)}) collective-permute-start(f32[2,9,128]{2,1,0:T(8,128)S(1)} %reshape.376), channel_id=1, source_target_pairs={{0,3},{1,0},{2,1},{3,2},{4,7},{5,4},{6,5},{7,6},{8,11},{9,8},{10,9... | collective-permute-start | bytes 27656 | tf_op jit(solution)/shard_map/ppermute | solution.py:148
  67.6 7.6 %collective-permute-start.11 = (f32[2,9,128]{2,1,0:T(8,128)S(1)}, f32[2,9,128]{2,1,0:T(8,128)S(1)}, u32[]{:S(2)}, u32[]{:S(2)}) collective-permute-start(f32[2,9,128]{2,1,0:T(8,128)S(1)} %reshape.376), channel_id=1, source_target_pairs={{0,2},{1,3},{2,0},{3,1},{4,6},{5,7},{6,4},{7,5},{8,10},{9,11},{10,... | collective-permute-start | bytes 27656 | tf_op jit(solution)/shard_map/ppermute | solution.py:148
  72.1 6.8 %collective-permute-start.12 = (f32[2,9,128]{2,1,0:T(8,128)S(1)}, f32[2,9,128]{2,1,0:T(8,128)S(1)}, u32[]{:S(2)}, u32[]{:S(2)}) collective-permute-start(f32[2,9,128]{2,1,0:T(8,128)S(1)} %reshape.376), channel_id=1, source_target_pairs={{0,1},{1,2},{2,3},{3,0},{4,5},{5,6},{6,7},{7,4},{8,9},{9,10},{10,1... | collective-permute-start | bytes 27656 | tf_op jit(solution)/shard_map/ppermute | solution.py:148
  74.9 8.5 %copy-start.4 = (f32[64,256]{1,0:T(8,128)S(1)}, f32[64,256]{1,0:T(8,128)}, u32[]{:S(2)}) copy-start(f32[64,256]{1,0:T(8,128)} %param.13) | copy-start | bytes 196612
  74.9 8.5 %copy-start.5 = (f32[2,64,256]{2,1,0:T(8,128)S(1)}, f32[2,64,256]{2,1,0:T(8,128)}, u32[]{:S(2)}) copy-start(f32[2,64,256]{2,1,0:T(8,128)} %param.14) | copy-start | bytes 393220
  79.0 4.6 %collective-permute-start.14 = (f32[768]{0:T(1024)S(1)}, f32[768]{0:T(1024)S(1)}, u32[]{:S(2)}, u32[]{:S(2)}) collective-permute-start(f32[768]{0:T(1024)S(1)} %reshape.380), channel_id=1, source_target_pairs={{16,0},{32,16},{48,32},{64,48},{80,64},{96,80},{112,96},{128,112},... | collective-permute-start | bytes 9224 | tf_op jit(solution)/shard_map/ppermute | solution.py:248
  81.0 6.1 %collective-permute-start.13 = (f32[768]{0:T(1024)S(1)}, f32[768]{0:T(1024)S(1)}, u32[]{:S(2)}, u32[]{:S(2)}) collective-permute-start(f32[768]{0:T(1024)S(1)} %reshape.378), channel_id=1, source_target_pairs={{0,16},{16,32},{32,48},{48,64},{64,80},{80,96},{96,112},{112,128},... | collective-permute-start | bytes 9224 | tf_op jit(solution)/shard_map/ppermute | solution.py:248
  87.1 3.9 %collective-permute-start.16 = (f32[1280]{0:T(1024)S(1)}, f32[1280]{0:T(1024)S(1)}, u32[]{:S(2)}, u32[]{:S(2)}) collective-permute-start(f32[1280]{0:T(1024)S(1)} %reshape.384), channel_id=1, source_target_pairs={{4,0},{8,4},{12,8},{5,1},{9,5},{13,9},{6,2},{10,6},{14,10},{7,3},{... | collective-permute-start | bytes 15368 | tf_op jit(solution)/shard_map/ppermute | solution.py:248
  89.5 5.5 %collective-permute-start.15 = (f32[1280]{0:T(1024)S(1)}, f32[1280]{0:T(1024)S(1)}, u32[]{:S(2)}, u32[]{:S(2)}) collective-permute-start(f32[1280]{0:T(1024)S(1)} %reshape.382), channel_id=1, source_target_pairs={{0,4},{4,8},{8,12},{1,5},{5,9},{9,13},{2,6},{6,10},{10,14},{3,7},{... | collective-permute-start | bytes 15368 | tf_op jit(solution)/shard_map/ppermute | solution.py:248

commit v4 on v3

--- a/solution.py
+++ b/solution.py
@@ -42,20 +42,18 @@
                 total = total + term
             vis_ref[tri] = total / 6.0 * weight
 
-        def tile_body(tile, carry):
-            row = pl.multiple_of((tile // 3) * 8, 8)
-            lane = pl.multiple_of((tile % 3) * 128, 128)
+        def tile_body(block, carry):
+            row = pl.multiple_of(block * 8, 8)
             for tri in range(2):
-                vals = [vals_ref[tri, beta, pl.ds(row, 8), pl.ds(lane, 128)] for beta in range(18)]
-                vis = vis_ref[tri, pl.ds(row, 8), pl.ds(lane, 128)]
+                vis = vis_ref[tri, pl.ds(row, 8), :]
                 for alpha in range(18):
-                    acc = kmat_ref[alpha, 0] * vals[0]
+                    acc = kmat_ref[alpha, 0] * vals_ref[tri, 0, pl.ds(row, 8), :]
                     for beta in range(1, 18):
-                        acc = acc + kmat_ref[alpha, beta] * vals[beta]
-                    resp_ref[tri, alpha, pl.ds(row, 8), pl.ds(lane, 128)] = acc * vis
+                        acc = acc + kmat_ref[alpha, beta] * vals_ref[tri, beta, pl.ds(row, 8), :]
+                    resp_ref[tri, alpha, pl.ds(row, 8), :] = acc * vis
             return carry
 
-        lax.fori_loop(0, 9, tile_body, 0)
+        lax.fori_loop(0, ROWS_PAD // 8, tile_body, 0)
         for height in range(2):
             own_layer = pair + height - 1
             if own_layer < 0 or own_layer > pairs - 2:
@@ -125,18 +123,18 @@
     row_of = jnp.where(live, index // cols, -1)
     col_of = jnp.where(live, index % cols, -1)
     pick_row = (row_of[:, None] == jnp.arange(rows, dtype=jnp.int32)[None]).astype(jnp.float32)
-    pick_col = col_of[:, None] == jnp.arange(cols, dtype=jnp.int32)[None]
+    pick_col = (col_of[:, None] == jnp.arange(cols, dtype=jnp.int32)[None]).astype(jnp.float32)
     return pick_row, pick_col
 
 
 def gather_slots(field, pick_row, pick_col):
-    rows_taken = jnp.einsum("sr,krc->ksc", pick_row, field, precision=HIGH)
-    return jnp.sum(jnp.where(pick_col[None], rows_taken, 0.0), axis=-1)
+    cols_taken = jnp.einsum("krc,sc->krs", field, pick_col, precision=HIGH)
+    return jnp.sum(jnp.where(pick_row.T[None] > 0.5, cols_taken, 0.0), axis=1)
 
 
 def scatter_slots(values, pick_row, pick_col):
-    spread = jnp.where(pick_col[None], values[:, :, None], 0.0)
-    return jnp.einsum("sr,ksc->krc", pick_row, spread, precision=HIGH)
+    weighted = pick_row[None] * values[:, :, None]
+    return jnp.einsum("ksr,sc->krc", weighted, pick_col, precision=HIGH)
 
 
 def layer_total(part):
@@ -309,7 +307,7 @@
     columns = iface_columns[0]
     col_row, col_col = slot_selectors(columns.reshape(-1), block_x, block_y)
     placed = scatter_slots(returned.reshape(2, -1), col_row, col_col)
-    marked = jnp.einsum("sr,sc->rc", col_row, col_col.astype(jnp.float32))
+    marked = jnp.einsum("sr,sc->rc", col_row, col_col)
     ring = jnp.concatenate([jnp.minimum(marked, 1.0)[None], placed], 0)
     field_ext = widened[:-1].reshape(4, depth_count, block_x + 2, block_y + 2)
     flag_cells = widened[-1, :-1, :-1]

time: 97.9 us -> 92.6 us (0.946)
  matrix products: 7.34 us -> 4.61 us
  Pallas kernels: 12.9 us -> 10.5 us
    dot_general x5, matrix products: 7.34 us -> 4.61 us  [the longest x2 2.4 us: gather_slots(): cols_taken = jnp.einsum('krc,sc->krs', field, pick_col, precision=HIGH)]
    pallas_call x1, Pallas kernels: 12.9 us -> 10.5 us  [fem_pallas(): pl.pallas_call(fem_kernel, out_shape=jax.ShapeDtypeStruct(body_force.shap...]
  transfers between devices with their start and end apart: 17 -> 17, of which waited for: 7 -> 7; matrix products, arithmetic and copies ran while one was open for 7% -> 6% of each run, Pallas kernels for 0% -> 0%
where the time goes in v4:
time: 92.6 us; the launch traced here: 91.9 us
  starting transfers between devices  41.4 us (45%)
  waiting for transfers between devices  24.5 us (26%)
  Pallas kernels  10.5 us (11%)
  other arithmetic  6.16 us (7%)
  matrix products  4.61 us (5%)
  local copies, waits for them, and re-layouts  3.32 us (4%)
  between operations  1.49 us (2%)
    ppermute x7, waiting for transfers between devices, exchange(): lax.ppermute(sent_up, axis, up)  20.7 us
    ppermute x7, starting transfers between devices, exchange(): lax.ppermute(sent_down, axis, down)  16 us
    ppermute x7, starting transfers between devices, exchange(): lax.ppermute(sent_up, axis, up)  15.1 us
    pallas_call x1, Pallas kernels, fem_pallas(): pl.pallas_call(fem_kernel, out_shape=jax.ShapeDtypeStruct(body_force.shap...  10.5 us
    ppermute x3, starting transfers between devices, layer_total(): received.append(lax.ppermute(part, 'layer', pairs))  10.2 us
    ppermute x3, waiting for transfers between devices, layer_total(): received.append(lax.ppermute(part, 'layer', pairs))  3.8 us
    dot_general x2, matrix products, gather_slots(): cols_taken = jnp.einsum('krc,sc->krs', field, pick_col, precision=HIGH)  2.4 us
    dot_general x2, matrix products, scatter_slots(): return jnp.einsum('ksr,sc->krc', weighted, pick_col, precision=HIGH)  1.87 us
  transfers between devices with their start and end apart: 17, of which 7 were waited for; matrix products, arithmetic and copies ran while one was open for 6% of the time, Pallas kernels for 0%

profile of v4, /device:TPU:408, one launch (start us, length us, event | category | flops | bytes accessed | tf_op | source)
XLA Modules:
  0.0 91.9 jit_solution(6128565198655309875)
XLA Ops:
  0.7 0.7 reduce.2
  1.5 1.7 %fusion.1 = f32[2,1152]{1,0:T(2,128)S(1)} fusion(f32[2,64,256]{2,1,0:T(8,128)} %param.11, s32[1152]{0:T(1024)S(1)} %get-tuple-element.42, pred[64,1152]{1,0:T(8,128)(4,1)S(1)} %convert_compare_fusion), kind=kOutput, calls=%fused_computation.3 | convolution fusion | flops 453572352 | bytes 218624 | tf_op jit(solution)/shard_map/krc,sc->krs/dot_general | solution.py:131
  3.5 3.6 %collective-permute-start.1 = (f32[4864]{0:T(1024)S(1)}, f32[4864]{0:T(1024)S(1)}, u32[]{:S(2)}, u32[]{:S(2)}) collective-permute-start(f32[4864]{0:T(1024)S(1)} %pad_maximum_fusion.24), channel_id=1, source_target_pairs={{16,0},{32,16},{48,32},{64,48},{80,64},{96,80},{112,96},{128,112},... | collective-permute-start | bytes 58376 | tf_op jit(solution)/shard_map/ppermute | solution.py:246
  7.1 1.9 %collective-permute-start = (f32[4864]{0:T(1024)S(1)}, f32[4864]{0:T(1024)S(1)}, u32[]{:S(2)}, u32[]{:S(2)}) collective-permute-start(f32[4864]{0:T(1024)S(1)} %pad_maximum_fusion.23), channel_id=1, source_target_pairs={{0,16},{16,32},{32,48},{48,64},{64,80},{80,96},{96,112},{112,128},... | collective-permute-start | bytes 58376 | tf_op jit(solution)/shard_map/ppermute | solution.py:246
  9.7 3.7 %collective-permute-done = f32[4864]{0:T(1024)S(1)} collective-permute-done((f32[4864]{0:T(1024)S(1)}, f32[4864]{0:T(1024)S(1)}, u32[]{:S(2)}, u32[]{:S(2)}) %collective-permute-start) | collective-permute-done | bytes 19488 | tf_op jit(solution)/shard_map/ppermute | solution.py:246
  14.4 2.6 %collective-permute-start.3 = (f32[1712]{0:T(1024)S(1)}, f32[1712]{0:T(1024)S(1)}, u32[]{:S(2)}, u32[]{:S(2)}) collective-permute-start(f32[1712]{0:T(1024)S(1)} %concatenate.68), channel_id=1, source_target_pairs={{4,0},{8,4},{12,8},{5,1},{9,5},{13,9},{6,2},{10,6},{14,10},{7,3},{... | collective-permute-start | bytes 20552 | tf_op jit(solution)/shard_map/ppermute | solution.py:246
  17.3 1.3 %collective-permute-start.2 = (f32[1712]{0:T(1024)S(1)}, f32[1712]{0:T(1024)S(1)}, u32[]{:S(2)}, u32[]{:S(2)}) collective-permute-start(f32[1712]{0:T(1024)S(1)} %concatenate.67), channel_id=1, source_target_pairs={{0,4},{4,8},{8,12},{1,5},{5,9},{9,13},{2,6},{6,10},{10,14},{3,7},{... | collective-permute-start | bytes 20552 | tf_op jit(solution)/shard_map/ppermute | solution.py:246
  18.6 0.7 add_convert_fusion.live_ref
  19.5 3.3 %collective-permute-done.2 = f32[1712]{0:T(1024)S(1)} collective-permute-done((f32[1712]{0:T(1024)S(1)}, f32[1712]{0:T(1024)S(1)}, u32[]{:S(2)}, u32[]{:S(2)}) %collective-permute-start.2) | collective-permute-done | bytes 6880 | tf_op jit(solution)/shard_map/ppermute | solution.py:246
  23.5 1.3 %collective-permute-start.9 = (f32[4,18,258]{2,1,0:T(8,128)S(1)}, f32[4,18,258]{2,1,0:T(8,128)S(1)}, u32[]{:S(2)}, u32[]{:S(2)}) collective-permute-start(f32[4,18,258]{2,1,0:T(8,128)S(1)} %get-tuple-element.23), channel_id=1, source_target_pairs={{1,0},{2,1},{3,2},{5,4},{6,5},{7,6},{9,8},{10,9},{11,10},{13,12},{... | collective-permute-start | bytes 222920 | tf_op jit(solution)/shard_map/ppermute | solution.py:246
  24.8 4.6 %collective-permute-start.8 = (f32[4,18,258]{2,1,0:T(8,128)S(1)}, f32[4,18,258]{2,1,0:T(8,128)S(1)}, u32[]{:S(2)}, u32[]{:S(2)}) collective-permute-start(f32[4,18,258]{2,1,0:T(8,128)S(1)} %get-tuple-element.22), channel_id=1, source_target_pairs={{0,1},{1,2},{2,3},{4,5},{5,6},{6,7},{8,9},{9,10},{10,11},{12,13},{... | collective-permute-start | bytes 222920 | tf_op jit(solution)/shard_map/ppermute | solution.py:246
  30.4 1.9 %collective-permute-start.5 = (f32[768]{0:T(1024)S(1)}, f32[768]{0:T(1024)S(1)}, u32[]{:S(2)}, u32[]{:S(2)}) collective-permute-start(f32[768]{0:T(1024)S(1)} %reshape.415), channel_id=1, source_target_pairs={{16,0},{32,16},{48,32},{64,48},{80,64},{96,80},{112,96},{128,112},... | collective-permute-start | bytes 9224 | tf_op jit(solution)/shard_map/ppermute | solution.py:246
  32.3 2.4 %collective-permute-start.4 = (f32[768]{0:T(1024)S(1)}, f32[768]{0:T(1024)S(1)}, u32[]{:S(2)}, u32[]{:S(2)}) collective-permute-start(f32[768]{0:T(1024)S(1)} %reshape.413), channel_id=1, source_target_pairs={{0,16},{16,32},{32,48},{48,64},{64,80},{80,96},{96,112},{112,128},... | collective-permute-start | bytes 9224 | tf_op jit(solution)/shard_map/ppermute | solution.py:246
  35.8 2.7 %collective-permute-done.4 = f32[768]{0:T(1024)S(1)} collective-permute-done((f32[768]{0:T(1024)S(1)}, f32[768]{0:T(1024)S(1)}, u32[]{:S(2)}, u32[]{:S(2)}) %collective-permute-start.4) | collective-permute-done | bytes 3104 | tf_op jit(solution)/shard_map/ppermute | solution.py:246
  38.8 2.4 %collective-permute-start.7 = (f32[54]{0:T(128)S(1)}, f32[54]{0:T(128)S(1)}, u32[]{:S(2)}, u32[]{:S(2)}) collective-permute-start(f32[54]{0:T(128)S(1)} %reshape.419), channel_id=1, source_target_pairs={{4,0},{8,4},{12,8},{5,1},{9,5},{13,9},{6,2},{10,6},{14,10},{7,3},{... | collective-permute-start | bytes 656 | tf_op jit(solution)/shard_map/ppermute | solution.py:246
  41.2 1.3 %collective-permute-start.6 = (f32[54]{0:T(128)S(1)}, f32[54]{0:T(128)S(1)}, u32[]{:S(2)}, u32[]{:S(2)}) collective-permute-start(f32[54]{0:T(128)S(1)} %reshape.417), channel_id=1, source_target_pairs={{0,4},{4,8},{8,12},{1,5},{5,9},{9,13},{2,6},{6,10},{10,14},{3,7},{... | collective-permute-start | bytes 656 | tf_op jit(solution)/shard_map/ppermute | solution.py:246
  43.2 3.4 %collective-permute-done.6 = f32[54]{0:T(128)S(1)} collective-permute-done((f32[54]{0:T(128)S(1)}, f32[54]{0:T(128)S(1)}, u32[]{:S(2)}, u32[]{:S(2)}) %collective-permute-start.6) | collective-permute-done | bytes 248 | tf_op jit(solution)/shard_map/ppermute | solution.py:246
  47.1 0.9 %select_maximum_fusion.fld_ref = f32[4,5,24,384]{3,2,1,0:T(8,128)} fusion(f32[2,5,18,258]{3,2,1,0:T(8,128)S(1)} %get-tuple-element.21, f32[2,5,18,258]{3,2,1,0:T(8,128)S(1)} %get-tuple-element.20), kind=kLoop, calls=%fused_computation.15 | loop fusion | flops 1474560 | bytes 1108800 | tf_op jit(solution)/shard_map/concatenate | solution.py:320
  48.0 10.5 %shard_map.122 = f32[3,3,16,256]{3,2,1,0:T(8,128)} custom-call(f32[4,5,24,384]{3,2,1,0:T(8,128)} %select_maximum_fusion.fld_ref, f32[24,384]{1,0:T(8,128)} %get-tuple-element.44.main_ref, f32[24,384]{1,0:T(8,128)} %get-tuple-element.43.weight_ref, f32[18,18]{1,0:T(8,128)} %kmat_ref.1, f32[2]{0:T(128)} %add_convert_fusion.live_ref, f32[3,3,16,256]{3,2,1,0:T(8,128)} %body_ref.1), custom_call_target="tpu_custom_call" | custom-call | tf_op jit(solution)/shard_map/pallas_call | solution.py:90
  58.6 0.9 slice_reduce_fusion.4
  59.5 0.7 fusion.14
  60.2 2.9 %collective-permute-start.10 = (f32[2,9,128]{2,1,0:T(8,128)S(1)}, f32[2,9,128]{2,1,0:T(8,128)S(1)}, u32[]{:S(2)}, u32[]{:S(2)}) collective-permute-start(f32[2,9,128]{2,1,0:T(8,128)S(1)} %reshape.424), channel_id=1, source_target_pairs={{0,3},{1,0},{2,1},{3,2},{4,7},{5,4},{6,5},{7,6},{8,11},{9,8},{10,9... | collective-permute-start | bytes 27656 | tf_op jit(solution)/shard_map/ppermute | solution.py:146
  63.1 4.5 %collective-permute-start.11 = (f32[2,9,128]{2,1,0:T(8,128)S(1)}, f32[2,9,128]{2,1,0:T(8,128)S(1)}, u32[]{:S(2)}, u32[]{:S(2)}) collective-permute-start(f32[2,9,128]{2,1,0:T(8,128)S(1)} %reshape.424), channel_id=1, source_target_pairs={{0,2},{1,3},{2,0},{3,1},{4,6},{5,7},{6,4},{7,5},{8,10},{9,11},{10,... | collective-permute-start | bytes 27656 | tf_op jit(solution)/shard_map/ppermute | solution.py:146
  67.6 2.8 %collective-permute-start.12 = (f32[2,9,128]{2,1,0:T(8,128)S(1)}, f32[2,9,128]{2,1,0:T(8,128)S(1)}, u32[]{:S(2)}, u32[]{:S(2)}) collective-permute-start(f32[2,9,128]{2,1,0:T(8,128)S(1)} %reshape.424), channel_id=1, source_target_pairs={{0,1},{1,2},{2,3},{3,0},{4,5},{5,6},{6,7},{7,4},{8,9},{9,10},{10,1... | collective-permute-start | bytes 27656 | tf_op jit(solution)/shard_map/ppermute | solution.py:146
  70.6 3.8 %collective-permute-done.12 = f32[2,9,128]{2,1,0:T(8,128)S(1)} collective-permute-done((f32[2,9,128]{2,1,0:T(8,128)S(1)}, f32[2,9,128]{2,1,0:T(8,128)S(1)}, u32[]{:S(2)}, u32[]{:S(2)}) %collective-permute-start.12) | collective-permute-done | bytes 9248 | tf_op jit(solution)/shard_map/ppermute | solution.py:146
  74.5 1.9 %collective-permute-start.14 = (f32[768]{0:T(1024)S(1)}, f32[768]{0:T(1024)S(1)}, u32[]{:S(2)}, u32[]{:S(2)}) collective-permute-start(f32[768]{0:T(1024)S(1)} %reshape.428), channel_id=1, source_target_pairs={{16,0},{32,16},{48,32},{64,48},{80,64},{96,80},{112,96},{128,112},... | collective-permute-start | bytes 9224 | tf_op jit(solution)/shard_map/ppermute | solution.py:246
  76.4 2.4 %collective-permute-start.13 = (f32[768]{0:T(1024)S(1)}, f32[768]{0:T(1024)S(1)}, u32[]{:S(2)}, u32[]{:S(2)}) collective-permute-start(f32[768]{0:T(1024)S(1)} %reshape.426), channel_id=1, source_target_pairs={{0,16},{16,32},{32,48},{48,64},{64,80},{80,96},{96,112},{112,128},... | collective-permute-start | bytes 9224 | tf_op jit(solution)/shard_map/ppermute | solution.py:246
  79.1 3.5 %collective-permute-done.13 = f32[768]{0:T(1024)S(1)} collective-permute-done((f32[768]{0:T(1024)S(1)}, f32[768]{0:T(1024)S(1)}, u32[]{:S(2)}, u32[]{:S(2)}) %collective-permute-start.13) | collective-permute-done | bytes 3104 | tf_op jit(solution)/shard_map/ppermute | solution.py:246
  82.6 2.4 %collective-permute-start.16 = (f32[1280]{0:T(1024)S(1)}, f32[1280]{0:T(1024)S(1)}, u32[]{:S(2)}, u32[]{:S(2)}) collective-permute-start(f32[1280]{0:T(1024)S(1)} %reshape.432), channel_id=1, source_target_pairs={{4,0},{8,4},{12,8},{5,1},{9,5},{13,9},{6,2},{10,6},{14,10},{7,3},{... | collective-permute-start | bytes 15368 | tf_op jit(solution)/shard_map/ppermute | solution.py:246
  85.0 1.3 %collective-permute-start.15 = (f32[1280]{0:T(1024)S(1)}, f32[1280]{0:T(1024)S(1)}, u32[]{:S(2)}, u32[]{:S(2)}) collective-permute-start(f32[1280]{0:T(1024)S(1)} %reshape.430), channel_id=1, source_target_pairs={{0,4},{4,8},{8,12},{1,5},{5,9},{9,13},{2,6},{6,10},{10,14},{3,7},{... | collective-permute-start | bytes 15368 | tf_op jit(solution)/shard_map/ppermute | solution.py:246
  86.5 4.0 %collective-permute-done.15 = f32[1280]{0:T(1024)S(1)} collective-permute-done((f32[1280]{0:T(1024)S(1)}, f32[1280]{0:T(1024)S(1)}, u32[]{:S(2)}, u32[]{:S(2)}) %collective-permute-start.15) | collective-permute-done | bytes 5152 | tf_op jit(solution)/shard_map/ppermute | solution.py:246
  90.6 1.3 %fusion.11 = f32[2,64,256]{2,1,0:T(8,128)} fusion(s32[1152]{0:T(1024)S(1)} %get-tuple-element.42, f32[2,1152]{1,0:T(2,128)S(1)} %bitcast.149, f32[1152,64]{0,1:T(8,128)S(1)} %fusion.27, f32[1,64,256]{2,1,0:T(8,128)S(1)} %fusion.35, f32[1,64,256]{2,1,0:T(8,128)S(1)} %fusion.41), kind=kOutput, calls=%fused_computation.11 | convolution fusion | flops 453492736 | bytes 570880 | tf_op jit(solution)/shard_map/ksr,sc->krc/dot_general | solution.py:137
  (137 shorter events, 7.2 us)
Async XLA Ops:
  0.6 2.6 %copy-start.6 = (s32[16,256]{1,0:T(8,128)S(1)}, s32[16,256]{1,0:T(8,128)}, u32[]{:S(2)}) copy-start(s32[16,256]{1,0:T(8,128)} %param.18) | copy-start | bytes 49156
  0.6 2.6 %copy-start.2 = (f32[3,16,256]{2,1,0:T(8,128)S(1)}, f32[3,16,256]{2,1,0:T(8,128)}, u32[]{:S(2)}) copy-start(f32[3,16,256]{2,1,0:T(8,128)} %param.16) | copy-start | bytes 147460
  0.7 2.6 %copy-start = (f32[3,3,16,256]{3,2,1,0:T(8,128)S(1)}, f32[3,3,16,256]{3,2,1,0:T(8,128)}, u32[]{:S(2)}) copy-start(f32[3,3,16,256]{3,2,1,0:T(8,128)} %param.15) | copy-start | bytes 442372
  1.4 2.0 %copy-start.1 = (f32[2,64,256]{2,1,0:T(8,128)S(1)}, f32[2,64,256]{2,1,0:T(8,128)}, u32[]{:S(2)}) copy-start(f32[2,64,256]{2,1,0:T(8,128)} %param.11) | copy-start | bytes 393220
  1.4 2.0 %copy-start.3 = (f32[64,256]{1,0:T(8,128)S(1)}, f32[64,256]{1,0:T(8,128)}, u32[]{:S(2)}) copy-start(f32[64,256]{1,0:T(8,128)} %param.12) | copy-start | bytes 196612
  1.5 7.5 %copy-start.7 = (s32[1,9,128]{2,0,1:T(1,128)S(1)}, s32[1,9,128]{2,0,1:T(1,128)}, u32[]{:S(2)}) copy-start(s32[1,9,128]{2,0,1:T(1,128)} %param.20) | copy-start | bytes 13828
  3.5 6.2 %collective-permute-start.1 = (f32[4864]{0:T(1024)S(1)}, f32[4864]{0:T(1024)S(1)}, u32[]{:S(2)}, u32[]{:S(2)}) collective-permute-start(f32[4864]{0:T(1024)S(1)} %pad_maximum_fusion.24), channel_id=1, source_target_pairs={{16,0},{32,16},{48,32},{64,48},{80,64},{96,80},{112,96},{128,112},... | collective-permute-start | bytes 58376 | tf_op jit(solution)/shard_map/ppermute | solution.py:246
  7.1 6.3 %collective-permute-start = (f32[4864]{0:T(1024)S(1)}, f32[4864]{0:T(1024)S(1)}, u32[]{:S(2)}, u32[]{:S(2)}) collective-permute-start(f32[4864]{0:T(1024)S(1)} %pad_maximum_fusion.23), channel_id=1, source_target_pairs={{0,16},{16,32},{32,48},{48,64},{64,80},{80,96},{96,112},{112,128},... | collective-permute-start | bytes 58376 | tf_op jit(solution)/shard_map/ppermute | solution.py:246
  14.4 4.8 %collective-permute-start.3 = (f32[1712]{0:T(1024)S(1)}, f32[1712]{0:T(1024)S(1)}, u32[]{:S(2)}, u32[]{:S(2)}) collective-permute-start(f32[1712]{0:T(1024)S(1)} %concatenate.68), channel_id=1, source_target_pairs={{4,0},{8,4},{12,8},{5,1},{9,5},{13,9},{6,2},{10,6},{14,10},{7,3},{... | collective-permute-start | bytes 20552 | tf_op jit(solution)/shard_map/ppermute | solution.py:246
  17.3 5.5 %collective-permute-start.2 = (f32[1712]{0:T(1024)S(1)}, f32[1712]{0:T(1024)S(1)}, u32[]{:S(2)}, u32[]{:S(2)}) collective-permute-start(f32[1712]{0:T(1024)S(1)} %concatenate.67), channel_id=1, source_target_pairs={{0,4},{4,8},{8,12},{1,5},{5,9},{9,13},{2,6},{6,10},{10,14},{3,7},{... | collective-permute-start | bytes 20552 | tf_op jit(solution)/shard_map/ppermute | solution.py:246
  23.5 23.5 %collective-permute-start.9 = (f32[4,18,258]{2,1,0:T(8,128)S(1)}, f32[4,18,258]{2,1,0:T(8,128)S(1)}, u32[]{:S(2)}, u32[]{:S(2)}) collective-permute-start(f32[4,18,258]{2,1,0:T(8,128)S(1)} %get-tuple-element.23), channel_id=1, source_target_pairs={{1,0},{2,1},{3,2},{5,4},{6,5},{7,6},{9,8},{10,9},{11,10},{13,12},{... | collective-permute-start | bytes 222920 | tf_op jit(solution)/shard_map/ppermute | solution.py:246
  24.8 22.2 %collective-permute-start.8 = (f32[4,18,258]{2,1,0:T(8,128)S(1)}, f32[4,18,258]{2,1,0:T(8,128)S(1)}, u32[]{:S(2)}, u32[]{:S(2)}) collective-permute-start(f32[4,18,258]{2,1,0:T(8,128)S(1)} %get-tuple-element.22), channel_id=1, source_target_pairs={{0,1},{1,2},{2,3},{4,5},{5,6},{6,7},{8,9},{9,10},{10,11},{12,13},{... | collective-permute-start | bytes 222920 | tf_op jit(solution)/shard_map/ppermute | solution.py:246
  30.4 5.4 %collective-permute-start.5 = (f32[768]{0:T(1024)S(1)}, f32[768]{0:T(1024)S(1)}, u32[]{:S(2)}, u32[]{:S(2)}) collective-permute-start(f32[768]{0:T(1024)S(1)} %reshape.415), channel_id=1, source_target_pairs={{16,0},{32,16},{48,32},{64,48},{80,64},{96,80},{112,96},{128,112},... | collective-permute-start | bytes 9224 | tf_op jit(solution)/shard_map/ppermute | solution.py:246
  32.3 6.1 %collective-permute-start.4 = (f32[768]{0:T(1024)S(1)}, f32[768]{0:T(1024)S(1)}, u32[]{:S(2)}, u32[]{:S(2)}) collective-permute-start(f32[768]{0:T(1024)S(1)} %reshape.413), channel_id=1, source_target_pairs={{0,16},{16,32},{32,48},{48,64},{64,80},{80,96},{96,112},{112,128},... | collective-permute-start | bytes 9224 | tf_op jit(solution)/shard_map/ppermute | solution.py:246
  38.8 4.4 %collective-permute-start.7 = (f32[54]{0:T(128)S(1)}, f32[54]{0:T(128)S(1)}, u32[]{:S(2)}, u32[]{:S(2)}) collective-permute-start(f32[54]{0:T(128)S(1)} %reshape.419), channel_id=1, source_target_pairs={{4,0},{8,4},{12,8},{5,1},{9,5},{13,9},{6,2},{10,6},{14,10},{7,3},{... | collective-permute-start | bytes 656 | tf_op jit(solution)/shard_map/ppermute | solution.py:246
  41.2 5.4 %collective-permute-start.6 = (f32[54]{0:T(128)S(1)}, f32[54]{0:T(128)S(1)}, u32[]{:S(2)}, u32[]{:S(2)}) collective-permute-start(f32[54]{0:T(128)S(1)} %reshape.417), channel_id=1, source_target_pairs={{0,4},{4,8},{8,12},{1,5},{5,9},{9,13},{2,6},{6,10},{10,14},{3,7},{... | collective-permute-start | bytes 656 | tf_op jit(solution)/shard_map/ppermute | solution.py:246
  60.2 10.4 %collective-permute-start.10 = (f32[2,9,128]{2,1,0:T(8,128)S(1)}, f32[2,9,128]{2,1,0:T(8,128)S(1)}, u32[]{:S(2)}, u32[]{:S(2)}) collective-permute-start(f32[2,9,128]{2,1,0:T(8,128)S(1)} %reshape.424), channel_id=1, source_target_pairs={{0,3},{1,0},{2,1},{3,2},{4,7},{5,4},{6,5},{7,6},{8,11},{9,8},{10,9... | collective-permute-start | bytes 27656 | tf_op jit(solution)/shard_map/ppermute | solution.py:146
  63.1 7.6 %collective-permute-start.11 = (f32[2,9,128]{2,1,0:T(8,128)S(1)}, f32[2,9,128]{2,1,0:T(8,128)S(1)}, u32[]{:S(2)}, u32[]{:S(2)}) collective-permute-start(f32[2,9,128]{2,1,0:T(8,128)S(1)} %reshape.424), channel_id=1, source_target_pairs={{0,2},{1,3},{2,0},{3,1},{4,6},{5,7},{6,4},{7,5},{8,10},{9,11},{10,... | collective-permute-start | bytes 27656 | tf_op jit(solution)/shard_map/ppermute | solution.py:146
  67.6 6.8 %collective-permute-start.12 = (f32[2,9,128]{2,1,0:T(8,128)S(1)}, f32[2,9,128]{2,1,0:T(8,128)S(1)}, u32[]{:S(2)}, u32[]{:S(2)}) collective-permute-start(f32[2,9,128]{2,1,0:T(8,128)S(1)} %reshape.424), channel_id=1, source_target_pairs={{0,1},{1,2},{2,3},{3,0},{4,5},{5,6},{6,7},{7,4},{8,9},{9,10},{10,1... | collective-permute-start | bytes 27656 | tf_op jit(solution)/shard_map/ppermute | solution.py:146
  70.4 8.5 %copy-start.4 = (f32[64,256]{1,0:T(8,128)S(1)}, f32[64,256]{1,0:T(8,128)}, u32[]{:S(2)}) copy-start(f32[64,256]{1,0:T(8,128)} %param.13) | copy-start | bytes 196612
  70.4 8.5 %copy-start.5 = (f32[2,64,256]{2,1,0:T(8,128)S(1)}, f32[2,64,256]{2,1,0:T(8,128)}, u32[]{:S(2)}) copy-start(f32[2,64,256]{2,1,0:T(8,128)} %param.14) | copy-start | bytes 393220
  74.5 4.6 %collective-permute-start.14 = (f32[768]{0:T(1024)S(1)}, f32[768]{0:T(1024)S(1)}, u32[]{:S(2)}, u32[]{:S(2)}) collective-permute-start(f32[768]{0:T(1024)S(1)} %reshape.428), channel_id=1, source_target_pairs={{16,0},{32,16},{48,32},{64,48},{80,64},{96,80},{112,96},{128,112},... | collective-permute-start | bytes 9224 | tf_op jit(solution)/shard_map/ppermute | solution.py:246
  76.4 6.1 %collective-permute-start.13 = (f32[768]{0:T(1024)S(1)}, f32[768]{0:T(1024)S(1)}, u32[]{:S(2)}, u32[]{:S(2)}) collective-permute-start(f32[768]{0:T(1024)S(1)} %reshape.426), channel_id=1, source_target_pairs={{0,16},{16,32},{32,48},{48,64},{64,80},{80,96},{96,112},{112,128},... | collective-permute-start | bytes 9224 | tf_op jit(solution)/shard_map/ppermute | solution.py:246
  82.6 3.9 %collective-permute-start.16 = (f32[1280]{0:T(1024)S(1)}, f32[1280]{0:T(1024)S(1)}, u32[]{:S(2)}, u32[]{:S(2)}) collective-permute-start(f32[1280]{0:T(1024)S(1)} %reshape.432), channel_id=1, source_target_pairs={{4,0},{8,4},{12,8},{5,1},{9,5},{13,9},{6,2},{10,6},{14,10},{7,3},{... | collective-permute-start | bytes 15368 | tf_op jit(solution)/shard_map/ppermute | solution.py:246
  85.0 5.5 %collective-permute-start.15 = (f32[1280]{0:T(1024)S(1)}, f32[1280]{0:T(1024)S(1)}, u32[]{:S(2)}, u32[]{:S(2)}) collective-permute-start(f32[1280]{0:T(1024)S(1)} %reshape.430), channel_id=1, source_target_pairs={{0,4},{4,8},{8,12},{1,5},{5,9},{9,13},{2,6},{6,10},{10,14},{3,7},{... | collective-permute-start | bytes 15368 | tf_op jit(solution)/shard_map/ppermute | solution.py:246

commit v5 on v4

--- a/solution.py
+++ b/solution.py
@@ -140,17 +140,13 @@
 def layer_total(part):
     count = lax.axis_size("layer")
     place = lax.axis_index("layer")
-    received = [part]
-    for shift in range(1, count):
-        pairs = [(i, (i + shift) % count) for i in range(count)]
-        received.append(lax.ppermute(part, "layer", pairs))
-    total = None
-    for source in range(count):
-        wanted = (place - source) % count
-        value = received[0]
-        for shift in range(1, count):
-            value = jnp.where(wanted == shift, received[shift], value)
-        total = value if total is None else total + value
+    total = part
+    step = 1
+    while step < count:
+        pairs = [(i, i ^ step) for i in range(count)]
+        other = lax.ppermute(total, "layer", pairs)
+        total = jnp.where((place & step) == 0, total + other, other + total)
+        step *= 2
     return total
 
 

time: 92.6 us -> 91.1 us (0.984)
  the two profiles are of different devices: /device:TPU:408 before, /device:TPU:410 now
where the time goes in v5:
time: 91.1 us; the launch traced here: 90.4 us
  starting transfers between devices  36.6 us (40%)
  waiting for transfers between devices  27.7 us (30%)
  Pallas kernels  10.5 us (12%)
  other arithmetic  6.17 us (7%)
  matrix products  4.61 us (5%)
  local copies, waits for them, and re-layouts  3.32 us (4%)
  between operations  1.46 us (2%)
    ppermute x7, waiting for transfers between devices, exchange(): lax.ppermute(sent_up, axis, up)  20.9 us
    ppermute x7, starting transfers between devices, exchange(): lax.ppermute(sent_down, axis, down)  17.2 us
    ppermute x7, starting transfers between devices, exchange(): lax.ppermute(sent_up, axis, up)  14 us
    pallas_call x1, Pallas kernels, fem_pallas(): pl.pallas_call(fem_kernel, out_shape=jax.ShapeDtypeStruct(body_force.shap...  10.5 us
    ppermute x2, waiting for transfers between devices, layer_total(): other = lax.ppermute(total, 'layer', pairs)  6.81 us
    ppermute x2, starting transfers between devices, layer_total(): other = lax.ppermute(total, 'layer', pairs)  5.45 us
    dot_general x2, matrix products, gather_slots(): cols_taken = jnp.einsum('krc,sc->krs', field, pick_col, precision=HIGH)  2.4 us
    dot_general x2, matrix products, scatter_slots(): return jnp.einsum('ksr,sc->krc', weighted, pick_col, precision=HIGH)  1.87 us
  transfers between devices with their start and end apart: 16, of which 8 were waited for; matrix products, arithmetic and copies ran while one was open for 6% of the time, Pallas kernels for 0%

profile of v5, /device:TPU:410, one launch (start us, length us, event | category | flops | bytes accessed | tf_op | source)
XLA Modules:
  0.0 90.4 jit_solution(10645861328863524944)
XLA Ops:
  0.7 0.7 reduce.2
  1.5 1.7 %fusion.1 = f32[2,1152]{1,0:T(2,128)S(1)} fusion(f32[2,64,256]{2,1,0:T(8,128)} %param.11, s32[1152]{0:T(1024)S(1)} %get-tuple-element.42, pred[64,1152]{1,0:T(8,128)(4,1)S(1)} %convert_compare_fusion), kind=kOutput, calls=%fused_computation.3 | convolution fusion | flops 453572352 | bytes 218624 | tf_op jit(solution)/shard_map/krc,sc->krs/dot_general | solution.py:131
  3.5 3.6 %collective-permute-start.1 = (f32[4864]{0:T(1024)S(1)}, f32[4864]{0:T(1024)S(1)}, u32[]{:S(2)}, u32[]{:S(2)}) collective-permute-start(f32[4864]{0:T(1024)S(1)} %pad_maximum_fusion.24), channel_id=1, source_target_pairs={{16,0},{32,16},{48,32},{64,48},{80,64},{96,80},{112,96},{128,112},... | collective-permute-start | bytes 58376 | tf_op jit(solution)/shard_map/ppermute | solution.py:242
  7.1 1.9 %collective-permute-start = (f32[4864]{0:T(1024)S(1)}, f32[4864]{0:T(1024)S(1)}, u32[]{:S(2)}, u32[]{:S(2)}) collective-permute-start(f32[4864]{0:T(1024)S(1)} %pad_maximum_fusion.23), channel_id=1, source_target_pairs={{0,16},{16,32},{32,48},{48,64},{64,80},{80,96},{96,112},{112,128},... | collective-permute-start | bytes 58376 | tf_op jit(solution)/shard_map/ppermute | solution.py:242
  9.7 3.7 %collective-permute-done = f32[4864]{0:T(1024)S(1)} collective-permute-done((f32[4864]{0:T(1024)S(1)}, f32[4864]{0:T(1024)S(1)}, u32[]{:S(2)}, u32[]{:S(2)}) %collective-permute-start) | collective-permute-done | bytes 19488 | tf_op jit(solution)/shard_map/ppermute | solution.py:242
  14.4 2.6 %collective-permute-start.3 = (f32[1712]{0:T(1024)S(1)}, f32[1712]{0:T(1024)S(1)}, u32[]{:S(2)}, u32[]{:S(2)}) collective-permute-start(f32[1712]{0:T(1024)S(1)} %concatenate.68), channel_id=1, source_target_pairs={{4,0},{8,4},{12,8},{5,1},{9,5},{13,9},{6,2},{10,6},{14,10},{7,3},{... | collective-permute-start | bytes 20552 | tf_op jit(solution)/shard_map/ppermute | solution.py:242
  17.3 1.3 %collective-permute-start.2 = (f32[1712]{0:T(1024)S(1)}, f32[1712]{0:T(1024)S(1)}, u32[]{:S(2)}, u32[]{:S(2)}) collective-permute-start(f32[1712]{0:T(1024)S(1)} %concatenate.67), channel_id=1, source_target_pairs={{0,4},{4,8},{8,12},{1,5},{5,9},{9,13},{2,6},{6,10},{10,14},{3,7},{... | collective-permute-start | bytes 20552 | tf_op jit(solution)/shard_map/ppermute | solution.py:242
  18.6 0.7 add_convert_fusion.live_ref
  19.5 3.3 %collective-permute-done.2 = f32[1712]{0:T(1024)S(1)} collective-permute-done((f32[1712]{0:T(1024)S(1)}, f32[1712]{0:T(1024)S(1)}, u32[]{:S(2)}, u32[]{:S(2)}) %collective-permute-start.2) | collective-permute-done | bytes 6880 | tf_op jit(solution)/shard_map/ppermute | solution.py:242
  23.5 2.4 %collective-permute-start.9 = (f32[4,18,258]{2,1,0:T(8,128)S(1)}, f32[4,18,258]{2,1,0:T(8,128)S(1)}, u32[]{:S(2)}, u32[]{:S(2)}) collective-permute-start(f32[4,18,258]{2,1,0:T(8,128)S(1)} %get-tuple-element.23), channel_id=1, source_target_pairs={{1,0},{2,1},{3,2},{5,4},{6,5},{7,6},{9,8},{10,9},{11,10},{13,12},{... | collective-permute-start | bytes 222920 | tf_op jit(solution)/shard_map/ppermute | solution.py:242
  25.9 3.4 %collective-permute-start.8 = (f32[4,18,258]{2,1,0:T(8,128)S(1)}, f32[4,18,258]{2,1,0:T(8,128)S(1)}, u32[]{:S(2)}, u32[]{:S(2)}) collective-permute-start(f32[4,18,258]{2,1,0:T(8,128)S(1)} %get-tuple-element.22), channel_id=1, source_target_pairs={{0,1},{1,2},{2,3},{4,5},{5,6},{6,7},{8,9},{9,10},{10,11},{12,13},{... | collective-permute-start | bytes 222920 | tf_op jit(solution)/shard_map/ppermute | solution.py:242
  30.4 1.9 %collective-permute-start.5 = (f32[768]{0:T(1024)S(1)}, f32[768]{0:T(1024)S(1)}, u32[]{:S(2)}, u32[]{:S(2)}) collective-permute-start(f32[768]{0:T(1024)S(1)} %reshape.415), channel_id=1, source_target_pairs={{16,0},{32,16},{48,32},{64,48},{80,64},{96,80},{112,96},{128,112},... | collective-permute-start | bytes 9224 | tf_op jit(solution)/shard_map/ppermute | solution.py:242
  32.3 2.4 %collective-permute-start.4 = (f32[768]{0:T(1024)S(1)}, f32[768]{0:T(1024)S(1)}, u32[]{:S(2)}, u32[]{:S(2)}) collective-permute-start(f32[768]{0:T(1024)S(1)} %reshape.413), channel_id=1, source_target_pairs={{0,16},{16,32},{32,48},{48,64},{64,80},{80,96},{96,112},{112,128},... | collective-permute-start | bytes 9224 | tf_op jit(solution)/shard_map/ppermute | solution.py:242
  35.5 2.9 %collective-permute-done.4 = f32[768]{0:T(1024)S(1)} collective-permute-done((f32[768]{0:T(1024)S(1)}, f32[768]{0:T(1024)S(1)}, u32[]{:S(2)}, u32[]{:S(2)}) %collective-permute-start.4) | collective-permute-done | bytes 3104 | tf_op jit(solution)/shard_map/ppermute | solution.py:242
  38.7 2.4 %collective-permute-start.7 = (f32[54]{0:T(128)S(1)}, f32[54]{0:T(128)S(1)}, u32[]{:S(2)}, u32[]{:S(2)}) collective-permute-start(f32[54]{0:T(128)S(1)} %reshape.419), channel_id=1, source_target_pairs={{4,0},{8,4},{12,8},{5,1},{9,5},{13,9},{6,2},{10,6},{14,10},{7,3},{... | collective-permute-start | bytes 656 | tf_op jit(solution)/shard_map/ppermute | solution.py:242
  41.2 1.3 %collective-permute-start.6 = (f32[54]{0:T(128)S(1)}, f32[54]{0:T(128)S(1)}, u32[]{:S(2)}, u32[]{:S(2)}) collective-permute-start(f32[54]{0:T(128)S(1)} %reshape.417), channel_id=1, source_target_pairs={{0,4},{4,8},{8,12},{1,5},{5,9},{9,13},{2,6},{6,10},{10,14},{3,7},{... | collective-permute-start | bytes 656 | tf_op jit(solution)/shard_map/ppermute | solution.py:242
  43.2 3.4 %collective-permute-done.6 = f32[54]{0:T(128)S(1)} collective-permute-done((f32[54]{0:T(128)S(1)}, f32[54]{0:T(128)S(1)}, u32[]{:S(2)}, u32[]{:S(2)}) %collective-permute-start.6) | collective-permute-done | bytes 248 | tf_op jit(solution)/shard_map/ppermute | solution.py:242
  47.1 1.0 %select_maximum_fusion.fld_ref = f32[4,5,24,384]{3,2,1,0:T(8,128)} fusion(f32[2,5,18,258]{3,2,1,0:T(8,128)S(1)} %get-tuple-element.21, f32[2,5,18,258]{3,2,1,0:T(8,128)S(1)} %get-tuple-element.20), kind=kLoop, calls=%fused_computation.15 | loop fusion | flops 1474560 | bytes 1108800 | tf_op jit(solution)/shard_map/concatenate | solution.py:316
  48.1 10.5 %shard_map.122 = f32[3,3,16,256]{3,2,1,0:T(8,128)} custom-call(f32[4,5,24,384]{3,2,1,0:T(8,128)} %select_maximum_fusion.fld_ref, f32[24,384]{1,0:T(8,128)} %get-tuple-element.44.main_ref, f32[24,384]{1,0:T(8,128)} %get-tuple-element.43.weight_ref, f32[18,18]{1,0:T(8,128)} %kmat_ref.1, f32[2]{0:T(128)} %add_convert_fusion.live_ref, f32[3,3,16,256]{3,2,1,0:T(8,128)} %body_ref.1), custom_call_target="tpu_custom_call" | custom-call | tf_op jit(solution)/shard_map/pallas_call | solution.py:90
  58.6 0.9 %slice_reduce_fusion.4 = f32[2,16,256]{2,1,0:T(8,128)S(1)} fusion(f32[3,3,16,256]{3,2,1,0:T(8,128)} %shard_map.122), kind=kLoop, calls=%fused_computation.60 | loop fusion | flops 16384 | bytes 131072 | tf_op jit(solution)/shard_map/reduce_sum | solution.py:333
  59.5 0.7 fusion.14
  60.2 2.4 %collective-permute-start.10 = (f32[2,9,128]{2,1,0:T(8,128)S(1)}, f32[2,9,128]{2,1,0:T(8,128)S(1)}, u32[]{:S(2)}, u32[]{:S(2)}) collective-permute-start(f32[2,9,128]{2,1,0:T(8,128)S(1)} %reshape.424), channel_id=1, source_target_pairs={{0,1},{1,0},{2,3},{3,2},{4,5},{5,4},{6,7},{7,6},{8,9},{9,8},{10,11... | collective-permute-start | bytes 27656 | tf_op jit(solution)/shard_map/ppermute | solution.py:147
  62.9 2.9 %collective-permute-done.10 = f32[2,9,128]{2,1,0:T(8,128)S(1)} collective-permute-done((f32[2,9,128]{2,1,0:T(8,128)S(1)}, f32[2,9,128]{2,1,0:T(8,128)S(1)}, u32[]{:S(2)}, u32[]{:S(2)}) %collective-permute-start.10) | collective-permute-done | bytes 9248 | tf_op jit(solution)/shard_map/ppermute | solution.py:147
  65.8 3.0 %collective-permute-start.11 = (f32[2,9,128]{2,1,0:T(8,128)S(1)}, f32[2,9,128]{2,1,0:T(8,128)S(1)}, u32[]{:S(2)}, u32[]{:S(2)}) collective-permute-start(f32[2,9,128]{2,1,0:T(8,128)S(1)} %add.173), channel_id=1, source_target_pairs={{0,2},{1,3},{2,0},{3,1},{4,6},{5,7},{6,4},{7,5},{8,10},{9,11},{10,... | collective-permute-start | bytes 27656 | tf_op jit(solution)/shard_map/ppermute | solution.py:147
  69.1 3.9 %collective-permute-done.11 = f32[2,9,128]{2,1,0:T(8,128)S(1)} collective-permute-done((f32[2,9,128]{2,1,0:T(8,128)S(1)}, f32[2,9,128]{2,1,0:T(8,128)S(1)}, u32[]{:S(2)}, u32[]{:S(2)}) %collective-permute-start.11) | collective-permute-done | bytes 9248 | tf_op jit(solution)/shard_map/ppermute | solution.py:147
  73.0 1.9 %collective-permute-start.13 = (f32[768]{0:T(1024)S(1)}, f32[768]{0:T(1024)S(1)}, u32[]{:S(2)}, u32[]{:S(2)}) collective-permute-start(f32[768]{0:T(1024)S(1)} %reshape.428), channel_id=1, source_target_pairs={{16,0},{32,16},{48,32},{64,48},{80,64},{96,80},{112,96},{128,112},... | collective-permute-start | bytes 9224 | tf_op jit(solution)/shard_map/ppermute | solution.py:242
  75.0 2.4 %collective-permute-start.12 = (f32[768]{0:T(1024)S(1)}, f32[768]{0:T(1024)S(1)}, u32[]{:S(2)}, u32[]{:S(2)}) collective-permute-start(f32[768]{0:T(1024)S(1)} %reshape.426), channel_id=1, source_target_pairs={{0,16},{16,32},{32,48},{48,64},{64,80},{80,96},{96,112},{112,128},... | collective-permute-start | bytes 9224 | tf_op jit(solution)/shard_map/ppermute | solution.py:242
  77.6 3.5 %collective-permute-done.12 = f32[768]{0:T(1024)S(1)} collective-permute-done((f32[768]{0:T(1024)S(1)}, f32[768]{0:T(1024)S(1)}, u32[]{:S(2)}, u32[]{:S(2)}) %collective-permute-start.12) | collective-permute-done | bytes 3104 | tf_op jit(solution)/shard_map/ppermute | solution.py:242
  81.1 2.4 %collective-permute-start.15 = (f32[1280]{0:T(1024)S(1)}, f32[1280]{0:T(1024)S(1)}, u32[]{:S(2)}, u32[]{:S(2)}) collective-permute-start(f32[1280]{0:T(1024)S(1)} %reshape.432), channel_id=1, source_target_pairs={{4,0},{8,4},{12,8},{5,1},{9,5},{13,9},{6,2},{10,6},{14,10},{7,3},{... | collective-permute-start | bytes 15368 | tf_op jit(solution)/shard_map/ppermute | solution.py:242
  83.5 1.3 %collective-permute-start.14 = (f32[1280]{0:T(1024)S(1)}, f32[1280]{0:T(1024)S(1)}, u32[]{:S(2)}, u32[]{:S(2)}) collective-permute-start(f32[1280]{0:T(1024)S(1)} %reshape.430), channel_id=1, source_target_pairs={{0,4},{4,8},{8,12},{1,5},{5,9},{9,13},{2,6},{6,10},{10,14},{3,7},{... | collective-permute-start | bytes 15368 | tf_op jit(solution)/shard_map/ppermute | solution.py:242
  85.0 4.0 %collective-permute-done.14 = f32[1280]{0:T(1024)S(1)} collective-permute-done((f32[1280]{0:T(1024)S(1)}, f32[1280]{0:T(1024)S(1)}, u32[]{:S(2)}, u32[]{:S(2)}) %collective-permute-start.14) | collective-permute-done | bytes 5152 | tf_op jit(solution)/shard_map/ppermute | solution.py:242
  89.1 1.3 %fusion.11 = f32[2,64,256]{2,1,0:T(8,128)} fusion(s32[1152]{0:T(1024)S(1)} %get-tuple-element.42, f32[2,1152]{1,0:T(2,128)S(1)} %bitcast.149, f32[1152,64]{0,1:T(8,128)S(1)} %fusion.27, f32[1,64,256]{2,1,0:T(8,128)S(1)} %fusion.35, f32[1,64,256]{2,1,0:T(8,128)S(1)} %fusion.41), kind=kOutput, calls=%fused_computation.11 | convolution fusion | flops 453492736 | bytes 570880 | tf_op jit(solution)/shard_map/ksr,sc->krc/dot_general | solution.py:137
  (136 shorter events, 7.1 us)
Async XLA Ops:
  0.6 2.6 %copy-start.6 = (s32[16,256]{1,0:T(8,128)S(1)}, s32[16,256]{1,0:T(8,128)}, u32[]{:S(2)}) copy-start(s32[16,256]{1,0:T(8,128)} %param.18) | copy-start | bytes 49156
  0.6 2.6 %copy-start.2 = (f32[3,16,256]{2,1,0:T(8,128)S(1)}, f32[3,16,256]{2,1,0:T(8,128)}, u32[]{:S(2)}) copy-start(f32[3,16,256]{2,1,0:T(8,128)} %param.16) | copy-start | bytes 147460
  0.7 2.6 %copy-start = (f32[3,3,16,256]{3,2,1,0:T(8,128)S(1)}, f32[3,3,16,256]{3,2,1,0:T(8,128)}, u32[]{:S(2)}) copy-start(f32[3,3,16,256]{3,2,1,0:T(8,128)} %param.15) | copy-start | bytes 442372
  1.4 2.0 %copy-start.1 = (f32[2,64,256]{2,1,0:T(8,128)S(1)}, f32[2,64,256]{2,1,0:T(8,128)}, u32[]{:S(2)}) copy-start(f32[2,64,256]{2,1,0:T(8,128)} %param.11) | copy-start | bytes 393220
  1.4 2.0 %copy-start.3 = (f32[64,256]{1,0:T(8,128)S(1)}, f32[64,256]{1,0:T(8,128)}, u32[]{:S(2)}) copy-start(f32[64,256]{1,0:T(8,128)} %param.12) | copy-start | bytes 196612
  1.5 7.5 %copy-start.7 = (s32[1,9,128]{2,0,1:T(1,128)S(1)}, s32[1,9,128]{2,0,1:T(1,128)}, u32[]{:S(2)}) copy-start(s32[1,9,128]{2,0,1:T(1,128)} %param.20) | copy-start | bytes 13828
  3.5 6.2 %collective-permute-start.1 = (f32[4864]{0:T(1024)S(1)}, f32[4864]{0:T(1024)S(1)}, u32[]{:S(2)}, u32[]{:S(2)}) collective-permute-start(f32[4864]{0:T(1024)S(1)} %pad_maximum_fusion.24), channel_id=1, source_target_pairs={{16,0},{32,16},{48,32},{64,48},{80,64},{96,80},{112,96},{128,112},... | collective-permute-start | bytes 58376 | tf_op jit(solution)/shard_map/ppermute | solution.py:242
  7.1 6.3 %collective-permute-start = (f32[4864]{0:T(1024)S(1)}, f32[4864]{0:T(1024)S(1)}, u32[]{:S(2)}, u32[]{:S(2)}) collective-permute-start(f32[4864]{0:T(1024)S(1)} %pad_maximum_fusion.23), channel_id=1, source_target_pairs={{0,16},{16,32},{32,48},{48,64},{64,80},{80,96},{96,112},{112,128},... | collective-permute-start | bytes 58376 | tf_op jit(solution)/shard_map/ppermute | solution.py:242
  14.4 4.9 %collective-permute-start.3 = (f32[1712]{0:T(1024)S(1)}, f32[1712]{0:T(1024)S(1)}, u32[]{:S(2)}, u32[]{:S(2)}) collective-permute-start(f32[1712]{0:T(1024)S(1)} %concatenate.68), channel_id=1, source_target_pairs={{4,0},{8,4},{12,8},{5,1},{9,5},{13,9},{6,2},{10,6},{14,10},{7,3},{... | collective-permute-start | bytes 20552 | tf_op jit(solution)/shard_map/ppermute | solution.py:242
  17.3 5.5 %collective-permute-start.2 = (f32[1712]{0:T(1024)S(1)}, f32[1712]{0:T(1024)S(1)}, u32[]{:S(2)}, u32[]{:S(2)}) collective-permute-start(f32[1712]{0:T(1024)S(1)} %concatenate.67), channel_id=1, source_target_pairs={{0,4},{4,8},{8,12},{1,5},{5,9},{9,13},{2,6},{6,10},{10,14},{3,7},{... | collective-permute-start | bytes 20552 | tf_op jit(solution)/shard_map/ppermute | solution.py:242
  23.5 23.5 %collective-permute-start.9 = (f32[4,18,258]{2,1,0:T(8,128)S(1)}, f32[4,18,258]{2,1,0:T(8,128)S(1)}, u32[]{:S(2)}, u32[]{:S(2)}) collective-permute-start(f32[4,18,258]{2,1,0:T(8,128)S(1)} %get-tuple-element.23), channel_id=1, source_target_pairs={{1,0},{2,1},{3,2},{5,4},{6,5},{7,6},{9,8},{10,9},{11,10},{13,12},{... | collective-permute-start | bytes 222920 | tf_op jit(solution)/shard_map/ppermute | solution.py:242
  25.9 21.1 %collective-permute-start.8 = (f32[4,18,258]{2,1,0:T(8,128)S(1)}, f32[4,18,258]{2,1,0:T(8,128)S(1)}, u32[]{:S(2)}, u32[]{:S(2)}) collective-permute-start(f32[4,18,258]{2,1,0:T(8,128)S(1)} %get-tuple-element.22), channel_id=1, source_target_pairs={{0,1},{1,2},{2,3},{4,5},{5,6},{6,7},{8,9},{9,10},{10,11},{12,13},{... | collective-permute-start | bytes 222920 | tf_op jit(solution)/shard_map/ppermute | solution.py:242
  30.4 5.1 %collective-permute-start.5 = (f32[768]{0:T(1024)S(1)}, f32[768]{0:T(1024)S(1)}, u32[]{:S(2)}, u32[]{:S(2)}) collective-permute-start(f32[768]{0:T(1024)S(1)} %reshape.415), channel_id=1, source_target_pairs={{16,0},{32,16},{48,32},{64,48},{80,64},{96,80},{112,96},{128,112},... | collective-permute-start | bytes 9224 | tf_op jit(solution)/shard_map/ppermute | solution.py:242
  32.3 6.1 %collective-permute-start.4 = (f32[768]{0:T(1024)S(1)}, f32[768]{0:T(1024)S(1)}, u32[]{:S(2)}, u32[]{:S(2)}) collective-permute-start(f32[768]{0:T(1024)S(1)} %reshape.413), channel_id=1, source_target_pairs={{0,16},{16,32},{32,48},{48,64},{64,80},{80,96},{96,112},{112,128},... | collective-permute-start | bytes 9224 | tf_op jit(solution)/shard_map/ppermute | solution.py:242
  38.7 4.4 %collective-permute-start.7 = (f32[54]{0:T(128)S(1)}, f32[54]{0:T(128)S(1)}, u32[]{:S(2)}, u32[]{:S(2)}) collective-permute-start(f32[54]{0:T(128)S(1)} %reshape.419), channel_id=1, source_target_pairs={{4,0},{8,4},{12,8},{5,1},{9,5},{13,9},{6,2},{10,6},{14,10},{7,3},{... | collective-permute-start | bytes 656 | tf_op jit(solution)/shard_map/ppermute | solution.py:242
  41.2 5.4 %collective-permute-start.6 = (f32[54]{0:T(128)S(1)}, f32[54]{0:T(128)S(1)}, u32[]{:S(2)}, u32[]{:S(2)}) collective-permute-start(f32[54]{0:T(128)S(1)} %reshape.417), channel_id=1, source_target_pairs={{0,4},{4,8},{8,12},{1,5},{5,9},{9,13},{2,6},{6,10},{10,14},{3,7},{... | collective-permute-start | bytes 656 | tf_op jit(solution)/shard_map/ppermute | solution.py:242
  60.2 5.6 %collective-permute-start.10 = (f32[2,9,128]{2,1,0:T(8,128)S(1)}, f32[2,9,128]{2,1,0:T(8,128)S(1)}, u32[]{:S(2)}, u32[]{:S(2)}) collective-permute-start(f32[2,9,128]{2,1,0:T(8,128)S(1)} %reshape.424), channel_id=1, source_target_pairs={{0,1},{1,0},{2,3},{3,2},{4,5},{5,4},{6,7},{7,6},{8,9},{9,8},{10,11... | collective-permute-start | bytes 27656 | tf_op jit(solution)/shard_map/ppermute | solution.py:147
  65.8 7.1 %collective-permute-start.11 = (f32[2,9,128]{2,1,0:T(8,128)S(1)}, f32[2,9,128]{2,1,0:T(8,128)S(1)}, u32[]{:S(2)}, u32[]{:S(2)}) collective-permute-start(f32[2,9,128]{2,1,0:T(8,128)S(1)} %add.173), channel_id=1, source_target_pairs={{0,2},{1,3},{2,0},{3,1},{4,6},{5,7},{6,4},{7,5},{8,10},{9,11},{10,... | collective-permute-start | bytes 27656 | tf_op jit(solution)/shard_map/ppermute | solution.py:147
  68.9 8.5 %copy-start.4 = (f32[64,256]{1,0:T(8,128)S(1)}, f32[64,256]{1,0:T(8,128)}, u32[]{:S(2)}) copy-start(f32[64,256]{1,0:T(8,128)} %param.13) | copy-start | bytes 196612
  68.9 8.5 %copy-start.5 = (f32[2,64,256]{2,1,0:T(8,128)S(1)}, f32[2,64,256]{2,1,0:T(8,128)}, u32[]{:S(2)}) copy-start(f32[2,64,256]{2,1,0:T(8,128)} %param.14) | copy-start | bytes 393220
  73.0 4.6 %collective-permute-start.13 = (f32[768]{0:T(1024)S(1)}, f32[768]{0:T(1024)S(1)}, u32[]{:S(2)}, u32[]{:S(2)}) collective-permute-start(f32[768]{0:T(1024)S(1)} %reshape.428), channel_id=1, source_target_pairs={{16,0},{32,16},{48,32},{64,48},{80,64},{96,80},{112,96},{128,112},... | collective-permute-start | bytes 9224 | tf_op jit(solution)/shard_map/ppermute | solution.py:242
  75.0 6.1 %collective-permute-start.12 = (f32[768]{0:T(1024)S(1)}, f32[768]{0:T(1024)S(1)}, u32[]{:S(2)}, u32[]{:S(2)}) collective-permute-start(f32[768]{0:T(1024)S(1)} %reshape.426), channel_id=1, source_target_pairs={{0,16},{16,32},{32,48},{48,64},{64,80},{80,96},{96,112},{112,128},... | collective-permute-start | bytes 9224 | tf_op jit(solution)/shard_map/ppermute | solution.py:242
  81.1 3.9 %collective-permute-start.15 = (f32[1280]{0:T(1024)S(1)}, f32[1280]{0:T(1024)S(1)}, u32[]{:S(2)}, u32[]{:S(2)}) collective-permute-start(f32[1280]{0:T(1024)S(1)} %reshape.432), channel_id=1, source_target_pairs={{4,0},{8,4},{12,8},{5,1},{9,5},{13,9},{6,2},{10,6},{14,10},{7,3},{... | collective-permute-start | bytes 15368 | tf_op jit(solution)/shard_map/ppermute | solution.py:242
  83.5 5.5 %collective-permute-start.14 = (f32[1280]{0:T(1024)S(1)}, f32[1280]{0:T(1024)S(1)}, u32[]{:S(2)}, u32[]{:S(2)}) collective-permute-start(f32[1280]{0:T(1024)S(1)} %reshape.430), channel_id=1, source_target_pairs={{0,4},{4,8},{8,12},{1,5},{5,9},{9,13},{2,6},{6,10},{10,14},{3,7},{... | collective-permute-start | bytes 15368 | tf_op jit(solution)/shard_map/ppermute | solution.py:242

commit v6 on v5

--- a/solution.py
+++ b/solution.py
@@ -139,15 +139,28 @@
 
 def layer_total(part):
     count = lax.axis_size("layer")
+    copies = jnp.broadcast_to(part[None], (count,) + part.shape)
+    gathered = lax.all_to_all(copies, "layer", 0, 0, tiled=True)
+    total = gathered[0]
+    for source in range(1, count):
+        total = total + gathered[source]
+    return total
+
+
+def layer_neighbours(top, bottom):
+    count = lax.axis_size("layer")
     place = lax.axis_index("layer")
-    total = part
-    step = 1
-    while step < count:
-        pairs = [(i, i ^ step) for i in range(count)]
-        other = lax.ppermute(total, "layer", pairs)
-        total = jnp.where((place & step) == 0, total + other, other + total)
-        step *= 2
-    return total
+    chunks = []
+    for target in range(count):
+        chunk = jnp.where(target == place + 1, top, jnp.where(target == place - 1, bottom, 0.0))
+        chunks.append(chunk[None])
+    received = lax.all_to_all(jnp.concatenate(chunks, 0), "layer", 0, 0, tiled=True)
+    below = jnp.zeros_like(top)
+    above = jnp.zeros_like(top)
+    for source in range(count):
+        below = jnp.where(source == place - 1, received[source], below)
+        above = jnp.where(source == place + 1, received[source], above)
+    return below, above
 
 
 def cell_dx(plane):
@@ -307,7 +320,7 @@
     ring = jnp.concatenate([jnp.minimum(marked, 1.0)[None], placed], 0)
     field_ext = widened[:-1].reshape(4, depth_count, block_x + 2, block_y + 2)
     flag_cells = widened[-1, :-1, :-1]
-    below_raw, above_raw = exchange("layer", field_ext[:, -1], field_ext[:, 0])
+    below_raw, above_raw = layer_neighbours(field_ext[:, -1], field_ext[:, 0])
     (ring_x,) = packed_halo((ring,), (1,), "mx")
     (ring_ext,) = packed_halo((ring_x,), (2,), "my")
     imposed_at = ring_ext[0] > 0.5

time: 91.1 us -> 88.7 us (0.974)
  the two profiles are of different devices: /device:TPU:410 before, /device:TPU:408 now
where the time goes in v6:
time: 88.7 us; the launch traced here: 88.1 us
  starting transfers between devices  34.4 us (39%)
  waiting for transfers between devices  26 us (29%)
  Pallas kernels  10.5 us (12%)
  other arithmetic  6.31 us (7%)
  local copies, waits for them, and re-layouts  4.83 us (5%)
  matrix products  4.61 us (5%)
  between operations  1.43 us (2%)
    ppermute x6, waiting for transfers between devices, exchange(): lax.ppermute(sent_up, axis, up)  20.7 us
    ppermute x6, starting transfers between devices, exchange(): lax.ppermute(sent_down, axis, down)  14.8 us
    ppermute x6, starting transfers between devices, exchange(): lax.ppermute(sent_up, axis, up)  10.6 us
    pallas_call x1, Pallas kernels, fem_pallas(): pl.pallas_call(fem_kernel, out_shape=jax.ShapeDtypeStruct(body_force.shap...  10.5 us
    all_to_all x1, waiting for transfers between devices, layer_total(): gathered = lax.all_to_all(copies, 'layer', 0, 0, tiled=True)  5.27 us
    all_to_all x1, starting transfers between devices, layer_total(): gathered = lax.all_to_all(copies, 'layer', 0, 0, tiled=True)  4.8 us
    all_to_all x1, starting transfers between devices, layer_neighbours(): lax.all_to_all(jnp.concatenate(chunks, 0), 'layer', 0, 0, tiled=True)  4.29 us
    dot_general x2, matrix products, gather_slots(): cols_taken = jnp.einsum('krc,sc->krs', field, pick_col, precision=HIGH)  2.4 us
  transfers between devices with their start and end apart: 14, of which 7 were waited for; matrix products, arithmetic and copies ran while one was open for 7% of the time, Pallas kernels for 0%

profile of v6, /device:TPU:408, one launch (start us, length us, event | category | flops | bytes accessed | tf_op | source)
XLA Modules:
  0.0 88.1 jit_solution(9619978309339412511)
XLA Ops:
  0.7 0.7 reduce.2
  1.5 1.7 %fusion.1 = f32[2,1152]{1,0:T(2,128)S(1)} fusion(f32[2,64,256]{2,1,0:T(8,128)} %param.11, s32[1152]{0:T(1024)S(1)} %get-tuple-element.49, pred[64,1152]{1,0:T(8,128)(4,1)S(1)} %convert_compare_fusion), kind=kOutput, calls=%fused_computation.3 | convolution fusion | flops 453572352 | bytes 218624 | tf_op jit(solution)/shard_map/krc,sc->krs/dot_general | solution.py:131
  3.5 3.6 %collective-permute-start.1 = (f32[4864]{0:T(1024)S(1)}, f32[4864]{0:T(1024)S(1)}, u32[]{:S(2)}, u32[]{:S(2)}) collective-permute-start(f32[4864]{0:T(1024)S(1)} %pad_maximum_fusion.25), channel_id=1, source_target_pairs={{16,0},{32,16},{48,32},{64,48},{80,64},{96,80},{112,96},{128,112},... | collective-permute-start | bytes 58376 | tf_op jit(solution)/shard_map/ppermute | solution.py:255
  7.1 1.9 %collective-permute-start = (f32[4864]{0:T(1024)S(1)}, f32[4864]{0:T(1024)S(1)}, u32[]{:S(2)}, u32[]{:S(2)}) collective-permute-start(f32[4864]{0:T(1024)S(1)} %pad_maximum_fusion.24), channel_id=1, source_target_pairs={{0,16},{16,32},{32,48},{48,64},{64,80},{80,96},{96,112},{112,128},... | collective-permute-start | bytes 58376 | tf_op jit(solution)/shard_map/ppermute | solution.py:255
  9.7 3.7 %collective-permute-done = f32[4864]{0:T(1024)S(1)} collective-permute-done((f32[4864]{0:T(1024)S(1)}, f32[4864]{0:T(1024)S(1)}, u32[]{:S(2)}, u32[]{:S(2)}) %collective-permute-start) | collective-permute-done | bytes 19488 | tf_op jit(solution)/shard_map/ppermute | solution.py:255
  14.4 2.6 %collective-permute-start.3 = (f32[1712]{0:T(1024)S(1)}, f32[1712]{0:T(1024)S(1)}, u32[]{:S(2)}, u32[]{:S(2)}) collective-permute-start(f32[1712]{0:T(1024)S(1)} %concatenate.71), channel_id=1, source_target_pairs={{4,0},{8,4},{12,8},{5,1},{9,5},{13,9},{6,2},{10,6},{14,10},{7,3},{... | collective-permute-start | bytes 20552 | tf_op jit(solution)/shard_map/ppermute | solution.py:255
  17.3 1.3 %collective-permute-start.2 = (f32[1712]{0:T(1024)S(1)}, f32[1712]{0:T(1024)S(1)}, u32[]{:S(2)}, u32[]{:S(2)}) collective-permute-start(f32[1712]{0:T(1024)S(1)} %concatenate.70), channel_id=1, source_target_pairs={{0,4},{4,8},{8,12},{1,5},{5,9},{9,13},{2,6},{6,10},{10,14},{3,7},{... | collective-permute-start | bytes 20552 | tf_op jit(solution)/shard_map/ppermute | solution.py:255
  18.6 0.7 add_convert_fusion.live_ref
  19.5 3.3 %collective-permute-done.2 = f32[1712]{0:T(1024)S(1)} collective-permute-done((f32[1712]{0:T(1024)S(1)}, f32[1712]{0:T(1024)S(1)}, u32[]{:S(2)}, u32[]{:S(2)}) %collective-permute-start.2) | collective-permute-done | bytes 6880 | tf_op jit(solution)/shard_map/ppermute | solution.py:255
  23.6 0.9 %copy.70 = f32[4,4,18,258]{3,1,2,0:T(4,128)} copy(f32[4,4,18,258]{3,2,1,0:T(8,128)S(1)} %pad_maximum_fusion.1) | data formatting | bytes 594432 | tf_op jit(solution)/shard_map/concatenate | solution.py:157
  24.4 4.3 %all-to-all-start = ((f32[4,4,18,258]{3,1,2,0:T(4,128)}), f32[4,4,18,258]{3,1,2,0:T(4,128)S(1)}, u32[]{:S(2)}, u32[]{:S(2)}) async-start(f32[4,4,18,258]{3,1,2,0:T(4,128)} %copy.70), calls=%async_computation | async-start | bytes 884736 | tf_op jit(solution)/shard_map/all_to_all | solution.py:157
  29.8 1.9 %collective-permute-start.5 = (f32[768]{0:T(1024)S(1)}, f32[768]{0:T(1024)S(1)}, u32[]{:S(2)}, u32[]{:S(2)}) collective-permute-start(f32[768]{0:T(1024)S(1)} %reshape.616), channel_id=1, source_target_pairs={{16,0},{32,16},{48,32},{64,48},{80,64},{96,80},{112,96},{128,112},... | collective-permute-start | bytes 9224 | tf_op jit(solution)/shard_map/ppermute | solution.py:255
  31.7 2.4 %collective-permute-start.4 = (f32[768]{0:T(1024)S(1)}, f32[768]{0:T(1024)S(1)}, u32[]{:S(2)}, u32[]{:S(2)}) collective-permute-start(f32[768]{0:T(1024)S(1)} %reshape.614), channel_id=1, source_target_pairs={{0,16},{16,32},{32,48},{48,64},{64,80},{80,96},{96,112},{112,128},... | collective-permute-start | bytes 9224 | tf_op jit(solution)/shard_map/ppermute | solution.py:255
  35.2 2.7 %collective-permute-done.4 = f32[768]{0:T(1024)S(1)} collective-permute-done((f32[768]{0:T(1024)S(1)}, f32[768]{0:T(1024)S(1)}, u32[]{:S(2)}, u32[]{:S(2)}) %collective-permute-start.4) | collective-permute-done | bytes 3104 | tf_op jit(solution)/shard_map/ppermute | solution.py:255
  38.2 2.4 %collective-permute-start.7 = (f32[54]{0:T(128)S(1)}, f32[54]{0:T(128)S(1)}, u32[]{:S(2)}, u32[]{:S(2)}) collective-permute-start(f32[54]{0:T(128)S(1)} %reshape.620), channel_id=1, source_target_pairs={{4,0},{8,4},{12,8},{5,1},{9,5},{13,9},{6,2},{10,6},{14,10},{7,3},{... | collective-permute-start | bytes 656 | tf_op jit(solution)/shard_map/ppermute | solution.py:255
  40.6 1.3 %collective-permute-start.6 = (f32[54]{0:T(128)S(1)}, f32[54]{0:T(128)S(1)}, u32[]{:S(2)}, u32[]{:S(2)}) collective-permute-start(f32[54]{0:T(128)S(1)} %reshape.618), channel_id=1, source_target_pairs={{0,4},{4,8},{8,12},{1,5},{5,9},{9,13},{2,6},{6,10},{10,14},{3,7},{... | collective-permute-start | bytes 656 | tf_op jit(solution)/shard_map/ppermute | solution.py:255
  41.9 0.6 pad_convert_fusion
  42.7 3.4 %collective-permute-done.6 = f32[54]{0:T(128)S(1)} collective-permute-done((f32[54]{0:T(128)S(1)}, f32[54]{0:T(128)S(1)}, u32[]{:S(2)}, u32[]{:S(2)}) %collective-permute-start.6) | collective-permute-done | bytes 248 | tf_op jit(solution)/shard_map/ppermute | solution.py:255
  46.6 0.9 %select_maximum_fusion.fld_ref = f32[4,5,24,384]{3,2,1,0:T(8,128)} fusion(f32[2,5,18,258]{3,2,1,0:T(8,128)S(1)} %get-tuple-element.21, f32[2,5,18,258]{3,2,1,0:T(8,128)S(1)} %get-tuple-element.20), kind=kLoop, calls=%fused_computation.15 | loop fusion | flops 1474560 | bytes 1108800 | tf_op jit(solution)/shard_map/concatenate | solution.py:329
  47.6 10.5 %shard_map.122 = f32[3,3,16,256]{3,2,1,0:T(8,128)} custom-call(f32[4,5,24,384]{3,2,1,0:T(8,128)} %select_maximum_fusion.fld_ref, f32[24,384]{1,0:T(8,128)} %get-tuple-element.51.main_ref, f32[24,384]{1,0:T(8,128)} %get-tuple-element.50.weight_ref, f32[18,18]{1,0:T(8,128)} %kmat_ref.1, f32[2]{0:T(128)} %add_convert_fusion.live_ref, f32[3,3,16,256]{3,2,1,0:T(8,128)} %body_ref.1), custom_call_target="tpu_custom_call" | custom-call | tf_op jit(solution)/shard_map/pallas_call | solution.py:90
  58.1 0.9 %slice_reduce_fusion.4 = f32[2,16,256]{2,1,0:T(8,128)S(1)} fusion(f32[3,3,16,256]{3,2,1,0:T(8,128)} %shard_map.122), kind=kLoop, calls=%fused_computation.81 | loop fusion | flops 16384 | bytes 131072 | tf_op jit(solution)/shard_map/reduce_sum | solution.py:346
  59.0 0.7 fusion.14
  59.7 0.6 broadcast_in_dim.104
  60.3 4.8 %all-to-all-start.1 = ((f32[4,2,9,128]{3,1,2,0:T(2,128)}), f32[4,2,9,128]{3,1,2,0:T(2,128)S(1)}, u32[]{:S(2)}, u32[]{:S(2)}) async-start(f32[4,2,9,128]{3,1,2,0:T(2,128)} %broadcast_in_dim.104), calls=%async_computation.1 | async-start | bytes 73728 | tf_op jit(solution)/shard_map/all_to_all | solution.py:143
  65.3 5.3 %all-to-all-done.1 = f32[4,2,9,128]{3,1,2,0:T(2,128)S(1)} async-done(((f32[4,2,9,128]{3,1,2,0:T(2,128)}), f32[4,2,9,128]{3,1,2,0:T(2,128)S(1)}, u32[]{:S(2)}, u32[]{:S(2)}) %all-to-all-start.1) | async-done | bytes 36896 | tf_op jit(solution)/shard_map/all_to_all | solution.py:143
  70.6 1.9 %collective-permute-start.9 = (f32[768]{0:T(1024)S(1)}, f32[768]{0:T(1024)S(1)}, u32[]{:S(2)}, u32[]{:S(2)}) collective-permute-start(f32[768]{0:T(1024)S(1)} %reshape.627), channel_id=1, source_target_pairs={{16,0},{32,16},{48,32},{64,48},{80,64},{96,80},{112,96},{128,112},... | collective-permute-start | bytes 9224 | tf_op jit(solution)/shard_map/ppermute | solution.py:255
  72.6 2.4 %collective-permute-start.8 = (f32[768]{0:T(1024)S(1)}, f32[768]{0:T(1024)S(1)}, u32[]{:S(2)}, u32[]{:S(2)}) collective-permute-start(f32[768]{0:T(1024)S(1)} %reshape.625), channel_id=1, source_target_pairs={{0,16},{16,32},{32,48},{48,64},{64,80},{80,96},{96,112},{112,128},... | collective-permute-start | bytes 9224 | tf_op jit(solution)/shard_map/ppermute | solution.py:255
  75.2 3.5 %collective-permute-done.8 = f32[768]{0:T(1024)S(1)} collective-permute-done((f32[768]{0:T(1024)S(1)}, f32[768]{0:T(1024)S(1)}, u32[]{:S(2)}, u32[]{:S(2)}) %collective-permute-start.8) | collective-permute-done | bytes 3104 | tf_op jit(solution)/shard_map/ppermute | solution.py:255
  78.8 2.4 %collective-permute-start.11 = (f32[1280]{0:T(1024)S(1)}, f32[1280]{0:T(1024)S(1)}, u32[]{:S(2)}, u32[]{:S(2)}) collective-permute-start(f32[1280]{0:T(1024)S(1)} %reshape.631), channel_id=1, source_target_pairs={{4,0},{8,4},{12,8},{5,1},{9,5},{13,9},{6,2},{10,6},{14,10},{7,3},{... | collective-permute-start | bytes 15368 | tf_op jit(solution)/shard_map/ppermute | solution.py:255
  81.2 1.3 %collective-permute-start.10 = (f32[1280]{0:T(1024)S(1)}, f32[1280]{0:T(1024)S(1)}, u32[]{:S(2)}, u32[]{:S(2)}) collective-permute-start(f32[1280]{0:T(1024)S(1)} %reshape.629), channel_id=1, source_target_pairs={{0,4},{4,8},{8,12},{1,5},{5,9},{9,13},{2,6},{6,10},{10,14},{3,7},{... | collective-permute-start | bytes 15368 | tf_op jit(solution)/shard_map/ppermute | solution.py:255
  82.7 4.0 %collective-permute-done.10 = f32[1280]{0:T(1024)S(1)} collective-permute-done((f32[1280]{0:T(1024)S(1)}, f32[1280]{0:T(1024)S(1)}, u32[]{:S(2)}, u32[]{:S(2)}) %collective-permute-start.10) | collective-permute-done | bytes 5152 | tf_op jit(solution)/shard_map/ppermute | solution.py:255
  86.7 1.3 %fusion.11 = f32[2,64,256]{2,1,0:T(8,128)} fusion(s32[1152]{0:T(1024)S(1)} %get-tuple-element.49, f32[2,1152]{1,0:T(2,128)S(1)} %bitcast.183, f32[1152,64]{0,1:T(8,128)S(1)} %fusion.27, f32[1,64,256]{2,1,0:T(8,128)S(1)} %fusion.42, f32[1,64,256]{2,1,0:T(8,128)S(1)} %fusion.48), kind=kOutput, calls=%fused_computation.11 | convolution fusion | flops 453492736 | bytes 570880 | tf_op jit(solution)/shard_map/ksr,sc->krc/dot_general | solution.py:137
  (135 shorter events, 6.7 us)
Async XLA Ops:
  0.6 2.6 %copy-start.6 = (s32[16,256]{1,0:T(8,128)S(1)}, s32[16,256]{1,0:T(8,128)}, u32[]{:S(2)}) copy-start(s32[16,256]{1,0:T(8,128)} %param.18) | copy-start | bytes 49156
  0.6 2.6 %copy-start.2 = (f32[3,16,256]{2,1,0:T(8,128)S(1)}, f32[3,16,256]{2,1,0:T(8,128)}, u32[]{:S(2)}) copy-start(f32[3,16,256]{2,1,0:T(8,128)} %param.16) | copy-start | bytes 147460
  0.7 2.6 %copy-start = (f32[3,3,16,256]{3,2,1,0:T(8,128)S(1)}, f32[3,3,16,256]{3,2,1,0:T(8,128)}, u32[]{:S(2)}) copy-start(f32[3,3,16,256]{3,2,1,0:T(8,128)} %param.15) | copy-start | bytes 442372
  1.4 2.0 %copy-start.1 = (f32[2,64,256]{2,1,0:T(8,128)S(1)}, f32[2,64,256]{2,1,0:T(8,128)}, u32[]{:S(2)}) copy-start(f32[2,64,256]{2,1,0:T(8,128)} %param.11) | copy-start | bytes 393220
  1.4 2.0 %copy-start.3 = (f32[64,256]{1,0:T(8,128)S(1)}, f32[64,256]{1,0:T(8,128)}, u32[]{:S(2)}) copy-start(f32[64,256]{1,0:T(8,128)} %param.12) | copy-start | bytes 196612
  1.5 7.5 %copy-start.7 = (s32[1,9,128]{2,0,1:T(1,128)S(1)}, s32[1,9,128]{2,0,1:T(1,128)}, u32[]{:S(2)}) copy-start(s32[1,9,128]{2,0,1:T(1,128)} %param.20) | copy-start | bytes 13828
  3.5 6.2 %collective-permute-start.1 = (f32[4864]{0:T(1024)S(1)}, f32[4864]{0:T(1024)S(1)}, u32[]{:S(2)}, u32[]{:S(2)}) collective-permute-start(f32[4864]{0:T(1024)S(1)} %pad_maximum_fusion.25), channel_id=1, source_target_pairs={{16,0},{32,16},{48,32},{64,48},{80,64},{96,80},{112,96},{128,112},... | collective-permute-start | bytes 58376 | tf_op jit(solution)/shard_map/ppermute | solution.py:255
  7.1 6.3 %collective-permute-start = (f32[4864]{0:T(1024)S(1)}, f32[4864]{0:T(1024)S(1)}, u32[]{:S(2)}, u32[]{:S(2)}) collective-permute-start(f32[4864]{0:T(1024)S(1)} %pad_maximum_fusion.24), channel_id=1, source_target_pairs={{0,16},{16,32},{32,48},{48,64},{64,80},{80,96},{96,112},{112,128},... | collective-permute-start | bytes 58376 | tf_op jit(solution)/shard_map/ppermute | solution.py:255
  14.4 4.8 %collective-permute-start.3 = (f32[1712]{0:T(1024)S(1)}, f32[1712]{0:T(1024)S(1)}, u32[]{:S(2)}, u32[]{:S(2)}) collective-permute-start(f32[1712]{0:T(1024)S(1)} %concatenate.71), channel_id=1, source_target_pairs={{4,0},{8,4},{12,8},{5,1},{9,5},{13,9},{6,2},{10,6},{14,10},{7,3},{... | collective-permute-start | bytes 20552 | tf_op jit(solution)/shard_map/ppermute | solution.py:255
  17.3 5.5 %collective-permute-start.2 = (f32[1712]{0:T(1024)S(1)}, f32[1712]{0:T(1024)S(1)}, u32[]{:S(2)}, u32[]{:S(2)}) collective-permute-start(f32[1712]{0:T(1024)S(1)} %concatenate.70), channel_id=1, source_target_pairs={{0,4},{4,8},{8,12},{1,5},{5,9},{9,13},{2,6},{6,10},{10,14},{3,7},{... | collective-permute-start | bytes 20552 | tf_op jit(solution)/shard_map/ppermute | solution.py:255
  24.4 21.9 %all-to-all-start = ((f32[4,4,18,258]{3,1,2,0:T(4,128)}), f32[4,4,18,258]{3,1,2,0:T(4,128)S(1)}, u32[]{:S(2)}, u32[]{:S(2)}) async-start(f32[4,4,18,258]{3,1,2,0:T(4,128)} %copy.70), calls=%async_computation | async-start | bytes 884736 | tf_op jit(solution)/shard_map/all_to_all | solution.py:157
  29.8 5.4 %collective-permute-start.5 = (f32[768]{0:T(1024)S(1)}, f32[768]{0:T(1024)S(1)}, u32[]{:S(2)}, u32[]{:S(2)}) collective-permute-start(f32[768]{0:T(1024)S(1)} %reshape.616), channel_id=1, source_target_pairs={{16,0},{32,16},{48,32},{64,48},{80,64},{96,80},{112,96},{128,112},... | collective-permute-start | bytes 9224 | tf_op jit(solution)/shard_map/ppermute | solution.py:255
  31.7 6.1 %collective-permute-start.4 = (f32[768]{0:T(1024)S(1)}, f32[768]{0:T(1024)S(1)}, u32[]{:S(2)}, u32[]{:S(2)}) collective-permute-start(f32[768]{0:T(1024)S(1)} %reshape.614), channel_id=1, source_target_pairs={{0,16},{16,32},{32,48},{48,64},{64,80},{80,96},{96,112},{112,128},... | collective-permute-start | bytes 9224 | tf_op jit(solution)/shard_map/ppermute | solution.py:255
  38.2 4.4 %collective-permute-start.7 = (f32[54]{0:T(128)S(1)}, f32[54]{0:T(128)S(1)}, u32[]{:S(2)}, u32[]{:S(2)}) collective-permute-start(f32[54]{0:T(128)S(1)} %reshape.620), channel_id=1, source_target_pairs={{4,0},{8,4},{12,8},{5,1},{9,5},{13,9},{6,2},{10,6},{14,10},{7,3},{... | collective-permute-start | bytes 656 | tf_op jit(solution)/shard_map/ppermute | solution.py:255
  40.6 5.4 %collective-permute-start.6 = (f32[54]{0:T(128)S(1)}, f32[54]{0:T(128)S(1)}, u32[]{:S(2)}, u32[]{:S(2)}) collective-permute-start(f32[54]{0:T(128)S(1)} %reshape.618), channel_id=1, source_target_pairs={{0,4},{4,8},{8,12},{1,5},{5,9},{9,13},{2,6},{6,10},{10,14},{3,7},{... | collective-permute-start | bytes 656 | tf_op jit(solution)/shard_map/ppermute | solution.py:255
  60.3 10.3 %all-to-all-start.1 = ((f32[4,2,9,128]{3,1,2,0:T(2,128)}), f32[4,2,9,128]{3,1,2,0:T(2,128)S(1)}, u32[]{:S(2)}, u32[]{:S(2)}) async-start(f32[4,2,9,128]{3,1,2,0:T(2,128)} %broadcast_in_dim.104), calls=%async_computation.1 | async-start | bytes 73728 | tf_op jit(solution)/shard_map/all_to_all | solution.py:143
  65.1 9.9 %copy-start.4 = (f32[64,256]{1,0:T(8,128)S(1)}, f32[64,256]{1,0:T(8,128)}, u32[]{:S(2)}) copy-start(f32[64,256]{1,0:T(8,128)} %param.13) | copy-start | bytes 196612
  65.1 9.9 %copy-start.5 = (f32[2,64,256]{2,1,0:T(8,128)S(1)}, f32[2,64,256]{2,1,0:T(8,128)}, u32[]{:S(2)}) copy-start(f32[2,64,256]{2,1,0:T(8,128)} %param.14) | copy-start | bytes 393220
  70.6 4.6 %collective-permute-start.9 = (f32[768]{0:T(1024)S(1)}, f32[768]{0:T(1024)S(1)}, u32[]{:S(2)}, u32[]{:S(2)}) collective-permute-start(f32[768]{0:T(1024)S(1)} %reshape.627), channel_id=1, source_target_pairs={{16,0},{32,16},{48,32},{64,48},{80,64},{96,80},{112,96},{128,112},... | collective-permute-start | bytes 9224 | tf_op jit(solution)/shard_map/ppermute | solution.py:255
  72.6 6.1 %collective-permute-start.8 = (f32[768]{0:T(1024)S(1)}, f32[768]{0:T(1024)S(1)}, u32[]{:S(2)}, u32[]{:S(2)}) collective-permute-start(f32[768]{0:T(1024)S(1)} %reshape.625), channel_id=1, source_target_pairs={{0,16},{16,32},{32,48},{48,64},{64,80},{80,96},{96,112},{112,128},... | collective-permute-start | bytes 9224 | tf_op jit(solution)/shard_map/ppermute | solution.py:255
  78.8 3.9 %collective-permute-start.11 = (f32[1280]{0:T(1024)S(1)}, f32[1280]{0:T(1024)S(1)}, u32[]{:S(2)}, u32[]{:S(2)}) collective-permute-start(f32[1280]{0:T(1024)S(1)} %reshape.631), channel_id=1, source_target_pairs={{4,0},{8,4},{12,8},{5,1},{9,5},{13,9},{6,2},{10,6},{14,10},{7,3},{... | collective-permute-start | bytes 15368 | tf_op jit(solution)/shard_map/ppermute | solution.py:255
  81.2 5.5 %collective-permute-start.10 = (f32[1280]{0:T(1024)S(1)}, f32[1280]{0:T(1024)S(1)}, u32[]{:S(2)}, u32[]{:S(2)}) collective-permute-start(f32[1280]{0:T(1024)S(1)} %reshape.629), channel_id=1, source_target_pairs={{0,4},{4,8},{8,12},{1,5},{5,9},{9,13},{2,6},{6,10},{10,14},{3,7},{... | collective-permute-start | bytes 15368 | tf_op jit(solution)/shard_map/ppermute | solution.py:255

commit v7 on v5

--- a/solution.py
+++ b/solution.py
@@ -139,14 +139,11 @@
 
 def layer_total(part):
     count = lax.axis_size("layer")
-    place = lax.axis_index("layer")
-    total = part
-    step = 1
-    while step < count:
-        pairs = [(i, i ^ step) for i in range(count)]
-        other = lax.ppermute(total, "layer", pairs)
-        total = jnp.where((place & step) == 0, total + other, other + total)
-        step *= 2
+    copies = jnp.broadcast_to(part[None], (count,) + part.shape)
+    gathered = lax.all_to_all(copies, "layer", 0, 0, tiled=True)
+    total = gathered[0]
+    for source in range(1, count):
+        total = total + gathered[source]
     return total
 
 
@@ -237,9 +234,22 @@
 
 def exchange(axis, sent_up, sent_down):
     count = lax.axis_size(axis)
-    up = [(i, i + 1) for i in range(count - 1)]
-    down = [(i + 1, i) for i in range(count - 1)]
-    return lax.ppermute(sent_up, axis, up), lax.ppermute(sent_down, axis, down)
+    if count > 4:
+        up = [(i, i + 1) for i in range(count - 1)]
+        down = [(i + 1, i) for i in range(count - 1)]
+        return lax.ppermute(sent_up, axis, up), lax.ppermute(sent_down, axis, down)
+    place = lax.axis_index(axis)
+    chunks = []
+    for target in range(count):
+        chunk = jnp.where(target == place + 1, sent_up, jnp.where(target == place - 1, sent_down, 0.0))
+        chunks.append(chunk[None])
+    received = lax.all_to_all(jnp.concatenate(chunks, 0), axis, 0, 0, tiled=True)
+    before = jnp.zeros_like(sent_up)
+    after = jnp.zeros_like(sent_down)
+    for source in range(count):
+        before = jnp.where(source == place - 1, received[source], before)
+        after = jnp.where(source == place + 1, received[source], after)
+    return before, after
 
 
 def packed_halo(arrays, dims, axis):

time: 91.1 us -> 98.7 us (1.083)
  the two profiles are of different devices: /device:TPU:410 before, /device:TPU:384 now
where the time goes in v7:
time: 98.7 us; the launch traced here: 98 us
  waiting for transfers between devices  34.9 us (35%)
  starting transfers between devices  32.6 us (33%)
  Pallas kernels  10.5 us (11%)
  other arithmetic  7.9 us (8%)
  local copies, waits for them, and re-layouts  6.1 us (6%)
  matrix products  4.61 us (5%)
  between operations  1.43 us (1%)
    all_to_all x4, waiting for transfers between devices, exchange(): lax.all_to_all(jnp.concatenate(chunks, 0), axis, 0, 0, tiled=True)  20.8 us
    all_to_all x4, starting transfers between devices, exchange(): lax.all_to_all(jnp.concatenate(chunks, 0), axis, 0, 0, tiled=True)  15.2 us
    pallas_call x1, Pallas kernels, fem_pallas(): pl.pallas_call(fem_kernel, out_shape=jax.ShapeDtypeStruct(body_force.shap...  10.5 us
    ppermute x3, waiting for transfers between devices, exchange(): lax.ppermute(sent_up, axis, up)  8.89 us
    ppermute x3, starting transfers between devices, exchange(): lax.ppermute(sent_down, axis, down)  7.41 us
    ppermute x3, starting transfers between devices, exchange(): lax.ppermute(sent_up, axis, up)  6.73 us
    all_to_all x1, waiting for transfers between devices, layer_total(): gathered = lax.all_to_all(copies, 'layer', 0, 0, tiled=True)  5.21 us
    all_to_all x1, starting transfers between devices, layer_total(): gathered = lax.all_to_all(copies, 'layer', 0, 0, tiled=True)  3.27 us
  transfers between devices with their start and end apart: 11, of which 8 were waited for; matrix products, arithmetic and copies ran while one was open for 6% of the time, Pallas kernels for 0%

profile of v7, /device:TPU:384, one launch (start us, length us, event | category | flops | bytes accessed | tf_op | source)
XLA Modules:
  0.0 98.0 jit_solution(3297467677756970316)
XLA Ops:
  0.7 0.7 reduce.2
  1.5 1.7 %fusion.1 = f32[2,1152]{1,0:T(2,128)S(1)} fusion(f32[2,64,256]{2,1,0:T(8,128)} %param.11, s32[1152]{0:T(1024)S(1)} %get-tuple-element.65, pred[64,1152]{1,0:T(8,128)(4,1)S(1)} %convert_compare_fusion), kind=kOutput, calls=%fused_computation.3 | convolution fusion | flops 453572352 | bytes 218624 | tf_op jit(solution)/shard_map/krc,sc->krs/dot_general | solution.py:131
  3.5 3.6 %collective-permute-start.1 = (f32[4864]{0:T(1024)S(1)}, f32[4864]{0:T(1024)S(1)}, u32[]{:S(2)}, u32[]{:S(2)}) collective-permute-start(f32[4864]{0:T(1024)S(1)} %pad_maximum_fusion.25), channel_id=1, source_target_pairs={{16,0},{32,16},{48,32},{64,48},{80,64},{96,80},{112,96},{128,112},... | collective-permute-start | bytes 58376 | tf_op jit(solution)/shard_map/ppermute | solution.py:240
  7.1 1.9 %collective-permute-start = (f32[4864]{0:T(1024)S(1)}, f32[4864]{0:T(1024)S(1)}, u32[]{:S(2)}, u32[]{:S(2)}) collective-permute-start(f32[4864]{0:T(1024)S(1)} %pad_maximum_fusion.24), channel_id=1, source_target_pairs={{0,16},{16,32},{32,48},{48,64},{64,80},{80,96},{96,112},{112,128},... | collective-permute-start | bytes 58376 | tf_op jit(solution)/shard_map/ppermute | solution.py:240
  9.6 0.6 pad_convert_fusion.weight_ref
  10.3 3.1 %collective-permute-done = f32[4864]{0:T(1024)S(1)} collective-permute-done((f32[4864]{0:T(1024)S(1)}, f32[4864]{0:T(1024)S(1)}, u32[]{:S(2)}, u32[]{:S(2)}) %collective-permute-start) | collective-permute-done | bytes 19488 | tf_op jit(solution)/shard_map/ppermute | solution.py:240
  14.7 0.6 copy.65
  15.3 4.5 %all-to-all-start = ((f32[4,1,1712]{2,1,0:T(1,128)}), f32[4,1,1712]{2,1,0:T(1,128)S(1)}, u32[]{:S(2)}, u32[]{:S(2)}) async-start(f32[4,1,1712]{2,1,0:T(1,128)} %copy.65), calls=%async_computation | async-start | bytes 57344 | tf_op jit(solution)/shard_map/all_to_all | solution.py:246
  19.8 0.6 add_convert_fusion.live_ref
  20.5 4.8 %all-to-all-done = f32[4,1,1712]{2,1,0:T(1,128)S(1)} async-done(((f32[4,1,1712]{2,1,0:T(1,128)}), f32[4,1,1712]{2,1,0:T(1,128)S(1)}, u32[]{:S(2)}, u32[]{:S(2)}) %all-to-all-start) | async-done | bytes 27424 | tf_op jit(solution)/shard_map/all_to_all | solution.py:246
  26.8 1.9 %collective-permute-start.3 = (f32[768]{0:T(1024)S(1)}, f32[768]{0:T(1024)S(1)}, u32[]{:S(2)}, u32[]{:S(2)}) collective-permute-start(f32[768]{0:T(1024)S(1)} %reshape.1406), channel_id=1, source_target_pairs={{16,0},{32,16},{48,32},{64,48},{80,64},{96,80},{112,96},{128,112},... | collective-permute-start | bytes 9224 | tf_op jit(solution)/shard_map/ppermute | solution.py:240
  28.8 2.4 %collective-permute-start.2 = (f32[768]{0:T(1024)S(1)}, f32[768]{0:T(1024)S(1)}, u32[]{:S(2)}, u32[]{:S(2)}) collective-permute-start(f32[768]{0:T(1024)S(1)} %reshape.1404), channel_id=1, source_target_pairs={{0,16},{16,32},{32,48},{48,64},{64,80},{80,96},{96,112},{112,128},... | collective-permute-start | bytes 9224 | tf_op jit(solution)/shard_map/ppermute | solution.py:240
  32.6 2.3 %collective-permute-done.2 = f32[768]{0:T(1024)S(1)} collective-permute-done((f32[768]{0:T(1024)S(1)}, f32[768]{0:T(1024)S(1)}, u32[]{:S(2)}, u32[]{:S(2)}) %collective-permute-start.2) | collective-permute-done | bytes 3104 | tf_op jit(solution)/shard_map/ppermute | solution.py:240
  36.1 3.2 %all-to-all-start.1 = ((f32[4,1,54]{2,1,0:T(1,128)}), f32[4,1,54]{2,1,0:T(1,128)S(1)}, u32[]{:S(2)}, u32[]{:S(2)}) async-start(f32[4,1,54]{2,1,0:T(1,128)} %bitcast.22), calls=%async_computation.1 | async-start | bytes 4096 | tf_op jit(solution)/shard_map/all_to_all | solution.py:246
  39.9 0.9 copy.81
  40.8 3.6 %all-to-all-done.1 = f32[4,1,54]{2,1,0:T(1,128)S(1)} async-done(((f32[4,1,54]{2,1,0:T(1,128)}), f32[4,1,54]{2,1,0:T(1,128)S(1)}, u32[]{:S(2)}, u32[]{:S(2)}) %all-to-all-start.1) | async-done | bytes 896 | tf_op jit(solution)/shard_map/all_to_all | solution.py:246
  44.5 4.3 %all-to-all-start.2 = ((f32[4,4,18,258]{3,1,2,0:T(4,128)}), f32[4,4,18,258]{3,1,2,0:T(4,128)S(1)}, u32[]{:S(2)}, u32[]{:S(2)}) async-start(f32[4,4,18,258]{3,1,2,0:T(4,128)} %copy.81), calls=%async_computation.2 | async-start | bytes 884736 | tf_op jit(solution)/shard_map/all_to_all | solution.py:246
  49.2 7.2 %all-to-all-done.2 = f32[4,4,18,258]{3,1,2,0:T(4,128)S(1)} async-done(((f32[4,4,18,258]{3,1,2,0:T(4,128)}), f32[4,4,18,258]{3,1,2,0:T(4,128)S(1)}, u32[]{:S(2)}, u32[]{:S(2)}) %all-to-all-start.2) | async-done | bytes 297248 | tf_op jit(solution)/shard_map/all_to_all | solution.py:246
  56.6 0.9 select_maximum_fusion.fld_ref
  57.6 10.5 %shard_map.122 = f32[3,3,16,256]{3,2,1,0:T(8,128)} custom-call(f32[4,5,24,384]{3,2,1,0:T(8,128)} %select_maximum_fusion.fld_ref, f32[24,384]{1,0:T(8,128)} %pad_convert_fusion.1.main_ref, f32[24,384]{1,0:T(8,128)} %pad_convert_fusion.weight_ref, f32[18,18]{1,0:T(8,128)} %kmat_ref.1, f32[2]{0:T(128)} %add_convert_fusion.live_ref, f32[3,3,16,256]{3,2,1,0:T(8,128)} %body_ref.1), custom_call_target="tpu_custom_call" | custom-call | tf_op jit(solution)/shard_map/pallas_call | solution.py:90
  68.1 0.9 slice_reduce_fusion.4
  69.0 0.7 fusion.14
  69.7 0.6 broadcast_in_dim.147
  70.3 3.3 %all-to-all-start.3 = ((f32[4,2,9,128]{3,1,2,0:T(2,128)}), f32[4,2,9,128]{3,1,2,0:T(2,128)S(1)}, u32[]{:S(2)}, u32[]{:S(2)}) async-start(f32[4,2,9,128]{3,1,2,0:T(2,128)} %broadcast_in_dim.147), calls=%async_computation.3 | async-start | bytes 73728 | tf_op jit(solution)/shard_map/all_to_all | solution.py:143
  73.8 5.2 %all-to-all-done.3 = f32[4,2,9,128]{3,1,2,0:T(2,128)S(1)} async-done(((f32[4,2,9,128]{3,1,2,0:T(2,128)}), f32[4,2,9,128]{3,1,2,0:T(2,128)S(1)}, u32[]{:S(2)}, u32[]{:S(2)}) %all-to-all-start.3) | async-done | bytes 36896 | tf_op jit(solution)/shard_map/all_to_all | solution.py:143
  79.1 1.9 %collective-permute-start.5 = (f32[768]{0:T(1024)S(1)}, f32[768]{0:T(1024)S(1)}, u32[]{:S(2)}, u32[]{:S(2)}) collective-permute-start(f32[768]{0:T(1024)S(1)} %reshape.1413), channel_id=1, source_target_pairs={{16,0},{32,16},{48,32},{64,48},{80,64},{96,80},{112,96},{128,112},... | collective-permute-start | bytes 9224 | tf_op jit(solution)/shard_map/ppermute | solution.py:240
  81.0 2.4 %collective-permute-start.4 = (f32[768]{0:T(1024)S(1)}, f32[768]{0:T(1024)S(1)}, u32[]{:S(2)}, u32[]{:S(2)}) collective-permute-start(f32[768]{0:T(1024)S(1)} %reshape.1411), channel_id=1, source_target_pairs={{0,16},{16,32},{32,48},{48,64},{64,80},{80,96},{96,112},{112,128},... | collective-permute-start | bytes 9224 | tf_op jit(solution)/shard_map/ppermute | solution.py:240
  83.7 3.5 %collective-permute-done.4 = f32[768]{0:T(1024)S(1)} collective-permute-done((f32[768]{0:T(1024)S(1)}, f32[768]{0:T(1024)S(1)}, u32[]{:S(2)}, u32[]{:S(2)}) %collective-permute-start.4) | collective-permute-done | bytes 3104 | tf_op jit(solution)/shard_map/ppermute | solution.py:240
  87.4 0.6 copy.97
  88.0 3.3 %all-to-all-start.4 = ((f32[4,1,1280]{2,1,0:T(1,128)}), f32[4,1,1280]{2,1,0:T(1,128)S(1)}, u32[]{:S(2)}, u32[]{:S(2)}) async-start(f32[4,1,1280]{2,1,0:T(1,128)} %copy.97), calls=%async_computation.4 | async-start | bytes 40960 | tf_op jit(solution)/shard_map/all_to_all | solution.py:246
  91.4 5.2 %all-to-all-done.4 = f32[4,1,1280]{2,1,0:T(1,128)S(1)} async-done(((f32[4,1,1280]{2,1,0:T(1,128)}), f32[4,1,1280]{2,1,0:T(1,128)S(1)}, u32[]{:S(2)}, u32[]{:S(2)}) %all-to-all-start.4) | async-done | bytes 20512 | tf_op jit(solution)/shard_map/all_to_all | solution.py:246
  96.7 1.3 %fusion.11 = f32[2,64,256]{2,1,0:T(8,128)} fusion(s32[1152]{0:T(1024)S(1)} %get-tuple-element.65, f32[2,1152]{1,0:T(2,128)S(1)} %bitcast.202, f32[1152,64]{0,1:T(8,128)S(1)} %fusion.27, f32[1,64,256]{2,1,0:T(8,128)S(1)} %fusion.42, f32[1,64,256]{2,1,0:T(8,128)S(1)} %fusion.48), kind=kOutput, calls=%fused_computation.11 | convolution fusion | flops 453492736 | bytes 570880 | tf_op jit(solution)/shard_map/ksr,sc->krc/dot_general | solution.py:137
  (140 shorter events, 8.2 us)
Async XLA Ops:
  0.6 2.6 %copy-start.6 = (s32[16,256]{1,0:T(8,128)S(1)}, s32[16,256]{1,0:T(8,128)}, u32[]{:S(2)}) copy-start(s32[16,256]{1,0:T(8,128)} %param.18) | copy-start | bytes 49156
  0.6 2.6 %copy-start.2 = (f32[3,16,256]{2,1,0:T(8,128)S(1)}, f32[3,16,256]{2,1,0:T(8,128)}, u32[]{:S(2)}) copy-start(f32[3,16,256]{2,1,0:T(8,128)} %param.16) | copy-start | bytes 147460
  0.7 2.6 %copy-start = (f32[3,3,16,256]{3,2,1,0:T(8,128)S(1)}, f32[3,3,16,256]{3,2,1,0:T(8,128)}, u32[]{:S(2)}) copy-start(f32[3,3,16,256]{3,2,1,0:T(8,128)} %param.15) | copy-start | bytes 442372
  1.4 2.0 %copy-start.1 = (f32[2,64,256]{2,1,0:T(8,128)S(1)}, f32[2,64,256]{2,1,0:T(8,128)}, u32[]{:S(2)}) copy-start(f32[2,64,256]{2,1,0:T(8,128)} %param.11) | copy-start | bytes 393220
  1.4 2.0 %copy-start.3 = (f32[64,256]{1,0:T(8,128)S(1)}, f32[64,256]{1,0:T(8,128)}, u32[]{:S(2)}) copy-start(f32[64,256]{1,0:T(8,128)} %param.12) | copy-start | bytes 196612
  1.5 7.5 %copy-start.7 = (s32[1,9,128]{2,0,1:T(1,128)S(1)}, s32[1,9,128]{2,0,1:T(1,128)}, u32[]{:S(2)}) copy-start(s32[1,9,128]{2,0,1:T(1,128)} %param.20) | copy-start | bytes 13828
  3.5 6.8 %collective-permute-start.1 = (f32[4864]{0:T(1024)S(1)}, f32[4864]{0:T(1024)S(1)}, u32[]{:S(2)}, u32[]{:S(2)}) collective-permute-start(f32[4864]{0:T(1024)S(1)} %pad_maximum_fusion.25), channel_id=1, source_target_pairs={{16,0},{32,16},{48,32},{64,48},{80,64},{96,80},{112,96},{128,112},... | collective-permute-start | bytes 58376 | tf_op jit(solution)/shard_map/ppermute | solution.py:240
  7.1 6.3 %collective-permute-start = (f32[4864]{0:T(1024)S(1)}, f32[4864]{0:T(1024)S(1)}, u32[]{:S(2)}, u32[]{:S(2)}) collective-permute-start(f32[4864]{0:T(1024)S(1)} %pad_maximum_fusion.24), channel_id=1, source_target_pairs={{0,16},{16,32},{32,48},{48,64},{64,80},{80,96},{96,112},{112,128},... | collective-permute-start | bytes 58376 | tf_op jit(solution)/shard_map/ppermute | solution.py:240
  15.3 9.9 %all-to-all-start = ((f32[4,1,1712]{2,1,0:T(1,128)}), f32[4,1,1712]{2,1,0:T(1,128)S(1)}, u32[]{:S(2)}, u32[]{:S(2)}) async-start(f32[4,1,1712]{2,1,0:T(1,128)} %copy.65), calls=%async_computation | async-start | bytes 57344 | tf_op jit(solution)/shard_map/all_to_all | solution.py:246
  26.8 5.8 %collective-permute-start.3 = (f32[768]{0:T(1024)S(1)}, f32[768]{0:T(1024)S(1)}, u32[]{:S(2)}, u32[]{:S(2)}) collective-permute-start(f32[768]{0:T(1024)S(1)} %reshape.1406), channel_id=1, source_target_pairs={{16,0},{32,16},{48,32},{64,48},{80,64},{96,80},{112,96},{128,112},... | collective-permute-start | bytes 9224 | tf_op jit(solution)/shard_map/ppermute | solution.py:240
  28.8 6.1 %collective-permute-start.2 = (f32[768]{0:T(1024)S(1)}, f32[768]{0:T(1024)S(1)}, u32[]{:S(2)}, u32[]{:S(2)}) collective-permute-start(f32[768]{0:T(1024)S(1)} %reshape.1404), channel_id=1, source_target_pairs={{0,16},{16,32},{32,48},{48,64},{64,80},{80,96},{96,112},{112,128},... | collective-permute-start | bytes 9224 | tf_op jit(solution)/shard_map/ppermute | solution.py:240
  36.1 8.4 %all-to-all-start.1 = ((f32[4,1,54]{2,1,0:T(1,128)}), f32[4,1,54]{2,1,0:T(1,128)S(1)}, u32[]{:S(2)}, u32[]{:S(2)}) async-start(f32[4,1,54]{2,1,0:T(1,128)} %bitcast.22), calls=%async_computation.1 | async-start | bytes 4096 | tf_op jit(solution)/shard_map/all_to_all | solution.py:246
  44.5 11.9 %all-to-all-start.2 = ((f32[4,4,18,258]{3,1,2,0:T(4,128)}), f32[4,4,18,258]{3,1,2,0:T(4,128)S(1)}, u32[]{:S(2)}, u32[]{:S(2)}) async-start(f32[4,4,18,258]{3,1,2,0:T(4,128)} %copy.81), calls=%async_computation.2 | async-start | bytes 884736 | tf_op jit(solution)/shard_map/all_to_all | solution.py:246
  70.3 8.7 %all-to-all-start.3 = ((f32[4,2,9,128]{3,1,2,0:T(2,128)}), f32[4,2,9,128]{3,1,2,0:T(2,128)S(1)}, u32[]{:S(2)}, u32[]{:S(2)}) async-start(f32[4,2,9,128]{3,1,2,0:T(2,128)} %broadcast_in_dim.147), calls=%async_computation.3 | async-start | bytes 73728 | tf_op jit(solution)/shard_map/all_to_all | solution.py:143
  73.6 9.9 %copy-start.4 = (f32[64,256]{1,0:T(8,128)S(1)}, f32[64,256]{1,0:T(8,128)}, u32[]{:S(2)}) copy-start(f32[64,256]{1,0:T(8,128)} %param.13) | copy-start | bytes 196612
  73.6 9.8 %copy-start.5 = (f32[2,64,256]{2,1,0:T(8,128)S(1)}, f32[2,64,256]{2,1,0:T(8,128)}, u32[]{:S(2)}) copy-start(f32[2,64,256]{2,1,0:T(8,128)} %param.14) | copy-start | bytes 393220
  79.1 4.6 %collective-permute-start.5 = (f32[768]{0:T(1024)S(1)}, f32[768]{0:T(1024)S(1)}, u32[]{:S(2)}, u32[]{:S(2)}) collective-permute-start(f32[768]{0:T(1024)S(1)} %reshape.1413), channel_id=1, source_target_pairs={{16,0},{32,16},{48,32},{64,48},{80,64},{96,80},{112,96},{128,112},... | collective-permute-start | bytes 9224 | tf_op jit(solution)/shard_map/ppermute | solution.py:240
  81.0 6.1 %collective-permute-start.4 = (f32[768]{0:T(1024)S(1)}, f32[768]{0:T(1024)S(1)}, u32[]{:S(2)}, u32[]{:S(2)}) collective-permute-start(f32[768]{0:T(1024)S(1)} %reshape.1411), channel_id=1, source_target_pairs={{0,16},{16,32},{32,48},{48,64},{64,80},{80,96},{96,112},{112,128},... | collective-permute-start | bytes 9224 | tf_op jit(solution)/shard_map/ppermute | solution.py:240
  88.0 8.6 %all-to-all-start.4 = ((f32[4,1,1280]{2,1,0:T(1,128)}), f32[4,1,1280]{2,1,0:T(1,128)S(1)}, u32[]{:S(2)}, u32[]{:S(2)}) async-start(f32[4,1,1280]{2,1,0:T(1,128)} %copy.97), calls=%async_computation.4 | async-start | bytes 40960 | tf_op jit(solution)/shard_map/all_to_all | solution.py:246

commit v8 on v6

--- a/solution.py
+++ b/solution.py
@@ -8,11 +8,13 @@
 ROWS_PAD, LANES_PAD = 24, 384
 
 
-def fem_kernel(fld_ref, main_ref, weight_ref, kmat_ref, live_ref, body_ref, out_ref, vals_ref, vis_ref, resp_ref):
+def fem_body(comps, fld_ref, main_ref, weight_ref, kmat_ref, live_ref, body_ref, out_ref, vals_ref, vis_ref, resp_ref):
     main = main_ref[...] > 0.5
     weight = weight_ref[...]
     zero = jnp.zeros((ROWS_PAD, LANES_PAD), jnp.float32)
-    out_ref[...] = -body_ref[...]
+    for comp in comps:
+        out_ref[comp] = -body_ref[comp]
+    rows_out = [height * 9 + comp * 3 + vertex for height in range(2) for comp in comps for vertex in range(3)]
     pairs = fld_ref.shape[1] - 1
     for pair in range(pairs):
         vis_parts = [[], []]
@@ -46,7 +48,7 @@
             row = pl.multiple_of(block * 8, 8)
             for tri in range(2):
                 vis = vis_ref[tri, pl.ds(row, 8), :]
-                for alpha in range(18):
+                for alpha in rows_out:
                     acc = kmat_ref[alpha, 0] * vals_ref[tri, 0, pl.ds(row, 8), :]
                     for beta in range(1, 18):
                         acc = acc + kmat_ref[alpha, beta] * vals_ref[tri, beta, pl.ds(row, 8), :]
@@ -63,7 +65,7 @@
                 scale = live_ref[0]
             if pair == pairs - 1 and height == 0:
                 scale = live_ref[1]
-            for comp in range(3):
+            for comp in comps:
                 base = height * 9 + comp * 3
                 one = [resp_ref[0, base + v] for v in range(3)]
                 two = [resp_ref[1, base + v] for v in range(3)]
@@ -80,39 +82,64 @@
                 out_ref[comp, own_layer] = out_ref[comp, own_layer] + part
 
 
-def fem_pallas(extended_layers, flag_cells, weight, element_matrix, below_live, above_live, body_force):
+def fem_horizontal(fld_ref, main_ref, weight_ref, kmat_ref, live_ref, body_ref, out_ref, depth_ref, vals_ref, vis_ref, resp_ref):
+    fem_body((0, 1), fld_ref, main_ref, weight_ref, kmat_ref, live_ref, body_ref, out_ref, vals_ref, vis_ref, resp_ref)
+    for comp in range(2):
+        total = out_ref[comp, 0]
+        for layer in range(1, out_ref.shape[1]):
+            total = total + out_ref[comp, layer]
+        depth_ref[comp] = total
+
+
+def fem_vertical(fld_ref, main_ref, weight_ref, kmat_ref, live_ref, body_ref, prev_ref, out_ref, vals_ref, vis_ref, resp_ref):
+    out_ref[0:2] = prev_ref[0:2]
+    fem_body((2,), fld_ref, main_ref, weight_ref, kmat_ref, live_ref, body_ref, out_ref, vals_ref, vis_ref, resp_ref)
+
+
+def fem_inputs(extended_layers, flag_cells, weight, below_live, above_live):
     comps, layers, rows, lanes = extended_layers.shape
     fld = jnp.pad(extended_layers, ((0, 0), (0, 0), (0, ROWS_PAD - rows), (0, LANES_PAD - lanes)))
     cell_rows, cell_lanes = flag_cells.shape
     main = jnp.pad((flag_cells == 0).astype(jnp.float32), ((0, ROWS_PAD - cell_rows), (0, LANES_PAD - cell_lanes)))
     wpad = jnp.pad(weight, ((0, ROWS_PAD - cell_rows), (0, LANES_PAD - cell_lanes)))
     live = jnp.stack([below_live, above_live]).astype(jnp.float32)
+    return fld, main, wpad, live
+
+
+def fem_scratch():
+    return [
+        pltpu.VMEM((2, 18, ROWS_PAD, LANES_PAD), jnp.float32),
+        pltpu.VMEM((2, ROWS_PAD, LANES_PAD), jnp.float32),
+        pltpu.VMEM((2, 18, ROWS_PAD, LANES_PAD), jnp.float32),
+    ]
+
+
+def fem_first(fld, main, wpad, element_matrix, live, body_force):
+    vmem = pl.BlockSpec(memory_space=pltpu.VMEM)
+    smem = pl.BlockSpec(memory_space=pltpu.SMEM)
+    depth_shape = (2,) + body_force.shape[2:]
     return pl.pallas_call(
-        fem_kernel,
+        fem_horizontal,
+        out_shape=(
+            jax.ShapeDtypeStruct(body_force.shape, jnp.float32),
+            jax.ShapeDtypeStruct(depth_shape, jnp.float32),
+        ),
+        in_specs=[vmem, vmem, vmem, smem, smem, vmem],
+        out_specs=(vmem, vmem),
+        scratch_shapes=fem_scratch(),
+    )(fld, main, wpad, element_matrix, live, body_force)
+
+
+def fem_second(fld, main, wpad, element_matrix, live, body_force, previous):
+    vmem = pl.BlockSpec(memory_space=pltpu.VMEM)
+    smem = pl.BlockSpec(memory_space=pltpu.SMEM)
+    return pl.pallas_call(
+        fem_vertical,
         out_shape=jax.ShapeDtypeStruct(body_force.shape, jnp.float32),
-        in_specs=[pl.BlockSpec(memory_space=pltpu.VMEM)] * 3
-        + [pl.BlockSpec(memory_space=pltpu.SMEM)] * 2
-        + [pl.BlockSpec(memory_space=pltpu.VMEM)],
-        out_specs=pl.BlockSpec(memory_space=pltpu.VMEM),
-        scratch_shapes=[
-            pltpu.VMEM((2, 18, ROWS_PAD, LANES_PAD), jnp.float32),
-            pltpu.VMEM((2, ROWS_PAD, LANES_PAD), jnp.float32),
-            pltpu.VMEM((2, 18, ROWS_PAD, LANES_PAD), jnp.float32),
-        ],
-    )(fld, main, wpad, element_matrix, live, body_force)
-
-
-def with_halo(array, sides, width):
-    for axis, dim in sides:
-        devices, length = (lax.axis_size(axis), array.shape[dim])
-        up = [(i, (i + 1) % devices) for i in range(devices - 1)]
-        down = [(j, i) for i, j in up]
-        last = lax.slice_in_dim(array, length - width, length, axis=dim)
-        initial = lax.slice_in_dim(array, 0, width, axis=dim)
-        before = lax.ppermute(last, axis, up)
-        after = lax.ppermute(initial, axis, down)
-        array = jnp.concatenate([before, array, after], axis=dim)
-    return array
+        in_specs=[vmem, vmem, vmem, smem, smem, vmem, vmem],
+        out_specs=vmem,
+        scratch_shapes=fem_scratch(),
+    )(fld, main, wpad, element_matrix, live, body_force, previous)
 
 
 HIGH = lax.Precision.HIGHEST
@@ -340,10 +367,9 @@
     layer_count = lax.axis_size("layer")
     below_live = (layer_index > 0).astype(jnp.float32)
     above_live = (layer_index < layer_count - 1).astype(jnp.float32)
-    stokes_residual = fem_pallas(
-        extended_layers, flag_cells, weight, element_matrix, below_live, above_live, body_force
-    )
-    depth_sum = jnp.sum(stokes_residual[:2], axis=1)
+    fld, main, wpad, live = fem_inputs(extended_layers, flag_cells, weight, below_live, above_live)
+    partial_residual, depth_sum = fem_first(fld, main, wpad, element_matrix, live, body_force)
+    stokes_residual = fem_second(fld, main, wpad, element_matrix, live, body_force, partial_residual)
     bucket = gather_slots(depth_sum, col_row, col_col).reshape(2, 9, slot_count)
     depth_total = layer_total(bucket)
     grid_back = depth_total.reshape(2, 3, 3, slot_count)

time: 88.7 us -> 92.8 us (1.046)
  the two profiles are of different devices: /device:TPU:408 before, /device:TPU:105 now
where the time goes in v8:
time: 92.8 us; the launch traced here: 92.2 us
  starting transfers between devices  46.1 us (50%)
  waiting for transfers between devices  15.4 us (17%)
  Pallas kernels  13.6 us (15%)
  other arithmetic  5.38 us (6%)
  matrix products  5.36 us (6%)
  local copies, waits for them, and re-layouts  4.84 us (5%)
  between operations  1.45 us (2%)
    ppermute x6, starting transfers between devices, exchange(): lax.ppermute(sent_up, axis, up)  25 us
    ppermute x6, starting transfers between devices, exchange(): lax.ppermute(sent_down, axis, down)  13.7 us
    ppermute x6, waiting for transfers between devices, exchange(): lax.ppermute(sent_down, axis, down)  10.7 us
    pallas_call x1, Pallas kernels, fem_first(): pl.pallas_call(fem_horizontal, out_shape=(jax.ShapeDtypeStruct(body_force...  8.01 us
    pallas_call x1, Pallas kernels, fem_second(): pl.pallas_call(fem_vertical, out_shape=jax.ShapeDtypeStruct(body_force.sh...  5.56 us
    all_to_all x1, waiting for transfers between devices, layer_total(): gathered = lax.all_to_all(copies, 'layer', 0, 0, tiled=True)  4.12 us
    all_to_all x1, starting transfers between devices, layer_neighbours(): lax.all_to_all(jnp.concatenate(chunks, 0), 'layer', 0, 0, tiled=True)  4.01 us
    all_to_all x1, starting transfers between devices, layer_total(): gathered = lax.all_to_all(copies, 'layer', 0, 0, tiled=True)  3.41 us
  transfers between devices with their start and end apart: 14, of which 6 were waited for; matrix products, arithmetic and copies ran while one was open for 7% of the time, Pallas kernels for 6%

profile of v8, /device:TPU:105, one launch (start us, length us, event | category | flops | bytes accessed | tf_op | source)
XLA Modules:
  0.0 92.2 jit_solution(14479705563094038823)
XLA Ops:
  0.7 0.7 reduce.2
  1.5 1.7 %fusion.1 = f32[2,1152]{1,0:T(2,128)S(1)} fusion(f32[2,64,256]{2,1,0:T(8,128)} %param.11, s32[1152]{0:T(1024)S(1)} %get-tuple-element.53, pred[64,1152]{1,0:T(8,128)(4,1)S(1)} %convert_compare_fusion), kind=kOutput, calls=%fused_computation.3 | convolution fusion | flops 453572352 | bytes 218624 | tf_op jit(solution)/shard_map/krc,sc->krs/dot_general | solution.py:158
  3.5 5.3 %collective-permute-start = (f32[4864]{0:T(1024)S(1)}, f32[4864]{0:T(1024)S(1)}, u32[]{:S(2)}, u32[]{:S(2)}) collective-permute-start(f32[4864]{0:T(1024)S(1)} %pad_maximum_fusion.24), channel_id=1, source_target_pairs={{0,16},{16,32},{32,48},{48,64},{64,80},{80,96},{96,112},{112,128},... | collective-permute-start | bytes 58376 | tf_op jit(solution)/shard_map/ppermute | solution.py:282
  8.8 1.9 %collective-permute-start.1 = (f32[4864]{0:T(1024)S(1)}, f32[4864]{0:T(1024)S(1)}, u32[]{:S(2)}, u32[]{:S(2)}) collective-permute-start(f32[4864]{0:T(1024)S(1)} %pad_maximum_fusion.25), channel_id=1, source_target_pairs={{16,0},{32,16},{48,32},{64,48},{80,64},{96,80},{112,96},{128,112},... | collective-permute-start | bytes 58376 | tf_op jit(solution)/shard_map/ppermute | solution.py:282
  11.4 3.7 %collective-permute-done.1 = f32[4864]{0:T(1024)S(1)} collective-permute-done((f32[4864]{0:T(1024)S(1)}, f32[4864]{0:T(1024)S(1)}, u32[]{:S(2)}, u32[]{:S(2)}) %collective-permute-start.1) | collective-permute-done | bytes 19488 | tf_op jit(solution)/shard_map/ppermute | solution.py:282
  16.2 3.2 %collective-permute-start.2 = (f32[1712]{0:T(1024)S(1)}, f32[1712]{0:T(1024)S(1)}, u32[]{:S(2)}, u32[]{:S(2)}) collective-permute-start(f32[1712]{0:T(1024)S(1)} %concatenate.70), channel_id=1, source_target_pairs={{0,4},{4,8},{8,12},{1,5},{5,9},{9,13},{2,6},{6,10},{10,14},{3,7},{... | collective-permute-start | bytes 20552 | tf_op jit(solution)/shard_map/ppermute | solution.py:282
  19.6 2.1 %collective-permute-start.3 = (f32[1712]{0:T(1024)S(1)}, f32[1712]{0:T(1024)S(1)}, u32[]{:S(2)}, u32[]{:S(2)}) collective-permute-start(f32[1712]{0:T(1024)S(1)} %concatenate.71), channel_id=1, source_target_pairs={{4,0},{8,4},{12,8},{5,1},{9,5},{13,9},{6,2},{10,6},{14,10},{7,3},{... | collective-permute-start | bytes 20552 | tf_op jit(solution)/shard_map/ppermute | solution.py:282
  21.7 0.7 add_convert_fusion.live_ref
  22.4 1.6 %collective-permute-done.3 = f32[1712]{0:T(1024)S(1)} collective-permute-done((f32[1712]{0:T(1024)S(1)}, f32[1712]{0:T(1024)S(1)}, u32[]{:S(2)}, u32[]{:S(2)}) %collective-permute-start.3) | collective-permute-done | bytes 6880 | tf_op jit(solution)/shard_map/ppermute | solution.py:282
  24.4 0.5 fusion.5
  25.0 3.4 %collective-permute-start.4 = (f32[768]{0:T(1024)S(1)}, f32[768]{0:T(1024)S(1)}, u32[]{:S(2)}, u32[]{:S(2)}) collective-permute-start(f32[768]{0:T(1024)S(1)} %reshape.614), channel_id=1, source_target_pairs={{0,16},{16,32},{32,48},{48,64},{64,80},{80,96},{96,112},{112,128},... | collective-permute-start | bytes 9224 | tf_op jit(solution)/shard_map/ppermute | solution.py:282
  28.4 1.9 %collective-permute-start.5 = (f32[768]{0:T(1024)S(1)}, f32[768]{0:T(1024)S(1)}, u32[]{:S(2)}, u32[]{:S(2)}) collective-permute-start(f32[768]{0:T(1024)S(1)} %reshape.616), channel_id=1, source_target_pairs={{16,0},{32,16},{48,32},{64,48},{80,64},{96,80},{112,96},{128,112},... | collective-permute-start | bytes 9224 | tf_op jit(solution)/shard_map/ppermute | solution.py:282
  32.3 0.9 copy.70
  33.2 4.0 %all-to-all-start = ((f32[4,4,18,258]{3,1,2,0:T(4,128)}), f32[4,4,18,258]{3,1,2,0:T(4,128)S(1)}, u32[]{:S(2)}, u32[]{:S(2)}) async-start(f32[4,4,18,258]{3,1,2,0:T(4,128)} %copy.70), calls=%async_computation | async-start | bytes 884736 | tf_op jit(solution)/shard_map/all_to_all | solution.py:184
  37.5 2.9 %collective-permute-start.6 = (f32[54]{0:T(128)S(1)}, f32[54]{0:T(128)S(1)}, u32[]{:S(2)}, u32[]{:S(2)}) collective-permute-start(f32[54]{0:T(128)S(1)} %reshape.618), channel_id=1, source_target_pairs={{0,4},{4,8},{8,12},{1,5},{5,9},{9,13},{2,6},{6,10},{10,14},{3,7},{... | collective-permute-start | bytes 656 | tf_op jit(solution)/shard_map/ppermute | solution.py:282
  40.5 2.4 %collective-permute-start.7 = (f32[54]{0:T(128)S(1)}, f32[54]{0:T(128)S(1)}, u32[]{:S(2)}, u32[]{:S(2)}) collective-permute-start(f32[54]{0:T(128)S(1)} %reshape.620), channel_id=1, source_target_pairs={{4,0},{8,4},{12,8},{5,1},{9,5},{13,9},{6,2},{10,6},{14,10},{7,3},{... | collective-permute-start | bytes 656 | tf_op jit(solution)/shard_map/ppermute | solution.py:282
  42.9 0.6 pad_convert_fusion
  43.6 1.4 %collective-permute-done.7 = f32[54]{0:T(128)S(1)} collective-permute-done((f32[54]{0:T(128)S(1)}, f32[54]{0:T(128)S(1)}, u32[]{:S(2)}, u32[]{:S(2)}) %collective-permute-start.7) | collective-permute-done | bytes 248 | tf_op jit(solution)/shard_map/ppermute | solution.py:282
  45.4 0.6 all-to-all-done
  46.2 0.9 %select_maximum_fusion.fld_ref = f32[4,5,24,384]{3,2,1,0:T(8,128)} fusion(f32[2,5,18,258]{3,2,1,0:T(8,128)S(1)} %get-tuple-element.25, f32[2,5,18,258]{3,2,1,0:T(8,128)S(1)} %get-tuple-element.24), kind=kLoop, calls=%fused_computation.15 | loop fusion | flops 1474560 | bytes 1108800 | tf_op jit(solution)/shard_map/concatenate | solution.py:356
  47.1 8.0 %shard_map.122 = (f32[3,3,16,256]{3,2,1,0:T(8,128)}, f32[2,16,256]{2,1,0:T(8,128)}) custom-call(f32[4,5,24,384]{3,2,1,0:T(8,128)} %select_maximum_fusion.fld_ref, f32[24,384]{1,0:T(8,128)} %get-tuple-element.55.main_ref, f32[24,384]{1,0:T(8,128)} %get-tuple-element.54.weight_ref, f32[18,18]{1,0:T(8,128)} %kmat_ref.3, f32[2]{0:T(128)} %add_convert_fusion.live_ref, ...), custom_call_target="tpu_custom_call" | custom-call | tf_op jit(solution)/shard_map/pallas_call | solution.py:121
  55.1 1.5 %fusion.14 = f32[2,1152]{1,0:T(2,128)S(1)} fusion(f32[2,16,256]{2,1,0:T(8,128)} %get-tuple-element.4, s32[1152]{0:T(1024)S(1)} %get-tuple-element.51, pred[16,1152]{1,0:T(8,128)(4,1)S(1)} %convert_compare_fusion.1), kind=kOutput, calls=%fused_computation.12 | convolution fusion | flops 113612544 | bytes 65024 | tf_op jit(solution)/shard_map/krc,sc->krs/dot_general | solution.py:158
  56.6 0.6 broadcast_in_dim.104
  57.3 3.4 %all-to-all-start.1 = ((f32[4,2,9,128]{3,1,2,0:T(2,128)}), f32[4,2,9,128]{3,1,2,0:T(2,128)S(1)}, u32[]{:S(2)}, u32[]{:S(2)}) async-start(f32[4,2,9,128]{3,1,2,0:T(2,128)} %broadcast_in_dim.104), calls=%async_computation.1 | async-start | bytes 73728 | tf_op jit(solution)/shard_map/all_to_all | solution.py:170
  60.9 4.1 %all-to-all-done.1 = f32[4,2,9,128]{3,1,2,0:T(2,128)S(1)} async-done(((f32[4,2,9,128]{3,1,2,0:T(2,128)}), f32[4,2,9,128]{3,1,2,0:T(2,128)S(1)}, u32[]{:S(2)}, u32[]{:S(2)}) %all-to-all-start.1) | async-done | bytes 36896 | tf_op jit(solution)/shard_map/all_to_all | solution.py:170
  65.0 8.3 %collective-permute-start.8 = (f32[768]{0:T(1024)S(1)}, f32[768]{0:T(1024)S(1)}, u32[]{:S(2)}, u32[]{:S(2)}) collective-permute-start(f32[768]{0:T(1024)S(1)} %reshape.625), channel_id=1, source_target_pairs={{0,16},{16,32},{32,48},{48,64},{64,80},{80,96},{96,112},{112,128},... | collective-permute-start | bytes 9224 | tf_op jit(solution)/shard_map/ppermute | solution.py:282
  73.3 1.9 %collective-permute-start.9 = (f32[768]{0:T(1024)S(1)}, f32[768]{0:T(1024)S(1)}, u32[]{:S(2)}, u32[]{:S(2)}) collective-permute-start(f32[768]{0:T(1024)S(1)} %reshape.627), channel_id=1, source_target_pairs={{16,0},{32,16},{48,32},{64,48},{80,64},{96,80},{112,96},{128,112},... | collective-permute-start | bytes 9224 | tf_op jit(solution)/shard_map/ppermute | solution.py:282
  75.5 4.0 %collective-permute-done.9 = f32[768]{0:T(1024)S(1)} collective-permute-done((f32[768]{0:T(1024)S(1)}, f32[768]{0:T(1024)S(1)}, u32[]{:S(2)}, u32[]{:S(2)}) %collective-permute-start.9) | collective-permute-done | bytes 3104 | tf_op jit(solution)/shard_map/ppermute | solution.py:282
  79.5 1.9 %collective-permute-start.10 = (f32[1280]{0:T(1024)S(1)}, f32[1280]{0:T(1024)S(1)}, u32[]{:S(2)}, u32[]{:S(2)}) collective-permute-start(f32[1280]{0:T(1024)S(1)} %reshape.629), channel_id=1, source_target_pairs={{0,4},{4,8},{8,12},{1,5},{5,9},{9,13},{2,6},{6,10},{10,14},{3,7},{... | collective-permute-start | bytes 15368 | tf_op jit(solution)/shard_map/ppermute | solution.py:282
  81.5 3.5 %collective-permute-start.11 = (f32[1280]{0:T(1024)S(1)}, f32[1280]{0:T(1024)S(1)}, u32[]{:S(2)}, u32[]{:S(2)}) collective-permute-start(f32[1280]{0:T(1024)S(1)} %reshape.631), channel_id=1, source_target_pairs={{4,0},{8,4},{12,8},{5,1},{9,5},{13,9},{6,2},{10,6},{14,10},{7,3},{... | collective-permute-start | bytes 15368 | tf_op jit(solution)/shard_map/ppermute | solution.py:282
  85.2 5.6 %shard_map.123 = f32[3,3,16,256]{3,2,1,0:T(8,128)} custom-call(f32[4,5,24,384]{3,2,1,0:T(8,128)} %select_maximum_fusion.fld_ref, f32[24,384]{1,0:T(8,128)} %get-tuple-element.55.main_ref, f32[24,384]{1,0:T(8,128)} %get-tuple-element.54.weight_ref, f32[18,18]{1,0:T(8,128)} %kmat_ref.3, f32[2]{0:T(128)} %add_convert_fusion.live_ref, ...), custom_call_target="tpu_custom_call" | custom-call | tf_op jit(solution)/shard_map/pallas_call | solution.py:136
  90.8 1.3 %fusion.11 = f32[2,64,256]{2,1,0:T(8,128)} fusion(s32[1152]{0:T(1024)S(1)} %get-tuple-element.53, f32[2,1152]{1,0:T(2,128)S(1)} %bitcast.183, f32[1152,64]{0,1:T(8,128)S(1)} %fusion.27, f32[1,64,256]{2,1,0:T(8,128)S(1)} %fusion.42, f32[1,64,256]{2,1,0:T(8,128)S(1)} %fusion.48), kind=kOutput, calls=%fused_computation.11 | convolution fusion | flops 453492736 | bytes 570880 | tf_op jit(solution)/shard_map/ksr,sc->krc/dot_general | solution.py:164
  (135 shorter events, 6.1 us)
Async XLA Ops:
  0.6 2.6 %copy-start.6 = (s32[16,256]{1,0:T(8,128)S(1)}, s32[16,256]{1,0:T(8,128)}, u32[]{:S(2)}) copy-start(s32[16,256]{1,0:T(8,128)} %param.18) | copy-start | bytes 49156
  0.6 2.6 %copy-start = (f32[3,3,16,256]{3,2,1,0:T(8,128)S(1)}, f32[3,3,16,256]{3,2,1,0:T(8,128)}, u32[]{:S(2)}) copy-start(f32[3,3,16,256]{3,2,1,0:T(8,128)} %param.15) | copy-start | bytes 442372
  0.7 2.6 %copy-start.2 = (f32[3,16,256]{2,1,0:T(8,128)S(1)}, f32[3,16,256]{2,1,0:T(8,128)}, u32[]{:S(2)}) copy-start(f32[3,16,256]{2,1,0:T(8,128)} %param.16) | copy-start | bytes 147460
  1.4 2.0 %copy-start.1 = (f32[2,64,256]{2,1,0:T(8,128)S(1)}, f32[2,64,256]{2,1,0:T(8,128)}, u32[]{:S(2)}) copy-start(f32[2,64,256]{2,1,0:T(8,128)} %param.11) | copy-start | bytes 393220
  1.4 2.0 %copy-start.3 = (f32[64,256]{1,0:T(8,128)S(1)}, f32[64,256]{1,0:T(8,128)}, u32[]{:S(2)}) copy-start(f32[64,256]{1,0:T(8,128)} %param.12) | copy-start | bytes 196612
  1.5 9.3 %copy-start.7 = (s32[1,9,128]{2,0,1:T(1,128)S(1)}, s32[1,9,128]{2,0,1:T(1,128)}, u32[]{:S(2)}) copy-start(s32[1,9,128]{2,0,1:T(1,128)} %param.20) | copy-start | bytes 13828
  3.5 7.9 %collective-permute-start = (f32[4864]{0:T(1024)S(1)}, f32[4864]{0:T(1024)S(1)}, u32[]{:S(2)}, u32[]{:S(2)}) collective-permute-start(f32[4864]{0:T(1024)S(1)} %pad_maximum_fusion.24), channel_id=1, source_target_pairs={{0,16},{16,32},{32,48},{48,64},{64,80},{80,96},{96,112},{112,128},... | collective-permute-start | bytes 58376 | tf_op jit(solution)/shard_map/ppermute | solution.py:282
  8.8 6.3 %collective-permute-start.1 = (f32[4864]{0:T(1024)S(1)}, f32[4864]{0:T(1024)S(1)}, u32[]{:S(2)}, u32[]{:S(2)}) collective-permute-start(f32[4864]{0:T(1024)S(1)} %pad_maximum_fusion.25), channel_id=1, source_target_pairs={{16,0},{32,16},{48,32},{64,48},{80,64},{96,80},{112,96},{128,112},... | collective-permute-start | bytes 58376 | tf_op jit(solution)/shard_map/ppermute | solution.py:282
  16.2 6.2 %collective-permute-start.2 = (f32[1712]{0:T(1024)S(1)}, f32[1712]{0:T(1024)S(1)}, u32[]{:S(2)}, u32[]{:S(2)}) collective-permute-start(f32[1712]{0:T(1024)S(1)} %concatenate.70), channel_id=1, source_target_pairs={{0,4},{4,8},{8,12},{1,5},{5,9},{9,13},{2,6},{6,10},{10,14},{3,7},{... | collective-permute-start | bytes 20552 | tf_op jit(solution)/shard_map/ppermute | solution.py:282
  19.6 4.4 %collective-permute-start.3 = (f32[1712]{0:T(1024)S(1)}, f32[1712]{0:T(1024)S(1)}, u32[]{:S(2)}, u32[]{:S(2)}) collective-permute-start(f32[1712]{0:T(1024)S(1)} %concatenate.71), channel_id=1, source_target_pairs={{4,0},{8,4},{12,8},{5,1},{9,5},{13,9},{6,2},{10,6},{14,10},{7,3},{... | collective-permute-start | bytes 20552 | tf_op jit(solution)/shard_map/ppermute | solution.py:282
  25.0 12.2 %collective-permute-start.4 = (f32[768]{0:T(1024)S(1)}, f32[768]{0:T(1024)S(1)}, u32[]{:S(2)}, u32[]{:S(2)}) collective-permute-start(f32[768]{0:T(1024)S(1)} %reshape.614), channel_id=1, source_target_pairs={{0,16},{16,32},{32,48},{48,64},{64,80},{80,96},{96,112},{112,128},... | collective-permute-start | bytes 9224 | tf_op jit(solution)/shard_map/ppermute | solution.py:282
  28.4 8.9 %collective-permute-start.5 = (f32[768]{0:T(1024)S(1)}, f32[768]{0:T(1024)S(1)}, u32[]{:S(2)}, u32[]{:S(2)}) collective-permute-start(f32[768]{0:T(1024)S(1)} %reshape.616), channel_id=1, source_target_pairs={{16,0},{32,16},{48,32},{64,48},{80,64},{96,80},{112,96},{128,112},... | collective-permute-start | bytes 9224 | tf_op jit(solution)/shard_map/ppermute | solution.py:282
  33.2 12.8 %all-to-all-start = ((f32[4,4,18,258]{3,1,2,0:T(4,128)}), f32[4,4,18,258]{3,1,2,0:T(4,128)S(1)}, u32[]{:S(2)}, u32[]{:S(2)}) async-start(f32[4,4,18,258]{3,1,2,0:T(4,128)} %copy.70), calls=%async_computation | async-start | bytes 884736 | tf_op jit(solution)/shard_map/all_to_all | solution.py:184
  37.5 6.0 %collective-permute-start.6 = (f32[54]{0:T(128)S(1)}, f32[54]{0:T(128)S(1)}, u32[]{:S(2)}, u32[]{:S(2)}) collective-permute-start(f32[54]{0:T(128)S(1)} %reshape.618), channel_id=1, source_target_pairs={{0,4},{4,8},{8,12},{1,5},{5,9},{9,13},{2,6},{6,10},{10,14},{3,7},{... | collective-permute-start | bytes 656 | tf_op jit(solution)/shard_map/ppermute | solution.py:282
  40.5 4.6 %collective-permute-start.7 = (f32[54]{0:T(128)S(1)}, f32[54]{0:T(128)S(1)}, u32[]{:S(2)}, u32[]{:S(2)}) collective-permute-start(f32[54]{0:T(128)S(1)} %reshape.620), channel_id=1, source_target_pairs={{4,0},{8,4},{12,8},{5,1},{9,5},{13,9},{6,2},{10,6},{14,10},{7,3},{... | collective-permute-start | bytes 656 | tf_op jit(solution)/shard_map/ppermute | solution.py:282
  57.3 7.7 %all-to-all-start.1 = ((f32[4,2,9,128]{3,1,2,0:T(2,128)}), f32[4,2,9,128]{3,1,2,0:T(2,128)S(1)}, u32[]{:S(2)}, u32[]{:S(2)}) async-start(f32[4,2,9,128]{3,1,2,0:T(2,128)} %broadcast_in_dim.104), calls=%async_computation.1 | async-start | bytes 73728 | tf_op jit(solution)/shard_map/all_to_all | solution.py:170
  60.7 14.6 %copy-start.4 = (f32[64,256]{1,0:T(8,128)S(1)}, f32[64,256]{1,0:T(8,128)}, u32[]{:S(2)}) copy-start(f32[64,256]{1,0:T(8,128)} %param.13) | copy-start | bytes 196612
  60.7 14.6 %copy-start.5 = (f32[2,64,256]{2,1,0:T(8,128)S(1)}, f32[2,64,256]{2,1,0:T(8,128)}, u32[]{:S(2)}) copy-start(f32[2,64,256]{2,1,0:T(8,128)} %param.14) | copy-start | bytes 393220
  65.0 10.4 %collective-permute-start.8 = (f32[768]{0:T(1024)S(1)}, f32[768]{0:T(1024)S(1)}, u32[]{:S(2)}, u32[]{:S(2)}) collective-permute-start(f32[768]{0:T(1024)S(1)} %reshape.625), channel_id=1, source_target_pairs={{0,16},{16,32},{32,48},{48,64},{64,80},{80,96},{96,112},{112,128},... | collective-permute-start | bytes 9224 | tf_op jit(solution)/shard_map/ppermute | solution.py:282
  73.3 6.1 %collective-permute-start.9 = (f32[768]{0:T(1024)S(1)}, f32[768]{0:T(1024)S(1)}, u32[]{:S(2)}, u32[]{:S(2)}) collective-permute-start(f32[768]{0:T(1024)S(1)} %reshape.627), channel_id=1, source_target_pairs={{16,0},{32,16},{48,32},{64,48},{80,64},{96,80},{112,96},{128,112},... | collective-permute-start | bytes 9224 | tf_op jit(solution)/shard_map/ppermute | solution.py:282
  79.5 11.2 %collective-permute-start.10 = (f32[1280]{0:T(1024)S(1)}, f32[1280]{0:T(1024)S(1)}, u32[]{:S(2)}, u32[]{:S(2)}) collective-permute-start(f32[1280]{0:T(1024)S(1)} %reshape.629), channel_id=1, source_target_pairs={{0,4},{4,8},{8,12},{1,5},{5,9},{9,13},{2,6},{6,10},{10,14},{3,7},{... | collective-permute-start | bytes 15368 | tf_op jit(solution)/shard_map/ppermute | solution.py:282
  81.5 9.3 %collective-permute-start.11 = (f32[1280]{0:T(1024)S(1)}, f32[1280]{0:T(1024)S(1)}, u32[]{:S(2)}, u32[]{:S(2)}) collective-permute-start(f32[1280]{0:T(1024)S(1)} %reshape.631), channel_id=1, source_target_pairs={{4,0},{8,4},{12,8},{5,1},{9,5},{13,9},{6,2},{10,6},{14,10},{7,3},{... | collective-permute-start | bytes 15368 | tf_op jit(solution)/shard_map/ppermute | solution.py:282

commit v9 on v8

--- a/solution.py
+++ b/solution.py
@@ -372,6 +372,7 @@
     stokes_residual = fem_second(fld, main, wpad, element_matrix, live, body_force, partial_residual)
     bucket = gather_slots(depth_sum, col_row, col_col).reshape(2, 9, slot_count)
     depth_total = layer_total(bucket)
+    depth_total, stokes_residual = lax.optimization_barrier((depth_total, stokes_residual))
     grid_back = depth_total.reshape(2, 3, 3, slot_count)
     (back_x,) = packed_halo((grid_back,), (1,), "mx")
     (extended_back,) = packed_halo((back_x,), (2,), "my")

time: 92.8 us -> 87 us (0.938)
  the two profiles are of different devices: /device:TPU:105 before, /device:TPU:410 now
where the time goes in v9:
time: 87 us; the launch traced here: 86.3 us
  starting transfers between devices  35 us (40%)
  waiting for transfers between devices  20.7 us (24%)
  Pallas kernels  13.6 us (16%)
  other arithmetic  5.41 us (6%)
  matrix products  5.36 us (6%)
  local copies, waits for them, and re-layouts  4.84 us (6%)
  between operations  1.44 us (2%)
    ppermute x6, waiting for transfers between devices, exchange(): lax.ppermute(sent_up, axis, up)  20.7 us
    ppermute x6, starting transfers between devices, exchange(): lax.ppermute(sent_down, axis, down)  14.8 us
    ppermute x6, starting transfers between devices, exchange(): lax.ppermute(sent_up, axis, up)  10.6 us
    pallas_call x1, Pallas kernels, fem_first(): pl.pallas_call(fem_horizontal, out_shape=(jax.ShapeDtypeStruct(body_force...  8.01 us
    pallas_call x1, Pallas kernels, fem_second(): pl.pallas_call(fem_vertical, out_shape=jax.ShapeDtypeStruct(body_force.sh...  5.61 us
    all_to_all x1, starting transfers between devices, layer_neighbours(): lax.all_to_all(jnp.concatenate(chunks, 0), 'layer', 0, 0, tiled=True)  4.82 us
    all_to_all x1, starting transfers between devices, layer_total(): gathered = lax.all_to_all(copies, 'layer', 0, 0, tiled=True)  4.8 us
    dot_general x2, matrix products, gather_slots(): cols_taken = jnp.einsum('krc,sc->krs', field, pick_col, precision=HIGH)  3.15 us
  transfers between devices with their start and end apart: 14, of which 6 were waited for; matrix products, arithmetic and copies ran while one was open for 7% of the time, Pallas kernels for 6%

profile of v9, /device:TPU:410, one launch (start us, length us, event | category | flops | bytes accessed | tf_op | source)
XLA Modules:
  0.0 86.3 jit_solution(14246952268068306999)
XLA Ops:
  0.7 0.7 reduce.2
  1.5 1.7 %fusion.1 = f32[2,1152]{1,0:T(2,128)S(1)} fusion(f32[2,64,256]{2,1,0:T(8,128)} %param.11, s32[1152]{0:T(1024)S(1)} %get-tuple-element.57, pred[64,1152]{1,0:T(8,128)(4,1)S(1)} %convert_compare_fusion), kind=kOutput, calls=%fused_computation.3 | convolution fusion | flops 453572352 | bytes 218624 | tf_op jit(solution)/shard_map/krc,sc->krs/dot_general | solution.py:158
  3.5 3.6 %collective-permute-start.1 = (f32[4864]{0:T(1024)S(1)}, f32[4864]{0:T(1024)S(1)}, u32[]{:S(2)}, u32[]{:S(2)}) collective-permute-start(f32[4864]{0:T(1024)S(1)} %pad_maximum_fusion.25), channel_id=1, source_target_pairs={{16,0},{32,16},{48,32},{64,48},{80,64},{96,80},{112,96},{128,112},... | collective-permute-start | bytes 58376 | tf_op jit(solution)/shard_map/ppermute | solution.py:282
  7.1 1.9 %collective-permute-start = (f32[4864]{0:T(1024)S(1)}, f32[4864]{0:T(1024)S(1)}, u32[]{:S(2)}, u32[]{:S(2)}) collective-permute-start(f32[4864]{0:T(1024)S(1)} %pad_maximum_fusion.24), channel_id=1, source_target_pairs={{0,16},{16,32},{32,48},{48,64},{64,80},{80,96},{96,112},{112,128},... | collective-permute-start | bytes 58376 | tf_op jit(solution)/shard_map/ppermute | solution.py:282
  9.7 3.7 %collective-permute-done = f32[4864]{0:T(1024)S(1)} collective-permute-done((f32[4864]{0:T(1024)S(1)}, f32[4864]{0:T(1024)S(1)}, u32[]{:S(2)}, u32[]{:S(2)}) %collective-permute-start) | collective-permute-done | bytes 19488 | tf_op jit(solution)/shard_map/ppermute | solution.py:282
  14.4 2.6 %collective-permute-start.3 = (f32[1712]{0:T(1024)S(1)}, f32[1712]{0:T(1024)S(1)}, u32[]{:S(2)}, u32[]{:S(2)}) collective-permute-start(f32[1712]{0:T(1024)S(1)} %concatenate.71), channel_id=1, source_target_pairs={{4,0},{8,4},{12,8},{5,1},{9,5},{13,9},{6,2},{10,6},{14,10},{7,3},{... | collective-permute-start | bytes 20552 | tf_op jit(solution)/shard_map/ppermute | solution.py:282
  17.3 1.3 %collective-permute-start.2 = (f32[1712]{0:T(1024)S(1)}, f32[1712]{0:T(1024)S(1)}, u32[]{:S(2)}, u32[]{:S(2)}) collective-permute-start(f32[1712]{0:T(1024)S(1)} %concatenate.70), channel_id=1, source_target_pairs={{0,4},{4,8},{8,12},{1,5},{5,9},{9,13},{2,6},{6,10},{10,14},{3,7},{... | collective-permute-start | bytes 20552 | tf_op jit(solution)/shard_map/ppermute | solution.py:282
  18.6 0.7 add_convert_fusion.live_ref
  19.5 3.3 %collective-permute-done.2 = f32[1712]{0:T(1024)S(1)} collective-permute-done((f32[1712]{0:T(1024)S(1)}, f32[1712]{0:T(1024)S(1)}, u32[]{:S(2)}, u32[]{:S(2)}) %collective-permute-start.2) | collective-permute-done | bytes 6880 | tf_op jit(solution)/shard_map/ppermute | solution.py:282
  23.6 0.9 %copy.70 = f32[4,4,18,258]{3,1,2,0:T(4,128)} copy(f32[4,4,18,258]{3,2,1,0:T(8,128)S(1)} %pad_maximum_fusion.1) | data formatting | bytes 594432 | tf_op jit(solution)/shard_map/concatenate | solution.py:184
  24.5 4.8 %all-to-all-start = ((f32[4,4,18,258]{3,1,2,0:T(4,128)}), f32[4,4,18,258]{3,1,2,0:T(4,128)S(1)}, u32[]{:S(2)}, u32[]{:S(2)}) async-start(f32[4,4,18,258]{3,1,2,0:T(4,128)} %copy.70), calls=%async_computation | async-start | bytes 884736 | tf_op jit(solution)/shard_map/all_to_all | solution.py:184
  29.7 0.5 fusion.5
  30.3 1.9 %collective-permute-start.5 = (f32[768]{0:T(1024)S(1)}, f32[768]{0:T(1024)S(1)}, u32[]{:S(2)}, u32[]{:S(2)}) collective-permute-start(f32[768]{0:T(1024)S(1)} %reshape.614), channel_id=1, source_target_pairs={{16,0},{32,16},{48,32},{64,48},{80,64},{96,80},{112,96},{128,112},... | collective-permute-start | bytes 9224 | tf_op jit(solution)/shard_map/ppermute | solution.py:282
  32.3 2.4 %collective-permute-start.4 = (f32[768]{0:T(1024)S(1)}, f32[768]{0:T(1024)S(1)}, u32[]{:S(2)}, u32[]{:S(2)}) collective-permute-start(f32[768]{0:T(1024)S(1)} %reshape.612), channel_id=1, source_target_pairs={{0,16},{16,32},{32,48},{48,64},{64,80},{80,96},{96,112},{112,128},... | collective-permute-start | bytes 9224 | tf_op jit(solution)/shard_map/ppermute | solution.py:282
  35.7 2.7 %collective-permute-done.4 = f32[768]{0:T(1024)S(1)} collective-permute-done((f32[768]{0:T(1024)S(1)}, f32[768]{0:T(1024)S(1)}, u32[]{:S(2)}, u32[]{:S(2)}) %collective-permute-start.4) | collective-permute-done | bytes 3104 | tf_op jit(solution)/shard_map/ppermute | solution.py:282
  38.7 2.4 %collective-permute-start.7 = (f32[54]{0:T(128)S(1)}, f32[54]{0:T(128)S(1)}, u32[]{:S(2)}, u32[]{:S(2)}) collective-permute-start(f32[54]{0:T(128)S(1)} %reshape.618), channel_id=1, source_target_pairs={{4,0},{8,4},{12,8},{5,1},{9,5},{13,9},{6,2},{10,6},{14,10},{7,3},{... | collective-permute-start | bytes 656 | tf_op jit(solution)/shard_map/ppermute | solution.py:282
  41.1 1.3 %collective-permute-start.6 = (f32[54]{0:T(128)S(1)}, f32[54]{0:T(128)S(1)}, u32[]{:S(2)}, u32[]{:S(2)}) collective-permute-start(f32[54]{0:T(128)S(1)} %reshape.616), channel_id=1, source_target_pairs={{0,4},{4,8},{8,12},{1,5},{5,9},{9,13},{2,6},{6,10},{10,14},{3,7},{... | collective-permute-start | bytes 656 | tf_op jit(solution)/shard_map/ppermute | solution.py:282
  42.4 0.6 pad_convert_fusion
  43.2 3.4 %collective-permute-done.6 = f32[54]{0:T(128)S(1)} collective-permute-done((f32[54]{0:T(128)S(1)}, f32[54]{0:T(128)S(1)}, u32[]{:S(2)}, u32[]{:S(2)}) %collective-permute-start.6) | collective-permute-done | bytes 248 | tf_op jit(solution)/shard_map/ppermute | solution.py:282
  47.2 0.9 %select_maximum_fusion.fld_ref = f32[4,5,24,384]{3,2,1,0:T(8,128)} fusion(f32[2,5,18,258]{3,2,1,0:T(8,128)S(1)} %get-tuple-element.29, f32[2,5,18,258]{3,2,1,0:T(8,128)S(1)} %get-tuple-element.28), kind=kLoop, calls=%fused_computation.15 | loop fusion | flops 1474560 | bytes 1108800 | tf_op jit(solution)/shard_map/concatenate | solution.py:356
  48.1 8.0 %shard_map.122 = (f32[3,3,16,256]{3,2,1,0:T(8,128)}, f32[2,16,256]{2,1,0:T(8,128)}) custom-call(f32[4,5,24,384]{3,2,1,0:T(8,128)} %select_maximum_fusion.fld_ref, f32[24,384]{1,0:T(8,128)} %get-tuple-element.59.main_ref, f32[24,384]{1,0:T(8,128)} %get-tuple-element.58.weight_ref, f32[18,18]{1,0:T(8,128)} %kmat_ref.3, f32[2]{0:T(128)} %add_convert_fusion.live_ref, ...), custom_call_target="tpu_custom_call" | custom-call | tf_op jit(solution)/shard_map/pallas_call | solution.py:121
  56.1 1.5 %fusion.14 = f32[2,1152]{1,0:T(2,128)S(1)} fusion(f32[2,16,256]{2,1,0:T(8,128)} %get-tuple-element.6, s32[1152]{0:T(1024)S(1)} %get-tuple-element.55, pred[16,1152]{1,0:T(8,128)(4,1)S(1)} %convert_compare_fusion.1), kind=kOutput, calls=%fused_computation.12 | convolution fusion | flops 113612544 | bytes 65024 | tf_op jit(solution)/shard_map/krc,sc->krs/dot_general | solution.py:158
  57.6 0.6 broadcast_in_dim.104
  58.2 4.8 %all-to-all-start.1 = ((f32[4,2,9,128]{3,1,2,0:T(2,128)}), f32[4,2,9,128]{3,1,2,0:T(2,128)S(1)}, u32[]{:S(2)}, u32[]{:S(2)}) async-start(f32[4,2,9,128]{3,1,2,0:T(2,128)} %broadcast_in_dim.104), calls=%async_computation.1 | async-start | bytes 73728 | tf_op jit(solution)/shard_map/all_to_all | solution.py:170
  63.2 5.6 %shard_map.123 = f32[3,3,16,256]{3,2,1,0:T(8,128)} custom-call(f32[4,5,24,384]{3,2,1,0:T(8,128)} %select_maximum_fusion.fld_ref, f32[24,384]{1,0:T(8,128)} %get-tuple-element.59.main_ref, f32[24,384]{1,0:T(8,128)} %get-tuple-element.58.weight_ref, f32[18,18]{1,0:T(8,128)} %kmat_ref.3, f32[2]{0:T(128)} %add_convert_fusion.live_ref, ...), custom_call_target="tpu_custom_call" | custom-call | tf_op jit(solution)/shard_map/pallas_call | solution.py:136
  68.9 1.9 %collective-permute-start.9 = (f32[768]{0:T(1024)S(1)}, f32[768]{0:T(1024)S(1)}, u32[]{:S(2)}, u32[]{:S(2)}) collective-permute-start(f32[768]{0:T(1024)S(1)} %reshape.626), channel_id=1, source_target_pairs={{16,0},{32,16},{48,32},{64,48},{80,64},{96,80},{112,96},{128,112},... | collective-permute-start | bytes 9224 | tf_op jit(solution)/shard_map/ppermute | solution.py:282
  70.8 2.4 %collective-permute-start.8 = (f32[768]{0:T(1024)S(1)}, f32[768]{0:T(1024)S(1)}, u32[]{:S(2)}, u32[]{:S(2)}) collective-permute-start(f32[768]{0:T(1024)S(1)} %reshape.624), channel_id=1, source_target_pairs={{0,16},{16,32},{32,48},{48,64},{64,80},{80,96},{96,112},{112,128},... | collective-permute-start | bytes 9224 | tf_op jit(solution)/shard_map/ppermute | solution.py:282
  73.5 3.5 %collective-permute-done.8 = f32[768]{0:T(1024)S(1)} collective-permute-done((f32[768]{0:T(1024)S(1)}, f32[768]{0:T(1024)S(1)}, u32[]{:S(2)}, u32[]{:S(2)}) %collective-permute-start.8) | collective-permute-done | bytes 3104 | tf_op jit(solution)/shard_map/ppermute | solution.py:282
  77.0 2.4 %collective-permute-start.11 = (f32[1280]{0:T(1024)S(1)}, f32[1280]{0:T(1024)S(1)}, u32[]{:S(2)}, u32[]{:S(2)}) collective-permute-start(f32[1280]{0:T(1024)S(1)} %reshape.630), channel_id=1, source_target_pairs={{4,0},{8,4},{12,8},{5,1},{9,5},{13,9},{6,2},{10,6},{14,10},{7,3},{... | collective-permute-start | bytes 15368 | tf_op jit(solution)/shard_map/ppermute | solution.py:282
  79.4 1.3 %collective-permute-start.10 = (f32[1280]{0:T(1024)S(1)}, f32[1280]{0:T(1024)S(1)}, u32[]{:S(2)}, u32[]{:S(2)}) collective-permute-start(f32[1280]{0:T(1024)S(1)} %reshape.628), channel_id=1, source_target_pairs={{0,4},{4,8},{8,12},{1,5},{5,9},{9,13},{2,6},{6,10},{10,14},{3,7},{... | collective-permute-start | bytes 15368 | tf_op jit(solution)/shard_map/ppermute | solution.py:282
  80.9 4.0 %collective-permute-done.10 = f32[1280]{0:T(1024)S(1)} collective-permute-done((f32[1280]{0:T(1024)S(1)}, f32[1280]{0:T(1024)S(1)}, u32[]{:S(2)}, u32[]{:S(2)}) %collective-permute-start.10) | collective-permute-done | bytes 5152 | tf_op jit(solution)/shard_map/ppermute | solution.py:282
  85.0 1.3 %fusion.11 = f32[2,64,256]{2,1,0:T(8,128)} fusion(s32[1152]{0:T(1024)S(1)} %get-tuple-element.57, f32[2,1152]{1,0:T(2,128)S(1)} %bitcast.185, f32[1152,64]{0,1:T(8,128)S(1)} %fusion.27, f32[1,64,256]{2,1,0:T(8,128)S(1)} %fusion.42, f32[1,64,256]{2,1,0:T(8,128)S(1)} %fusion.48), kind=kOutput, calls=%fused_computation.11 | convolution fusion | flops 453492736 | bytes 570880 | tf_op jit(solution)/shard_map/ksr,sc->krc/dot_general | solution.py:164
  (135 shorter events, 6.1 us)
Async XLA Ops:
  0.6 2.6 %copy-start.6 = (s32[16,256]{1,0:T(8,128)S(1)}, s32[16,256]{1,0:T(8,128)}, u32[]{:S(2)}) copy-start(s32[16,256]{1,0:T(8,128)} %param.18) | copy-start | bytes 49156
  0.6 2.6 %copy-start.2 = (f32[3,16,256]{2,1,0:T(8,128)S(1)}, f32[3,16,256]{2,1,0:T(8,128)}, u32[]{:S(2)}) copy-start(f32[3,16,256]{2,1,0:T(8,128)} %param.16) | copy-start | bytes 147460
  0.7 2.6 %copy-start = (f32[3,3,16,256]{3,2,1,0:T(8,128)S(1)}, f32[3,3,16,256]{3,2,1,0:T(8,128)}, u32[]{:S(2)}) copy-start(f32[3,3,16,256]{3,2,1,0:T(8,128)} %param.15) | copy-start | bytes 442372
  1.4 2.0 %copy-start.1 = (f32[2,64,256]{2,1,0:T(8,128)S(1)}, f32[2,64,256]{2,1,0:T(8,128)}, u32[]{:S(2)}) copy-start(f32[2,64,256]{2,1,0:T(8,128)} %param.11) | copy-start | bytes 393220
  1.4 2.0 %copy-start.3 = (f32[64,256]{1,0:T(8,128)S(1)}, f32[64,256]{1,0:T(8,128)}, u32[]{:S(2)}) copy-start(f32[64,256]{1,0:T(8,128)} %param.12) | copy-start | bytes 196612
  1.5 7.5 %copy-start.7 = (s32[1,9,128]{2,0,1:T(1,128)S(1)}, s32[1,9,128]{2,0,1:T(1,128)}, u32[]{:S(2)}) copy-start(s32[1,9,128]{2,0,1:T(1,128)} %param.20) | copy-start | bytes 13828
  3.5 6.2 %collective-permute-start.1 = (f32[4864]{0:T(1024)S(1)}, f32[4864]{0:T(1024)S(1)}, u32[]{:S(2)}, u32[]{:S(2)}) collective-permute-start(f32[4864]{0:T(1024)S(1)} %pad_maximum_fusion.25), channel_id=1, source_target_pairs={{16,0},{32,16},{48,32},{64,48},{80,64},{96,80},{112,96},{128,112},... | collective-permute-start | bytes 58376 | tf_op jit(solution)/shard_map/ppermute | solution.py:282
  7.1 6.3 %collective-permute-start = (f32[4864]{0:T(1024)S(1)}, f32[4864]{0:T(1024)S(1)}, u32[]{:S(2)}, u32[]{:S(2)}) collective-permute-start(f32[4864]{0:T(1024)S(1)} %pad_maximum_fusion.24), channel_id=1, source_target_pairs={{0,16},{16,32},{32,48},{48,64},{64,80},{80,96},{96,112},{112,128},... | collective-permute-start | bytes 58376 | tf_op jit(solution)/shard_map/ppermute | solution.py:282
  14.4 4.8 %collective-permute-start.3 = (f32[1712]{0:T(1024)S(1)}, f32[1712]{0:T(1024)S(1)}, u32[]{:S(2)}, u32[]{:S(2)}) collective-permute-start(f32[1712]{0:T(1024)S(1)} %concatenate.71), channel_id=1, source_target_pairs={{4,0},{8,4},{12,8},{5,1},{9,5},{13,9},{6,2},{10,6},{14,10},{7,3},{... | collective-permute-start | bytes 20552 | tf_op jit(solution)/shard_map/ppermute | solution.py:282
  17.3 5.5 %collective-permute-start.2 = (f32[1712]{0:T(1024)S(1)}, f32[1712]{0:T(1024)S(1)}, u32[]{:S(2)}, u32[]{:S(2)}) collective-permute-start(f32[1712]{0:T(1024)S(1)} %concatenate.70), channel_id=1, source_target_pairs={{0,4},{4,8},{8,12},{1,5},{5,9},{9,13},{2,6},{6,10},{10,14},{3,7},{... | collective-permute-start | bytes 20552 | tf_op jit(solution)/shard_map/ppermute | solution.py:282
  24.5 22.5 %all-to-all-start = ((f32[4,4,18,258]{3,1,2,0:T(4,128)}), f32[4,4,18,258]{3,1,2,0:T(4,128)S(1)}, u32[]{:S(2)}, u32[]{:S(2)}) async-start(f32[4,4,18,258]{3,1,2,0:T(4,128)} %copy.70), calls=%async_computation | async-start | bytes 884736 | tf_op jit(solution)/shard_map/all_to_all | solution.py:184
  30.3 5.4 %collective-permute-start.5 = (f32[768]{0:T(1024)S(1)}, f32[768]{0:T(1024)S(1)}, u32[]{:S(2)}, u32[]{:S(2)}) collective-permute-start(f32[768]{0:T(1024)S(1)} %reshape.614), channel_id=1, source_target_pairs={{16,0},{32,16},{48,32},{64,48},{80,64},{96,80},{112,96},{128,112},... | collective-permute-start | bytes 9224 | tf_op jit(solution)/shard_map/ppermute | solution.py:282
  32.3 6.1 %collective-permute-start.4 = (f32[768]{0:T(1024)S(1)}, f32[768]{0:T(1024)S(1)}, u32[]{:S(2)}, u32[]{:S(2)}) collective-permute-start(f32[768]{0:T(1024)S(1)} %reshape.612), channel_id=1, source_target_pairs={{0,16},{16,32},{32,48},{48,64},{64,80},{80,96},{96,112},{112,128},... | collective-permute-start | bytes 9224 | tf_op jit(solution)/shard_map/ppermute | solution.py:282
  38.7 4.4 %collective-permute-start.7 = (f32[54]{0:T(128)S(1)}, f32[54]{0:T(128)S(1)}, u32[]{:S(2)}, u32[]{:S(2)}) collective-permute-start(f32[54]{0:T(128)S(1)} %reshape.618), channel_id=1, source_target_pairs={{4,0},{8,4},{12,8},{5,1},{9,5},{13,9},{6,2},{10,6},{14,10},{7,3},{... | collective-permute-start | bytes 656 | tf_op jit(solution)/shard_map/ppermute | solution.py:282
  41.1 5.4 %collective-permute-start.6 = (f32[54]{0:T(128)S(1)}, f32[54]{0:T(128)S(1)}, u32[]{:S(2)}, u32[]{:S(2)}) collective-permute-start(f32[54]{0:T(128)S(1)} %reshape.616), channel_id=1, source_target_pairs={{0,4},{4,8},{8,12},{1,5},{5,9},{9,13},{2,6},{6,10},{10,14},{3,7},{... | collective-permute-start | bytes 656 | tf_op jit(solution)/shard_map/ppermute | solution.py:282
  58.2 10.6 %all-to-all-start.1 = ((f32[4,2,9,128]{3,1,2,0:T(2,128)}), f32[4,2,9,128]{3,1,2,0:T(2,128)S(1)}, u32[]{:S(2)}, u32[]{:S(2)}) async-start(f32[4,2,9,128]{3,1,2,0:T(2,128)} %broadcast_in_dim.104), calls=%async_computation.1 | async-start | bytes 73728 | tf_op jit(solution)/shard_map/all_to_all | solution.py:170
  63.2 10.0 %copy-start.4 = (f32[64,256]{1,0:T(8,128)S(1)}, f32[64,256]{1,0:T(8,128)}, u32[]{:S(2)}) copy-start(f32[64,256]{1,0:T(8,128)} %param.13) | copy-start | bytes 196612
  63.2 10.0 %copy-start.5 = (f32[2,64,256]{2,1,0:T(8,128)S(1)}, f32[2,64,256]{2,1,0:T(8,128)}, u32[]{:S(2)}) copy-start(f32[2,64,256]{2,1,0:T(8,128)} %param.14) | copy-start | bytes 393220
  68.9 4.6 %collective-permute-start.9 = (f32[768]{0:T(1024)S(1)}, f32[768]{0:T(1024)S(1)}, u32[]{:S(2)}, u32[]{:S(2)}) collective-permute-start(f32[768]{0:T(1024)S(1)} %reshape.626), channel_id=1, source_target_pairs={{16,0},{32,16},{48,32},{64,48},{80,64},{96,80},{112,96},{128,112},... | collective-permute-start | bytes 9224 | tf_op jit(solution)/shard_map/ppermute | solution.py:282
  70.8 6.1 %collective-permute-start.8 = (f32[768]{0:T(1024)S(1)}, f32[768]{0:T(1024)S(1)}, u32[]{:S(2)}, u32[]{:S(2)}) collective-permute-start(f32[768]{0:T(1024)S(1)} %reshape.624), channel_id=1, source_target_pairs={{0,16},{16,32},{32,48},{48,64},{64,80},{80,96},{96,112},{112,128},... | collective-permute-start | bytes 9224 | tf_op jit(solution)/shard_map/ppermute | solution.py:282
  77.0 3.9 %collective-permute-start.11 = (f32[1280]{0:T(1024)S(1)}, f32[1280]{0:T(1024)S(1)}, u32[]{:S(2)}, u32[]{:S(2)}) collective-permute-start(f32[1280]{0:T(1024)S(1)} %reshape.630), channel_id=1, source_target_pairs={{4,0},{8,4},{12,8},{5,1},{9,5},{13,9},{6,2},{10,6},{14,10},{7,3},{... | collective-permute-start | bytes 15368 | tf_op jit(solution)/shard_map/ppermute | solution.py:282
  79.4 5.5 %collective-permute-start.10 = (f32[1280]{0:T(1024)S(1)}, f32[1280]{0:T(1024)S(1)}, u32[]{:S(2)}, u32[]{:S(2)}) collective-permute-start(f32[1280]{0:T(1024)S(1)} %reshape.628), channel_id=1, source_target_pairs={{0,4},{4,8},{8,12},{1,5},{5,9},{9,13},{2,6},{6,10},{10,14},{3,7},{... | collective-permute-start | bytes 15368 | tf_op jit(solution)/shard_map/ppermute | solution.py:282

commit v10 on v9

--- a/solution.py
+++ b/solution.py
@@ -1,3 +1,5 @@
+import functools
+
 import jax
 import jax.numpy as jnp
 from jax import lax
@@ -8,20 +10,35 @@
 ROWS_PAD, LANES_PAD = 24, 384
 
 
-def fem_body(comps, fld_ref, main_ref, weight_ref, kmat_ref, live_ref, body_ref, out_ref, vals_ref, vis_ref, resp_ref):
-    main = main_ref[...] > 0.5
-    weight = weight_ref[...]
+def cell_weight(grid):
+    block_x, block_y, count_x, count_y = grid
+    rows = lax.broadcasted_iota(jnp.int32, (ROWS_PAD, LANES_PAD), 0)
+    lanes = lax.broadcasted_iota(jnp.int32, (ROWS_PAD, LANES_PAD), 1)
+    global_x = lax.axis_index("mx") * block_x + rows - 1
+    global_y = lax.axis_index("my") * block_y + lanes - 1
+    valid = (global_x >= 0) & (global_x <= count_x * block_x - 2) & (rows <= block_x)
+    valid = valid & (global_y >= 0) & (global_y <= count_y * block_y - 2) & (lanes <= block_y)
+    return valid.astype(jnp.float32)
+
+
+def fem_body(comps, grid, fld_ref, kmat_ref, body_ref, out_ref, vals_ref, vis_ref, resp_ref):
+    layers = (fld_ref.shape[0] - 1) // 4
+    main = fld_ref[4 * layers] == 0.0
+    weight = cell_weight(grid)
+    layer_index = lax.axis_index("layer")
+    below_live = (layer_index > 0).astype(jnp.float32)
+    above_live = (layer_index < lax.axis_size("layer") - 1).astype(jnp.float32)
     zero = jnp.zeros((ROWS_PAD, LANES_PAD), jnp.float32)
     for comp in comps:
         out_ref[comp] = -body_ref[comp]
     rows_out = [height * 9 + comp * 3 + vertex for height in range(2) for comp in comps for vertex in range(3)]
-    pairs = fld_ref.shape[1] - 1
+    pairs = layers - 1
     for pair in range(pairs):
         vis_parts = [[], []]
         for height in range(2):
             layer = pair + height
             for comp in range(4):
-                plane = fld_ref[comp, layer]
+                plane = fld_ref[comp * layers + layer]
                 below = pltpu.roll(plane, ROWS_PAD - 1, 0)
                 right = pltpu.roll(plane, LANES_PAD - 1, 1)
                 diag = pltpu.roll(below, LANES_PAD - 1, 1)
@@ -62,9 +79,9 @@
                 continue
             scale = None
             if pair == 0 and height == 1:
-                scale = live_ref[0]
+                scale = below_live
             if pair == pairs - 1 and height == 0:
-                scale = live_ref[1]
+                scale = above_live
             for comp in comps:
                 base = height * 9 + comp * 3
                 one = [resp_ref[0, base + v] for v in range(3)]
@@ -82,8 +99,8 @@
                 out_ref[comp, own_layer] = out_ref[comp, own_layer] + part
 
 
-def fem_horizontal(fld_ref, main_ref, weight_ref, kmat_ref, live_ref, body_ref, out_ref, depth_ref, vals_ref, vis_ref, resp_ref):
-    fem_body((0, 1), fld_ref, main_ref, weight_ref, kmat_ref, live_ref, body_ref, out_ref, vals_ref, vis_ref, resp_ref)
+def fem_horizontal(grid, fld_ref, kmat_ref, body_ref, out_ref, depth_ref, vals_ref, vis_ref, resp_ref):
+    fem_body((0, 1), grid, fld_ref, kmat_ref, body_ref, out_ref, vals_ref, vis_ref, resp_ref)
     for comp in range(2):
         total = out_ref[comp, 0]
         for layer in range(1, out_ref.shape[1]):
@@ -91,19 +108,15 @@
         depth_ref[comp] = total
 
 
-def fem_vertical(fld_ref, main_ref, weight_ref, kmat_ref, live_ref, body_ref, prev_ref, out_ref, vals_ref, vis_ref, resp_ref):
+def fem_vertical(grid, fld_ref, kmat_ref, body_ref, prev_ref, out_ref, vals_ref, vis_ref, resp_ref):
     out_ref[0:2] = prev_ref[0:2]
-    fem_body((2,), fld_ref, main_ref, weight_ref, kmat_ref, live_ref, body_ref, out_ref, vals_ref, vis_ref, resp_ref)
-
-
-def fem_inputs(extended_layers, flag_cells, weight, below_live, above_live):
+    fem_body((2,), grid, fld_ref, kmat_ref, body_ref, out_ref, vals_ref, vis_ref, resp_ref)
+
+
+def fem_inputs(extended_layers, diag_ext):
     comps, layers, rows, lanes = extended_layers.shape
-    fld = jnp.pad(extended_layers, ((0, 0), (0, 0), (0, ROWS_PAD - rows), (0, LANES_PAD - lanes)))
-    cell_rows, cell_lanes = flag_cells.shape
-    main = jnp.pad((flag_cells == 0).astype(jnp.float32), ((0, ROWS_PAD - cell_rows), (0, LANES_PAD - cell_lanes)))
-    wpad = jnp.pad(weight, ((0, ROWS_PAD - cell_rows), (0, LANES_PAD - cell_lanes)))
-    live = jnp.stack([below_live, above_live]).astype(jnp.float32)
-    return fld, main, wpad, live
+    planes = jnp.concatenate([extended_layers.reshape(comps * layers, rows, lanes), diag_ext[None]], 0)
+    return jnp.pad(planes, ((0, 0), (0, ROWS_PAD - rows), (0, LANES_PAD - lanes)))
 
 
 def fem_scratch():
@@ -114,32 +127,32 @@
     ]
 
 
-def fem_first(fld, main, wpad, element_matrix, live, body_force):
+def fem_first(grid, fld, element_matrix, body_force):
     vmem = pl.BlockSpec(memory_space=pltpu.VMEM)
     smem = pl.BlockSpec(memory_space=pltpu.SMEM)
     depth_shape = (2,) + body_force.shape[2:]
     return pl.pallas_call(
-        fem_horizontal,
+        functools.partial(fem_horizontal, grid),
         out_shape=(
             jax.ShapeDtypeStruct(body_force.shape, jnp.float32),
             jax.ShapeDtypeStruct(depth_shape, jnp.float32),
         ),
-        in_specs=[vmem, vmem, vmem, smem, smem, vmem],
+        in_specs=[vmem, smem, vmem],
         out_specs=(vmem, vmem),
         scratch_shapes=fem_scratch(),
-    )(fld, main, wpad, element_matrix, live, body_force)
-
-
-def fem_second(fld, main, wpad, element_matrix, live, body_force, previous):
+    )(fld, element_matrix, body_force)
+
+
+def fem_second(grid, fld, element_matrix, body_force, previous):
     vmem = pl.BlockSpec(memory_space=pltpu.VMEM)
     smem = pl.BlockSpec(memory_space=pltpu.SMEM)
     return pl.pallas_call(
-        fem_vertical,
+        functools.partial(fem_vertical, grid),
         out_shape=jax.ShapeDtypeStruct(body_force.shape, jnp.float32),
-        in_specs=[vmem, vmem, vmem, smem, smem, vmem, vmem],
+        in_specs=[vmem, smem, vmem, vmem],
         out_specs=vmem,
         scratch_shapes=fem_scratch(),
-    )(fld, main, wpad, element_matrix, live, body_force, previous)
+    )(fld, element_matrix, body_force, previous)
 
 
 HIGH = lax.Precision.HIGHEST
@@ -346,7 +359,6 @@
     marked = jnp.einsum("sr,sc->rc", col_row, col_col)
     ring = jnp.concatenate([jnp.minimum(marked, 1.0)[None], placed], 0)
     field_ext = widened[:-1].reshape(4, depth_count, block_x + 2, block_y + 2)
-    flag_cells = widened[-1, :-1, :-1]
     below_raw, above_raw = layer_neighbours(field_ext[:, -1], field_ext[:, 0])
     (ring_x,) = packed_halo((ring,), (1,), "mx")
     (ring_ext,) = packed_halo((ring_x,), (2,), "my")
@@ -354,22 +366,10 @@
     all_layers = jnp.concatenate([below_raw[:, None], field_ext, above_raw[:, None]], 1)
     uv_ext = jnp.where(imposed_at[None, None], ring_ext[1:3, None], all_layers[:2])
     extended_layers = jnp.concatenate([uv_ext, all_layers[2:]], 0)
-    count_x = lax.axis_size("mx")
-    count_y = lax.axis_size("my")
-    place_x = lax.axis_index("mx")
-    place_y = lax.axis_index("my")
-    global_x = place_x * block_x + jnp.arange(block_x + 1, dtype=jnp.int32) - 1
-    global_y = place_y * block_y + jnp.arange(block_y + 1, dtype=jnp.int32) - 1
-    valid_x = (global_x >= 0) & (global_x <= count_x * block_x - 2)
-    valid_y = (global_y >= 0) & (global_y <= count_y * block_y - 2)
-    weight = (valid_x[:, None] & valid_y[None, :]).astype(jnp.float32)
-    layer_index = lax.axis_index("layer")
-    layer_count = lax.axis_size("layer")
-    below_live = (layer_index > 0).astype(jnp.float32)
-    above_live = (layer_index < layer_count - 1).astype(jnp.float32)
-    fld, main, wpad, live = fem_inputs(extended_layers, flag_cells, weight, below_live, above_live)
-    partial_residual, depth_sum = fem_first(fld, main, wpad, element_matrix, live, body_force)
-    stokes_residual = fem_second(fld, main, wpad, element_matrix, live, body_force, partial_residual)
+    grid = (block_x, block_y, lax.axis_size("mx"), lax.axis_size("my"))
+    fld = fem_inputs(extended_layers, widened[-1])
+    partial_residual, depth_sum = fem_first(grid, fld, element_matrix, body_force)
+    stokes_residual = fem_second(grid, fld, element_matrix, body_force, partial_residual)
     bucket = gather_slots(depth_sum, col_row, col_col).reshape(2, 9, slot_count)
     depth_total = layer_total(bucket)
     depth_total, stokes_residual = lax.optimization_barrier((depth_total, stokes_residual))

time: 87 us -> 87.2 us (level)
  waiting for transfers between devices: 20.7 us -> 22.1 us
  other arithmetic: 5.41 us -> 4.12 us
    ppermute x6, waiting for transfers between devices: 20.7 us -> 22.1 us  [exchange(): lax.ppermute(sent_up, axis, up)]
    pad x0 -> x1, local copies, waits for them, and re-layouts: none -> 0.93 us  [fem_inputs(): jnp.pad(planes, ((0, 0), (0, ROWS_PAD - rows), (0, LANES_PAD - lanes)))]
    concatenate x1, other arithmetic: 0.95 us -> 0.06 us  [per_device(): extended_layers = jnp.concatenate([uv_ext, all_layers[2:]], 0)]
    concatenate x1 -> x0, local copies, waits for them, and re-layouts: 0.89 us -> none  [layer_neighbours(): jnp.concatenate(chunks, 0)]
  transfers between devices with their start and end apart: 14 -> 14, of which waited for: 6 -> 6; matrix products, arithmetic and copies ran while one was open for 7% -> 5% of each run, Pallas kernels for 6% -> 6%
where the time goes in v10:
time: 87.2 us; the launch traced here: 86.5 us
  starting transfers between devices  35 us (40%)
  waiting for transfers between devices  22.1 us (25%)
  Pallas kernels  13.6 us (16%)
  matrix products  5.36 us (6%)
  local copies, waits for them, and re-layouts  4.93 us (6%)
  other arithmetic  4.12 us (5%)
  between operations  1.44 us (2%)
    ppermute x6, waiting for transfers between devices, exchange(): lax.ppermute(sent_up, axis, up)  22.1 us
    ppermute x6, starting transfers between devices, exchange(): lax.ppermute(sent_down, axis, down)  14.8 us
    ppermute x6, starting transfers between devices, exchange(): lax.ppermute(sent_up, axis, up)  10.6 us
    pallas_call x1, Pallas kernels, fem_first(): pl.pallas_call(functools.partial(fem_horizontal, grid), out_shape=(jax.Sh...  8 us
    pallas_call x1, Pallas kernels, fem_second(): pl.pallas_call(functools.partial(fem_vertical, grid), out_shape=jax.Shape...  5.58 us
    all_to_all x1, starting transfers between devices, layer_neighbours(): lax.all_to_all(jnp.concatenate(chunks, 0), 'layer', 0, 0, tiled=True)  4.83 us
    all_to_all x1, starting transfers between devices, layer_total(): gathered = lax.all_to_all(copies, 'layer', 0, 0, tiled=True)  4.8 us
    dot_general x2, matrix products, gather_slots(): cols_taken = jnp.einsum('krc,sc->krs', field, pick_col, precision=HIGH)  3.15 us
  transfers between devices with their start and end apart: 14, of which 6 were waited for; matrix products, arithmetic and copies ran while one was open for 5% of the time, Pallas kernels for 6%

profile of v10, /device:TPU:410, one launch (start us, length us, event | category | flops | bytes accessed | tf_op | source)
XLA Modules:
  0.0 86.5 jit_solution(7007405094216791979)
XLA Ops:
  0.7 0.8 reduce.2
  1.6 1.7 %fusion.1 = f32[2,1152]{1,0:T(2,128)S(1)} fusion(f32[2,64,256]{2,1,0:T(8,128)} %param.11, s32[1152]{0:T(1024)S(1)} %get-tuple-element.56, pred[64,1152]{1,0:T(8,128)(4,1)S(1)} %convert_compare_fusion), kind=kOutput, calls=%fused_computation.3 | convolution fusion | flops 453572352 | bytes 218624 | tf_op jit(solution)/shard_map/krc,sc->krs/dot_general | solution.py:171
  3.5 3.6 %collective-permute-start.1 = (f32[4864]{0:T(1024)S(1)}, f32[4864]{0:T(1024)S(1)}, u32[]{:S(2)}, u32[]{:S(2)}) collective-permute-start(f32[4864]{0:T(1024)S(1)} %pad_maximum_fusion.16), channel_id=1, source_target_pairs={{16,0},{32,16},{48,32},{64,48},{80,64},{96,80},{112,96},{128,112},... | collective-permute-start | bytes 58376 | tf_op jit(solution)/shard_map/ppermute | solution.py:295
  7.1 1.9 %collective-permute-start = (f32[4864]{0:T(1024)S(1)}, f32[4864]{0:T(1024)S(1)}, u32[]{:S(2)}, u32[]{:S(2)}) collective-permute-start(f32[4864]{0:T(1024)S(1)} %pad_maximum_fusion.15), channel_id=1, source_target_pairs={{0,16},{16,32},{32,48},{48,64},{64,80},{80,96},{96,112},{112,128},... | collective-permute-start | bytes 58376 | tf_op jit(solution)/shard_map/ppermute | solution.py:295
  9.2 4.2 %collective-permute-done = f32[4864]{0:T(1024)S(1)} collective-permute-done((f32[4864]{0:T(1024)S(1)}, f32[4864]{0:T(1024)S(1)}, u32[]{:S(2)}, u32[]{:S(2)}) %collective-permute-start) | collective-permute-done | bytes 19488 | tf_op jit(solution)/shard_map/ppermute | solution.py:295
  14.5 2.6 %collective-permute-start.3 = (f32[1712]{0:T(1024)S(1)}, f32[1712]{0:T(1024)S(1)}, u32[]{:S(2)}, u32[]{:S(2)}) collective-permute-start(f32[1712]{0:T(1024)S(1)} %concatenate.71), channel_id=1, source_target_pairs={{4,0},{8,4},{12,8},{5,1},{9,5},{13,9},{6,2},{10,6},{14,10},{7,3},{... | collective-permute-start | bytes 20552 | tf_op jit(solution)/shard_map/ppermute | solution.py:295
  17.4 1.3 %collective-permute-start.2 = (f32[1712]{0:T(1024)S(1)}, f32[1712]{0:T(1024)S(1)}, u32[]{:S(2)}, u32[]{:S(2)}) collective-permute-start(f32[1712]{0:T(1024)S(1)} %concatenate.70), channel_id=1, source_target_pairs={{0,4},{4,8},{8,12},{1,5},{5,9},{9,13},{2,6},{6,10},{10,14},{3,7},{... | collective-permute-start | bytes 20552 | tf_op jit(solution)/shard_map/ppermute | solution.py:295
  18.6 0.3 fusion.18
  19.3 3.6 %collective-permute-done.2 = f32[1712]{0:T(1024)S(1)} collective-permute-done((f32[1712]{0:T(1024)S(1)}, f32[1712]{0:T(1024)S(1)}, u32[]{:S(2)}, u32[]{:S(2)}) %collective-permute-start.2) | collective-permute-done | bytes 6880 | tf_op jit(solution)/shard_map/ppermute | solution.py:295
  23.2 0.3 pad_maximum_fusion.2
  23.7 0.9 %pad_maximum_fusion.3 = f32[4,4,18,258]{3,1,2,0:T(4,128)} fusion(f32[1,4,18,258]{3,1,2,0:T(4,128)S(1)} %get-tuple-element.40, f32[1,4,18,258]{3,1,2,0:T(4,128)S(1)} %get-tuple-element.39, f32[1,4,18,258]{3,1,2,0:T(4,128)S(1)} %get-tuple-element.38, f32[1,4,18,258]{3,1,2,0:T(4,128)S(1)} %get-tuple-element.37), kind=kLoop, calls=%fused_computation.36 | loop fusion | flops 222912 | bytes 594432 | tf_op jit(solution)/shard_map/concatenate | solution.py:197
  24.6 4.8 %all-to-all-start = ((f32[4,4,18,258]{3,1,2,0:T(4,128)}), f32[4,4,18,258]{3,1,2,0:T(4,128)S(1)}, u32[]{:S(2)}, u32[]{:S(2)}) async-start(f32[4,4,18,258]{3,1,2,0:T(4,128)} %pad_maximum_fusion.3), calls=%async_computation | async-start | bytes 884736 | tf_op jit(solution)/shard_map/all_to_all | solution.py:197
  29.9 0.5 fusion.5
  30.4 1.9 %collective-permute-start.5 = (f32[768]{0:T(1024)S(1)}, f32[768]{0:T(1024)S(1)}, u32[]{:S(2)}, u32[]{:S(2)}) collective-permute-start(f32[768]{0:T(1024)S(1)} %reshape.597), channel_id=1, source_target_pairs={{16,0},{32,16},{48,32},{64,48},{80,64},{96,80},{112,96},{128,112},... | collective-permute-start | bytes 9224 | tf_op jit(solution)/shard_map/ppermute | solution.py:295
  32.4 2.4 %collective-permute-start.4 = (f32[768]{0:T(1024)S(1)}, f32[768]{0:T(1024)S(1)}, u32[]{:S(2)}, u32[]{:S(2)}) collective-permute-start(f32[768]{0:T(1024)S(1)} %reshape.595), channel_id=1, source_target_pairs={{0,16},{16,32},{32,48},{48,64},{64,80},{80,96},{96,112},{112,128},... | collective-permute-start | bytes 9224 | tf_op jit(solution)/shard_map/ppermute | solution.py:295
  35.5 3.0 %collective-permute-done.4 = f32[768]{0:T(1024)S(1)} collective-permute-done((f32[768]{0:T(1024)S(1)}, f32[768]{0:T(1024)S(1)}, u32[]{:S(2)}, u32[]{:S(2)}) %collective-permute-start.4) | collective-permute-done | bytes 3104 | tf_op jit(solution)/shard_map/ppermute | solution.py:295
  38.8 2.4 %collective-permute-start.7 = (f32[54]{0:T(128)S(1)}, f32[54]{0:T(128)S(1)}, u32[]{:S(2)}, u32[]{:S(2)}) collective-permute-start(f32[54]{0:T(128)S(1)} %reshape.601), channel_id=1, source_target_pairs={{4,0},{8,4},{12,8},{5,1},{9,5},{13,9},{6,2},{10,6},{14,10},{7,3},{... | collective-permute-start | bytes 656 | tf_op jit(solution)/shard_map/ppermute | solution.py:295
  41.2 1.3 %collective-permute-start.6 = (f32[54]{0:T(128)S(1)}, f32[54]{0:T(128)S(1)}, u32[]{:S(2)}, u32[]{:S(2)}) collective-permute-start(f32[54]{0:T(128)S(1)} %reshape.599), channel_id=1, source_target_pairs={{0,4},{4,8},{8,12},{1,5},{5,9},{9,13},{2,6},{6,10},{10,14},{3,7},{... | collective-permute-start | bytes 656 | tf_op jit(solution)/shard_map/ppermute | solution.py:295
  42.9 3.7 %collective-permute-done.6 = f32[54]{0:T(128)S(1)} collective-permute-done((f32[54]{0:T(128)S(1)}, f32[54]{0:T(128)S(1)}, u32[]{:S(2)}, u32[]{:S(2)}) %collective-permute-start.6) | collective-permute-done | bytes 248 | tf_op jit(solution)/shard_map/ppermute | solution.py:295
  47.4 0.9 %pad.4.fld_ref = f32[21,24,384]{2,1,0:T(8,128)} pad(f32[21,18,258]{2,1,0:T(8,128)S(1)} %fusion.19, f32[]{:T(128)} %constant.67.clone.1), padding=0_0x0_6x0_126 | pad | bytes 1164244 | tf_op jit(solution)/shard_map/jit(_pad)/pad | solution.py:119
  48.4 8.0 %shard_map.122 = (f32[3,3,16,256]{3,2,1,0:T(8,128)}, f32[2,16,256]{2,1,0:T(8,128)}) custom-call(f32[21,24,384]{2,1,0:T(8,128)} %pad.4.fld_ref, f32[18,18]{1,0:T(8,128)} %kmat_ref.3, f32[3,3,16,256]{3,2,1,0:T(8,128)} %body_ref.3), custom_call_target="tpu_custom_call" | custom-call | tf_op jit(solution)/shard_map/pallas_call | solution.py:134
  56.4 1.5 %fusion.14 = f32[2,1152]{1,0:T(2,128)S(1)} fusion(f32[2,16,256]{2,1,0:T(8,128)} %get-tuple-element.6, s32[1152]{0:T(1024)S(1)} %get-tuple-element.54, pred[16,1152]{1,0:T(8,128)(4,1)S(1)} %convert_compare_fusion.1), kind=kOutput, calls=%fused_computation.12 | convolution fusion | flops 113612544 | bytes 65024 | tf_op jit(solution)/shard_map/krc,sc->krs/dot_general | solution.py:171
  57.8 0.6 broadcast_in_dim.102
  58.5 4.8 %all-to-all-start.1 = ((f32[4,2,9,128]{3,1,2,0:T(2,128)}), f32[4,2,9,128]{3,1,2,0:T(2,128)S(1)}, u32[]{:S(2)}, u32[]{:S(2)}) async-start(f32[4,2,9,128]{3,1,2,0:T(2,128)} %broadcast_in_dim.102), calls=%async_computation.1 | async-start | bytes 73728 | tf_op jit(solution)/shard_map/all_to_all | solution.py:183
  63.5 5.6 %shard_map.123 = f32[3,3,16,256]{3,2,1,0:T(8,128)} custom-call(f32[21,24,384]{2,1,0:T(8,128)} %pad.4.fld_ref, f32[18,18]{1,0:T(8,128)} %kmat_ref.3, f32[3,3,16,256]{3,2,1,0:T(8,128)} %body_ref.3, f32[3,3,16,256]{3,2,1,0:T(8,128)} %get-tuple-element.7.prev_ref), custom_call_target="tpu_custom_call" | custom-call | tf_op jit(solution)/shard_map/pallas_call | solution.py:149
  69.1 1.9 %collective-permute-start.9 = (f32[768]{0:T(1024)S(1)}, f32[768]{0:T(1024)S(1)}, u32[]{:S(2)}, u32[]{:S(2)}) collective-permute-start(f32[768]{0:T(1024)S(1)} %reshape.610), channel_id=1, source_target_pairs={{16,0},{32,16},{48,32},{64,48},{80,64},{96,80},{112,96},{128,112},... | collective-permute-start | bytes 9224 | tf_op jit(solution)/shard_map/ppermute | solution.py:295
  71.1 2.4 %collective-permute-start.8 = (f32[768]{0:T(1024)S(1)}, f32[768]{0:T(1024)S(1)}, u32[]{:S(2)}, u32[]{:S(2)}) collective-permute-start(f32[768]{0:T(1024)S(1)} %reshape.608), channel_id=1, source_target_pairs={{0,16},{16,32},{32,48},{48,64},{64,80},{80,96},{96,112},{112,128},... | collective-permute-start | bytes 9224 | tf_op jit(solution)/shard_map/ppermute | solution.py:295
  73.7 3.5 %collective-permute-done.8 = f32[768]{0:T(1024)S(1)} collective-permute-done((f32[768]{0:T(1024)S(1)}, f32[768]{0:T(1024)S(1)}, u32[]{:S(2)}, u32[]{:S(2)}) %collective-permute-start.8) | collective-permute-done | bytes 3104 | tf_op jit(solution)/shard_map/ppermute | solution.py:295
  77.2 2.4 %collective-permute-start.11 = (f32[1280]{0:T(1024)S(1)}, f32[1280]{0:T(1024)S(1)}, u32[]{:S(2)}, u32[]{:S(2)}) collective-permute-start(f32[1280]{0:T(1024)S(1)} %reshape.614), channel_id=1, source_target_pairs={{4,0},{8,4},{12,8},{5,1},{9,5},{13,9},{6,2},{10,6},{14,10},{7,3},{... | collective-permute-start | bytes 15368 | tf_op jit(solution)/shard_map/ppermute | solution.py:295
  79.6 1.3 %collective-permute-start.10 = (f32[1280]{0:T(1024)S(1)}, f32[1280]{0:T(1024)S(1)}, u32[]{:S(2)}, u32[]{:S(2)}) collective-permute-start(f32[1280]{0:T(1024)S(1)} %reshape.612), channel_id=1, source_target_pairs={{0,4},{4,8},{8,12},{1,5},{5,9},{9,13},{2,6},{6,10},{10,14},{3,7},{... | collective-permute-start | bytes 15368 | tf_op jit(solution)/shard_map/ppermute | solution.py:295
  81.1 4.0 %collective-permute-done.10 = f32[1280]{0:T(1024)S(1)} collective-permute-done((f32[1280]{0:T(1024)S(1)}, f32[1280]{0:T(1024)S(1)}, u32[]{:S(2)}, u32[]{:S(2)}) %collective-permute-start.10) | collective-permute-done | bytes 5152 | tf_op jit(solution)/shard_map/ppermute | solution.py:295
  85.2 1.3 %fusion.11 = f32[2,64,256]{2,1,0:T(8,128)} fusion(s32[1152]{0:T(1024)S(1)} %get-tuple-element.56, f32[2,1152]{1,0:T(2,128)S(1)} %bitcast.150, f32[1152,64]{0,1:T(8,128)S(1)} %fusion.36, f32[1,64,256]{2,1,0:T(8,128)S(1)} %fusion.44, f32[1,64,256]{2,1,0:T(8,128)S(1)} %fusion.50), kind=kOutput, calls=%fused_computation.11 | convolution fusion | flops 453492736 | bytes 570880 | tf_op jit(solution)/shard_map/ksr,sc->krc/dot_general | solution.py:177
  (132 shorter events, 5.5 us)
Async XLA Ops:
  0.6 2.8 %copy-start.1 = (f32[2,64,256]{2,1,0:T(8,128)S(1)}, f32[2,64,256]{2,1,0:T(8,128)}, u32[]{:S(2)}) copy-start(f32[2,64,256]{2,1,0:T(8,128)} %param.11) | copy-start | bytes 393220
  0.6 2.7 %copy-start.6 = (s32[16,256]{1,0:T(8,128)S(1)}, s32[16,256]{1,0:T(8,128)}, u32[]{:S(2)}) copy-start(s32[16,256]{1,0:T(8,128)} %param.18) | copy-start | bytes 49156
  0.7 2.7 %copy-start.2 = (f32[3,16,256]{2,1,0:T(8,128)S(1)}, f32[3,16,256]{2,1,0:T(8,128)}, u32[]{:S(2)}) copy-start(f32[3,16,256]{2,1,0:T(8,128)} %param.16) | copy-start | bytes 147460
  0.7 2.7 %copy-start = (f32[3,3,16,256]{3,2,1,0:T(8,128)S(1)}, f32[3,3,16,256]{3,2,1,0:T(8,128)}, u32[]{:S(2)}) copy-start(f32[3,3,16,256]{3,2,1,0:T(8,128)} %param.15) | copy-start | bytes 442372
  0.7 2.8 %copy-start.3 = (f32[64,256]{1,0:T(8,128)S(1)}, f32[64,256]{1,0:T(8,128)}, u32[]{:S(2)}) copy-start(f32[64,256]{1,0:T(8,128)} %param.12) | copy-start | bytes 196612
  1.6 7.5 %copy-start.7 = (s32[1,9,128]{2,0,1:T(1,128)S(1)}, s32[1,9,128]{2,0,1:T(1,128)}, u32[]{:S(2)}) copy-start(s32[1,9,128]{2,0,1:T(1,128)} %param.20) | copy-start | bytes 13828
  3.5 5.7 %collective-permute-start.1 = (f32[4864]{0:T(1024)S(1)}, f32[4864]{0:T(1024)S(1)}, u32[]{:S(2)}, u32[]{:S(2)}) collective-permute-start(f32[4864]{0:T(1024)S(1)} %pad_maximum_fusion.16), channel_id=1, source_target_pairs={{16,0},{32,16},{48,32},{64,48},{80,64},{96,80},{112,96},{128,112},... | collective-permute-start | bytes 58376 | tf_op jit(solution)/shard_map/ppermute | solution.py:295
  7.1 6.3 %collective-permute-start = (f32[4864]{0:T(1024)S(1)}, f32[4864]{0:T(1024)S(1)}, u32[]{:S(2)}, u32[]{:S(2)}) collective-permute-start(f32[4864]{0:T(1024)S(1)} %pad_maximum_fusion.15), channel_id=1, source_target_pairs={{0,16},{16,32},{32,48},{48,64},{64,80},{80,96},{96,112},{112,128},... | collective-permute-start | bytes 58376 | tf_op jit(solution)/shard_map/ppermute | solution.py:295
  14.5 4.5 %collective-permute-start.3 = (f32[1712]{0:T(1024)S(1)}, f32[1712]{0:T(1024)S(1)}, u32[]{:S(2)}, u32[]{:S(2)}) collective-permute-start(f32[1712]{0:T(1024)S(1)} %concatenate.71), channel_id=1, source_target_pairs={{4,0},{8,4},{12,8},{5,1},{9,5},{13,9},{6,2},{10,6},{14,10},{7,3},{... | collective-permute-start | bytes 20552 | tf_op jit(solution)/shard_map/ppermute | solution.py:295
  17.4 5.5 %collective-permute-start.2 = (f32[1712]{0:T(1024)S(1)}, f32[1712]{0:T(1024)S(1)}, u32[]{:S(2)}, u32[]{:S(2)}) collective-permute-start(f32[1712]{0:T(1024)S(1)} %concatenate.70), channel_id=1, source_target_pairs={{0,4},{4,8},{8,12},{1,5},{5,9},{9,13},{2,6},{6,10},{10,14},{3,7},{... | collective-permute-start | bytes 20552 | tf_op jit(solution)/shard_map/ppermute | solution.py:295
  24.6 22.5 %all-to-all-start = ((f32[4,4,18,258]{3,1,2,0:T(4,128)}), f32[4,4,18,258]{3,1,2,0:T(4,128)S(1)}, u32[]{:S(2)}, u32[]{:S(2)}) async-start(f32[4,4,18,258]{3,1,2,0:T(4,128)} %pad_maximum_fusion.3), calls=%async_computation | async-start | bytes 884736 | tf_op jit(solution)/shard_map/all_to_all | solution.py:197
  30.4 5.0 %collective-permute-start.5 = (f32[768]{0:T(1024)S(1)}, f32[768]{0:T(1024)S(1)}, u32[]{:S(2)}, u32[]{:S(2)}) collective-permute-start(f32[768]{0:T(1024)S(1)} %reshape.597), channel_id=1, source_target_pairs={{16,0},{32,16},{48,32},{64,48},{80,64},{96,80},{112,96},{128,112},... | collective-permute-start | bytes 9224 | tf_op jit(solution)/shard_map/ppermute | solution.py:295
  32.4 6.1 %collective-permute-start.4 = (f32[768]{0:T(1024)S(1)}, f32[768]{0:T(1024)S(1)}, u32[]{:S(2)}, u32[]{:S(2)}) collective-permute-start(f32[768]{0:T(1024)S(1)} %reshape.595), channel_id=1, source_target_pairs={{0,16},{16,32},{32,48},{48,64},{64,80},{80,96},{96,112},{112,128},... | collective-permute-start | bytes 9224 | tf_op jit(solution)/shard_map/ppermute | solution.py:295
  38.8 4.0 %collective-permute-start.7 = (f32[54]{0:T(128)S(1)}, f32[54]{0:T(128)S(1)}, u32[]{:S(2)}, u32[]{:S(2)}) collective-permute-start(f32[54]{0:T(128)S(1)} %reshape.601), channel_id=1, source_target_pairs={{4,0},{8,4},{12,8},{5,1},{9,5},{13,9},{6,2},{10,6},{14,10},{7,3},{... | collective-permute-start | bytes 656 | tf_op jit(solution)/shard_map/ppermute | solution.py:295
  41.2 5.4 %collective-permute-start.6 = (f32[54]{0:T(128)S(1)}, f32[54]{0:T(128)S(1)}, u32[]{:S(2)}, u32[]{:S(2)}) collective-permute-start(f32[54]{0:T(128)S(1)} %reshape.599), channel_id=1, source_target_pairs={{0,4},{4,8},{8,12},{1,5},{5,9},{9,13},{2,6},{6,10},{10,14},{3,7},{... | collective-permute-start | bytes 656 | tf_op jit(solution)/shard_map/ppermute | solution.py:295
  58.5 10.6 %all-to-all-start.1 = ((f32[4,2,9,128]{3,1,2,0:T(2,128)}), f32[4,2,9,128]{3,1,2,0:T(2,128)S(1)}, u32[]{:S(2)}, u32[]{:S(2)}) async-start(f32[4,2,9,128]{3,1,2,0:T(2,128)} %broadcast_in_dim.102), calls=%async_computation.1 | async-start | bytes 73728 | tf_op jit(solution)/shard_map/all_to_all | solution.py:183
  63.5 10.0 %copy-start.4 = (f32[64,256]{1,0:T(8,128)S(1)}, f32[64,256]{1,0:T(8,128)}, u32[]{:S(2)}) copy-start(f32[64,256]{1,0:T(8,128)} %param.13) | copy-start | bytes 196612
  63.5 10.0 %copy-start.5 = (f32[2,64,256]{2,1,0:T(8,128)S(1)}, f32[2,64,256]{2,1,0:T(8,128)}, u32[]{:S(2)}) copy-start(f32[2,64,256]{2,1,0:T(8,128)} %param.14) | copy-start | bytes 393220
  69.1 4.6 %collective-permute-start.9 = (f32[768]{0:T(1024)S(1)}, f32[768]{0:T(1024)S(1)}, u32[]{:S(2)}, u32[]{:S(2)}) collective-permute-start(f32[768]{0:T(1024)S(1)} %reshape.610), channel_id=1, source_target_pairs={{16,0},{32,16},{48,32},{64,48},{80,64},{96,80},{112,96},{128,112},... | collective-permute-start | bytes 9224 | tf_op jit(solution)/shard_map/ppermute | solution.py:295
  71.1 6.1 %collective-permute-start.8 = (f32[768]{0:T(1024)S(1)}, f32[768]{0:T(1024)S(1)}, u32[]{:S(2)}, u32[]{:S(2)}) collective-permute-start(f32[768]{0:T(1024)S(1)} %reshape.608), channel_id=1, source_target_pairs={{0,16},{16,32},{32,48},{48,64},{64,80},{80,96},{96,112},{112,128},... | collective-permute-start | bytes 9224 | tf_op jit(solution)/shard_map/ppermute | solution.py:295
  77.2 3.9 %collective-permute-start.11 = (f32[1280]{0:T(1024)S(1)}, f32[1280]{0:T(1024)S(1)}, u32[]{:S(2)}, u32[]{:S(2)}) collective-permute-start(f32[1280]{0:T(1024)S(1)} %reshape.614), channel_id=1, source_target_pairs={{4,0},{8,4},{12,8},{5,1},{9,5},{13,9},{6,2},{10,6},{14,10},{7,3},{... | collective-permute-start | bytes 15368 | tf_op jit(solution)/shard_map/ppermute | solution.py:295
  79.6 5.5 %collective-permute-start.10 = (f32[1280]{0:T(1024)S(1)}, f32[1280]{0:T(1024)S(1)}, u32[]{:S(2)}, u32[]{:S(2)}) collective-permute-start(f32[1280]{0:T(1024)S(1)} %reshape.612), channel_id=1, source_target_pairs={{0,4},{4,8},{8,12},{1,5},{5,9},{9,13},{2,6},{6,10},{10,14},{3,7},{... | collective-permute-start | bytes 15368 | tf_op jit(solution)/shard_map/ppermute | solution.py:295

commit v11 on v10

--- a/solution.py
+++ b/solution.py
@@ -33,42 +33,41 @@
         out_ref[comp] = -body_ref[comp]
     rows_out = [height * 9 + comp * 3 + vertex for height in range(2) for comp in comps for vertex in range(3)]
     pairs = layers - 1
+
+    def layer_views(layer):
+        slot = layer % 2
+        for comp in range(4):
+            plane = fld_ref[comp * layers + layer]
+            below = pltpu.roll(plane, ROWS_PAD - 1, 0)
+            right = pltpu.roll(plane, LANES_PAD - 1, 1)
+            diag = pltpu.roll(below, LANES_PAD - 1, 1)
+            far = jnp.where(main, diag, right)
+            near = jnp.where(main, plane, below)
+            for tri, views in enumerate(((plane, below, far), (near, diag, right))):
+                for vertex in range(3):
+                    vals_ref[slot, tri, comp * 3 + vertex] = views[vertex]
+
+    layer_views(0)
     for pair in range(pairs):
-        vis_parts = [[], []]
-        for height in range(2):
-            layer = pair + height
-            for comp in range(4):
-                plane = fld_ref[comp * layers + layer]
-                below = pltpu.roll(plane, ROWS_PAD - 1, 0)
-                right = pltpu.roll(plane, LANES_PAD - 1, 1)
-                diag = pltpu.roll(below, LANES_PAD - 1, 1)
-                far = jnp.where(main, diag, right)
-                near = jnp.where(main, plane, below)
-                if comp < 3:
-                    base = height * 9 + comp * 3
-                    vals_ref[0, base] = plane
-                    vals_ref[0, base + 1] = below
-                    vals_ref[0, base + 2] = far
-                    vals_ref[1, base] = near
-                    vals_ref[1, base + 1] = diag
-                    vals_ref[1, base + 2] = right
-                else:
-                    vis_parts[0] += [plane, below, far]
-                    vis_parts[1] += [near, diag, right]
+        layer_views(pair + 1)
+        slots = (pair % 2, (pair + 1) % 2)
         for tri in range(2):
-            total = vis_parts[tri][0]
-            for term in vis_parts[tri][1:]:
-                total = total + term
+            total = None
+            for height in range(2):
+                for vertex in range(3):
+                    term = vals_ref[slots[height], tri, 9 + vertex]
+                    total = term if total is None else total + term
             vis_ref[tri] = total / 6.0 * weight
 
         def tile_body(block, carry):
             row = pl.multiple_of(block * 8, 8)
             for tri in range(2):
                 vis = vis_ref[tri, pl.ds(row, 8), :]
+                values = [vals_ref[slots[beta // 9], tri, beta % 9, pl.ds(row, 8), :] for beta in range(18)]
                 for alpha in rows_out:
-                    acc = kmat_ref[alpha, 0] * vals_ref[tri, 0, pl.ds(row, 8), :]
+                    acc = kmat_ref[alpha, 0] * values[0]
                     for beta in range(1, 18):
-                        acc = acc + kmat_ref[alpha, beta] * vals_ref[tri, beta, pl.ds(row, 8), :]
+                        acc = acc + kmat_ref[alpha, beta] * values[beta]
                     resp_ref[tri, alpha, pl.ds(row, 8), :] = acc * vis
             return carry
 
@@ -121,7 +120,7 @@
 
 def fem_scratch():
     return [
-        pltpu.VMEM((2, 18, ROWS_PAD, LANES_PAD), jnp.float32),
+        pltpu.VMEM((2, 2, 12, ROWS_PAD, LANES_PAD), jnp.float32),
         pltpu.VMEM((2, ROWS_PAD, LANES_PAD), jnp.float32),
         pltpu.VMEM((2, 18, ROWS_PAD, LANES_PAD), jnp.float32),
     ]

time: 87.2 us -> 86.7 us (level)
  no operation moved by 1% of the time
where the time goes in v11:
time: 86.7 us; the launch traced here: 86 us
  starting transfers between devices  35 us (40%)
  waiting for transfers between devices  22.1 us (25%)
  Pallas kernels  13.1 us (15%)
  matrix products  5.36 us (6%)
  local copies, waits for them, and re-layouts  4.93 us (6%)
  other arithmetic  4.12 us (5%)
  between operations  1.44 us (2%)
    ppermute x6, waiting for transfers between devices, exchange(): lax.ppermute(sent_up, axis, up)  22.1 us
    ppermute x6, starting transfers between devices, exchange(): lax.ppermute(sent_down, axis, down)  14.8 us
    ppermute x6, starting transfers between devices, exchange(): lax.ppermute(sent_up, axis, up)  10.6 us
    pallas_call x1, Pallas kernels, fem_first(): pl.pallas_call(functools.partial(fem_horizontal, grid), out_shape=(jax.Sh...  7.76 us
    pallas_call x1, Pallas kernels, fem_second(): pl.pallas_call(functools.partial(fem_vertical, grid), out_shape=jax.Shape...  5.32 us
    all_to_all x1, starting transfers between devices, layer_neighbours(): lax.all_to_all(jnp.concatenate(chunks, 0), 'layer', 0, 0, tiled=True)  4.83 us
    all_to_all x1, starting transfers between devices, layer_total(): gathered = lax.all_to_all(copies, 'layer', 0, 0, tiled=True)  4.8 us
    dot_general x2, matrix products, gather_slots(): cols_taken = jnp.einsum('krc,sc->krs', field, pick_col, precision=HIGH)  3.15 us
  transfers between devices with their start and end apart: 14, of which 6 were waited for; matrix products, arithmetic and copies ran while one was open for 5% of the time, Pallas kernels for 6%

profile of v11, /device:TPU:410, one launch (start us, length us, event | category | flops | bytes accessed | tf_op | source)
XLA Modules:
  0.0 86.0 jit_solution(6626591510674274493)
XLA Ops:
  0.7 0.8 reduce.2
  1.6 1.7 %fusion.1 = f32[2,1152]{1,0:T(2,128)S(1)} fusion(f32[2,64,256]{2,1,0:T(8,128)} %param.11, s32[1152]{0:T(1024)S(1)} %get-tuple-element.56, pred[64,1152]{1,0:T(8,128)(4,1)S(1)} %convert_compare_fusion), kind=kOutput, calls=%fused_computation.3 | convolution fusion | flops 453572352 | bytes 218624 | tf_op jit(solution)/shard_map/krc,sc->krs/dot_general | solution.py:170
  3.5 3.6 %collective-permute-start.1 = (f32[4864]{0:T(1024)S(1)}, f32[4864]{0:T(1024)S(1)}, u32[]{:S(2)}, u32[]{:S(2)}) collective-permute-start(f32[4864]{0:T(1024)S(1)} %pad_maximum_fusion.16), channel_id=1, source_target_pairs={{16,0},{32,16},{48,32},{64,48},{80,64},{96,80},{112,96},{128,112},... | collective-permute-start | bytes 58376 | tf_op jit(solution)/shard_map/ppermute | solution.py:294
  7.1 1.9 %collective-permute-start = (f32[4864]{0:T(1024)S(1)}, f32[4864]{0:T(1024)S(1)}, u32[]{:S(2)}, u32[]{:S(2)}) collective-permute-start(f32[4864]{0:T(1024)S(1)} %pad_maximum_fusion.15), channel_id=1, source_target_pairs={{0,16},{16,32},{32,48},{48,64},{64,80},{80,96},{96,112},{112,128},... | collective-permute-start | bytes 58376 | tf_op jit(solution)/shard_map/ppermute | solution.py:294
  9.2 4.2 %collective-permute-done = f32[4864]{0:T(1024)S(1)} collective-permute-done((f32[4864]{0:T(1024)S(1)}, f32[4864]{0:T(1024)S(1)}, u32[]{:S(2)}, u32[]{:S(2)}) %collective-permute-start) | collective-permute-done | bytes 19488 | tf_op jit(solution)/shard_map/ppermute | solution.py:294
  14.5 2.6 %collective-permute-start.3 = (f32[1712]{0:T(1024)S(1)}, f32[1712]{0:T(1024)S(1)}, u32[]{:S(2)}, u32[]{:S(2)}) collective-permute-start(f32[1712]{0:T(1024)S(1)} %concatenate.71), channel_id=1, source_target_pairs={{4,0},{8,4},{12,8},{5,1},{9,5},{13,9},{6,2},{10,6},{14,10},{7,3},{... | collective-permute-start | bytes 20552 | tf_op jit(solution)/shard_map/ppermute | solution.py:294
  17.4 1.3 %collective-permute-start.2 = (f32[1712]{0:T(1024)S(1)}, f32[1712]{0:T(1024)S(1)}, u32[]{:S(2)}, u32[]{:S(2)}) collective-permute-start(f32[1712]{0:T(1024)S(1)} %concatenate.70), channel_id=1, source_target_pairs={{0,4},{4,8},{8,12},{1,5},{5,9},{9,13},{2,6},{6,10},{10,14},{3,7},{... | collective-permute-start | bytes 20552 | tf_op jit(solution)/shard_map/ppermute | solution.py:294
  18.6 0.3 fusion.18
  19.3 3.6 %collective-permute-done.2 = f32[1712]{0:T(1024)S(1)} collective-permute-done((f32[1712]{0:T(1024)S(1)}, f32[1712]{0:T(1024)S(1)}, u32[]{:S(2)}, u32[]{:S(2)}) %collective-permute-start.2) | collective-permute-done | bytes 6880 | tf_op jit(solution)/shard_map/ppermute | solution.py:294
  23.2 0.3 pad_maximum_fusion.2
  23.7 0.9 %pad_maximum_fusion.3 = f32[4,4,18,258]{3,1,2,0:T(4,128)} fusion(f32[1,4,18,258]{3,1,2,0:T(4,128)S(1)} %get-tuple-element.40, f32[1,4,18,258]{3,1,2,0:T(4,128)S(1)} %get-tuple-element.39, f32[1,4,18,258]{3,1,2,0:T(4,128)S(1)} %get-tuple-element.38, f32[1,4,18,258]{3,1,2,0:T(4,128)S(1)} %get-tuple-element.37), kind=kLoop, calls=%fused_computation.36 | loop fusion | flops 222912 | bytes 594432 | tf_op jit(solution)/shard_map/concatenate | solution.py:196
  24.6 4.8 %all-to-all-start = ((f32[4,4,18,258]{3,1,2,0:T(4,128)}), f32[4,4,18,258]{3,1,2,0:T(4,128)S(1)}, u32[]{:S(2)}, u32[]{:S(2)}) async-start(f32[4,4,18,258]{3,1,2,0:T(4,128)} %pad_maximum_fusion.3), calls=%async_computation | async-start | bytes 884736 | tf_op jit(solution)/shard_map/all_to_all | solution.py:196
  29.9 0.5 fusion.5
  30.4 1.9 %collective-permute-start.5 = (f32[768]{0:T(1024)S(1)}, f32[768]{0:T(1024)S(1)}, u32[]{:S(2)}, u32[]{:S(2)}) collective-permute-start(f32[768]{0:T(1024)S(1)} %reshape.597), channel_id=1, source_target_pairs={{16,0},{32,16},{48,32},{64,48},{80,64},{96,80},{112,96},{128,112},... | collective-permute-start | bytes 9224 | tf_op jit(solution)/shard_map/ppermute | solution.py:294
  32.4 2.4 %collective-permute-start.4 = (f32[768]{0:T(1024)S(1)}, f32[768]{0:T(1024)S(1)}, u32[]{:S(2)}, u32[]{:S(2)}) collective-permute-start(f32[768]{0:T(1024)S(1)} %reshape.595), channel_id=1, source_target_pairs={{0,16},{16,32},{32,48},{48,64},{64,80},{80,96},{96,112},{112,128},... | collective-permute-start | bytes 9224 | tf_op jit(solution)/shard_map/ppermute | solution.py:294
  35.5 3.0 %collective-permute-done.4 = f32[768]{0:T(1024)S(1)} collective-permute-done((f32[768]{0:T(1024)S(1)}, f32[768]{0:T(1024)S(1)}, u32[]{:S(2)}, u32[]{:S(2)}) %collective-permute-start.4) | collective-permute-done | bytes 3104 | tf_op jit(solution)/shard_map/ppermute | solution.py:294
  38.8 2.4 %collective-permute-start.7 = (f32[54]{0:T(128)S(1)}, f32[54]{0:T(128)S(1)}, u32[]{:S(2)}, u32[]{:S(2)}) collective-permute-start(f32[54]{0:T(128)S(1)} %reshape.601), channel_id=1, source_target_pairs={{4,0},{8,4},{12,8},{5,1},{9,5},{13,9},{6,2},{10,6},{14,10},{7,3},{... | collective-permute-start | bytes 656 | tf_op jit(solution)/shard_map/ppermute | solution.py:294
  41.2 1.3 %collective-permute-start.6 = (f32[54]{0:T(128)S(1)}, f32[54]{0:T(128)S(1)}, u32[]{:S(2)}, u32[]{:S(2)}) collective-permute-start(f32[54]{0:T(128)S(1)} %reshape.599), channel_id=1, source_target_pairs={{0,4},{4,8},{8,12},{1,5},{5,9},{9,13},{2,6},{6,10},{10,14},{3,7},{... | collective-permute-start | bytes 656 | tf_op jit(solution)/shard_map/ppermute | solution.py:294
  42.9 3.7 %collective-permute-done.6 = f32[54]{0:T(128)S(1)} collective-permute-done((f32[54]{0:T(128)S(1)}, f32[54]{0:T(128)S(1)}, u32[]{:S(2)}, u32[]{:S(2)}) %collective-permute-start.6) | collective-permute-done | bytes 248 | tf_op jit(solution)/shard_map/ppermute | solution.py:294
  47.4 0.9 %pad.4.fld_ref = f32[21,24,384]{2,1,0:T(8,128)} pad(f32[21,18,258]{2,1,0:T(8,128)S(1)} %fusion.19, f32[]{:T(128)} %constant.67.clone.1), padding=0_0x0_6x0_126 | pad | bytes 1164244 | tf_op jit(solution)/shard_map/jit(_pad)/pad | solution.py:118
  48.4 7.8 %shard_map.122 = (f32[3,3,16,256]{3,2,1,0:T(8,128)}, f32[2,16,256]{2,1,0:T(8,128)}) custom-call(f32[21,24,384]{2,1,0:T(8,128)} %pad.4.fld_ref, f32[18,18]{1,0:T(8,128)} %kmat_ref.3, f32[3,3,16,256]{3,2,1,0:T(8,128)} %body_ref.3), custom_call_target="tpu_custom_call" | custom-call | tf_op jit(solution)/shard_map/pallas_call | solution.py:133
  56.1 1.5 %fusion.14 = f32[2,1152]{1,0:T(2,128)S(1)} fusion(f32[2,16,256]{2,1,0:T(8,128)} %get-tuple-element.6, s32[1152]{0:T(1024)S(1)} %get-tuple-element.54, pred[16,1152]{1,0:T(8,128)(4,1)S(1)} %convert_compare_fusion.1), kind=kOutput, calls=%fused_computation.12 | convolution fusion | flops 113612544 | bytes 65024 | tf_op jit(solution)/shard_map/krc,sc->krs/dot_general | solution.py:170
  57.6 0.6 broadcast_in_dim.102
  58.2 4.8 %all-to-all-start.1 = ((f32[4,2,9,128]{3,1,2,0:T(2,128)}), f32[4,2,9,128]{3,1,2,0:T(2,128)S(1)}, u32[]{:S(2)}, u32[]{:S(2)}) async-start(f32[4,2,9,128]{3,1,2,0:T(2,128)} %broadcast_in_dim.102), calls=%async_computation.1 | async-start | bytes 73728 | tf_op jit(solution)/shard_map/all_to_all | solution.py:182
  63.2 5.3 %shard_map.123 = f32[3,3,16,256]{3,2,1,0:T(8,128)} custom-call(f32[21,24,384]{2,1,0:T(8,128)} %pad.4.fld_ref, f32[18,18]{1,0:T(8,128)} %kmat_ref.3, f32[3,3,16,256]{3,2,1,0:T(8,128)} %body_ref.3, f32[3,3,16,256]{3,2,1,0:T(8,128)} %get-tuple-element.7.prev_ref), custom_call_target="tpu_custom_call" | custom-call | tf_op jit(solution)/shard_map/pallas_call | solution.py:148
  68.6 1.9 %collective-permute-start.9 = (f32[768]{0:T(1024)S(1)}, f32[768]{0:T(1024)S(1)}, u32[]{:S(2)}, u32[]{:S(2)}) collective-permute-start(f32[768]{0:T(1024)S(1)} %reshape.610), channel_id=1, source_target_pairs={{16,0},{32,16},{48,32},{64,48},{80,64},{96,80},{112,96},{128,112},... | collective-permute-start | bytes 9224 | tf_op jit(solution)/shard_map/ppermute | solution.py:294
  70.6 2.4 %collective-permute-start.8 = (f32[768]{0:T(1024)S(1)}, f32[768]{0:T(1024)S(1)}, u32[]{:S(2)}, u32[]{:S(2)}) collective-permute-start(f32[768]{0:T(1024)S(1)} %reshape.608), channel_id=1, source_target_pairs={{0,16},{16,32},{32,48},{48,64},{64,80},{80,96},{96,112},{112,128},... | collective-permute-start | bytes 9224 | tf_op jit(solution)/shard_map/ppermute | solution.py:294
  73.2 3.5 %collective-permute-done.8 = f32[768]{0:T(1024)S(1)} collective-permute-done((f32[768]{0:T(1024)S(1)}, f32[768]{0:T(1024)S(1)}, u32[]{:S(2)}, u32[]{:S(2)}) %collective-permute-start.8) | collective-permute-done | bytes 3104 | tf_op jit(solution)/shard_map/ppermute | solution.py:294
  76.7 2.4 %collective-permute-start.11 = (f32[1280]{0:T(1024)S(1)}, f32[1280]{0:T(1024)S(1)}, u32[]{:S(2)}, u32[]{:S(2)}) collective-permute-start(f32[1280]{0:T(1024)S(1)} %reshape.614), channel_id=1, source_target_pairs={{4,0},{8,4},{12,8},{5,1},{9,5},{13,9},{6,2},{10,6},{14,10},{7,3},{... | collective-permute-start | bytes 15368 | tf_op jit(solution)/shard_map/ppermute | solution.py:294
  79.1 1.3 %collective-permute-start.10 = (f32[1280]{0:T(1024)S(1)}, f32[1280]{0:T(1024)S(1)}, u32[]{:S(2)}, u32[]{:S(2)}) collective-permute-start(f32[1280]{0:T(1024)S(1)} %reshape.612), channel_id=1, source_target_pairs={{0,4},{4,8},{8,12},{1,5},{5,9},{9,13},{2,6},{6,10},{10,14},{3,7},{... | collective-permute-start | bytes 15368 | tf_op jit(solution)/shard_map/ppermute | solution.py:294
  80.6 4.0 %collective-permute-done.10 = f32[1280]{0:T(1024)S(1)} collective-permute-done((f32[1280]{0:T(1024)S(1)}, f32[1280]{0:T(1024)S(1)}, u32[]{:S(2)}, u32[]{:S(2)}) %collective-permute-start.10) | collective-permute-done | bytes 5152 | tf_op jit(solution)/shard_map/ppermute | solution.py:294
  84.7 1.3 %fusion.11 = f32[2,64,256]{2,1,0:T(8,128)} fusion(s32[1152]{0:T(1024)S(1)} %get-tuple-element.56, f32[2,1152]{1,0:T(2,128)S(1)} %bitcast.150, f32[1152,64]{0,1:T(8,128)S(1)} %fusion.36, f32[1,64,256]{2,1,0:T(8,128)S(1)} %fusion.44, f32[1,64,256]{2,1,0:T(8,128)S(1)} %fusion.50), kind=kOutput, calls=%fused_computation.11 | convolution fusion | flops 453492736 | bytes 570880 | tf_op jit(solution)/shard_map/ksr,sc->krc/dot_general | solution.py:176
  (132 shorter events, 5.5 us)
Async XLA Ops:
  0.6 2.8 %copy-start.1 = (f32[2,64,256]{2,1,0:T(8,128)S(1)}, f32[2,64,256]{2,1,0:T(8,128)}, u32[]{:S(2)}) copy-start(f32[2,64,256]{2,1,0:T(8,128)} %param.11) | copy-start | bytes 393220
  0.6 2.7 %copy-start.6 = (s32[16,256]{1,0:T(8,128)S(1)}, s32[16,256]{1,0:T(8,128)}, u32[]{:S(2)}) copy-start(s32[16,256]{1,0:T(8,128)} %param.18) | copy-start | bytes 49156
  0.7 2.7 %copy-start.2 = (f32[3,16,256]{2,1,0:T(8,128)S(1)}, f32[3,16,256]{2,1,0:T(8,128)}, u32[]{:S(2)}) copy-start(f32[3,16,256]{2,1,0:T(8,128)} %param.16) | copy-start | bytes 147460
  0.7 2.7 %copy-start = (f32[3,3,16,256]{3,2,1,0:T(8,128)S(1)}, f32[3,3,16,256]{3,2,1,0:T(8,128)}, u32[]{:S(2)}) copy-start(f32[3,3,16,256]{3,2,1,0:T(8,128)} %param.15) | copy-start | bytes 442372
  0.7 2.8 %copy-start.3 = (f32[64,256]{1,0:T(8,128)S(1)}, f32[64,256]{1,0:T(8,128)}, u32[]{:S(2)}) copy-start(f32[64,256]{1,0:T(8,128)} %param.12) | copy-start | bytes 196612
  1.6 7.5 %copy-start.7 = (s32[1,9,128]{2,0,1:T(1,128)S(1)}, s32[1,9,128]{2,0,1:T(1,128)}, u32[]{:S(2)}) copy-start(s32[1,9,128]{2,0,1:T(1,128)} %param.20) | copy-start | bytes 13828
  3.5 5.7 %collective-permute-start.1 = (f32[4864]{0:T(1024)S(1)}, f32[4864]{0:T(1024)S(1)}, u32[]{:S(2)}, u32[]{:S(2)}) collective-permute-start(f32[4864]{0:T(1024)S(1)} %pad_maximum_fusion.16), channel_id=1, source_target_pairs={{16,0},{32,16},{48,32},{64,48},{80,64},{96,80},{112,96},{128,112},... | collective-permute-start | bytes 58376 | tf_op jit(solution)/shard_map/ppermute | solution.py:294
  7.1 6.3 %collective-permute-start = (f32[4864]{0:T(1024)S(1)}, f32[4864]{0:T(1024)S(1)}, u32[]{:S(2)}, u32[]{:S(2)}) collective-permute-start(f32[4864]{0:T(1024)S(1)} %pad_maximum_fusion.15), channel_id=1, source_target_pairs={{0,16},{16,32},{32,48},{48,64},{64,80},{80,96},{96,112},{112,128},... | collective-permute-start | bytes 58376 | tf_op jit(solution)/shard_map/ppermute | solution.py:294
  14.5 4.5 %collective-permute-start.3 = (f32[1712]{0:T(1024)S(1)}, f32[1712]{0:T(1024)S(1)}, u32[]{:S(2)}, u32[]{:S(2)}) collective-permute-start(f32[1712]{0:T(1024)S(1)} %concatenate.71), channel_id=1, source_target_pairs={{4,0},{8,4},{12,8},{5,1},{9,5},{13,9},{6,2},{10,6},{14,10},{7,3},{... | collective-permute-start | bytes 20552 | tf_op jit(solution)/shard_map/ppermute | solution.py:294
  17.4 5.5 %collective-permute-start.2 = (f32[1712]{0:T(1024)S(1)}, f32[1712]{0:T(1024)S(1)}, u32[]{:S(2)}, u32[]{:S(2)}) collective-permute-start(f32[1712]{0:T(1024)S(1)} %concatenate.70), channel_id=1, source_target_pairs={{0,4},{4,8},{8,12},{1,5},{5,9},{9,13},{2,6},{6,10},{10,14},{3,7},{... | collective-permute-start | bytes 20552 | tf_op jit(solution)/shard_map/ppermute | solution.py:294
  24.6 22.5 %all-to-all-start = ((f32[4,4,18,258]{3,1,2,0:T(4,128)}), f32[4,4,18,258]{3,1,2,0:T(4,128)S(1)}, u32[]{:S(2)}, u32[]{:S(2)}) async-start(f32[4,4,18,258]{3,1,2,0:T(4,128)} %pad_maximum_fusion.3), calls=%async_computation | async-start | bytes 884736 | tf_op jit(solution)/shard_map/all_to_all | solution.py:196
  30.4 5.0 %collective-permute-start.5 = (f32[768]{0:T(1024)S(1)}, f32[768]{0:T(1024)S(1)}, u32[]{:S(2)}, u32[]{:S(2)}) collective-permute-start(f32[768]{0:T(1024)S(1)} %reshape.597), channel_id=1, source_target_pairs={{16,0},{32,16},{48,32},{64,48},{80,64},{96,80},{112,96},{128,112},... | collective-permute-start | bytes 9224 | tf_op jit(solution)/shard_map/ppermute | solution.py:294
  32.4 6.1 %collective-permute-start.4 = (f32[768]{0:T(1024)S(1)}, f32[768]{0:T(1024)S(1)}, u32[]{:S(2)}, u32[]{:S(2)}) collective-permute-start(f32[768]{0:T(1024)S(1)} %reshape.595), channel_id=1, source_target_pairs={{0,16},{16,32},{32,48},{48,64},{64,80},{80,96},{96,112},{112,128},... | collective-permute-start | bytes 9224 | tf_op jit(solution)/shard_map/ppermute | solution.py:294
  38.8 4.0 %collective-permute-start.7 = (f32[54]{0:T(128)S(1)}, f32[54]{0:T(128)S(1)}, u32[]{:S(2)}, u32[]{:S(2)}) collective-permute-start(f32[54]{0:T(128)S(1)} %reshape.601), channel_id=1, source_target_pairs={{4,0},{8,4},{12,8},{5,1},{9,5},{13,9},{6,2},{10,6},{14,10},{7,3},{... | collective-permute-start | bytes 656 | tf_op jit(solution)/shard_map/ppermute | solution.py:294
  41.2 5.4 %collective-permute-start.6 = (f32[54]{0:T(128)S(1)}, f32[54]{0:T(128)S(1)}, u32[]{:S(2)}, u32[]{:S(2)}) collective-permute-start(f32[54]{0:T(128)S(1)} %reshape.599), channel_id=1, source_target_pairs={{0,4},{4,8},{8,12},{1,5},{5,9},{9,13},{2,6},{6,10},{10,14},{3,7},{... | collective-permute-start | bytes 656 | tf_op jit(solution)/shard_map/ppermute | solution.py:294
  58.2 10.3 %all-to-all-start.1 = ((f32[4,2,9,128]{3,1,2,0:T(2,128)}), f32[4,2,9,128]{3,1,2,0:T(2,128)S(1)}, u32[]{:S(2)}, u32[]{:S(2)}) async-start(f32[4,2,9,128]{3,1,2,0:T(2,128)} %broadcast_in_dim.102), calls=%async_computation.1 | async-start | bytes 73728 | tf_op jit(solution)/shard_map/all_to_all | solution.py:182
  63.2 9.8 %copy-start.4 = (f32[64,256]{1,0:T(8,128)S(1)}, f32[64,256]{1,0:T(8,128)}, u32[]{:S(2)}) copy-start(f32[64,256]{1,0:T(8,128)} %param.13) | copy-start | bytes 196612
  63.2 9.8 %copy-start.5 = (f32[2,64,256]{2,1,0:T(8,128)S(1)}, f32[2,64,256]{2,1,0:T(8,128)}, u32[]{:S(2)}) copy-start(f32[2,64,256]{2,1,0:T(8,128)} %param.14) | copy-start | bytes 393220
  68.6 4.6 %collective-permute-start.9 = (f32[768]{0:T(1024)S(1)}, f32[768]{0:T(1024)S(1)}, u32[]{:S(2)}, u32[]{:S(2)}) collective-permute-start(f32[768]{0:T(1024)S(1)} %reshape.610), channel_id=1, source_target_pairs={{16,0},{32,16},{48,32},{64,48},{80,64},{96,80},{112,96},{128,112},... | collective-permute-start | bytes 9224 | tf_op jit(solution)/shard_map/ppermute | solution.py:294
  70.6 6.1 %collective-permute-start.8 = (f32[768]{0:T(1024)S(1)}, f32[768]{0:T(1024)S(1)}, u32[]{:S(2)}, u32[]{:S(2)}) collective-permute-start(f32[768]{0:T(1024)S(1)} %reshape.608), channel_id=1, source_target_pairs={{0,16},{16,32},{32,48},{48,64},{64,80},{80,96},{96,112},{112,128},... | collective-permute-start | bytes 9224 | tf_op jit(solution)/shard_map/ppermute | solution.py:294
  76.7 3.9 %collective-permute-start.11 = (f32[1280]{0:T(1024)S(1)}, f32[1280]{0:T(1024)S(1)}, u32[]{:S(2)}, u32[]{:S(2)}) collective-permute-start(f32[1280]{0:T(1024)S(1)} %reshape.614), channel_id=1, source_target_pairs={{4,0},{8,4},{12,8},{5,1},{9,5},{13,9},{6,2},{10,6},{14,10},{7,3},{... | collective-permute-start | bytes 15368 | tf_op jit(solution)/shard_map/ppermute | solution.py:294
  79.1 5.5 %collective-permute-start.10 = (f32[1280]{0:T(1024)S(1)}, f32[1280]{0:T(1024)S(1)}, u32[]{:S(2)}, u32[]{:S(2)}) collective-permute-start(f32[1280]{0:T(1024)S(1)} %reshape.612), channel_id=1, source_target_pairs={{0,4},{4,8},{8,12},{1,5},{5,9},{9,13},{2,6},{6,10},{10,14},{3,7},{... | collective-permute-start | bytes 15368 | tf_op jit(solution)/shard_map/ppermute | solution.py:294

commit v12 on v11

--- a/solution.py
+++ b/solution.py
@@ -21,9 +21,23 @@
     return valid.astype(jnp.float32)
 
 
-def fem_body(comps, grid, fld_ref, kmat_ref, body_ref, out_ref, vals_ref, vis_ref, resp_ref):
-    layers = (fld_ref.shape[0] - 1) // 4
-    main = fld_ref[4 * layers] == 0.0
+def fem_body(comps, grid, own_ref, below_ref, above_ref, ring_ref, kmat_ref, body_ref, out_ref, vals_ref, vis_ref, resp_ref):
+    own_layers = (own_ref.shape[0] - 1) // 4
+    layers = own_layers + 2
+    main = own_ref[4 * own_layers] == 0.0
+    imposed = ring_ref[0] > 0.5
+
+    def plane_of(comp, layer):
+        if layer == 0:
+            plane = below_ref[comp]
+        elif layer == layers - 1:
+            plane = above_ref[comp]
+        else:
+            plane = own_ref[comp * own_layers + layer - 1]
+        if comp < 2:
+            plane = jnp.where(imposed, ring_ref[1 + comp], plane)
+        return plane
+
     weight = cell_weight(grid)
     layer_index = lax.axis_index("layer")
     below_live = (layer_index > 0).astype(jnp.float32)
@@ -37,7 +51,7 @@
     def layer_views(layer):
         slot = layer % 2
         for comp in range(4):
-            plane = fld_ref[comp * layers + layer]
+            plane = plane_of(comp, layer)
             below = pltpu.roll(plane, ROWS_PAD - 1, 0)
             right = pltpu.roll(plane, LANES_PAD - 1, 1)
             diag = pltpu.roll(below, LANES_PAD - 1, 1)
@@ -98,8 +112,8 @@
                 out_ref[comp, own_layer] = out_ref[comp, own_layer] + part
 
 
-def fem_horizontal(grid, fld_ref, kmat_ref, body_ref, out_ref, depth_ref, vals_ref, vis_ref, resp_ref):
-    fem_body((0, 1), grid, fld_ref, kmat_ref, body_ref, out_ref, vals_ref, vis_ref, resp_ref)
+def fem_horizontal(grid, own_ref, below_ref, above_ref, ring_ref, kmat_ref, body_ref, out_ref, depth_ref, vals_ref, vis_ref, resp_ref):
+    fem_body((0, 1), grid, own_ref, below_ref, above_ref, ring_ref, kmat_ref, body_ref, out_ref, vals_ref, vis_ref, resp_ref)
     for comp in range(2):
         total = out_ref[comp, 0]
         for layer in range(1, out_ref.shape[1]):
@@ -107,14 +121,13 @@
         depth_ref[comp] = total
 
 
-def fem_vertical(grid, fld_ref, kmat_ref, body_ref, prev_ref, out_ref, vals_ref, vis_ref, resp_ref):
+def fem_vertical(grid, own_ref, below_ref, above_ref, ring_ref, kmat_ref, body_ref, prev_ref, out_ref, vals_ref, vis_ref, resp_ref):
     out_ref[0:2] = prev_ref[0:2]
-    fem_body((2,), grid, fld_ref, kmat_ref, body_ref, out_ref, vals_ref, vis_ref, resp_ref)
-
-
-def fem_inputs(extended_layers, diag_ext):
-    comps, layers, rows, lanes = extended_layers.shape
-    planes = jnp.concatenate([extended_layers.reshape(comps * layers, rows, lanes), diag_ext[None]], 0)
+    fem_body((2,), grid, own_ref, below_ref, above_ref, ring_ref, kmat_ref, body_ref, out_ref, vals_ref, vis_ref, resp_ref)
+
+
+def padded_planes(planes):
+    rows, lanes = planes.shape[-2:]
     return jnp.pad(planes, ((0, 0), (0, ROWS_PAD - rows), (0, LANES_PAD - lanes)))
 
 
@@ -126,7 +139,7 @@
     ]
 
 
-def fem_first(grid, fld, element_matrix, body_force):
+def fem_first(grid, fields, element_matrix, body_force):
     vmem = pl.BlockSpec(memory_space=pltpu.VMEM)
     smem = pl.BlockSpec(memory_space=pltpu.SMEM)
     depth_shape = (2,) + body_force.shape[2:]
@@ -136,22 +149,22 @@
             jax.ShapeDtypeStruct(body_force.shape, jnp.float32),
             jax.ShapeDtypeStruct(depth_shape, jnp.float32),
         ),
-        in_specs=[vmem, smem, vmem],
+        in_specs=[vmem] * 4 + [smem, vmem],
         out_specs=(vmem, vmem),
         scratch_shapes=fem_scratch(),
-    )(fld, element_matrix, body_force)
-
-
-def fem_second(grid, fld, element_matrix, body_force, previous):
+    )(*fields, element_matrix, body_force)
+
+
+def fem_second(grid, fields, element_matrix, body_force, previous):
     vmem = pl.BlockSpec(memory_space=pltpu.VMEM)
     smem = pl.BlockSpec(memory_space=pltpu.SMEM)
     return pl.pallas_call(
         functools.partial(fem_vertical, grid),
         out_shape=jax.ShapeDtypeStruct(body_force.shape, jnp.float32),
-        in_specs=[vmem, smem, vmem, vmem],
+        in_specs=[vmem] * 4 + [smem, vmem, vmem],
         out_specs=vmem,
         scratch_shapes=fem_scratch(),
-    )(fld, element_matrix, body_force, previous)
+    )(*fields, element_matrix, body_force, previous)
 
 
 HIGH = lax.Precision.HIGHEST
@@ -361,14 +374,10 @@
     below_raw, above_raw = layer_neighbours(field_ext[:, -1], field_ext[:, 0])
     (ring_x,) = packed_halo((ring,), (1,), "mx")
     (ring_ext,) = packed_halo((ring_x,), (2,), "my")
-    imposed_at = ring_ext[0] > 0.5
-    all_layers = jnp.concatenate([below_raw[:, None], field_ext, above_raw[:, None]], 1)
-    uv_ext = jnp.where(imposed_at[None, None], ring_ext[1:3, None], all_layers[:2])
-    extended_layers = jnp.concatenate([uv_ext, all_layers[2:]], 0)
+    fields = (padded_planes(widened), padded_planes(below_raw), padded_planes(above_raw), padded_planes(ring_ext))
     grid = (block_x, block_y, lax.axis_size("mx"), lax.axis_size("my"))
-    fld = fem_inputs(extended_layers, widened[-1])
-    partial_residual, depth_sum = fem_first(grid, fld, element_matrix, body_force)
-    stokes_residual = fem_second(grid, fld, element_matrix, body_force, partial_residual)
+    partial_residual, depth_sum = fem_first(grid, fields, element_matrix, body_force)
+    stokes_residual = fem_second(grid, fields, element_matrix, body_force, partial_residual)
     bucket = gather_slots(depth_sum, col_row, col_col).reshape(2, 9, slot_count)
     depth_total = layer_total(bucket)
     depth_total, stokes_residual = lax.optimization_barrier((depth_total, stokes_residual))

time: 86.7 us -> 87.6 us (1.010)
  local copies, waits for them, and re-layouts: 4.93 us -> 7.02 us
    pad x1 -> x3, local copies, waits for them, and re-layouts: 0.93 us -> 2.14 us  [padded_planes(): jnp.pad(planes, ((0, 0), (0, ROWS_PAD - rows), (0, LANES_PAD - lanes)))]
    concatenate x0 -> x1, local copies, waits for them, and re-layouts: none -> 0.89 us  [layer_neighbours(): jnp.concatenate(chunks, 0)]
  transfers between devices with their start and end apart: 14 -> 14, of which waited for: 6 -> 6; matrix products, arithmetic and copies ran while one was open for 5% -> 7% of each run, Pallas kernels for 6% -> 6%
where the time goes in v12:
time: 87.6 us; the launch traced here: 86.9 us
  starting transfers between devices  35 us (40%)
  waiting for transfers between devices  21.4 us (24%)
  Pallas kernels  13.3 us (15%)
  local copies, waits for them, and re-layouts  7.02 us (8%)
  matrix products  5.41 us (6%)
  other arithmetic  3.46 us (4%)
  between operations  1.39 us (2%)
    ppermute x6, waiting for transfers between devices, exchange(): lax.ppermute(sent_up, axis, up)  21.3 us
    ppermute x6, starting transfers between devices, exchange(): lax.ppermute(sent_down, axis, down)  14.8 us
    ppermute x6, starting transfers between devices, exchange(): lax.ppermute(sent_up, axis, up)  10.6 us
    pallas_call x1, Pallas kernels, fem_first(): pl.pallas_call(functools.partial(fem_horizontal, grid), out_shape=(jax.Sh...  7.87 us
    pallas_call x1, Pallas kernels, fem_second(): pl.pallas_call(functools.partial(fem_vertical, grid), out_shape=jax.Shape...  5.43 us
    all_to_all x1, starting transfers between devices, layer_neighbours(): lax.all_to_all(jnp.concatenate(chunks, 0), 'layer', 0, 0, tiled=True)  4.82 us
    all_to_all x1, starting transfers between devices, layer_total(): gathered = lax.all_to_all(copies, 'layer', 0, 0, tiled=True)  4.8 us
    dot_general x2, matrix products, gather_slots(): cols_taken = jnp.einsum('krc,sc->krs', field, pick_col, precision=HIGH)  3.2 us
  transfers between devices with their start and end apart: 14, of which 6 were waited for; matrix products, arithmetic and copies ran while one was open for 7% of the time, Pallas kernels for 6%

profile of v12, /device:TPU:410, one launch (start us, length us, event | category | flops | bytes accessed | tf_op | source)
XLA Modules:
  0.0 86.9 jit_solution(14420901289975774365)
XLA Ops:
  0.6 0.7 reduce.2
  1.5 1.7 %fusion.1 = f32[2,1152]{1,0:T(2,128)S(1)} fusion(f32[2,64,256]{2,1,0:T(8,128)} %param.11, s32[1152]{0:T(1024)S(1)} %get-tuple-element.55, pred[64,1152]{1,0:T(8,128)(4,1)S(1)} %convert_compare_fusion), kind=kOutput, calls=%fused_computation.3 | convolution fusion | flops 453572352 | bytes 218624 | tf_op jit(solution)/shard_map/krc,sc->krs/dot_general | solution.py:183
  3.5 3.6 %collective-permute-start.1 = (f32[4864]{0:T(1024)S(1)}, f32[4864]{0:T(1024)S(1)}, u32[]{:S(2)}, u32[]{:S(2)}) collective-permute-start(f32[4864]{0:T(1024)S(1)} %pad_maximum_fusion.9), channel_id=1, source_target_pairs={{16,0},{32,16},{48,32},{64,48},{80,64},{96,80},{112,96},{128,112},... | collective-permute-start | bytes 58376 | tf_op jit(solution)/shard_map/ppermute | solution.py:307
  7.1 1.9 %collective-permute-start = (f32[4864]{0:T(1024)S(1)}, f32[4864]{0:T(1024)S(1)}, u32[]{:S(2)}, u32[]{:S(2)}) collective-permute-start(f32[4864]{0:T(1024)S(1)} %pad_maximum_fusion.8), channel_id=1, source_target_pairs={{0,16},{16,32},{32,48},{48,64},{64,80},{80,96},{96,112},{112,128},... | collective-permute-start | bytes 58376 | tf_op jit(solution)/shard_map/ppermute | solution.py:307
  9.2 4.2 %collective-permute-done = f32[4864]{0:T(1024)S(1)} collective-permute-done((f32[4864]{0:T(1024)S(1)}, f32[4864]{0:T(1024)S(1)}, u32[]{:S(2)}, u32[]{:S(2)}) %collective-permute-start) | collective-permute-done | bytes 19488 | tf_op jit(solution)/shard_map/ppermute | solution.py:307
  14.4 2.6 %collective-permute-start.3 = (f32[1712]{0:T(1024)S(1)}, f32[1712]{0:T(1024)S(1)}, u32[]{:S(2)}, u32[]{:S(2)}) collective-permute-start(f32[1712]{0:T(1024)S(1)} %concatenate.62), channel_id=1, source_target_pairs={{4,0},{8,4},{12,8},{5,1},{9,5},{13,9},{6,2},{10,6},{14,10},{7,3},{... | collective-permute-start | bytes 20552 | tf_op jit(solution)/shard_map/ppermute | solution.py:307
  17.3 1.3 %collective-permute-start.2 = (f32[1712]{0:T(1024)S(1)}, f32[1712]{0:T(1024)S(1)}, u32[]{:S(2)}, u32[]{:S(2)}) collective-permute-start(f32[1712]{0:T(1024)S(1)} %concatenate.61), channel_id=1, source_target_pairs={{0,4},{4,8},{8,12},{1,5},{5,9},{9,13},{2,6},{6,10},{10,14},{3,7},{... | collective-permute-start | bytes 20552 | tf_op jit(solution)/shard_map/ppermute | solution.py:307
  19.3 3.6 %collective-permute-done.2 = f32[1712]{0:T(1024)S(1)} collective-permute-done((f32[1712]{0:T(1024)S(1)}, f32[1712]{0:T(1024)S(1)}, u32[]{:S(2)}, u32[]{:S(2)}) %collective-permute-start.2) | collective-permute-done | bytes 6880 | tf_op jit(solution)/shard_map/ppermute | solution.py:307
  23.6 0.9 %copy.61 = f32[4,4,18,258]{3,1,2,0:T(4,128)} copy(f32[4,4,18,258]{3,2,1,0:T(8,128)S(1)} %pad_maximum_fusion) | data formatting | bytes 594432 | tf_op jit(solution)/shard_map/concatenate | solution.py:209
  24.5 4.8 %all-to-all-start = ((f32[4,4,18,258]{3,1,2,0:T(4,128)}), f32[4,4,18,258]{3,1,2,0:T(4,128)S(1)}, u32[]{:S(2)}, u32[]{:S(2)}) async-start(f32[4,4,18,258]{3,1,2,0:T(4,128)} %copy.61), calls=%async_computation | async-start | bytes 884736 | tf_op jit(solution)/shard_map/all_to_all | solution.py:209
  30.4 1.9 %collective-permute-start.5 = (f32[768]{0:T(1024)S(1)}, f32[768]{0:T(1024)S(1)}, u32[]{:S(2)}, u32[]{:S(2)}) collective-permute-start(f32[768]{0:T(1024)S(1)} %reshape.509), channel_id=1, source_target_pairs={{16,0},{32,16},{48,32},{64,48},{80,64},{96,80},{112,96},{128,112},... | collective-permute-start | bytes 9224 | tf_op jit(solution)/shard_map/ppermute | solution.py:307
  32.4 2.4 %collective-permute-start.4 = (f32[768]{0:T(1024)S(1)}, f32[768]{0:T(1024)S(1)}, u32[]{:S(2)}, u32[]{:S(2)}) collective-permute-start(f32[768]{0:T(1024)S(1)} %reshape.507), channel_id=1, source_target_pairs={{0,16},{16,32},{32,48},{48,64},{64,80},{80,96},{96,112},{112,128},... | collective-permute-start | bytes 9224 | tf_op jit(solution)/shard_map/ppermute | solution.py:307
  35.7 2.8 %collective-permute-done.4 = f32[768]{0:T(1024)S(1)} collective-permute-done((f32[768]{0:T(1024)S(1)}, f32[768]{0:T(1024)S(1)}, u32[]{:S(2)}, u32[]{:S(2)}) %collective-permute-start.4) | collective-permute-done | bytes 3104 | tf_op jit(solution)/shard_map/ppermute | solution.py:307
  38.8 2.4 %collective-permute-start.7 = (f32[54]{0:T(128)S(1)}, f32[54]{0:T(128)S(1)}, u32[]{:S(2)}, u32[]{:S(2)}) collective-permute-start(f32[54]{0:T(128)S(1)} %reshape.513), channel_id=1, source_target_pairs={{4,0},{8,4},{12,8},{5,1},{9,5},{13,9},{6,2},{10,6},{14,10},{7,3},{... | collective-permute-start | bytes 656 | tf_op jit(solution)/shard_map/ppermute | solution.py:307
  41.2 1.3 %collective-permute-start.6 = (f32[54]{0:T(128)S(1)}, f32[54]{0:T(128)S(1)}, u32[]{:S(2)}, u32[]{:S(2)}) collective-permute-start(f32[54]{0:T(128)S(1)} %reshape.511), channel_id=1, source_target_pairs={{0,4},{4,8},{8,12},{1,5},{5,9},{9,13},{2,6},{6,10},{10,14},{3,7},{... | collective-permute-start | bytes 656 | tf_op jit(solution)/shard_map/ppermute | solution.py:307
  42.5 0.8 pad.15.own_ref
  43.4 3.2 %collective-permute-done.6 = f32[54]{0:T(128)S(1)} collective-permute-done((f32[54]{0:T(128)S(1)}, f32[54]{0:T(128)S(1)}, u32[]{:S(2)}, u32[]{:S(2)}) %collective-permute-start.6) | collective-permute-done | bytes 248 | tf_op jit(solution)/shard_map/ppermute | solution.py:307
  46.8 0.8 select_maximum_fusion.ring_ref
  47.7 0.7 pad.16.below_ref
  48.3 0.7 pad.17.above_ref
  49.0 7.9 %shard_map.122 = (f32[3,3,16,256]{3,2,1,0:T(8,128)}, f32[2,16,256]{2,1,0:T(8,128)}) custom-call(f32[13,24,384]{2,1,0:T(8,128)} %pad.15.own_ref, f32[4,24,384]{2,1,0:T(8,128)} %pad.16.below_ref, f32[4,24,384]{2,1,0:T(8,128)} %pad.17.above_ref, f32[3,24,384]{2,1,0:T(8,128)} %select_maximum_fusion.ring_ref, f32[18,18]{1,0:T(8,128)} %kmat_ref.3, ...), custom_call_target="tpu_custom_call" | custom-call | tf_op jit(solution)/shard_map/pallas_call | solution.py:146
  56.9 1.5 %fusion.14 = f32[2,1152]{1,0:T(2,128)S(1)} fusion(f32[2,16,256]{2,1,0:T(8,128)} %get-tuple-element.6, s32[1152]{0:T(1024)S(1)} %get-tuple-element.53, pred[16,1152]{1,0:T(8,128)(4,1)S(1)} %convert_compare_fusion.1), kind=kOutput, calls=%fused_computation.12 | convolution fusion | flops 113612544 | bytes 65024 | tf_op jit(solution)/shard_map/krc,sc->krs/dot_general | solution.py:183
  58.4 0.6 broadcast_in_dim.80
  59.0 4.8 %all-to-all-start.1 = ((f32[4,2,9,128]{3,1,2,0:T(2,128)}), f32[4,2,9,128]{3,1,2,0:T(2,128)S(1)}, u32[]{:S(2)}, u32[]{:S(2)}) async-start(f32[4,2,9,128]{3,1,2,0:T(2,128)} %broadcast_in_dim.80), calls=%async_computation.1 | async-start | bytes 73728 | tf_op jit(solution)/shard_map/all_to_all | solution.py:195
  64.0 5.4 %shard_map.123 = f32[3,3,16,256]{3,2,1,0:T(8,128)} custom-call(f32[13,24,384]{2,1,0:T(8,128)} %pad.15.own_ref, f32[4,24,384]{2,1,0:T(8,128)} %pad.16.below_ref, f32[4,24,384]{2,1,0:T(8,128)} %pad.17.above_ref, f32[3,24,384]{2,1,0:T(8,128)} %select_maximum_fusion.ring_ref, f32[18,18]{1,0:T(8,128)} %kmat_ref.3, f32[3,3,16,256]{3,2,1,0:T(8,128)} %body_ref.3, ...), custom_call_target="tpu_custom_call" | custom-call | tf_op jit(solution)/shard_map/pallas_call | solution.py:161
  69.5 1.9 %collective-permute-start.9 = (f32[768]{0:T(1024)S(1)}, f32[768]{0:T(1024)S(1)}, u32[]{:S(2)}, u32[]{:S(2)}) collective-permute-start(f32[768]{0:T(1024)S(1)} %reshape.518), channel_id=1, source_target_pairs={{16,0},{32,16},{48,32},{64,48},{80,64},{96,80},{112,96},{128,112},... | collective-permute-start | bytes 9224 | tf_op jit(solution)/shard_map/ppermute | solution.py:307
  71.4 2.4 %collective-permute-start.8 = (f32[768]{0:T(1024)S(1)}, f32[768]{0:T(1024)S(1)}, u32[]{:S(2)}, u32[]{:S(2)}) collective-permute-start(f32[768]{0:T(1024)S(1)} %reshape.516), channel_id=1, source_target_pairs={{0,16},{16,32},{32,48},{48,64},{64,80},{80,96},{96,112},{112,128},... | collective-permute-start | bytes 9224 | tf_op jit(solution)/shard_map/ppermute | solution.py:307
  74.1 3.5 %collective-permute-done.8 = f32[768]{0:T(1024)S(1)} collective-permute-done((f32[768]{0:T(1024)S(1)}, f32[768]{0:T(1024)S(1)}, u32[]{:S(2)}, u32[]{:S(2)}) %collective-permute-start.8) | collective-permute-done | bytes 3104 | tf_op jit(solution)/shard_map/ppermute | solution.py:307
  77.6 2.4 %collective-permute-start.11 = (f32[1280]{0:T(1024)S(1)}, f32[1280]{0:T(1024)S(1)}, u32[]{:S(2)}, u32[]{:S(2)}) collective-permute-start(f32[1280]{0:T(1024)S(1)} %reshape.522), channel_id=1, source_target_pairs={{4,0},{8,4},{12,8},{5,1},{9,5},{13,9},{6,2},{10,6},{14,10},{7,3},{... | collective-permute-start | bytes 15368 | tf_op jit(solution)/shard_map/ppermute | solution.py:307
  80.0 1.3 %collective-permute-start.10 = (f32[1280]{0:T(1024)S(1)}, f32[1280]{0:T(1024)S(1)}, u32[]{:S(2)}, u32[]{:S(2)}) collective-permute-start(f32[1280]{0:T(1024)S(1)} %reshape.520), channel_id=1, source_target_pairs={{0,4},{4,8},{8,12},{1,5},{5,9},{9,13},{2,6},{6,10},{10,14},{3,7},{... | collective-permute-start | bytes 15368 | tf_op jit(solution)/shard_map/ppermute | solution.py:307
  81.5 4.0 %collective-permute-done.10 = f32[1280]{0:T(1024)S(1)} collective-permute-done((f32[1280]{0:T(1024)S(1)}, f32[1280]{0:T(1024)S(1)}, u32[]{:S(2)}, u32[]{:S(2)}) %collective-permute-start.10) | collective-permute-done | bytes 5152 | tf_op jit(solution)/shard_map/ppermute | solution.py:307
  85.6 1.3 %fusion.11 = f32[2,64,256]{2,1,0:T(8,128)} fusion(s32[1152]{0:T(1024)S(1)} %get-tuple-element.55, f32[2,1152]{1,0:T(2,128)S(1)} %bitcast.175, f32[1152,64]{0,1:T(8,128)S(1)} %fusion.27, f32[1,64,256]{2,1,0:T(8,128)S(1)} %fusion.54, f32[1,64,256]{2,1,0:T(8,128)S(1)} %fusion.60), kind=kOutput, calls=%fused_computation.11 | convolution fusion | flops 453492736 | bytes 570880 | tf_op jit(solution)/shard_map/ksr,sc->krc/dot_general | solution.py:189
  (129 shorter events, 6.3 us)
Async XLA Ops:
  0.6 2.7 %copy-start.6 = (s32[16,256]{1,0:T(8,128)S(1)}, s32[16,256]{1,0:T(8,128)}, u32[]{:S(2)}) copy-start(s32[16,256]{1,0:T(8,128)} %param.18) | copy-start | bytes 49156
  1.4 1.9 %copy-start = (f32[3,3,16,256]{3,2,1,0:T(8,128)S(1)}, f32[3,3,16,256]{3,2,1,0:T(8,128)}, u32[]{:S(2)}) copy-start(f32[3,3,16,256]{3,2,1,0:T(8,128)} %param.15) | copy-start | bytes 442372
  1.4 1.9 %copy-start.3 = (f32[3,16,256]{2,1,0:T(8,128)S(1)}, f32[3,16,256]{2,1,0:T(8,128)}, u32[]{:S(2)}) copy-start(f32[3,16,256]{2,1,0:T(8,128)} %param.16) | copy-start | bytes 147460
  1.5 1.9 %copy-start.1 = (f32[2,64,256]{2,1,0:T(8,128)S(1)}, f32[2,64,256]{2,1,0:T(8,128)}, u32[]{:S(2)}) copy-start(f32[2,64,256]{2,1,0:T(8,128)} %param.11) | copy-start | bytes 393220
  1.5 1.9 %copy-start.2 = (f32[64,256]{1,0:T(8,128)S(1)}, f32[64,256]{1,0:T(8,128)}, u32[]{:S(2)}) copy-start(f32[64,256]{1,0:T(8,128)} %param.12) | copy-start | bytes 196612
  3.2 5.9 %copy-start.7 = (s32[1,9,128]{2,0,1:T(1,128)S(1)}, s32[1,9,128]{2,0,1:T(1,128)}, u32[]{:S(2)}) copy-start(s32[1,9,128]{2,0,1:T(1,128)} %param.20) | copy-start | bytes 13828
  3.5 5.7 %collective-permute-start.1 = (f32[4864]{0:T(1024)S(1)}, f32[4864]{0:T(1024)S(1)}, u32[]{:S(2)}, u32[]{:S(2)}) collective-permute-start(f32[4864]{0:T(1024)S(1)} %pad_maximum_fusion.9), channel_id=1, source_target_pairs={{16,0},{32,16},{48,32},{64,48},{80,64},{96,80},{112,96},{128,112},... | collective-permute-start | bytes 58376 | tf_op jit(solution)/shard_map/ppermute | solution.py:307
  7.1 6.3 %collective-permute-start = (f32[4864]{0:T(1024)S(1)}, f32[4864]{0:T(1024)S(1)}, u32[]{:S(2)}, u32[]{:S(2)}) collective-permute-start(f32[4864]{0:T(1024)S(1)} %pad_maximum_fusion.8), channel_id=1, source_target_pairs={{0,16},{16,32},{32,48},{48,64},{64,80},{80,96},{96,112},{112,128},... | collective-permute-start | bytes 58376 | tf_op jit(solution)/shard_map/ppermute | solution.py:307
  14.4 4.5 %collective-permute-start.3 = (f32[1712]{0:T(1024)S(1)}, f32[1712]{0:T(1024)S(1)}, u32[]{:S(2)}, u32[]{:S(2)}) collective-permute-start(f32[1712]{0:T(1024)S(1)} %concatenate.62), channel_id=1, source_target_pairs={{4,0},{8,4},{12,8},{5,1},{9,5},{13,9},{6,2},{10,6},{14,10},{7,3},{... | collective-permute-start | bytes 20552 | tf_op jit(solution)/shard_map/ppermute | solution.py:307
  17.3 5.5 %collective-permute-start.2 = (f32[1712]{0:T(1024)S(1)}, f32[1712]{0:T(1024)S(1)}, u32[]{:S(2)}, u32[]{:S(2)}) collective-permute-start(f32[1712]{0:T(1024)S(1)} %concatenate.61), channel_id=1, source_target_pairs={{0,4},{4,8},{8,12},{1,5},{5,9},{9,13},{2,6},{6,10},{10,14},{3,7},{... | collective-permute-start | bytes 20552 | tf_op jit(solution)/shard_map/ppermute | solution.py:307
  24.5 23.0 %all-to-all-start = ((f32[4,4,18,258]{3,1,2,0:T(4,128)}), f32[4,4,18,258]{3,1,2,0:T(4,128)S(1)}, u32[]{:S(2)}, u32[]{:S(2)}) async-start(f32[4,4,18,258]{3,1,2,0:T(4,128)} %copy.61), calls=%async_computation | async-start | bytes 884736 | tf_op jit(solution)/shard_map/all_to_all | solution.py:209
  30.4 5.3 %collective-permute-start.5 = (f32[768]{0:T(1024)S(1)}, f32[768]{0:T(1024)S(1)}, u32[]{:S(2)}, u32[]{:S(2)}) collective-permute-start(f32[768]{0:T(1024)S(1)} %reshape.509), channel_id=1, source_target_pairs={{16,0},{32,16},{48,32},{64,48},{80,64},{96,80},{112,96},{128,112},... | collective-permute-start | bytes 9224 | tf_op jit(solution)/shard_map/ppermute | solution.py:307
  32.4 6.1 %collective-permute-start.4 = (f32[768]{0:T(1024)S(1)}, f32[768]{0:T(1024)S(1)}, u32[]{:S(2)}, u32[]{:S(2)}) collective-permute-start(f32[768]{0:T(1024)S(1)} %reshape.507), channel_id=1, source_target_pairs={{0,16},{16,32},{32,48},{48,64},{64,80},{80,96},{96,112},{112,128},... | collective-permute-start | bytes 9224 | tf_op jit(solution)/shard_map/ppermute | solution.py:307
  38.8 4.5 %collective-permute-start.7 = (f32[54]{0:T(128)S(1)}, f32[54]{0:T(128)S(1)}, u32[]{:S(2)}, u32[]{:S(2)}) collective-permute-start(f32[54]{0:T(128)S(1)} %reshape.513), channel_id=1, source_target_pairs={{4,0},{8,4},{12,8},{5,1},{9,5},{13,9},{6,2},{10,6},{14,10},{7,3},{... | collective-permute-start | bytes 656 | tf_op jit(solution)/shard_map/ppermute | solution.py:307
  41.2 5.4 %collective-permute-start.6 = (f32[54]{0:T(128)S(1)}, f32[54]{0:T(128)S(1)}, u32[]{:S(2)}, u32[]{:S(2)}) collective-permute-start(f32[54]{0:T(128)S(1)} %reshape.511), channel_id=1, source_target_pairs={{0,4},{4,8},{8,12},{1,5},{5,9},{9,13},{2,6},{6,10},{10,14},{3,7},{... | collective-permute-start | bytes 656 | tf_op jit(solution)/shard_map/ppermute | solution.py:307
  59.0 10.4 %all-to-all-start.1 = ((f32[4,2,9,128]{3,1,2,0:T(2,128)}), f32[4,2,9,128]{3,1,2,0:T(2,128)S(1)}, u32[]{:S(2)}, u32[]{:S(2)}) async-start(f32[4,2,9,128]{3,1,2,0:T(2,128)} %broadcast_in_dim.80), calls=%async_computation.1 | async-start | bytes 73728 | tf_op jit(solution)/shard_map/all_to_all | solution.py:195
  64.0 9.9 %copy-start.4 = (f32[64,256]{1,0:T(8,128)S(1)}, f32[64,256]{1,0:T(8,128)}, u32[]{:S(2)}) copy-start(f32[64,256]{1,0:T(8,128)} %param.13) | copy-start | bytes 196612
  64.0 9.9 %copy-start.5 = (f32[2,64,256]{2,1,0:T(8,128)S(1)}, f32[2,64,256]{2,1,0:T(8,128)}, u32[]{:S(2)}) copy-start(f32[2,64,256]{2,1,0:T(8,128)} %param.14) | copy-start | bytes 393220
  69.5 4.6 %collective-permute-start.9 = (f32[768]{0:T(1024)S(1)}, f32[768]{0:T(1024)S(1)}, u32[]{:S(2)}, u32[]{:S(2)}) collective-permute-start(f32[768]{0:T(1024)S(1)} %reshape.518), channel_id=1, source_target_pairs={{16,0},{32,16},{48,32},{64,48},{80,64},{96,80},{112,96},{128,112},... | collective-permute-start | bytes 9224 | tf_op jit(solution)/shard_map/ppermute | solution.py:307
  71.4 6.1 %collective-permute-start.8 = (f32[768]{0:T(1024)S(1)}, f32[768]{0:T(1024)S(1)}, u32[]{:S(2)}, u32[]{:S(2)}) collective-permute-start(f32[768]{0:T(1024)S(1)} %reshape.516), channel_id=1, source_target_pairs={{0,16},{16,32},{32,48},{48,64},{64,80},{80,96},{96,112},{112,128},... | collective-permute-start | bytes 9224 | tf_op jit(solution)/shard_map/ppermute | solution.py:307
  77.6 3.9 %collective-permute-start.11 = (f32[1280]{0:T(1024)S(1)}, f32[1280]{0:T(1024)S(1)}, u32[]{:S(2)}, u32[]{:S(2)}) collective-permute-start(f32[1280]{0:T(1024)S(1)} %reshape.522), channel_id=1, source_target_pairs={{4,0},{8,4},{12,8},{5,1},{9,5},{13,9},{6,2},{10,6},{14,10},{7,3},{... | collective-permute-start | bytes 15368 | tf_op jit(solution)/shard_map/ppermute | solution.py:307
  80.0 5.5 %collective-permute-start.10 = (f32[1280]{0:T(1024)S(1)}, f32[1280]{0:T(1024)S(1)}, u32[]{:S(2)}, u32[]{:S(2)}) collective-permute-start(f32[1280]{0:T(1024)S(1)} %reshape.520), channel_id=1, source_target_pairs={{0,4},{4,8},{8,12},{1,5},{5,9},{9,13},{2,6},{6,10},{10,14},{3,7},{... | collective-permute-start | bytes 15368 | tf_op jit(solution)/shard_map/ppermute | solution.py:307

commit v13 on v11

--- a/solution.py
+++ b/solution.py
@@ -176,12 +176,10 @@
     return jnp.einsum("ksr,sc->krc", weighted, pick_col, precision=HIGH)
 
 
-def layer_total(part):
-    count = lax.axis_size("layer")
-    copies = jnp.broadcast_to(part[None], (count,) + part.shape)
+def layer_total(copies):
     gathered = lax.all_to_all(copies, "layer", 0, 0, tiled=True)
     total = gathered[0]
-    for source in range(1, count):
+    for source in range(1, copies.shape[0]):
         total = total + gathered[source]
     return total
 
@@ -369,8 +367,11 @@
     fld = fem_inputs(extended_layers, widened[-1])
     partial_residual, depth_sum = fem_first(grid, fld, element_matrix, body_force)
     stokes_residual = fem_second(grid, fld, element_matrix, body_force, partial_residual)
-    bucket = gather_slots(depth_sum, col_row, col_col).reshape(2, 9, slot_count)
-    depth_total = layer_total(bucket)
+    count = lax.axis_size("layer")
+    cols_taken = jnp.einsum("krc,sc->krs", depth_sum, col_col, precision=HIGH)
+    spread = jnp.broadcast_to(cols_taken[None], (count,) + cols_taken.shape)
+    copies = jnp.sum(jnp.where(col_row.T[None, None] > 0.5, spread, 0.0), axis=2)
+    depth_total = layer_total(copies.reshape(count, 2, 9, slot_count))
     depth_total, stokes_residual = lax.optimization_barrier((depth_total, stokes_residual))
     grid_back = depth_total.reshape(2, 3, 3, slot_count)
     (back_x,) = packed_halo((grid_back,), (1,), "mx")

time: 86.7 us -> 86.8 us (level)
    dot_general x2 -> x1, matrix products: 3.15 us -> 1.68 us  [gather_slots(): cols_taken = jnp.einsum('krc,sc->krs', field, pick_col, precision=HIGH)]
    dot_general x0 -> x1, matrix products: none -> 1.46 us  [per_device(): cols_taken = jnp.einsum('krc,sc->krs', depth_sum, col_col, precision=HIGH)]
where the time goes in v13:
time: 86.8 us; the launch traced here: 86.1 us
  starting transfers between devices  35 us (40%)
  waiting for transfers between devices  22.1 us (25%)
  Pallas kernels  13.1 us (15%)
  matrix products  5.34 us (6%)
  other arithmetic  4.8 us (6%)
  local copies, waits for them, and re-layouts  4.3 us (5%)
  between operations  1.43 us (2%)
    ppermute x6, waiting for transfers between devices, exchange(): lax.ppermute(sent_up, axis, up)  22.1 us
    ppermute x6, starting transfers between devices, exchange(): lax.ppermute(sent_down, axis, down)  14.8 us
    ppermute x6, starting transfers between devices, exchange(): lax.ppermute(sent_up, axis, up)  10.6 us
    pallas_call x1, Pallas kernels, fem_first(): pl.pallas_call(functools.partial(fem_horizontal, grid), out_shape=(jax.Sh...  7.76 us
    pallas_call x1, Pallas kernels, fem_second(): pl.pallas_call(functools.partial(fem_vertical, grid), out_shape=jax.Shape...  5.32 us
    all_to_all x1, starting transfers between devices, layer_neighbours(): lax.all_to_all(jnp.concatenate(chunks, 0), 'layer', 0, 0, tiled=True)  4.83 us
    all_to_all x1, starting transfers between devices, layer_total(): gathered = lax.all_to_all(copies, 'layer', 0, 0, tiled=True)  4.8 us
    dot_general x2, matrix products, scatter_slots(): return jnp.einsum('ksr,sc->krc', weighted, pick_col, precision=HIGH)  1.87 us
  transfers between devices with their start and end apart: 14, of which 6 were waited for; matrix products, arithmetic and copies ran while one was open for 5% of the time, Pallas kernels for 6%

profile of v13, /device:TPU:410, one launch (start us, length us, event | category | flops | bytes accessed | tf_op | source)
XLA Modules:
  0.0 86.1 jit_solution(1186699727068607564)
XLA Ops:
  0.7 0.8 reduce.2
  1.6 1.7 %fusion.1 = f32[2,1152]{1,0:T(2,128)S(1)} fusion(f32[2,64,256]{2,1,0:T(8,128)} %param.11, s32[1152]{0:T(1024)S(1)} %get-tuple-element.56, pred[64,1152]{1,0:T(8,128)(4,1)S(1)} %convert_compare_fusion), kind=kOutput, calls=%fused_computation.2 | convolution fusion | flops 453572352 | bytes 218624 | tf_op jit(solution)/shard_map/krc,sc->krs/dot_general | solution.py:170
  3.5 3.6 %collective-permute-start.1 = (f32[4864]{0:T(1024)S(1)}, f32[4864]{0:T(1024)S(1)}, u32[]{:S(2)}, u32[]{:S(2)}) collective-permute-start(f32[4864]{0:T(1024)S(1)} %pad_maximum_fusion.16), channel_id=1, source_target_pairs={{16,0},{32,16},{48,32},{64,48},{80,64},{96,80},{112,96},{128,112},... | collective-permute-start | bytes 58376 | tf_op jit(solution)/shard_map/ppermute | solution.py:292
  7.1 1.9 %collective-permute-start = (f32[4864]{0:T(1024)S(1)}, f32[4864]{0:T(1024)S(1)}, u32[]{:S(2)}, u32[]{:S(2)}) collective-permute-start(f32[4864]{0:T(1024)S(1)} %pad_maximum_fusion.15), channel_id=1, source_target_pairs={{0,16},{16,32},{32,48},{48,64},{64,80},{80,96},{96,112},{112,128},... | collective-permute-start | bytes 58376 | tf_op jit(solution)/shard_map/ppermute | solution.py:292
  9.2 4.2 %collective-permute-done = f32[4864]{0:T(1024)S(1)} collective-permute-done((f32[4864]{0:T(1024)S(1)}, f32[4864]{0:T(1024)S(1)}, u32[]{:S(2)}, u32[]{:S(2)}) %collective-permute-start) | collective-permute-done | bytes 19488 | tf_op jit(solution)/shard_map/ppermute | solution.py:292
  14.5 2.6 %collective-permute-start.3 = (f32[1712]{0:T(1024)S(1)}, f32[1712]{0:T(1024)S(1)}, u32[]{:S(2)}, u32[]{:S(2)}) collective-permute-start(f32[1712]{0:T(1024)S(1)} %concatenate.71), channel_id=1, source_target_pairs={{4,0},{8,4},{12,8},{5,1},{9,5},{13,9},{6,2},{10,6},{14,10},{7,3},{... | collective-permute-start | bytes 20552 | tf_op jit(solution)/shard_map/ppermute | solution.py:292
  17.4 1.3 %collective-permute-start.2 = (f32[1712]{0:T(1024)S(1)}, f32[1712]{0:T(1024)S(1)}, u32[]{:S(2)}, u32[]{:S(2)}) collective-permute-start(f32[1712]{0:T(1024)S(1)} %concatenate.70), channel_id=1, source_target_pairs={{0,4},{4,8},{8,12},{1,5},{5,9},{9,13},{2,6},{6,10},{10,14},{3,7},{... | collective-permute-start | bytes 20552 | tf_op jit(solution)/shard_map/ppermute | solution.py:292
  18.6 0.3 fusion.16
  19.3 3.6 %collective-permute-done.2 = f32[1712]{0:T(1024)S(1)} collective-permute-done((f32[1712]{0:T(1024)S(1)}, f32[1712]{0:T(1024)S(1)}, u32[]{:S(2)}, u32[]{:S(2)}) %collective-permute-start.2) | collective-permute-done | bytes 6880 | tf_op jit(solution)/shard_map/ppermute | solution.py:292
  23.2 0.3 pad_maximum_fusion.2
  23.7 0.9 %pad_maximum_fusion.3 = f32[4,4,18,258]{3,1,2,0:T(4,128)} fusion(f32[1,4,18,258]{3,1,2,0:T(4,128)S(1)} %get-tuple-element.40, f32[1,4,18,258]{3,1,2,0:T(4,128)S(1)} %get-tuple-element.39, f32[1,4,18,258]{3,1,2,0:T(4,128)S(1)} %get-tuple-element.38, f32[1,4,18,258]{3,1,2,0:T(4,128)S(1)} %get-tuple-element.37), kind=kLoop, calls=%fused_computation.36 | loop fusion | flops 222912 | bytes 594432 | tf_op jit(solution)/shard_map/concatenate | solution.py:194
  24.6 4.8 %all-to-all-start = ((f32[4,4,18,258]{3,1,2,0:T(4,128)}), f32[4,4,18,258]{3,1,2,0:T(4,128)S(1)}, u32[]{:S(2)}, u32[]{:S(2)}) async-start(f32[4,4,18,258]{3,1,2,0:T(4,128)} %pad_maximum_fusion.3), calls=%async_computation | async-start | bytes 884736 | tf_op jit(solution)/shard_map/all_to_all | solution.py:194
  29.9 0.5 fusion.6
  30.4 1.9 %collective-permute-start.5 = (f32[768]{0:T(1024)S(1)}, f32[768]{0:T(1024)S(1)}, u32[]{:S(2)}, u32[]{:S(2)}) collective-permute-start(f32[768]{0:T(1024)S(1)} %reshape.600), channel_id=1, source_target_pairs={{16,0},{32,16},{48,32},{64,48},{80,64},{96,80},{112,96},{128,112},... | collective-permute-start | bytes 9224 | tf_op jit(solution)/shard_map/ppermute | solution.py:292
  32.4 2.4 %collective-permute-start.4 = (f32[768]{0:T(1024)S(1)}, f32[768]{0:T(1024)S(1)}, u32[]{:S(2)}, u32[]{:S(2)}) collective-permute-start(f32[768]{0:T(1024)S(1)} %reshape.598), channel_id=1, source_target_pairs={{0,16},{16,32},{32,48},{48,64},{64,80},{80,96},{96,112},{112,128},... | collective-permute-start | bytes 9224 | tf_op jit(solution)/shard_map/ppermute | solution.py:292
  35.5 3.0 %collective-permute-done.4 = f32[768]{0:T(1024)S(1)} collective-permute-done((f32[768]{0:T(1024)S(1)}, f32[768]{0:T(1024)S(1)}, u32[]{:S(2)}, u32[]{:S(2)}) %collective-permute-start.4) | collective-permute-done | bytes 3104 | tf_op jit(solution)/shard_map/ppermute | solution.py:292
  38.8 2.4 %collective-permute-start.7 = (f32[54]{0:T(128)S(1)}, f32[54]{0:T(128)S(1)}, u32[]{:S(2)}, u32[]{:S(2)}) collective-permute-start(f32[54]{0:T(128)S(1)} %reshape.604), channel_id=1, source_target_pairs={{4,0},{8,4},{12,8},{5,1},{9,5},{13,9},{6,2},{10,6},{14,10},{7,3},{... | collective-permute-start | bytes 656 | tf_op jit(solution)/shard_map/ppermute | solution.py:292
  41.2 1.3 %collective-permute-start.6 = (f32[54]{0:T(128)S(1)}, f32[54]{0:T(128)S(1)}, u32[]{:S(2)}, u32[]{:S(2)}) collective-permute-start(f32[54]{0:T(128)S(1)} %reshape.602), channel_id=1, source_target_pairs={{0,4},{4,8},{8,12},{1,5},{5,9},{9,13},{2,6},{6,10},{10,14},{3,7},{... | collective-permute-start | bytes 656 | tf_op jit(solution)/shard_map/ppermute | solution.py:292
  42.9 3.7 %collective-permute-done.6 = f32[54]{0:T(128)S(1)} collective-permute-done((f32[54]{0:T(128)S(1)}, f32[54]{0:T(128)S(1)}, u32[]{:S(2)}, u32[]{:S(2)}) %collective-permute-start.6) | collective-permute-done | bytes 248 | tf_op jit(solution)/shard_map/ppermute | solution.py:292
  47.4 0.9 %pad.4.fld_ref = f32[21,24,384]{2,1,0:T(8,128)} pad(f32[21,18,258]{2,1,0:T(8,128)S(1)} %fusion.17, f32[]{:T(128)} %constant.67.clone.1), padding=0_0x0_6x0_126 | pad | bytes 1164244 | tf_op jit(solution)/shard_map/jit(_pad)/pad | solution.py:118
  48.4 7.8 %shard_map.122 = (f32[3,3,16,256]{3,2,1,0:T(8,128)}, f32[2,16,256]{2,1,0:T(8,128)}) custom-call(f32[21,24,384]{2,1,0:T(8,128)} %pad.4.fld_ref, f32[18,18]{1,0:T(8,128)} %kmat_ref.3, f32[3,3,16,256]{3,2,1,0:T(8,128)} %body_ref.3), custom_call_target="tpu_custom_call" | custom-call | tf_op jit(solution)/shard_map/pallas_call | solution.py:133
  56.1 1.5 %fusion.4 = f32[2,16,1152]{2,1,0:T(8,128)S(1)} fusion(f32[2,16,256]{2,1,0:T(8,128)} %get-tuple-element.6, s32[1152]{0:T(1024)S(1)} %get-tuple-element.54), kind=kOutput, calls=%fused_computation.6 | convolution fusion | flops 113541120 | bytes 184832 | tf_op jit(solution)/shard_map/krc,sc->krs/dot_general | solution.py:371
  57.6 0.7 select_reduce_fusion
  58.2 4.8 %all-to-all-start.1 = ((f32[4,2,9,128]{3,1,2,0:T(2,128)}), f32[4,2,9,128]{3,1,2,0:T(2,128)S(1)}, u32[]{:S(2)}, u32[]{:S(2)}) async-start(f32[4,2,9,128]{3,1,2,0:T(2,128)} %bitcast.25), calls=%async_computation.1 | async-start | bytes 73728 | tf_op jit(solution)/shard_map/all_to_all | solution.py:180
  63.3 5.3 %shard_map.123 = f32[3,3,16,256]{3,2,1,0:T(8,128)} custom-call(f32[21,24,384]{2,1,0:T(8,128)} %pad.4.fld_ref, f32[18,18]{1,0:T(8,128)} %kmat_ref.3, f32[3,3,16,256]{3,2,1,0:T(8,128)} %body_ref.3, f32[3,3,16,256]{3,2,1,0:T(8,128)} %get-tuple-element.7.prev_ref), custom_call_target="tpu_custom_call" | custom-call | tf_op jit(solution)/shard_map/pallas_call | solution.py:148
  68.6 1.9 %collective-permute-start.9 = (f32[768]{0:T(1024)S(1)}, f32[768]{0:T(1024)S(1)}, u32[]{:S(2)}, u32[]{:S(2)}) collective-permute-start(f32[768]{0:T(1024)S(1)} %reshape.614), channel_id=1, source_target_pairs={{16,0},{32,16},{48,32},{64,48},{80,64},{96,80},{112,96},{128,112},... | collective-permute-start | bytes 9224 | tf_op jit(solution)/shard_map/ppermute | solution.py:292
  70.6 2.4 %collective-permute-start.8 = (f32[768]{0:T(1024)S(1)}, f32[768]{0:T(1024)S(1)}, u32[]{:S(2)}, u32[]{:S(2)}) collective-permute-start(f32[768]{0:T(1024)S(1)} %reshape.612), channel_id=1, source_target_pairs={{0,16},{16,32},{32,48},{48,64},{64,80},{80,96},{96,112},{112,128},... | collective-permute-start | bytes 9224 | tf_op jit(solution)/shard_map/ppermute | solution.py:292
  73.2 3.5 %collective-permute-done.8 = f32[768]{0:T(1024)S(1)} collective-permute-done((f32[768]{0:T(1024)S(1)}, f32[768]{0:T(1024)S(1)}, u32[]{:S(2)}, u32[]{:S(2)}) %collective-permute-start.8) | collective-permute-done | bytes 3104 | tf_op jit(solution)/shard_map/ppermute | solution.py:292
  76.8 2.4 %collective-permute-start.11 = (f32[1280]{0:T(1024)S(1)}, f32[1280]{0:T(1024)S(1)}, u32[]{:S(2)}, u32[]{:S(2)}) collective-permute-start(f32[1280]{0:T(1024)S(1)} %reshape.618), channel_id=1, source_target_pairs={{4,0},{8,4},{12,8},{5,1},{9,5},{13,9},{6,2},{10,6},{14,10},{7,3},{... | collective-permute-start | bytes 15368 | tf_op jit(solution)/shard_map/ppermute | solution.py:292
  79.2 1.3 %collective-permute-start.10 = (f32[1280]{0:T(1024)S(1)}, f32[1280]{0:T(1024)S(1)}, u32[]{:S(2)}, u32[]{:S(2)}) collective-permute-start(f32[1280]{0:T(1024)S(1)} %reshape.616), channel_id=1, source_target_pairs={{0,4},{4,8},{8,12},{1,5},{5,9},{9,13},{2,6},{6,10},{10,14},{3,7},{... | collective-permute-start | bytes 15368 | tf_op jit(solution)/shard_map/ppermute | solution.py:292
  80.7 4.0 %collective-permute-done.10 = f32[1280]{0:T(1024)S(1)} collective-permute-done((f32[1280]{0:T(1024)S(1)}, f32[1280]{0:T(1024)S(1)}, u32[]{:S(2)}, u32[]{:S(2)}) %collective-permute-start.10) | collective-permute-done | bytes 5152 | tf_op jit(solution)/shard_map/ppermute | solution.py:292
  84.7 1.3 %fusion.12 = f32[2,64,256]{2,1,0:T(8,128)} fusion(s32[1152]{0:T(1024)S(1)} %get-tuple-element.56, f32[2,1152]{1,0:T(2,128)S(1)} %bitcast.148, f32[1152,64]{0,1:T(8,128)S(1)} %fusion.34, f32[1,64,256]{2,1,0:T(8,128)S(1)} %fusion.42, f32[1,64,256]{2,1,0:T(8,128)S(1)} %fusion.48), kind=kOutput, calls=%fused_computation.11 | convolution fusion | flops 453492736 | bytes 570880 | tf_op jit(solution)/shard_map/ksr,sc->krc/dot_general | solution.py:176
  (132 shorter events, 5.5 us)
Async XLA Ops:
  0.6 2.8 %copy-start.1 = (f32[2,64,256]{2,1,0:T(8,128)S(1)}, f32[2,64,256]{2,1,0:T(8,128)}, u32[]{:S(2)}) copy-start(f32[2,64,256]{2,1,0:T(8,128)} %param.11) | copy-start | bytes 393220
  0.6 2.7 %copy-start.6 = (s32[16,256]{1,0:T(8,128)S(1)}, s32[16,256]{1,0:T(8,128)}, u32[]{:S(2)}) copy-start(s32[16,256]{1,0:T(8,128)} %param.18) | copy-start | bytes 49156
  0.7 2.7 %copy-start.2 = (f32[3,16,256]{2,1,0:T(8,128)S(1)}, f32[3,16,256]{2,1,0:T(8,128)}, u32[]{:S(2)}) copy-start(f32[3,16,256]{2,1,0:T(8,128)} %param.16) | copy-start | bytes 147460
  0.7 2.7 %copy-start = (f32[3,3,16,256]{3,2,1,0:T(8,128)S(1)}, f32[3,3,16,256]{3,2,1,0:T(8,128)}, u32[]{:S(2)}) copy-start(f32[3,3,16,256]{3,2,1,0:T(8,128)} %param.15) | copy-start | bytes 442372
  0.7 2.8 %copy-start.3 = (f32[64,256]{1,0:T(8,128)S(1)}, f32[64,256]{1,0:T(8,128)}, u32[]{:S(2)}) copy-start(f32[64,256]{1,0:T(8,128)} %param.12) | copy-start | bytes 196612
  1.6 7.5 %copy-start.7 = (s32[1,9,128]{2,0,1:T(1,128)S(1)}, s32[1,9,128]{2,0,1:T(1,128)}, u32[]{:S(2)}) copy-start(s32[1,9,128]{2,0,1:T(1,128)} %param.20) | copy-start | bytes 13828
  3.5 5.7 %collective-permute-start.1 = (f32[4864]{0:T(1024)S(1)}, f32[4864]{0:T(1024)S(1)}, u32[]{:S(2)}, u32[]{:S(2)}) collective-permute-start(f32[4864]{0:T(1024)S(1)} %pad_maximum_fusion.16), channel_id=1, source_target_pairs={{16,0},{32,16},{48,32},{64,48},{80,64},{96,80},{112,96},{128,112},... | collective-permute-start | bytes 58376 | tf_op jit(solution)/shard_map/ppermute | solution.py:292
  7.1 6.3 %collective-permute-start = (f32[4864]{0:T(1024)S(1)}, f32[4864]{0:T(1024)S(1)}, u32[]{:S(2)}, u32[]{:S(2)}) collective-permute-start(f32[4864]{0:T(1024)S(1)} %pad_maximum_fusion.15), channel_id=1, source_target_pairs={{0,16},{16,32},{32,48},{48,64},{64,80},{80,96},{96,112},{112,128},... | collective-permute-start | bytes 58376 | tf_op jit(solution)/shard_map/ppermute | solution.py:292
  14.5 4.5 %collective-permute-start.3 = (f32[1712]{0:T(1024)S(1)}, f32[1712]{0:T(1024)S(1)}, u32[]{:S(2)}, u32[]{:S(2)}) collective-permute-start(f32[1712]{0:T(1024)S(1)} %concatenate.71), channel_id=1, source_target_pairs={{4,0},{8,4},{12,8},{5,1},{9,5},{13,9},{6,2},{10,6},{14,10},{7,3},{... | collective-permute-start | bytes 20552 | tf_op jit(solution)/shard_map/ppermute | solution.py:292
  17.4 5.5 %collective-permute-start.2 = (f32[1712]{0:T(1024)S(1)}, f32[1712]{0:T(1024)S(1)}, u32[]{:S(2)}, u32[]{:S(2)}) collective-permute-start(f32[1712]{0:T(1024)S(1)} %concatenate.70), channel_id=1, source_target_pairs={{0,4},{4,8},{8,12},{1,5},{5,9},{9,13},{2,6},{6,10},{10,14},{3,7},{... | collective-permute-start | bytes 20552 | tf_op jit(solution)/shard_map/ppermute | solution.py:292
  24.6 22.5 %all-to-all-start = ((f32[4,4,18,258]{3,1,2,0:T(4,128)}), f32[4,4,18,258]{3,1,2,0:T(4,128)S(1)}, u32[]{:S(2)}, u32[]{:S(2)}) async-start(f32[4,4,18,258]{3,1,2,0:T(4,128)} %pad_maximum_fusion.3), calls=%async_computation | async-start | bytes 884736 | tf_op jit(solution)/shard_map/all_to_all | solution.py:194
  30.4 5.0 %collective-permute-start.5 = (f32[768]{0:T(1024)S(1)}, f32[768]{0:T(1024)S(1)}, u32[]{:S(2)}, u32[]{:S(2)}) collective-permute-start(f32[768]{0:T(1024)S(1)} %reshape.600), channel_id=1, source_target_pairs={{16,0},{32,16},{48,32},{64,48},{80,64},{96,80},{112,96},{128,112},... | collective-permute-start | bytes 9224 | tf_op jit(solution)/shard_map/ppermute | solution.py:292
  32.4 6.1 %collective-permute-start.4 = (f32[768]{0:T(1024)S(1)}, f32[768]{0:T(1024)S(1)}, u32[]{:S(2)}, u32[]{:S(2)}) collective-permute-start(f32[768]{0:T(1024)S(1)} %reshape.598), channel_id=1, source_target_pairs={{0,16},{16,32},{32,48},{48,64},{64,80},{80,96},{96,112},{112,128},... | collective-permute-start | bytes 9224 | tf_op jit(solution)/shard_map/ppermute | solution.py:292
  38.8 4.0 %collective-permute-start.7 = (f32[54]{0:T(128)S(1)}, f32[54]{0:T(128)S(1)}, u32[]{:S(2)}, u32[]{:S(2)}) collective-permute-start(f32[54]{0:T(128)S(1)} %reshape.604), channel_id=1, source_target_pairs={{4,0},{8,4},{12,8},{5,1},{9,5},{13,9},{6,2},{10,6},{14,10},{7,3},{... | collective-permute-start | bytes 656 | tf_op jit(solution)/shard_map/ppermute | solution.py:292
  41.2 5.4 %collective-permute-start.6 = (f32[54]{0:T(128)S(1)}, f32[54]{0:T(128)S(1)}, u32[]{:S(2)}, u32[]{:S(2)}) collective-permute-start(f32[54]{0:T(128)S(1)} %reshape.602), channel_id=1, source_target_pairs={{0,4},{4,8},{8,12},{1,5},{5,9},{9,13},{2,6},{6,10},{10,14},{3,7},{... | collective-permute-start | bytes 656 | tf_op jit(solution)/shard_map/ppermute | solution.py:292
  58.2 10.3 %all-to-all-start.1 = ((f32[4,2,9,128]{3,1,2,0:T(2,128)}), f32[4,2,9,128]{3,1,2,0:T(2,128)S(1)}, u32[]{:S(2)}, u32[]{:S(2)}) async-start(f32[4,2,9,128]{3,1,2,0:T(2,128)} %bitcast.25), calls=%async_computation.1 | async-start | bytes 73728 | tf_op jit(solution)/shard_map/all_to_all | solution.py:180
  63.2 9.8 %copy-start.4 = (f32[64,256]{1,0:T(8,128)S(1)}, f32[64,256]{1,0:T(8,128)}, u32[]{:S(2)}) copy-start(f32[64,256]{1,0:T(8,128)} %param.13) | copy-start | bytes 196612
  63.3 9.8 %copy-start.5 = (f32[2,64,256]{2,1,0:T(8,128)S(1)}, f32[2,64,256]{2,1,0:T(8,128)}, u32[]{:S(2)}) copy-start(f32[2,64,256]{2,1,0:T(8,128)} %param.14) | copy-start | bytes 393220
  68.6 4.6 %collective-permute-start.9 = (f32[768]{0:T(1024)S(1)}, f32[768]{0:T(1024)S(1)}, u32[]{:S(2)}, u32[]{:S(2)}) collective-permute-start(f32[768]{0:T(1024)S(1)} %reshape.614), channel_id=1, source_target_pairs={{16,0},{32,16},{48,32},{64,48},{80,64},{96,80},{112,96},{128,112},... | collective-permute-start | bytes 9224 | tf_op jit(solution)/shard_map/ppermute | solution.py:292
  70.6 6.1 %collective-permute-start.8 = (f32[768]{0:T(1024)S(1)}, f32[768]{0:T(1024)S(1)}, u32[]{:S(2)}, u32[]{:S(2)}) collective-permute-start(f32[768]{0:T(1024)S(1)} %reshape.612), channel_id=1, source_target_pairs={{0,16},{16,32},{32,48},{48,64},{64,80},{80,96},{96,112},{112,128},... | collective-permute-start | bytes 9224 | tf_op jit(solution)/shard_map/ppermute | solution.py:292
  76.8 3.9 %collective-permute-start.11 = (f32[1280]{0:T(1024)S(1)}, f32[1280]{0:T(1024)S(1)}, u32[]{:S(2)}, u32[]{:S(2)}) collective-permute-start(f32[1280]{0:T(1024)S(1)} %reshape.618), channel_id=1, source_target_pairs={{4,0},{8,4},{12,8},{5,1},{9,5},{13,9},{6,2},{10,6},{14,10},{7,3},{... | collective-permute-start | bytes 15368 | tf_op jit(solution)/shard_map/ppermute | solution.py:292
  79.2 5.5 %collective-permute-start.10 = (f32[1280]{0:T(1024)S(1)}, f32[1280]{0:T(1024)S(1)}, u32[]{:S(2)}, u32[]{:S(2)}) collective-permute-start(f32[1280]{0:T(1024)S(1)} %reshape.616), channel_id=1, source_target_pairs={{0,4},{4,8},{8,12},{1,5},{5,9},{9,13},{2,6},{6,10},{10,14},{3,7},{... | collective-permute-start | bytes 15368 | tf_op jit(solution)/shard_map/ppermute | solution.py:292

commit v14 on v11

--- a/solution.py
+++ b/solution.py
@@ -167,13 +167,13 @@
 
 
 def gather_slots(field, pick_row, pick_col):
-    cols_taken = jnp.einsum("krc,sc->krs", field, pick_col, precision=HIGH)
+    cols_taken = jnp.einsum("krc,sc->krs", field, pick_col, precision=lax.Precision.HIGH)
     return jnp.sum(jnp.where(pick_row.T[None] > 0.5, cols_taken, 0.0), axis=1)
 
 
 def scatter_slots(values, pick_row, pick_col):
     weighted = pick_row[None] * values[:, :, None]
-    return jnp.einsum("ksr,sc->krc", weighted, pick_col, precision=HIGH)
+    return jnp.einsum("ksr,sc->krc", weighted, pick_col, precision=lax.Precision.HIGH)
 
 
 def layer_total(part):

time: 86.7 us -> 86 us (level)
  no operation moved by 1% of the time
where the time goes in v14:
time: 86 us; the launch traced here: 85.3 us
  starting transfers between devices  35 us (41%)
  waiting for transfers between devices  22.1 us (26%)
  Pallas kernels  13.1 us (15%)
  local copies, waits for them, and re-layouts  4.93 us (6%)
  matrix products  4.67 us (5%)
  other arithmetic  4.12 us (5%)
  between operations  1.44 us (2%)
    ppermute x6, waiting for transfers between devices, exchange(): lax.ppermute(sent_up, axis, up)  22.1 us
    ppermute x6, starting transfers between devices, exchange(): lax.ppermute(sent_down, axis, down)  14.8 us
    ppermute x6, starting transfers between devices, exchange(): lax.ppermute(sent_up, axis, up)  10.6 us
    pallas_call x1, Pallas kernels, fem_first(): pl.pallas_call(functools.partial(fem_horizontal, grid), out_shape=(jax.Sh...  7.76 us
    pallas_call x1, Pallas kernels, fem_second(): pl.pallas_call(functools.partial(fem_vertical, grid), out_shape=jax.Shape...  5.32 us
    all_to_all x1, starting transfers between devices, layer_neighbours(): lax.all_to_all(jnp.concatenate(chunks, 0), 'layer', 0, 0, tiled=True)  4.82 us
    all_to_all x1, starting transfers between devices, layer_total(): gathered = lax.all_to_all(copies, 'layer', 0, 0, tiled=True)  4.8 us
    dot_general x2, matrix products, gather_slots(): jnp.einsum('krc,sc->krs', field, pick_col, precision=lax.Precision.HIGH)  2.81 us
  transfers between devices with their start and end apart: 14, of which 6 were waited for; matrix products, arithmetic and copies ran while one was open for 5% of the time, Pallas kernels for 6%

profile of v14, /device:TPU:410, one launch (start us, length us, event | category | flops | bytes accessed | tf_op | source)
XLA Modules:
  0.0 85.3 jit_solution(11330199083806465491)
XLA Ops:
  0.7 0.8 reduce.2
  1.6 1.5 %fusion.1 = f32[2,1152]{1,0:T(2,128)S(1)} fusion(f32[2,64,256]{2,1,0:T(8,128)} %param.11, s32[1152]{0:T(1024)S(1)} %get-tuple-element.56, pred[64,1152]{1,0:T(8,128)(4,1)S(1)} %convert_compare_fusion), kind=kOutput, calls=%fused_computation.3 | convolution fusion | flops 227079936 | bytes 218624 | tf_op jit(solution)/shard_map/krc,sc->krs/dot_general | solution.py:170
  3.3 3.6 %collective-permute-start.1 = (f32[4864]{0:T(1024)S(1)}, f32[4864]{0:T(1024)S(1)}, u32[]{:S(2)}, u32[]{:S(2)}) collective-permute-start(f32[4864]{0:T(1024)S(1)} %pad_maximum_fusion.16), channel_id=1, source_target_pairs={{16,0},{32,16},{48,32},{64,48},{80,64},{96,80},{112,96},{128,112},... | collective-permute-start | bytes 58376 | tf_op jit(solution)/shard_map/ppermute | solution.py:294
  7.0 1.9 %collective-permute-start = (f32[4864]{0:T(1024)S(1)}, f32[4864]{0:T(1024)S(1)}, u32[]{:S(2)}, u32[]{:S(2)}) collective-permute-start(f32[4864]{0:T(1024)S(1)} %pad_maximum_fusion.15), channel_id=1, source_target_pairs={{0,16},{16,32},{32,48},{48,64},{64,80},{80,96},{96,112},{112,128},... | collective-permute-start | bytes 58376 | tf_op jit(solution)/shard_map/ppermute | solution.py:294
  9.1 4.2 %collective-permute-done = f32[4864]{0:T(1024)S(1)} collective-permute-done((f32[4864]{0:T(1024)S(1)}, f32[4864]{0:T(1024)S(1)}, u32[]{:S(2)}, u32[]{:S(2)}) %collective-permute-start) | collective-permute-done | bytes 19488 | tf_op jit(solution)/shard_map/ppermute | solution.py:294
  14.3 2.6 %collective-permute-start.3 = (f32[1712]{0:T(1024)S(1)}, f32[1712]{0:T(1024)S(1)}, u32[]{:S(2)}, u32[]{:S(2)}) collective-permute-start(f32[1712]{0:T(1024)S(1)} %concatenate.71), channel_id=1, source_target_pairs={{4,0},{8,4},{12,8},{5,1},{9,5},{13,9},{6,2},{10,6},{14,10},{7,3},{... | collective-permute-start | bytes 20552 | tf_op jit(solution)/shard_map/ppermute | solution.py:294
  17.2 1.3 %collective-permute-start.2 = (f32[1712]{0:T(1024)S(1)}, f32[1712]{0:T(1024)S(1)}, u32[]{:S(2)}, u32[]{:S(2)}) collective-permute-start(f32[1712]{0:T(1024)S(1)} %concatenate.70), channel_id=1, source_target_pairs={{0,4},{4,8},{8,12},{1,5},{5,9},{9,13},{2,6},{6,10},{10,14},{3,7},{... | collective-permute-start | bytes 20552 | tf_op jit(solution)/shard_map/ppermute | solution.py:294
  18.5 0.3 fusion.18
  19.1 3.6 %collective-permute-done.2 = f32[1712]{0:T(1024)S(1)} collective-permute-done((f32[1712]{0:T(1024)S(1)}, f32[1712]{0:T(1024)S(1)}, u32[]{:S(2)}, u32[]{:S(2)}) %collective-permute-start.2) | collective-permute-done | bytes 6880 | tf_op jit(solution)/shard_map/ppermute | solution.py:294
  23.0 0.3 pad_maximum_fusion.2
  23.5 0.9 %pad_maximum_fusion.3 = f32[4,4,18,258]{3,1,2,0:T(4,128)} fusion(f32[1,4,18,258]{3,1,2,0:T(4,128)S(1)} %get-tuple-element.40, f32[1,4,18,258]{3,1,2,0:T(4,128)S(1)} %get-tuple-element.39, f32[1,4,18,258]{3,1,2,0:T(4,128)S(1)} %get-tuple-element.38, f32[1,4,18,258]{3,1,2,0:T(4,128)S(1)} %get-tuple-element.37), kind=kLoop, calls=%fused_computation.36 | loop fusion | flops 222912 | bytes 594432 | tf_op jit(solution)/shard_map/concatenate | solution.py:196
  24.4 4.8 %all-to-all-start = ((f32[4,4,18,258]{3,1,2,0:T(4,128)}), f32[4,4,18,258]{3,1,2,0:T(4,128)S(1)}, u32[]{:S(2)}, u32[]{:S(2)}) async-start(f32[4,4,18,258]{3,1,2,0:T(4,128)} %pad_maximum_fusion.3), calls=%async_computation | async-start | bytes 884736 | tf_op jit(solution)/shard_map/all_to_all | solution.py:196
  29.7 0.4 fusion.5
  30.1 1.9 %collective-permute-start.5 = (f32[768]{0:T(1024)S(1)}, f32[768]{0:T(1024)S(1)}, u32[]{:S(2)}, u32[]{:S(2)}) collective-permute-start(f32[768]{0:T(1024)S(1)} %reshape.597), channel_id=1, source_target_pairs={{16,0},{32,16},{48,32},{64,48},{80,64},{96,80},{112,96},{128,112},... | collective-permute-start | bytes 9224 | tf_op jit(solution)/shard_map/ppermute | solution.py:294
  32.1 2.4 %collective-permute-start.4 = (f32[768]{0:T(1024)S(1)}, f32[768]{0:T(1024)S(1)}, u32[]{:S(2)}, u32[]{:S(2)}) collective-permute-start(f32[768]{0:T(1024)S(1)} %reshape.595), channel_id=1, source_target_pairs={{0,16},{16,32},{32,48},{48,64},{64,80},{80,96},{96,112},{112,128},... | collective-permute-start | bytes 9224 | tf_op jit(solution)/shard_map/ppermute | solution.py:294
  35.2 3.0 %collective-permute-done.4 = f32[768]{0:T(1024)S(1)} collective-permute-done((f32[768]{0:T(1024)S(1)}, f32[768]{0:T(1024)S(1)}, u32[]{:S(2)}, u32[]{:S(2)}) %collective-permute-start.4) | collective-permute-done | bytes 3104 | tf_op jit(solution)/shard_map/ppermute | solution.py:294
  38.5 2.4 %collective-permute-start.7 = (f32[54]{0:T(128)S(1)}, f32[54]{0:T(128)S(1)}, u32[]{:S(2)}, u32[]{:S(2)}) collective-permute-start(f32[54]{0:T(128)S(1)} %reshape.601), channel_id=1, source_target_pairs={{4,0},{8,4},{12,8},{5,1},{9,5},{13,9},{6,2},{10,6},{14,10},{7,3},{... | collective-permute-start | bytes 656 | tf_op jit(solution)/shard_map/ppermute | solution.py:294
  40.9 1.3 %collective-permute-start.6 = (f32[54]{0:T(128)S(1)}, f32[54]{0:T(128)S(1)}, u32[]{:S(2)}, u32[]{:S(2)}) collective-permute-start(f32[54]{0:T(128)S(1)} %reshape.599), channel_id=1, source_target_pairs={{0,4},{4,8},{8,12},{1,5},{5,9},{9,13},{2,6},{6,10},{10,14},{3,7},{... | collective-permute-start | bytes 656 | tf_op jit(solution)/shard_map/ppermute | solution.py:294
  42.6 3.7 %collective-permute-done.6 = f32[54]{0:T(128)S(1)} collective-permute-done((f32[54]{0:T(128)S(1)}, f32[54]{0:T(128)S(1)}, u32[]{:S(2)}, u32[]{:S(2)}) %collective-permute-start.6) | collective-permute-done | bytes 248 | tf_op jit(solution)/shard_map/ppermute | solution.py:294
  47.1 0.9 %pad.4.fld_ref = f32[21,24,384]{2,1,0:T(8,128)} pad(f32[21,18,258]{2,1,0:T(8,128)S(1)} %fusion.19, f32[]{:T(128)} %constant.67.clone.1), padding=0_0x0_6x0_126 | pad | bytes 1164244 | tf_op jit(solution)/shard_map/jit(_pad)/pad | solution.py:118
  48.0 7.8 %shard_map.122 = (f32[3,3,16,256]{3,2,1,0:T(8,128)}, f32[2,16,256]{2,1,0:T(8,128)}) custom-call(f32[21,24,384]{2,1,0:T(8,128)} %pad.4.fld_ref, f32[18,18]{1,0:T(8,128)} %kmat_ref.3, f32[3,3,16,256]{3,2,1,0:T(8,128)} %body_ref.3), custom_call_target="tpu_custom_call" | custom-call | tf_op jit(solution)/shard_map/pallas_call | solution.py:133
  55.8 1.3 %fusion.14 = f32[2,1152]{1,0:T(2,128)S(1)} fusion(f32[2,16,256]{2,1,0:T(8,128)} %get-tuple-element.6, s32[1152]{0:T(1024)S(1)} %get-tuple-element.54, pred[16,1152]{1,0:T(8,128)(4,1)S(1)} %convert_compare_fusion.1), kind=kOutput, calls=%fused_computation.12 | convolution fusion | flops 56989440 | bytes 65024 | tf_op jit(solution)/shard_map/krc,sc->krs/dot_general | solution.py:170
  57.1 0.6 broadcast_in_dim.102
  57.7 4.8 %all-to-all-start.1 = ((f32[4,2,9,128]{3,1,2,0:T(2,128)}), f32[4,2,9,128]{3,1,2,0:T(2,128)S(1)}, u32[]{:S(2)}, u32[]{:S(2)}) async-start(f32[4,2,9,128]{3,1,2,0:T(2,128)} %broadcast_in_dim.102), calls=%async_computation.1 | async-start | bytes 73728 | tf_op jit(solution)/shard_map/all_to_all | solution.py:182
  62.7 5.3 %shard_map.123 = f32[3,3,16,256]{3,2,1,0:T(8,128)} custom-call(f32[21,24,384]{2,1,0:T(8,128)} %pad.4.fld_ref, f32[18,18]{1,0:T(8,128)} %kmat_ref.3, f32[3,3,16,256]{3,2,1,0:T(8,128)} %body_ref.3, f32[3,3,16,256]{3,2,1,0:T(8,128)} %get-tuple-element.7.prev_ref), custom_call_target="tpu_custom_call" | custom-call | tf_op jit(solution)/shard_map/pallas_call | solution.py:148
  68.1 1.9 %collective-permute-start.9 = (f32[768]{0:T(1024)S(1)}, f32[768]{0:T(1024)S(1)}, u32[]{:S(2)}, u32[]{:S(2)}) collective-permute-start(f32[768]{0:T(1024)S(1)} %reshape.610), channel_id=1, source_target_pairs={{16,0},{32,16},{48,32},{64,48},{80,64},{96,80},{112,96},{128,112},... | collective-permute-start | bytes 9224 | tf_op jit(solution)/shard_map/ppermute | solution.py:294
  70.1 2.4 %collective-permute-start.8 = (f32[768]{0:T(1024)S(1)}, f32[768]{0:T(1024)S(1)}, u32[]{:S(2)}, u32[]{:S(2)}) collective-permute-start(f32[768]{0:T(1024)S(1)} %reshape.608), channel_id=1, source_target_pairs={{0,16},{16,32},{32,48},{48,64},{64,80},{80,96},{96,112},{112,128},... | collective-permute-start | bytes 9224 | tf_op jit(solution)/shard_map/ppermute | solution.py:294
  72.7 3.5 %collective-permute-done.8 = f32[768]{0:T(1024)S(1)} collective-permute-done((f32[768]{0:T(1024)S(1)}, f32[768]{0:T(1024)S(1)}, u32[]{:S(2)}, u32[]{:S(2)}) %collective-permute-start.8) | collective-permute-done | bytes 3104 | tf_op jit(solution)/shard_map/ppermute | solution.py:294
  76.2 2.4 %collective-permute-start.11 = (f32[1280]{0:T(1024)S(1)}, f32[1280]{0:T(1024)S(1)}, u32[]{:S(2)}, u32[]{:S(2)}) collective-permute-start(f32[1280]{0:T(1024)S(1)} %reshape.614), channel_id=1, source_target_pairs={{4,0},{8,4},{12,8},{5,1},{9,5},{13,9},{6,2},{10,6},{14,10},{7,3},{... | collective-permute-start | bytes 15368 | tf_op jit(solution)/shard_map/ppermute | solution.py:294
  78.6 1.3 %collective-permute-start.10 = (f32[1280]{0:T(1024)S(1)}, f32[1280]{0:T(1024)S(1)}, u32[]{:S(2)}, u32[]{:S(2)}) collective-permute-start(f32[1280]{0:T(1024)S(1)} %reshape.612), channel_id=1, source_target_pairs={{0,4},{4,8},{8,12},{1,5},{5,9},{9,13},{2,6},{6,10},{10,14},{3,7},{... | collective-permute-start | bytes 15368 | tf_op jit(solution)/shard_map/ppermute | solution.py:294
  80.1 4.0 %collective-permute-done.10 = f32[1280]{0:T(1024)S(1)} collective-permute-done((f32[1280]{0:T(1024)S(1)}, f32[1280]{0:T(1024)S(1)}, u32[]{:S(2)}, u32[]{:S(2)}) %collective-permute-start.10) | collective-permute-done | bytes 5152 | tf_op jit(solution)/shard_map/ppermute | solution.py:294
  84.2 1.1 %fusion.11 = f32[2,64,256]{2,1,0:T(8,128)} fusion(s32[1152]{0:T(1024)S(1)} %get-tuple-element.56, f32[2,1152]{1,0:T(2,128)S(1)} %bitcast.150, f32[1152,64]{0,1:T(8,128)S(1)} %fusion.36, f32[1,64,256]{2,1,0:T(8,128)S(1)} %fusion.44, f32[1,64,256]{2,1,0:T(8,128)S(1)} %fusion.50), kind=kOutput, calls=%fused_computation.11 | convolution fusion | flops 227000320 | bytes 570880 | tf_op jit(solution)/shard_map/ksr,sc->krc/dot_general | solution.py:176
  (132 shorter events, 5.5 us)
Async XLA Ops:
  0.6 2.6 %copy-start.1 = (f32[2,64,256]{2,1,0:T(8,128)S(1)}, f32[2,64,256]{2,1,0:T(8,128)}, u32[]{:S(2)}) copy-start(f32[2,64,256]{2,1,0:T(8,128)} %param.11) | copy-start | bytes 393220
  0.6 2.5 %copy-start.6 = (s32[16,256]{1,0:T(8,128)S(1)}, s32[16,256]{1,0:T(8,128)}, u32[]{:S(2)}) copy-start(s32[16,256]{1,0:T(8,128)} %param.18) | copy-start | bytes 49156
  0.7 2.5 %copy-start.2 = (f32[3,16,256]{2,1,0:T(8,128)S(1)}, f32[3,16,256]{2,1,0:T(8,128)}, u32[]{:S(2)}) copy-start(f32[3,16,256]{2,1,0:T(8,128)} %param.16) | copy-start | bytes 147460
  0.7 2.5 %copy-start = (f32[3,3,16,256]{3,2,1,0:T(8,128)S(1)}, f32[3,3,16,256]{3,2,1,0:T(8,128)}, u32[]{:S(2)}) copy-start(f32[3,3,16,256]{3,2,1,0:T(8,128)} %param.15) | copy-start | bytes 442372
  0.7 2.6 %copy-start.3 = (f32[64,256]{1,0:T(8,128)S(1)}, f32[64,256]{1,0:T(8,128)}, u32[]{:S(2)}) copy-start(f32[64,256]{1,0:T(8,128)} %param.12) | copy-start | bytes 196612
  1.6 7.4 %copy-start.7 = (s32[1,9,128]{2,0,1:T(1,128)S(1)}, s32[1,9,128]{2,0,1:T(1,128)}, u32[]{:S(2)}) copy-start(s32[1,9,128]{2,0,1:T(1,128)} %param.20) | copy-start | bytes 13828
  3.3 5.7 %collective-permute-start.1 = (f32[4864]{0:T(1024)S(1)}, f32[4864]{0:T(1024)S(1)}, u32[]{:S(2)}, u32[]{:S(2)}) collective-permute-start(f32[4864]{0:T(1024)S(1)} %pad_maximum_fusion.16), channel_id=1, source_target_pairs={{16,0},{32,16},{48,32},{64,48},{80,64},{96,80},{112,96},{128,112},... | collective-permute-start | bytes 58376 | tf_op jit(solution)/shard_map/ppermute | solution.py:294
  7.0 6.3 %collective-permute-start = (f32[4864]{0:T(1024)S(1)}, f32[4864]{0:T(1024)S(1)}, u32[]{:S(2)}, u32[]{:S(2)}) collective-permute-start(f32[4864]{0:T(1024)S(1)} %pad_maximum_fusion.15), channel_id=1, source_target_pairs={{0,16},{16,32},{32,48},{48,64},{64,80},{80,96},{96,112},{112,128},... | collective-permute-start | bytes 58376 | tf_op jit(solution)/shard_map/ppermute | solution.py:294
  14.3 4.5 %collective-permute-start.3 = (f32[1712]{0:T(1024)S(1)}, f32[1712]{0:T(1024)S(1)}, u32[]{:S(2)}, u32[]{:S(2)}) collective-permute-start(f32[1712]{0:T(1024)S(1)} %concatenate.71), channel_id=1, source_target_pairs={{4,0},{8,4},{12,8},{5,1},{9,5},{13,9},{6,2},{10,6},{14,10},{7,3},{... | collective-permute-start | bytes 20552 | tf_op jit(solution)/shard_map/ppermute | solution.py:294
  17.2 5.5 %collective-permute-start.2 = (f32[1712]{0:T(1024)S(1)}, f32[1712]{0:T(1024)S(1)}, u32[]{:S(2)}, u32[]{:S(2)}) collective-permute-start(f32[1712]{0:T(1024)S(1)} %concatenate.70), channel_id=1, source_target_pairs={{0,4},{4,8},{8,12},{1,5},{5,9},{9,13},{2,6},{6,10},{10,14},{3,7},{... | collective-permute-start | bytes 20552 | tf_op jit(solution)/shard_map/ppermute | solution.py:294
  24.4 22.3 %all-to-all-start = ((f32[4,4,18,258]{3,1,2,0:T(4,128)}), f32[4,4,18,258]{3,1,2,0:T(4,128)S(1)}, u32[]{:S(2)}, u32[]{:S(2)}) async-start(f32[4,4,18,258]{3,1,2,0:T(4,128)} %pad_maximum_fusion.3), calls=%async_computation | async-start | bytes 884736 | tf_op jit(solution)/shard_map/all_to_all | solution.py:196
  30.1 5.0 %collective-permute-start.5 = (f32[768]{0:T(1024)S(1)}, f32[768]{0:T(1024)S(1)}, u32[]{:S(2)}, u32[]{:S(2)}) collective-permute-start(f32[768]{0:T(1024)S(1)} %reshape.597), channel_id=1, source_target_pairs={{16,0},{32,16},{48,32},{64,48},{80,64},{96,80},{112,96},{128,112},... | collective-permute-start | bytes 9224 | tf_op jit(solution)/shard_map/ppermute | solution.py:294
  32.1 6.1 %collective-permute-start.4 = (f32[768]{0:T(1024)S(1)}, f32[768]{0:T(1024)S(1)}, u32[]{:S(2)}, u32[]{:S(2)}) collective-permute-start(f32[768]{0:T(1024)S(1)} %reshape.595), channel_id=1, source_target_pairs={{0,16},{16,32},{32,48},{48,64},{64,80},{80,96},{96,112},{112,128},... | collective-permute-start | bytes 9224 | tf_op jit(solution)/shard_map/ppermute | solution.py:294
  38.5 4.0 %collective-permute-start.7 = (f32[54]{0:T(128)S(1)}, f32[54]{0:T(128)S(1)}, u32[]{:S(2)}, u32[]{:S(2)}) collective-permute-start(f32[54]{0:T(128)S(1)} %reshape.601), channel_id=1, source_target_pairs={{4,0},{8,4},{12,8},{5,1},{9,5},{13,9},{6,2},{10,6},{14,10},{7,3},{... | collective-permute-start | bytes 656 | tf_op jit(solution)/shard_map/ppermute | solution.py:294
  40.9 5.4 %collective-permute-start.6 = (f32[54]{0:T(128)S(1)}, f32[54]{0:T(128)S(1)}, u32[]{:S(2)}, u32[]{:S(2)}) collective-permute-start(f32[54]{0:T(128)S(1)} %reshape.599), channel_id=1, source_target_pairs={{0,4},{4,8},{8,12},{1,5},{5,9},{9,13},{2,6},{6,10},{10,14},{3,7},{... | collective-permute-start | bytes 656 | tf_op jit(solution)/shard_map/ppermute | solution.py:294
  57.7 10.3 %all-to-all-start.1 = ((f32[4,2,9,128]{3,1,2,0:T(2,128)}), f32[4,2,9,128]{3,1,2,0:T(2,128)S(1)}, u32[]{:S(2)}, u32[]{:S(2)}) async-start(f32[4,2,9,128]{3,1,2,0:T(2,128)} %broadcast_in_dim.102), calls=%async_computation.1 | async-start | bytes 73728 | tf_op jit(solution)/shard_map/all_to_all | solution.py:182
  62.7 9.8 %copy-start.4 = (f32[64,256]{1,0:T(8,128)S(1)}, f32[64,256]{1,0:T(8,128)}, u32[]{:S(2)}) copy-start(f32[64,256]{1,0:T(8,128)} %param.13) | copy-start | bytes 196612
  62.7 9.8 %copy-start.5 = (f32[2,64,256]{2,1,0:T(8,128)S(1)}, f32[2,64,256]{2,1,0:T(8,128)}, u32[]{:S(2)}) copy-start(f32[2,64,256]{2,1,0:T(8,128)} %param.14) | copy-start | bytes 393220
  68.1 4.6 %collective-permute-start.9 = (f32[768]{0:T(1024)S(1)}, f32[768]{0:T(1024)S(1)}, u32[]{:S(2)}, u32[]{:S(2)}) collective-permute-start(f32[768]{0:T(1024)S(1)} %reshape.610), channel_id=1, source_target_pairs={{16,0},{32,16},{48,32},{64,48},{80,64},{96,80},{112,96},{128,112},... | collective-permute-start | bytes 9224 | tf_op jit(solution)/shard_map/ppermute | solution.py:294
  70.1 6.1 %collective-permute-start.8 = (f32[768]{0:T(1024)S(1)}, f32[768]{0:T(1024)S(1)}, u32[]{:S(2)}, u32[]{:S(2)}) collective-permute-start(f32[768]{0:T(1024)S(1)} %reshape.608), channel_id=1, source_target_pairs={{0,16},{16,32},{32,48},{48,64},{64,80},{80,96},{96,112},{112,128},... | collective-permute-start | bytes 9224 | tf_op jit(solution)/shard_map/ppermute | solution.py:294
  76.2 3.9 %collective-permute-start.11 = (f32[1280]{0:T(1024)S(1)}, f32[1280]{0:T(1024)S(1)}, u32[]{:S(2)}, u32[]{:S(2)}) collective-permute-start(f32[1280]{0:T(1024)S(1)} %reshape.614), channel_id=1, source_target_pairs={{4,0},{8,4},{12,8},{5,1},{9,5},{13,9},{6,2},{10,6},{14,10},{7,3},{... | collective-permute-start | bytes 15368 | tf_op jit(solution)/shard_map/ppermute | solution.py:294
  78.6 5.5 %collective-permute-start.10 = (f32[1280]{0:T(1024)S(1)}, f32[1280]{0:T(1024)S(1)}, u32[]{:S(2)}, u32[]{:S(2)}) collective-permute-start(f32[1280]{0:T(1024)S(1)} %reshape.612), channel_id=1, source_target_pairs={{0,4},{4,8},{8,12},{1,5},{5,9},{9,13},{2,6},{6,10},{10,14},{3,7},{... | collective-permute-start | bytes 15368 | tf_op jit(solution)/shard_map/ppermute | solution.py:294
